TPU v7x, 512 devices: a whole 4x8x8 slice. The times are simulated.
512 devices in a mesh: gx: 32 (over z, y_hi, core), gy: 16 (over x, y_lo).
Axes of the slice: x: 4, y: 8 (y_hi: 2, y_lo: 4; y = y_hi * 4 + y_lo), z: 8, core: 2. Of those that a mesh axis runs over, the one named last changes fastest.
Arguments:
- design: float32 [256, 128, 128], P('gx', 'gy'), may hold values from 0.06 to 0.9
- passive: int32 [256, 128, 128], P('gx', 'gy'), may hold values 0 or 1
- basis_pairs: float32 [4, 2, 3, 256, 128, 128], P(None, None, None, 'gx', 'gy'), may hold values from -6 to 6
- supports: int32 [256, 128, 128], P('gx', 'gy'), may hold values 0 or 1
- stiffness: float32 [24, 24], replicated, may hold values from -1.25 to 1.25
- mass_matrix: float32 [24, 24], replicated, may hold values from -1.25 to 1.25
- volume_fraction: float32 [64], replicated, may hold values from 0.26 to 0.36
Outputs:
- sensitivity: float32 [256, 128, 128], P('gx', 'gy')
- design_next: float32 [256, 128, 128], P('gx', 'gy')
All inputs are finite; a program needn't handle non-finite values. No bound on the sum of `passive` or of `supports` on one device may be relied on, other than what follows from the above.
Results may differ from a plain program's by a relative error of at most 0.0003.
Values sent between devices are 32-bit elements; how exact they have to be, the bound alone decides.
No kernel may reach another device: no remote copies, remote signals or barrier semaphores. Data moves between devices by JAX's collectives and lax.ppermute only.
A program may use at most 64 MiB of HBM per device.

v0:
```python
import math

import jax
import jax.numpy as jnp
from jax import lax
from jax.sharding import PartitionSpec as P

BISECT = 6
REGIONS = 64


PENALTY_SCALE = 3.0 * (1.0 - 0.001)
OMEGA_SQUARED = 0.5
MOVE_LIMIT = 0.2


def with_halo(cells, sides, width):
    for axis, dim in sides:
        count = lax.axis_size(axis)
        ends = count - 1
        head = lax.slice_in_dim(cells, 0, width, axis=dim)
        tail = lax.slice_in_dim(cells, cells.shape[dim] - width, cells.shape[dim], axis=dim)
        cells = jnp.concatenate(
            [
                lax.ppermute(tail, axis, [(i, (i + 1) % count) for i in range(ends)]),
                cells,
                lax.ppermute(head, axis, [((i + 1) % count, i) for i in range(ends)]),
            ],
            axis=dim,
        )
    return cells


def from_behind(value, axis, steps):
    count = lax.axis_size(axis)
    initial, last = (max(0, -steps), min(count, count - steps))
    return lax.ppermute(value, axis, [(source, source + steps) for source in range(initial, last)])


def filter_taps():
    tap_list = []
    for offset_x in range(-2, 3):
        for offset_y in range(-2, 3):
            for offset_z in range(-2, 3):
                weight = 3.0 - math.sqrt(
                    offset_x * offset_x + offset_y * offset_y + offset_z * offset_z
                )
                if weight > 0.0:
                    tap_list.append((offset_x, offset_y, offset_z, weight))
    return tap_list


def stencil(padded, block_shape):
    result = jnp.zeros(block_shape, jnp.float32)
    for offset_x, offset_y, offset_z, weight in filter_taps():
        result = (
            result
            + weight
            * padded[
                2 + offset_x : 2 + offset_x + block_shape[0],
                2 + offset_y : 2 + offset_y + block_shape[1],
                2 + offset_z : 2 + offset_z + block_shape[2],
            ]
        )
    return result


def element_terms(extended, stiffness, mass_matrix):
    pair_count = extended.shape[0]
    cells_x = extended.shape[3] - 1
    cells_y = extended.shape[4] - 1
    cells_z = extended.shape[5] - 1
    stiff_energy = jnp.zeros((cells_x * cells_y * cells_z,), jnp.float32)
    mass_energy = jnp.zeros((cells_x * cells_y * cells_z,), jnp.float32)
    for pair_index in range(pair_count):
        vectors = []
        for member in range(2):
            row_list = []
            for corner_x in (0, 1):
                for corner_y in (0, 1):
                    for corner_z in (0, 1):
                        for component in range(3):
                            row_list.append(
                                extended[
                                    pair_index,
                                    member,
                                    component,
                                    corner_x : corner_x + cells_x,
                                    corner_y : corner_y + cells_y,
                                    corner_z : corner_z + cells_z,
                                ].reshape(-1)
                            )
            vectors.append(jnp.stack(row_list))
        state_rows, adjoint_rows = vectors
        stiff_energy = stiff_energy + jnp.sum(
            state_rows * jnp.dot(stiffness, adjoint_rows, precision=lax.Precision.HIGHEST), axis=0
        )
        mass_energy = mass_energy + jnp.sum(
            state_rows * jnp.dot(mass_matrix, adjoint_rows, precision=lax.Precision.HIGHEST), axis=0
        )
    return (
        stiff_energy.reshape(cells_x, cells_y, cells_z),
        mass_energy.reshape(cells_x, cells_y, cells_z),
    )


def shards(design, passive, basis_pairs, supports, stiffness, mass_matrix, volume_fraction):
    block_shape = design.shape
    size_x, size_y, size_z = block_shape
    devices_x = lax.axis_size("gx")
    devices_y = lax.axis_size("gy")
    index_x = lax.axis_index("gx")
    index_y = lax.axis_index("gy")
    grid_x = size_x * devices_x
    grid_y = size_y * devices_y
    spread_x = jnp.arange(size_x + 4, dtype=jnp.int32) + index_x * size_x - 2
    spread_y = jnp.arange(size_y + 4, dtype=jnp.int32) + index_y * size_y - 2
    valid_x = ((spread_x >= 0) & (spread_x < grid_x)).astype(jnp.float32)
    valid_y = ((spread_y >= 0) & (spread_y < grid_y)).astype(jnp.float32)
    valid_z = jnp.pad(jnp.ones((size_z,), jnp.float32), 2)
    inside = valid_x[:, None, None] * valid_y[None, :, None] * valid_z[None, None, :]
    weight_sum = stencil(inside, block_shape)
    design_wide = with_halo(design, (("gx", 0), ("gy", 1)), 2)
    design_wide = jnp.pad(design_wide, ((0, 0), (0, 0), (2, 2)))
    physical = jnp.where(passive == 1, 1.0, stencil(design_wide, block_shape) / weight_sum)
    fields = basis_pairs * (1 - supports).astype(jnp.float32)
    rim_first = from_behind(fields[:, :, :, :1], "gx", -1)
    widened = jnp.concatenate([fields, rim_first], axis=3)
    rim_second = from_behind(widened[:, :, :, :, :1], "gy", -1)
    extended = jnp.concatenate([widened, rim_second], axis=4)
    extended = jnp.pad(extended, ((0, 0), (0, 0), (0, 0), (0, 0), (0, 0), (0, 1)))
    stiff_energy, mass_energy = element_terms(extended, stiffness, mass_matrix)
    raw_sensitivity = -(
        PENALTY_SCALE * physical * physical * stiff_energy - OMEGA_SQUARED * mass_energy
    )
    raw_sensitivity = jnp.where(passive == 1, 0.0, raw_sensitivity)
    scaled_wide = with_halo(raw_sensitivity / weight_sum, (("gx", 0), ("gy", 1)), 2)
    scaled_wide = jnp.pad(scaled_wide, ((0, 0), (0, 0), (2, 2)))
    sensitivity = stencil(scaled_wide, block_shape)
    benefit = jnp.maximum(-sensitivity, 0.0)
    floor_value = jnp.maximum(design - MOVE_LIMIT, 0.0)
    ceiling = jnp.minimum(design + MOVE_LIMIT, 1.0)
    band_cells = size_z // REGIONS
    target = volume_fraction * float(grid_x * grid_y * band_cells)

    def candidate(multiplier):
        per_cell = jnp.repeat(multiplier, band_cells)[None, None, :]
        trial = design * jnp.sqrt(benefit / per_cell)
        return jnp.where(passive == 1, 1.0, jnp.minimum(ceiling, jnp.maximum(floor_value, trial)))

    def region_sum(field):
        return jnp.sum(field, axis=(0, 1)).reshape(REGIONS, band_cells).sum(axis=1)

    levels = 1

    def bisect_round(round_index, bracket):
        low_end, high_end = bracket
        level_nodes = [(low_end, high_end)]
        midpoints = []
        next_nodes = []
        for node_low, node_high in level_nodes:
            middle = jnp.sqrt(node_low * node_high)
            midpoints.append(middle)
            next_nodes.append((node_low, middle))
            next_nodes.append((middle, node_high))
        partial_volumes = jnp.stack([region_sum(candidate(middle)) for middle in midpoints])
        volumes = lax.psum(partial_volumes, ("gx", "gy"))
        position = jnp.zeros((REGIONS,), jnp.int32)
        middle = jnp.sqrt(low_end * high_end)
        heap_index = position + (2**0 - 1)
        chosen = jnp.take_along_axis(volumes, heap_index[None, :], axis=0)[0]
        heavier = chosen > target
        low_end = jnp.where(heavier, middle, low_end)
        high_end = jnp.where(heavier, high_end, middle)
        return (low_end, high_end)

    start = (jnp.full((REGIONS,), 0.0001, jnp.float32), jnp.full((REGIONS,), 10000.0, jnp.float32))
    low_end, high_end = lax.fori_loop(0, BISECT // levels, bisect_round, start)
    design_next = candidate(jnp.sqrt(low_end * high_end))
    return (sensitivity, design_next)


def solution(mesh):
    placed = (
        P("gx", "gy", None),
        P("gx", "gy", None),
        P(None, None, None, "gx", "gy", None),
        P("gx", "gy", None),
        P(),
        P(),
        P(),
    )
    return jax.shard_map(
        shards,
        mesh=mesh,
        in_specs=placed,
        out_specs=(P("gx", "gy", None), P("gx", "gy", None)),
        check_vma=False,
    )
```

profile of v0, /device:TPU:6, one launch (start us, length us, event | category | flops | bytes accessed | tf_op | source)
XLA Modules:
  0.0 709.5 jit_solution(10859632898439551738)
XLA Ops:
  1.4 1.3 collective-permute-start.1
  2.7 3.0 collective-permute-start
  7.7 1.3 collective-permute-start.4
  10.0 3.5 collective-permute-start.2
  13.5 5.1 collective-permute-start.3
  18.7 1.3 collective-permute-done.3
  20.7 6.9 collective-permute-start.5
  36.8 3.7 stack.27
  40.5 5.8 stack.28
  46.4 2.7 fusion.12
  49.0 1.5 fusion.8
  50.5 3.7 stack.34
  54.2 5.8 stack.33
  60.0 2.7 fusion.15
  62.7 1.5 fusion.11
  66.2 3.6 stack.30
  70.0 3.6 stack.29
  75.7 3.4 stack.32
  79.2 3.4 stack.31
  85.7 5.7 collective-permute-start.6
  91.4 1.3 collective-permute-start.7
  92.7 9.6 %collective-permute-done.7 = f32[2,8,128]{2,1,0:T(8,128)S(1)} collective-permute-done((f32[2,8,128]{2,1,0:T(8,128)S(1)}, f32[2,8,128]{2,1,0:T(8,128)S(1)}, u32[]{:S(2)}, u32[]{:S(2)}) %collective-permute-start.7) | collective-permute-done | bytes 8224 | tf_op jit(solution)/shard_map/ppermute | solution.py:27
  102.3 1.9 collective-permute-start.8
  104.3 7.1 collective-permute-start.9
  111.4 1.3 collective-permute-done.9
  113.5 595.1 %while.13 = (s32[]{:T(128)}, f32[64]{0:T(128)S(1)}, f32[64]{0:T(128)S(1)}, s32[8,8,128]{2,1,0:T(8,128)S(1)}, f32[8,8,128]{2,1,0:T(8,128)S(1)}, /*index=5*/f32[8,...) while((s32[]{:T(128)}, f32[64]{0:T(128)S(1)}, ...), condition=%wide.region_12.13_spmd.clone, body=%wide.region_8.12_spmd.clone.sunk | while | flops 57923 | bytes 172676 | solution.py:178
  114.1 112.8 %psum.9 = f32[1,64]{1,0:T(1,128)S(1)} all-reduce(f32[1,64]{1,0:T(1,128)S(1)} %bitcast.455), channel_id=1, replica_groups=mesh['gx'=32,'gy'=16] {'gx','gy'}, use_global_device_ids=true, to_apply=%region_11.11 | all-reduce | flops 64 | bytes 512 | tf_op jit(solution)/shard_map/while/body/eval_jaxpr/psum | solution.py:167
  228.2 94.7 %psum.9 = f32[1,64]{1,0:T(1,128)S(1)} all-reduce(f32[1,64]{1,0:T(1,128)S(1)} %bitcast.455), channel_id=1, replica_groups=mesh['gx'=32,'gy'=16] {'gx','gy'}, use_global_device_ids=true, to_apply=%region_11.11 | all-reduce | flops 64 | bytes 512 | tf_op jit(solution)/shard_map/while/body/eval_jaxpr/psum | solution.py:167
  324.3 95.0 %psum.9 = f32[1,64]{1,0:T(1,128)S(1)} all-reduce(f32[1,64]{1,0:T(1,128)S(1)} %bitcast.455), channel_id=1, replica_groups=mesh['gx'=32,'gy'=16] {'gx','gy'}, use_global_device_ids=true, to_apply=%region_11.11 | all-reduce | flops 64 | bytes 512 | tf_op jit(solution)/shard_map/while/body/eval_jaxpr/psum | solution.py:167
  420.7 94.7 %psum.9 = f32[1,64]{1,0:T(1,128)S(1)} all-reduce(f32[1,64]{1,0:T(1,128)S(1)} %bitcast.455), channel_id=1, replica_groups=mesh['gx'=32,'gy'=16] {'gx','gy'}, use_global_device_ids=true, to_apply=%region_11.11 | all-reduce | flops 64 | bytes 512 | tf_op jit(solution)/shard_map/while/body/eval_jaxpr/psum | solution.py:167
  516.7 95.0 %psum.9 = f32[1,64]{1,0:T(1,128)S(1)} all-reduce(f32[1,64]{1,0:T(1,128)S(1)} %bitcast.455), channel_id=1, replica_groups=mesh['gx'=32,'gy'=16] {'gx','gy'}, use_global_device_ids=true, to_apply=%region_11.11 | all-reduce | flops 64 | bytes 512 | tf_op jit(solution)/shard_map/while/body/eval_jaxpr/psum | solution.py:167
  613.1 94.7 %psum.9 = f32[1,64]{1,0:T(1,128)S(1)} all-reduce(f32[1,64]{1,0:T(1,128)S(1)} %bitcast.455), channel_id=1, replica_groups=mesh['gx'=32,'gy'=16] {'gx','gy'}, use_global_device_ids=true, to_apply=%region_11.11 | all-reduce | flops 64 | bytes 512 | tf_op jit(solution)/shard_map/while/body/eval_jaxpr/psum | solution.py:167
  (224 shorter events, 29.7 us)
Async XLA Ops:
  0.6 45.7 %copy-start = (f32[24,24]{1,0:T(8,128)S(1)}, f32[24,24]{1,0:T(8,128)}, u32[]{:S(2)}) copy-start(f32[24,24]{1,0:T(8,128)} %param.14) | copy-start | bytes 6916
  0.6 9.3 %copy-start.3 = (f32[8,8,128]{2,1,0:T(8,128)S(1)}, f32[8,8,128]{2,1,0:T(8,128)}, u32[]{:S(2)}) copy-start(f32[8,8,128]{2,1,0:T(8,128)} %param.9) | copy-start | bytes 98308
  1.4 8.6 %collective-permute-start.1 = (f32[2,8,128]{2,1,0:T(8,128)S(1)}, f32[2,8,128]{2,1,0:T(8,128)S(1)}, u32[]{:S(2)}, u32[]{:S(2)}) collective-permute-start(f32[2,8,128]{2,1,0:T(8,128)S(1)} %get-tuple-element.311), channel_id=1, source_target_pairs={{16,0},{32,16},{48,32},{64,48},{80,64},{96,80},{112,96},{128,112},... | collective-permute-start | bytes 24584 | tf_op jit(solution)/shard_map/ppermute | solution.py:27
  2.7 7.3 %collective-permute-start = (f32[2,8,128]{2,1,0:T(8,128)S(1)}, f32[2,8,128]{2,1,0:T(8,128)S(1)}, u32[]{:S(2)}, u32[]{:S(2)}) collective-permute-start(f32[2,8,128]{2,1,0:T(8,128)S(1)} %get-tuple-element.312), channel_id=1, source_target_pairs={{0,16},{16,32},{32,48},{48,64},{64,80},{80,96},{96,112},{112,128},... | collective-permute-start | bytes 24584 | tf_op jit(solution)/shard_map/ppermute | solution.py:25
  7.7 12.4 %collective-permute-start.4 = (f32[4,2,3,1,8,128]{5,4,3,2,1,0:T(8,128)S(1)}, f32[4,2,3,1,8,128]{5,4,3,2,1,0:T(8,128)S(1)}, u32[]{:S(2)}, u32[]{:S(2)}) collective-permute-start(f32[4,2,3,1,8,128]{5,4,3,2,1,0:T(8,128)S(1)} %slice.2402), channel_id=1, source_target_pairs={{16,0},{32,16},{48,32},{64,48},{80,64},{96,80},{112,96},{128,112},... | collective-permute-start | bytes 294920 | tf_op jit(solution)/shard_map/ppermute | solution.py:37
  10.0 8.7 %collective-permute-start.2 = (f32[12,2,128]{2,1,0:T(2,128)S(1)}, f32[12,2,128]{2,1,0:T(2,128)S(1)}, u32[]{:S(2)}, u32[]{:S(2)}) collective-permute-start(f32[12,2,128]{2,1,0:T(2,128)S(1)} %get-tuple-element.302), channel_id=1, source_target_pairs={{0,1},{1,2},{2,3},{3,4},{4,5},{5,6},{6,7},{7,8},{8,9},{9,10},{10,1... | collective-permute-start | bytes 36872 | tf_op jit(solution)/shard_map/ppermute | solution.py:25
  13.5 6.4 collective-permute-start.3
  20.7 10.1 %collective-permute-start.5 = (f32[4,2,3,9,1,128]{5,3,4,2,1,0:T(8,128)S(1)}, f32[4,2,3,9,1,128]{5,3,4,2,1,0:T(8,128)S(1)}, u32[]{:S(2)}, u32[]{:S(2)}) collective-permute-start(f32[4,2,3,9,1,128]{5,3,4,2,1,0:T(8,128)S(1)} %copy.107), channel_id=1, source_target_pairs={{1,0},{2,1},{3,2},{4,3},{5,4},{6,5},{7,6},{8,7},{9,8},{10,9},{11,1... | collective-permute-start | bytes 331784 | tf_op jit(solution)/shard_map/ppermute | solution.py:37
  40.5 8.5 %copy-start.5 = (f32[24,24]{1,0:T(8,128)S(1)}, f32[24,24]{1,0:T(8,128)}, u32[]{:S(2)}) copy-start(f32[24,24]{1,0:T(8,128)} %param.13) | copy-start | bytes 6916
  65.1 4.7 copy-start.13
  65.1 4.8 copy-start.14
  65.1 4.8 copy-start.15
  65.1 4.8 copy-start.16
  65.1 4.8 copy-start.17
  65.1 4.8 copy-start.18
  65.1 4.8 copy-start.19
  65.1 4.8 copy-start.20
  65.1 4.8 copy-start.21
  65.1 4.8 copy-start.22
  65.2 4.8 copy-start.23
  74.6 4.5 copy-start.34
  74.6 4.5 copy-start.35
  74.6 4.5 copy-start.36
  74.6 4.5 copy-start.40
  74.6 4.5 copy-start.41
  74.6 4.5 copy-start.42
  84.4 26.9 %copy-start.57 = (f32[64]{0:T(128)S(1)}, f32[64]{0:T(128)}, u32[]{:S(2)}) copy-start(f32[64]{0:T(128)} %param.15) | copy-start | bytes 772
  85.7 7.0 collective-permute-start.6
  91.4 10.9 %collective-permute-start.7 = (f32[2,8,128]{2,1,0:T(8,128)S(1)}, f32[2,8,128]{2,1,0:T(8,128)S(1)}, u32[]{:S(2)}, u32[]{:S(2)}) collective-permute-start(f32[2,8,128]{2,1,0:T(8,128)S(1)} %get-tuple-element.310), channel_id=1, source_target_pairs={{16,0},{32,16},{48,32},{64,48},{80,64},{96,80},{112,96},{128,112},... | collective-permute-start | bytes 24584 | tf_op jit(solution)/shard_map/ppermute | solution.py:27
  102.3 9.1 %collective-permute-start.8 = (f32[12,2,128]{2,1,0:T(2,128)S(1)}, f32[12,2,128]{2,1,0:T(2,128)S(1)}, u32[]{:S(2)}, u32[]{:S(2)}) collective-permute-start(f32[12,2,128]{2,1,0:T(2,128)S(1)} %get-tuple-element.300), channel_id=1, source_target_pairs={{0,1},{1,2},{2,3},{3,4},{4,5},{5,6},{6,7},{7,8},{8,9},{9,10},{10,1... | collective-permute-start | bytes 36872 | tf_op jit(solution)/shard_map/ppermute | solution.py:25
  104.3 8.5 %collective-permute-start.9 = (f32[12,2,128]{2,1,0:T(2,128)S(1)}, f32[12,2,128]{2,1,0:T(2,128)S(1)}, u32[]{:S(2)}, u32[]{:S(2)}) collective-permute-start(f32[12,2,128]{2,1,0:T(2,128)S(1)} %get-tuple-element.301), channel_id=1, source_target_pairs={{1,0},{2,1},{3,2},{4,3},{5,4},{6,5},{7,6},{8,7},{9,8},{10,9},{11,1... | collective-permute-start | bytes 36872 | tf_op jit(solution)/shard_map/ppermute | solution.py:27
  113.5 595.3 %copy-start.33 = (f32[8,8,128]{2,1,0:T(8,128)}, f32[8,8,128]{2,1,0:T(8,128)S(1)}, u32[]{:S(2)}) copy-start(f32[8,8,128]{2,1,0:T(8,128)S(1)} %get-tuple-element.101) | copy-start | bytes 98308
  (36 other events, 82.4 us)
where the time goes:
time: 714 us; the launch traced here: 709 us
  blocking collectives  587 us (82%)
  local copies, waits for them, and re-layouts  50.1 us (7%)
  starting transfers between devices  37 us (5%)
  waiting for transfers between devices  13.1 us (2%)
  matrix products  11.6 us (2%)
  other arithmetic  8.48 us (1%)
    psum x6, blocking collectives, bisect_round(): volumes = lax.psum(partial_volumes, ('gx', 'gy'))  587 us
    another operation x8, local copies, waits for them, and re-layouts, element_terms(): vectors.append(jnp.stack(row_list))  33.2 us
    ppermute x4, starting transfers between devices, with_halo(): lax.ppermute(head, axis, [((i + 1) % count, i) for i in range(ends)])  14.7 us
  transfers between devices with their start and end apart: 10, of which 4 were waited for; matrix products, arithmetic and copies ran while one was open for 1% of the time, Pallas kernels for 0%

commit v1 on v0

--- a/solution.py
+++ b/solution.py
@@ -151,31 +151,43 @@
     def region_sum(field):
         return jnp.sum(field, axis=(0, 1)).reshape(REGIONS, band_cells).sum(axis=1)
 
-    levels = 1
+    levels = BISECT
 
     def bisect_round(round_index, bracket):
         low_end, high_end = bracket
         level_nodes = [(low_end, high_end)]
         midpoints = []
-        next_nodes = []
-        for node_low, node_high in level_nodes:
-            middle = jnp.sqrt(node_low * node_high)
-            midpoints.append(middle)
-            next_nodes.append((node_low, middle))
-            next_nodes.append((middle, node_high))
-        partial_volumes = jnp.stack([region_sum(candidate(middle)) for middle in midpoints])
+        for depth in range(levels):
+            next_nodes = []
+            for node_low, node_high in level_nodes:
+                middle = jnp.sqrt(node_low * node_high)
+                midpoints.append(middle)
+                next_nodes.append((node_low, middle))
+                next_nodes.append((middle, node_high))
+            level_nodes = next_nodes
+        trial_multipliers = jnp.stack(midpoints)
+        per_cell = jnp.repeat(trial_multipliers, band_cells, axis=1)[:, None, None, :]
+        trial = design[None] * jnp.sqrt(benefit[None] / per_cell)
+        fields_of = jnp.where(
+            passive[None] == 1, 1.0, jnp.minimum(ceiling[None], jnp.maximum(floor_value[None], trial))
+        )
+        partial_volumes = (
+            jnp.sum(fields_of, axis=(1, 2)).reshape(len(midpoints), REGIONS, band_cells).sum(axis=2)
+        )
         volumes = lax.psum(partial_volumes, ("gx", "gy"))
         position = jnp.zeros((REGIONS,), jnp.int32)
-        middle = jnp.sqrt(low_end * high_end)
-        heap_index = position + (2**0 - 1)
-        chosen = jnp.take_along_axis(volumes, heap_index[None, :], axis=0)[0]
-        heavier = chosen > target
-        low_end = jnp.where(heavier, middle, low_end)
-        high_end = jnp.where(heavier, high_end, middle)
+        for depth in range(levels):
+            middle = jnp.sqrt(low_end * high_end)
+            heap_index = position + (2**depth - 1)
+            chosen = jnp.take_along_axis(volumes, heap_index[None, :], axis=0)[0]
+            heavier = chosen > target
+            low_end = jnp.where(heavier, middle, low_end)
+            high_end = jnp.where(heavier, high_end, middle)
+            position = 2 * position + heavier.astype(jnp.int32)
         return (low_end, high_end)
 
     start = (jnp.full((REGIONS,), 0.0001, jnp.float32), jnp.full((REGIONS,), 10000.0, jnp.float32))
-    low_end, high_end = lax.fori_loop(0, BISECT // levels, bisect_round, start)
+    low_end, high_end = bisect_round(0, start)
     design_next = candidate(jnp.sqrt(low_end * high_end))
     return (sensitivity, design_next)
 

time: 714 us -> 236 us (0.33)
  blocking collectives: 587 us -> 113 us
    psum x6 -> x1, blocking collectives: 587 us -> 113 us  [bisect_round(): volumes = lax.psum(partial_volumes, ('gx', 'gy'))]
  transfers between devices with their start and end apart: 10 -> 10, of which waited for: 4 -> 4; matrix products, arithmetic and copies ran while one was open for 1% -> 3% of each run, Pallas kernels for 0% -> 0%
where the time goes in v1:
time: 236 us; the launch traced here: 232 us
  blocking collectives  113 us (48%)
  local copies, waits for them, and re-layouts  46.5 us (20%)
  starting transfers between devices  37 us (16%)
  waiting for transfers between devices  12.6 us (5%)
  matrix products  11.7 us (5%)
  other arithmetic  9.3 us (4%)
    psum x1, blocking collectives, bisect_round(): volumes = lax.psum(partial_volumes, ('gx', 'gy'))  113 us
    another operation x8, local copies, waits for them, and re-layouts, element_terms(): vectors.append(jnp.stack(row_list))  31 us
    ppermute x4, starting transfers between devices, with_halo(): lax.ppermute(head, axis, [((i + 1) % count, i) for i in range(ends)])  14.7 us
    ppermute x4, starting transfers between devices, with_halo(): lax.ppermute(tail, axis, [(i, (i + 1) % count) for i in range(ends)])  14.1 us
    ppermute x4, waiting for transfers between devices, with_halo(): lax.ppermute(head, axis, [((i + 1) % count, i) for i in range(ends)])  11.7 us
    slice x9, local copies, waits for them, and re-layouts, element_terms(): extended[pair_index, member, component, corner_x:corner_x + cells_x, corn...  8.41 us
    ppermute x2, starting transfers between devices, from_behind(): lax.ppermute(value, axis, [(source, source + steps) for source in range(i...  8.19 us
    dot_general x4, matrix products, element_terms(): jnp.dot(mass_matrix, adjoint_rows, precision=lax.Precision.HIGHEST)  7.02 us
  transfers between devices with their start and end apart: 10, of which 4 were waited for; matrix products, arithmetic and copies ran while one was open for 3% of the time, Pallas kernels for 0%

profile of v1, /device:TPU:6, one launch (start us, length us, event | category | flops | bytes accessed | tf_op | source)
XLA Modules:
  0.0 232.1 jit_solution(4660837941216454200)
XLA Ops:
  1.4 1.3 collective-permute-start.1
  2.7 3.0 %collective-permute-start = (f32[2,8,128]{2,1,0:T(8,128)S(1)}, f32[2,8,128]{2,1,0:T(8,128)S(1)}, u32[]{:S(2)}, u32[]{:S(2)}) collective-permute-start(f32[2,8,128]{2,1,0:T(8,128)S(1)} %get-tuple-element.215), channel_id=1, source_target_pairs={{0,16},{16,32},{32,48},{48,64},{64,80},{80,96},{96,112},{112,128},... | collective-permute-start | bytes 24584 | tf_op jit(solution)/shard_map/ppermute | solution.py:25
  6.5 1.2 broadcast_multiply_fusion
  7.7 1.3 collective-permute-start.4
  10.8 3.5 %collective-permute-start.2 = (f32[12,2,128]{2,1,0:T(2,128)S(1)}, f32[12,2,128]{2,1,0:T(2,128)S(1)}, u32[]{:S(2)}, u32[]{:S(2)}) collective-permute-start(f32[12,2,128]{2,1,0:T(2,128)S(1)} %get-tuple-element.205), channel_id=1, source_target_pairs={{0,1},{1,2},{2,3},{3,4},{4,5},{5,6},{6,7},{7,8},{8,9},{9,10},{10,1... | collective-permute-start | bytes 36872 | tf_op jit(solution)/shard_map/ppermute | solution.py:25
  14.3 5.1 %collective-permute-start.3 = (f32[12,2,128]{2,1,0:T(2,128)S(1)}, f32[12,2,128]{2,1,0:T(2,128)S(1)}, u32[]{:S(2)}, u32[]{:S(2)}) collective-permute-start(f32[12,2,128]{2,1,0:T(2,128)S(1)} %get-tuple-element.206), channel_id=1, source_target_pairs={{1,0},{2,1},{3,2},{4,3},{5,4},{6,5},{7,6},{8,7},{9,8},{10,9},{11,1... | collective-permute-start | bytes 36872 | tf_op jit(solution)/shard_map/ppermute | solution.py:27
  21.0 6.9 %collective-permute-start.5 = (f32[4,2,3,9,1,128]{5,3,4,2,1,0:T(8,128)S(1)}, f32[4,2,3,9,1,128]{5,3,4,2,1,0:T(8,128)S(1)}, u32[]{:S(2)}, u32[]{:S(2)}) collective-permute-start(f32[4,2,3,9,1,128]{5,3,4,2,1,0:T(8,128)S(1)} %copy.114), channel_id=1, source_target_pairs={{1,0},{2,1},{3,2},{4,3},{5,4},{6,5},{7,6},{8,7},{9,8},{10,9},{11,1... | collective-permute-start | bytes 331784 | tf_op jit(solution)/shard_map/ppermute | solution.py:37
  32.2 1.0 pad_slice_fusion.79
  33.2 1.1 pad_slice_fusion.48
  35.1 1.1 fusion.373
  37.2 3.7 %stack.24 = f32[24,8192]{1,0:T(8,128)S(1)} concatenate(f32[1,8192]{1,0:T(1,128)} %bitcast.576, f32[1,8192]{1,0:T(1,128)} %bitcast.575, f32[1,8192]{1,0:T(1,128)} %bitcast.574, f32[1,8192]{1,0:T(1,128)} %bitcast.624, f32[1,8192]{1,0:T(1,128)} %bitcast.497, f32[1,8192]{1,0:T(1,128)} %bitcast.498, f32[1,8192]{1,0:T(1,128)} %bitcast.623, f32[1,8192]{1,0:T(1,128)} %bitcast.622, ...), dimensions={0} | concatenate | bytes 1572864 | tf_op jit(solution)/shard_map/stack | solution.py:93
  40.9 5.8 %stack.25 = f32[24,8192]{1,0:T(8,128)} concatenate(f32[1,8192]{1,0:T(1,128)} %bitcast.571, f32[1,8192]{1,0:T(1,128)} %bitcast.570, f32[1,8192]{1,0:T(1,128)} %bitcast.588, f32[1,8192]{1,0:T(1,128)} %bitcast.468, f32[1,8192]{1,0:T(1,128)} %bitcast.469, f32[1,8192]{1,0:T(1,128)} %bitcast.470, f32[1,8192]{1,0:T(1,128)} %bitcast.617, f32[1,8192]{1,0:T(1,128)} %bitcast.616, ...), dimensions={0} | concatenate | bytes 1572864 | tf_op jit(solution)/shard_map/stack | solution.py:93
  46.7 2.7 %fusion.17 = f32[8192]{0:T(1024)} fusion(f32[24,8192]{1,0:T(8,128)S(1)} %stack.24, f32[24,8192]{1,0:T(8,128)} %stack.25, f32[24,24]{1,0:T(8,128)S(1)} %copy-done), kind=kOutput, calls=%fused_computation.153 | convolution fusion | flops 57008128 | bytes 1607936 | tf_op jit(solution)/shard_map/dot_general | solution.py:99
  49.4 1.5 fusion.13
  50.9 3.7 %stack.31 = f32[24,8192]{1,0:T(8,128)S(1)} concatenate(f32[1,8192]{1,0:T(1,128)} %bitcast.564, f32[1,8192]{1,0:T(1,128)} %bitcast.584, f32[1,8192]{1,0:T(1,128)} %bitcast.580, f32[1,8192]{1,0:T(1,128)} %bitcast.514, f32[1,8192]{1,0:T(1,128)} %bitcast.515, f32[1,8192]{1,0:T(1,128)} %bitcast.516, f32[1,8192]{1,0:T(1,128)} %bitcast.531, f32[1,8192]{1,0:T(1,128)} %bitcast.530, ...), dimensions={0} | concatenate | bytes 1572864 | tf_op jit(solution)/shard_map/stack | solution.py:93
  54.6 5.8 %stack.30 = f32[24,8192]{1,0:T(8,128)} concatenate(f32[1,8192]{1,0:T(1,128)} %bitcast.558, f32[1,8192]{1,0:T(1,128)} %bitcast.557, f32[1,8192]{1,0:T(1,128)} %bitcast.556, f32[1,8192]{1,0:T(1,128)} %bitcast.466, f32[1,8192]{1,0:T(1,128)} %bitcast.479, f32[1,8192]{1,0:T(1,128)} %bitcast.480, f32[1,8192]{1,0:T(1,128)} %bitcast.513, f32[1,8192]{1,0:T(1,128)} %bitcast.512, ...), dimensions={0} | concatenate | bytes 1572864 | tf_op jit(solution)/shard_map/stack | solution.py:93
  60.4 2.7 %fusion.20 = f32[8192]{0:T(1024)} fusion(f32[24,8192]{1,0:T(8,128)} %stack.30, f32[24,8192]{1,0:T(8,128)S(1)} %stack.31, f32[24,24]{1,0:T(8,128)S(1)} %copy-done), kind=kOutput, calls=%fused_computation.156 | convolution fusion | flops 57008128 | bytes 1607936 | tf_op jit(solution)/shard_map/dot_general | solution.py:99
  63.1 1.5 fusion.16
  65.5 1.0 pad_slice_fusion.49
  66.6 3.7 %stack.27 = f32[24,8192]{1,0:T(8,128)S(1)} concatenate(f32[1,8192]{1,0:T(1,128)} %bitcast.569, f32[1,8192]{1,0:T(1,128)} %bitcast.568, f32[1,8192]{1,0:T(1,128)} %bitcast.567, f32[1,8192]{1,0:T(1,128)} %bitcast.534, f32[1,8192]{1,0:T(1,128)} %bitcast.535, f32[1,8192]{1,0:T(1,128)} %bitcast.536, f32[1,8192]{1,0:T(1,128)} %bitcast.610, f32[1,8192]{1,0:T(1,128)} %bitcast.609, ...), dimensions={0} | concatenate | bytes 1572864 | tf_op jit(solution)/shard_map/stack | solution.py:93
  70.4 3.6 %stack.26 = f32[24,8192]{1,0:T(8,128)S(1)} concatenate(f32[1,8192]{1,0:T(1,128)S(1)} %bitcast.563, f32[1,8192]{1,0:T(1,128)S(1)} %bitcast.562, f32[1,8192]{1,0:T(1,128)S(1)} %bitcast.561, f32[1,8192]{1,0:T(1,128)S(1)} %bitcast.450, f32[1,8192]{1,0:T(1,128)S(1)} %bitcast.451, f32[1,8192]{1,0:T(1,128)S(1)} %bitcast.452, f32[1,8192]{1,0:T(1,128)} %bitcast.611, f32[1,8192]{1,0:T(1,128)} %bitcast.607, ...), dimensions={0} | concatenate | bytes 1572864 | tf_op jit(solution)/shard_map/stack | solution.py:93
  76.1 3.4 %stack.29 = f32[24,8192]{1,0:T(8,128)S(1)} concatenate(f32[1,8192]{1,0:T(1,128)S(1)} %bitcast.549, f32[1,8192]{1,0:T(1,128)S(1)} %bitcast.548, f32[1,8192]{1,0:T(1,128)S(1)} %bitcast.547, f32[1,8192]{1,0:T(1,128)S(1)} %bitcast.438, f32[1,8192]{1,0:T(1,128)S(1)} %bitcast.439, f32[1,8192]{1,0:T(1,128)S(1)} %bitcast.440, f32[1,8192]{1,0:T(1,128)} %bitcast.602, f32[1,8192]{1,0:T(1,128)} %bitcast.601, ...), dimensions={0} | concatenate | bytes 1572864 | tf_op jit(solution)/shard_map/stack | solution.py:93
  79.6 1.2 stack.28
  82.6 1.2 fusion.98
  83.9 5.7 %collective-permute-start.6 = (f32[2,8,128]{2,1,0:T(8,128)S(1)}, f32[2,8,128]{2,1,0:T(8,128)S(1)}, u32[]{:S(2)}, u32[]{:S(2)}) collective-permute-start(f32[2,8,128]{2,1,0:T(8,128)S(1)} %get-tuple-element.212), channel_id=1, source_target_pairs={{0,16},{16,32},{32,48},{48,64},{64,80},{80,96},{96,112},{112,128},... | collective-permute-start | bytes 24584 | tf_op jit(solution)/shard_map/ppermute | solution.py:25
  89.6 1.3 collective-permute-start.7
  90.9 9.6 %collective-permute-done.7 = f32[2,8,128]{2,1,0:T(8,128)S(1)} collective-permute-done((f32[2,8,128]{2,1,0:T(8,128)S(1)}, f32[2,8,128]{2,1,0:T(8,128)S(1)}, u32[]{:S(2)}, u32[]{:S(2)}) %collective-permute-start.7) | collective-permute-done | bytes 8224 | tf_op jit(solution)/shard_map/ppermute | solution.py:27
  100.5 1.9 collective-permute-start.8
  102.5 7.1 %collective-permute-start.9 = (f32[12,2,128]{2,1,0:T(2,128)S(1)}, f32[12,2,128]{2,1,0:T(2,128)S(1)}, u32[]{:S(2)}, u32[]{:S(2)}) collective-permute-start(f32[12,2,128]{2,1,0:T(2,128)S(1)} %get-tuple-element.204), channel_id=1, source_target_pairs={{1,0},{2,1},{3,2},{4,3},{5,4},{6,5},{7,6},{8,7},{9,8},{10,9},{11,1... | collective-permute-start | bytes 36872 | tf_op jit(solution)/shard_map/ppermute | solution.py:27
  109.7 1.2 collective-permute-done.9
  111.7 0.9 fusion.12
  113.0 113.2 %psum.7 = f32[63,64]{1,0:T(8,128)S(1)} all-reduce(f32[63,64]{1,0:T(8,128)S(1)} %copy.118), channel_id=1, replica_groups=mesh['gx'=32,'gy'=16] {'gx','gy'}, use_global_device_ids=true, to_apply=%region_10.11 | all-reduce | flops 4032 | bytes 32256 | tf_op jit(solution)/shard_map/psum | solution.py:177
  (198 shorter events, 22.6 us)
Async XLA Ops:
  0.6 46.1 %copy-start = (f32[24,24]{1,0:T(8,128)S(1)}, f32[24,24]{1,0:T(8,128)}, u32[]{:S(2)}) copy-start(f32[24,24]{1,0:T(8,128)} %param.14) | copy-start | bytes 6916
  0.6 9.5 %copy-start.3 = (f32[8,8,128]{2,1,0:T(8,128)S(1)}, f32[8,8,128]{2,1,0:T(8,128)}, u32[]{:S(2)}) copy-start(f32[8,8,128]{2,1,0:T(8,128)} %param.9) | copy-start | bytes 98308
  1.4 9.3 %collective-permute-start.1 = (f32[2,8,128]{2,1,0:T(8,128)S(1)}, f32[2,8,128]{2,1,0:T(8,128)S(1)}, u32[]{:S(2)}, u32[]{:S(2)}) collective-permute-start(f32[2,8,128]{2,1,0:T(8,128)S(1)} %get-tuple-element.214), channel_id=1, source_target_pairs={{16,0},{32,16},{48,32},{64,48},{80,64},{96,80},{112,96},{128,112},... | collective-permute-start | bytes 24584 | tf_op jit(solution)/shard_map/ppermute | solution.py:27
  2.7 7.4 %collective-permute-start = (f32[2,8,128]{2,1,0:T(8,128)S(1)}, f32[2,8,128]{2,1,0:T(8,128)S(1)}, u32[]{:S(2)}, u32[]{:S(2)}) collective-permute-start(f32[2,8,128]{2,1,0:T(8,128)S(1)} %get-tuple-element.215), channel_id=1, source_target_pairs={{0,16},{16,32},{32,48},{48,64},{64,80},{80,96},{96,112},{112,128},... | collective-permute-start | bytes 24584 | tf_op jit(solution)/shard_map/ppermute | solution.py:25
  7.7 13.2 %collective-permute-start.4 = (f32[4,2,3,1,8,128]{5,4,3,2,1,0:T(8,128)S(1)}, f32[4,2,3,1,8,128]{5,4,3,2,1,0:T(8,128)S(1)}, u32[]{:S(2)}, u32[]{:S(2)}) collective-permute-start(f32[4,2,3,1,8,128]{5,4,3,2,1,0:T(8,128)S(1)} %slice.2424), channel_id=1, source_target_pairs={{16,0},{32,16},{48,32},{64,48},{80,64},{96,80},{112,96},{128,112},... | collective-permute-start | bytes 294920 | tf_op jit(solution)/shard_map/ppermute | solution.py:37
  10.8 9.1 %collective-permute-start.2 = (f32[12,2,128]{2,1,0:T(2,128)S(1)}, f32[12,2,128]{2,1,0:T(2,128)S(1)}, u32[]{:S(2)}, u32[]{:S(2)}) collective-permute-start(f32[12,2,128]{2,1,0:T(2,128)S(1)} %get-tuple-element.205), channel_id=1, source_target_pairs={{0,1},{1,2},{2,3},{3,4},{4,5},{5,6},{6,7},{7,8},{8,9},{9,10},{10,1... | collective-permute-start | bytes 36872 | tf_op jit(solution)/shard_map/ppermute | solution.py:25
  14.3 6.4 %collective-permute-start.3 = (f32[12,2,128]{2,1,0:T(2,128)S(1)}, f32[12,2,128]{2,1,0:T(2,128)S(1)}, u32[]{:S(2)}, u32[]{:S(2)}) collective-permute-start(f32[12,2,128]{2,1,0:T(2,128)S(1)} %get-tuple-element.206), channel_id=1, source_target_pairs={{1,0},{2,1},{3,2},{4,3},{5,4},{6,5},{7,6},{8,7},{9,8},{10,9},{11,1... | collective-permute-start | bytes 36872 | tf_op jit(solution)/shard_map/ppermute | solution.py:27
  21.0 10.1 %collective-permute-start.5 = (f32[4,2,3,9,1,128]{5,3,4,2,1,0:T(8,128)S(1)}, f32[4,2,3,9,1,128]{5,3,4,2,1,0:T(8,128)S(1)}, u32[]{:S(2)}, u32[]{:S(2)}) collective-permute-start(f32[4,2,3,9,1,128]{5,3,4,2,1,0:T(8,128)S(1)} %copy.114), channel_id=1, source_target_pairs={{1,0},{2,1},{3,2},{4,3},{5,4},{6,5},{7,6},{8,7},{9,8},{10,9},{11,1... | collective-permute-start | bytes 331784 | tf_op jit(solution)/shard_map/ppermute | solution.py:37
  40.9 8.5 %copy-start.4 = (f32[24,24]{1,0:T(8,128)S(1)}, f32[24,24]{1,0:T(8,128)}, u32[]{:S(2)}) copy-start(f32[24,24]{1,0:T(8,128)} %param.13) | copy-start | bytes 6916
  65.4 4.8 %copy-start.10 = (f32[1,1,1,8,8,128]{5,4,3,2,1,0:T(8,128)S(1)}, f32[1,1,1,8,8,128]{5,4,3,2,1,0:T(8,128)}, u32[]{:S(2)}) copy-start(f32[1,1,1,8,8,128]{5,4,3,2,1,0:T(8,128)} %get-tuple-element.17) | copy-start | bytes 98308
  65.4 4.8 %copy-start.11 = (f32[1,1,1,8,8,128]{5,4,3,2,1,0:T(8,128)S(1)}, f32[1,1,1,8,8,128]{5,4,3,2,1,0:T(8,128)}, u32[]{:S(2)}) copy-start(f32[1,1,1,8,8,128]{5,4,3,2,1,0:T(8,128)} %get-tuple-element.18) | copy-start | bytes 98308
  65.4 4.8 %copy-start.12 = (f32[1,1,1,8,8,128]{5,4,3,2,1,0:T(8,128)S(1)}, f32[1,1,1,8,8,128]{5,4,3,2,1,0:T(8,128)}, u32[]{:S(2)}) copy-start(f32[1,1,1,8,8,128]{5,4,3,2,1,0:T(8,128)} %get-tuple-element.19) | copy-start | bytes 98308
  65.5 4.8 %copy-start.13 = (f32[1,1,1,8,8,128]{5,4,3,2,1,0:T(8,128)S(1)}, f32[1,1,1,8,8,128]{5,4,3,2,1,0:T(8,128)}, u32[]{:S(2)}) copy-start(f32[1,1,1,8,8,128]{5,4,3,2,1,0:T(8,128)} %get-tuple-element.20) | copy-start | bytes 98308
  65.5 4.8 %copy-start.14 = (f32[1,1,1,8,8,128]{5,4,3,2,1,0:T(8,128)S(1)}, f32[1,1,1,8,8,128]{5,4,3,2,1,0:T(8,128)}, u32[]{:S(2)}) copy-start(f32[1,1,1,8,8,128]{5,4,3,2,1,0:T(8,128)} %get-tuple-element.21) | copy-start | bytes 98308
  65.5 4.8 %copy-start.15 = (f32[1,1,1,8,8,128]{5,4,3,2,1,0:T(8,128)S(1)}, f32[1,1,1,8,8,128]{5,4,3,2,1,0:T(8,128)}, u32[]{:S(2)}) copy-start(f32[1,1,1,8,8,128]{5,4,3,2,1,0:T(8,128)} %get-tuple-element.22) | copy-start | bytes 98308
  65.5 4.8 %copy-start.16 = (f32[1,1,1,8,8,128]{5,4,3,2,1,0:T(8,128)S(1)}, f32[1,1,1,8,8,128]{5,4,3,2,1,0:T(8,128)}, u32[]{:S(2)}) copy-start(f32[1,1,1,8,8,128]{5,4,3,2,1,0:T(8,128)} %get-tuple-element.23) | copy-start | bytes 98308
  65.5 4.8 %copy-start.17 = (f32[1,1,1,8,8,128]{5,4,3,2,1,0:T(8,128)S(1)}, f32[1,1,1,8,8,128]{5,4,3,2,1,0:T(8,128)}, u32[]{:S(2)}) copy-start(f32[1,1,1,8,8,128]{5,4,3,2,1,0:T(8,128)} %get-tuple-element.24) | copy-start | bytes 98308
  65.5 4.8 %copy-start.18 = (f32[1,1,1,8,8,128]{5,4,3,2,1,0:T(8,128)S(1)}, f32[1,1,1,8,8,128]{5,4,3,2,1,0:T(8,128)}, u32[]{:S(2)}) copy-start(f32[1,1,1,8,8,128]{5,4,3,2,1,0:T(8,128)} %get-tuple-element.25) | copy-start | bytes 98308
  65.5 4.8 %copy-start.19 = (f32[1,1,1,8,8,128]{5,4,3,2,1,0:T(8,128)S(1)}, f32[1,1,1,8,8,128]{5,4,3,2,1,0:T(8,128)}, u32[]{:S(2)}) copy-start(f32[1,1,1,8,8,128]{5,4,3,2,1,0:T(8,128)} %get-tuple-element.26) | copy-start | bytes 98308
  65.5 4.8 %copy-start.20 = (f32[1,1,1,8,8,128]{5,4,3,2,1,0:T(8,128)S(1)}, f32[1,1,1,8,8,128]{5,4,3,2,1,0:T(8,128)}, u32[]{:S(2)}) copy-start(f32[1,1,1,8,8,128]{5,4,3,2,1,0:T(8,128)} %get-tuple-element.27) | copy-start | bytes 98308
  75.0 4.5 %copy-start.31 = (f32[1,1,1,8,8,128]{5,4,3,2,1,0:T(8,128)S(1)}, f32[1,1,1,8,8,128]{5,4,3,2,1,0:T(8,128)}, u32[]{:S(2)}) copy-start(f32[1,1,1,8,8,128]{5,4,3,2,1,0:T(8,128)} %get-tuple-element.194) | copy-start | bytes 98308
  75.0 4.5 %copy-start.32 = (f32[1,1,1,8,8,128]{5,4,3,2,1,0:T(8,128)S(1)}, f32[1,1,1,8,8,128]{5,4,3,2,1,0:T(8,128)}, u32[]{:S(2)}) copy-start(f32[1,1,1,8,8,128]{5,4,3,2,1,0:T(8,128)} %get-tuple-element.195) | copy-start | bytes 98308
  75.0 4.5 %copy-start.33 = (f32[1,1,1,8,8,128]{5,4,3,2,1,0:T(8,128)S(1)}, f32[1,1,1,8,8,128]{5,4,3,2,1,0:T(8,128)}, u32[]{:S(2)}) copy-start(f32[1,1,1,8,8,128]{5,4,3,2,1,0:T(8,128)} %get-tuple-element.196) | copy-start | bytes 98308
  75.0 4.5 %copy-start.37 = (f32[1,1,1,8,8,128]{5,4,3,2,1,0:T(8,128)S(1)}, f32[1,1,1,8,8,128]{5,4,3,2,1,0:T(8,128)}, u32[]{:S(2)}) copy-start(f32[1,1,1,8,8,128]{5,4,3,2,1,0:T(8,128)} %get-tuple-element.165) | copy-start | bytes 98308
  82.6 8.3 %copy-start.60 = (s32[1,64,1]{1,2,0:T(1,128)S(1)}, s32[1,64,1]{1,2,0:T(1,128)}, u32[]{:S(2)}) copy-start(s32[1,64,1]{1,2,0:T(1,128)} %broadcast_bitcast_fusion) | copy-start | bytes 772
  82.6 26.9 %copy-start.56 = (f32[63,64]{0,1:T(8,128)S(1)}, f32[63,64]{0,1:T(8,128)}, u32[]{:S(2)}) copy-start(f32[63,64]{0,1:T(8,128)} %constant.25.clone.1) | copy-start | bytes 48388
  83.9 7.0 %collective-permute-start.6 = (f32[2,8,128]{2,1,0:T(8,128)S(1)}, f32[2,8,128]{2,1,0:T(8,128)S(1)}, u32[]{:S(2)}, u32[]{:S(2)}) collective-permute-start(f32[2,8,128]{2,1,0:T(8,128)S(1)} %get-tuple-element.212), channel_id=1, source_target_pairs={{0,16},{16,32},{32,48},{48,64},{64,80},{80,96},{96,112},{112,128},... | collective-permute-start | bytes 24584 | tf_op jit(solution)/shard_map/ppermute | solution.py:25
  89.6 10.9 %collective-permute-start.7 = (f32[2,8,128]{2,1,0:T(8,128)S(1)}, f32[2,8,128]{2,1,0:T(8,128)S(1)}, u32[]{:S(2)}, u32[]{:S(2)}) collective-permute-start(f32[2,8,128]{2,1,0:T(8,128)S(1)} %get-tuple-element.213), channel_id=1, source_target_pairs={{16,0},{32,16},{48,32},{64,48},{80,64},{96,80},{112,96},{128,112},... | collective-permute-start | bytes 24584 | tf_op jit(solution)/shard_map/ppermute | solution.py:27
  100.5 9.2 %collective-permute-start.8 = (f32[12,2,128]{2,1,0:T(2,128)S(1)}, f32[12,2,128]{2,1,0:T(2,128)S(1)}, u32[]{:S(2)}, u32[]{:S(2)}) collective-permute-start(f32[12,2,128]{2,1,0:T(2,128)S(1)} %get-tuple-element.203), channel_id=1, source_target_pairs={{0,1},{1,2},{2,3},{3,4},{4,5},{5,6},{6,7},{7,8},{8,9},{9,10},{10,1... | collective-permute-start | bytes 36872 | tf_op jit(solution)/shard_map/ppermute | solution.py:25
  102.5 8.5 %collective-permute-start.9 = (f32[12,2,128]{2,1,0:T(2,128)S(1)}, f32[12,2,128]{2,1,0:T(2,128)S(1)}, u32[]{:S(2)}, u32[]{:S(2)}) collective-permute-start(f32[12,2,128]{2,1,0:T(2,128)S(1)} %get-tuple-element.204), channel_id=1, source_target_pairs={{1,0},{2,1},{3,2},{4,3},{5,4},{6,5},{7,6},{8,7},{9,8},{10,9},{11,1... | collective-permute-start | bytes 36872 | tf_op jit(solution)/shard_map/ppermute | solution.py:27
  111.1 115.8 %copy-start.59 = (f32[64]{0:T(128)S(1)}, f32[64]{0:T(128)}, u32[]{:S(2)}) copy-start(f32[64]{0:T(128)} %param.15) | copy-start | bytes 772
  111.7 119.8 %copy-start.30 = (f32[8,8,128]{2,1,0:T(8,128)}, f32[8,8,128]{2,1,0:T(8,128)S(1)}, u32[]{:S(2)}) copy-start(f32[8,8,128]{2,1,0:T(8,128)S(1)} %get-tuple-element.6) | copy-start | bytes 98308
  (39 other events, 106.4 us)

commit v2 on v1

--- a/solution.py
+++ b/solution.py
@@ -35,6 +35,15 @@
     count = lax.axis_size(axis)
     initial, last = (max(0, -steps), min(count, count - steps))
     return lax.ppermute(value, axis, [(source, source + steps) for source in range(initial, last)])
+
+
+def butterfly_sum(value, axis):
+    count = lax.axis_size(axis)
+    stride = 1
+    while stride < count:
+        value = value + lax.ppermute(value, axis, [(i, i ^ stride) for i in range(count)])
+        stride *= 2
+    return value
 
 
 def filter_taps():
@@ -174,7 +183,7 @@
         partial_volumes = (
             jnp.sum(fields_of, axis=(1, 2)).reshape(len(midpoints), REGIONS, band_cells).sum(axis=2)
         )
-        volumes = lax.psum(partial_volumes, ("gx", "gy"))
+        volumes = butterfly_sum(butterfly_sum(partial_volumes, "gy"), "gx")
         position = jnp.zeros((REGIONS,), jnp.int32)
         for depth in range(levels):
             middle = jnp.sqrt(low_end * high_end)

time: 236 us -> 195 us (0.83)
  blocking collectives: 113 us -> 0 us
  starting transfers between devices: 37 us -> 86.2 us
  waiting for transfers between devices: 12.6 us -> 36.4 us
    psum x1 -> x0, blocking collectives: 113 us -> none  [bisect_round(): volumes = lax.psum(partial_volumes, ('gx', 'gy'))]
    ppermute x0 -> x9, starting transfers between devices: none -> 49.1 us  [butterfly_sum(): lax.ppermute(value, axis, [(i, i ^ stride) for i in range(count)])]
    ppermute x0 -> x9, waiting for transfers between devices: none -> 23.3 us  [butterfly_sum(): lax.ppermute(value, axis, [(i, i ^ stride) for i in range(count)])]
  transfers between devices with their start and end apart: 10 -> 19, of which waited for: 4 -> 13; matrix products, arithmetic and copies ran while one was open for 3% -> 3% of each run, Pallas kernels for 0% -> 0%
where the time goes in v2:
time: 195 us; the launch traced here: 191 us
  starting transfers between devices  86.2 us (44%)
  local copies, waits for them, and re-layouts  45.7 us (23%)
  waiting for transfers between devices  36.4 us (19%)
  matrix products  11.7 us (6%)
  other arithmetic  9.28 us (5%)
  between operations  1.96 us (1%)
    ppermute x9, starting transfers between devices, butterfly_sum(): lax.ppermute(value, axis, [(i, i ^ stride) for i in range(count)])  49.1 us
    another operation x8, local copies, waits for them, and re-layouts, element_terms(): vectors.append(jnp.stack(row_list))  30.8 us
    ppermute x9, waiting for transfers between devices, butterfly_sum(): lax.ppermute(value, axis, [(i, i ^ stride) for i in range(count)])  23.3 us
    ppermute x4, starting transfers between devices, with_halo(): lax.ppermute(head, axis, [((i + 1) % count, i) for i in range(ends)])  14.7 us
    ppermute x4, starting transfers between devices, with_halo(): lax.ppermute(tail, axis, [(i, (i + 1) % count) for i in range(ends)])  14.1 us
    ppermute x4, waiting for transfers between devices, with_halo(): lax.ppermute(head, axis, [((i + 1) % count, i) for i in range(ends)])  12.1 us
    slice x9, local copies, waits for them, and re-layouts, element_terms(): extended[pair_index, member, component, corner_x:corner_x + cells_x, corn...  8.25 us
    ppermute x2, starting transfers between devices, from_behind(): lax.ppermute(value, axis, [(source, source + steps) for source in range(i...  8.19 us
  transfers between devices with their start and end apart: 19, of which 13 were waited for; matrix products, arithmetic and copies ran while one was open for 3% of the time, Pallas kernels for 0%

profile of v2, /device:TPU:6, one launch (start us, length us, event | category | flops | bytes accessed | tf_op | source)
XLA Modules:
  0.0 191.2 jit_solution(5509111839711941599)
XLA Ops:
  2.7 3.0 %collective-permute-start = (f32[2,8,128]{2,1,0:T(8,128)S(1)}, f32[2,8,128]{2,1,0:T(8,128)S(1)}, u32[]{:S(2)}, u32[]{:S(2)}) collective-permute-start(f32[2,8,128]{2,1,0:T(8,128)S(1)} %get-tuple-element.215), channel_id=1, source_target_pairs={{0,16},{16,32},{32,48},{48,64},{64,80},{80,96},{96,112},{112,128},... | collective-permute-start | bytes 24584 | tf_op jit(solution)/shard_map/ppermute | solution.py:25
  10.6 3.5 %collective-permute-start.2 = (f32[12,2,128]{2,1,0:T(2,128)S(1)}, f32[12,2,128]{2,1,0:T(2,128)S(1)}, u32[]{:S(2)}, u32[]{:S(2)}) collective-permute-start(f32[12,2,128]{2,1,0:T(2,128)S(1)} %get-tuple-element.205), channel_id=1, source_target_pairs={{0,1},{1,2},{2,3},{3,4},{4,5},{5,6},{6,7},{7,8},{8,9},{9,10},{10,1... | collective-permute-start | bytes 36872 | tf_op jit(solution)/shard_map/ppermute | solution.py:25
  14.1 5.1 %collective-permute-start.3 = (f32[12,2,128]{2,1,0:T(2,128)S(1)}, f32[12,2,128]{2,1,0:T(2,128)S(1)}, u32[]{:S(2)}, u32[]{:S(2)}) collective-permute-start(f32[12,2,128]{2,1,0:T(2,128)S(1)} %get-tuple-element.206), channel_id=1, source_target_pairs={{1,0},{2,1},{3,2},{4,3},{5,4},{6,5},{7,6},{8,7},{9,8},{10,9},{11,1... | collective-permute-start | bytes 36872 | tf_op jit(solution)/shard_map/ppermute | solution.py:27
  20.9 6.9 %collective-permute-start.5 = (f32[4,2,3,9,1,128]{5,3,4,2,1,0:T(8,128)S(1)}, f32[4,2,3,9,1,128]{5,3,4,2,1,0:T(8,128)S(1)}, u32[]{:S(2)}, u32[]{:S(2)}) collective-permute-start(f32[4,2,3,9,1,128]{5,3,4,2,1,0:T(8,128)S(1)} %copy.116), channel_id=1, source_target_pairs={{1,0},{2,1},{3,2},{4,3},{5,4},{6,5},{7,6},{8,7},{9,8},{10,9},{11,1... | collective-permute-start | bytes 331784 | tf_op jit(solution)/shard_map/ppermute | solution.py:37
  36.9 3.7 %stack.24 = f32[24,8192]{1,0:T(8,128)S(1)} concatenate(f32[1,8192]{1,0:T(1,128)} %bitcast.576, f32[1,8192]{1,0:T(1,128)} %bitcast.575, f32[1,8192]{1,0:T(1,128)} %bitcast.574, f32[1,8192]{1,0:T(1,128)} %bitcast.624, f32[1,8192]{1,0:T(1,128)} %bitcast.497, f32[1,8192]{1,0:T(1,128)} %bitcast.498, f32[1,8192]{1,0:T(1,128)} %bitcast.623, f32[1,8192]{1,0:T(1,128)} %bitcast.622, ...), dimensions={0} | concatenate | bytes 1572864 | tf_op jit(solution)/shard_map/stack | solution.py:102
  40.6 5.8 %stack.25 = f32[24,8192]{1,0:T(8,128)} concatenate(f32[1,8192]{1,0:T(1,128)} %bitcast.571, f32[1,8192]{1,0:T(1,128)} %bitcast.570, f32[1,8192]{1,0:T(1,128)} %bitcast.588, f32[1,8192]{1,0:T(1,128)} %bitcast.468, f32[1,8192]{1,0:T(1,128)} %bitcast.469, f32[1,8192]{1,0:T(1,128)} %bitcast.470, f32[1,8192]{1,0:T(1,128)} %bitcast.617, f32[1,8192]{1,0:T(1,128)} %bitcast.616, ...), dimensions={0} | concatenate | bytes 1572864 | tf_op jit(solution)/shard_map/stack | solution.py:102
  46.4 2.7 %fusion.17 = f32[8192]{0:T(1024)} fusion(f32[24,8192]{1,0:T(8,128)S(1)} %stack.24, f32[24,8192]{1,0:T(8,128)} %stack.25, f32[24,24]{1,0:T(8,128)S(1)} %copy-done), kind=kOutput, calls=%fused_computation.153 | convolution fusion | flops 57008128 | bytes 1607936 | tf_op jit(solution)/shard_map/dot_general | solution.py:108
  50.6 3.7 %stack.31 = f32[24,8192]{1,0:T(8,128)S(1)} concatenate(f32[1,8192]{1,0:T(1,128)} %bitcast.564, f32[1,8192]{1,0:T(1,128)} %bitcast.584, f32[1,8192]{1,0:T(1,128)} %bitcast.580, f32[1,8192]{1,0:T(1,128)} %bitcast.514, f32[1,8192]{1,0:T(1,128)} %bitcast.515, f32[1,8192]{1,0:T(1,128)} %bitcast.516, f32[1,8192]{1,0:T(1,128)} %bitcast.531, f32[1,8192]{1,0:T(1,128)} %bitcast.530, ...), dimensions={0} | concatenate | bytes 1572864 | tf_op jit(solution)/shard_map/stack | solution.py:102
  54.3 5.8 %stack.30 = f32[24,8192]{1,0:T(8,128)} concatenate(f32[1,8192]{1,0:T(1,128)} %bitcast.558, f32[1,8192]{1,0:T(1,128)} %bitcast.557, f32[1,8192]{1,0:T(1,128)} %bitcast.556, f32[1,8192]{1,0:T(1,128)} %bitcast.466, f32[1,8192]{1,0:T(1,128)} %bitcast.479, f32[1,8192]{1,0:T(1,128)} %bitcast.480, f32[1,8192]{1,0:T(1,128)} %bitcast.513, f32[1,8192]{1,0:T(1,128)} %bitcast.512, ...), dimensions={0} | concatenate | bytes 1572864 | tf_op jit(solution)/shard_map/stack | solution.py:102
  60.1 2.7 %fusion.20 = f32[8192]{0:T(1024)} fusion(f32[24,8192]{1,0:T(8,128)} %stack.30, f32[24,8192]{1,0:T(8,128)S(1)} %stack.31, f32[24,24]{1,0:T(8,128)S(1)} %copy-done), kind=kOutput, calls=%fused_computation.156 | convolution fusion | flops 57008128 | bytes 1607936 | tf_op jit(solution)/shard_map/dot_general | solution.py:108
  66.2 3.6 %stack.27 = f32[24,8192]{1,0:T(8,128)S(1)} concatenate(f32[1,8192]{1,0:T(1,128)} %bitcast.569, f32[1,8192]{1,0:T(1,128)} %bitcast.568, f32[1,8192]{1,0:T(1,128)} %bitcast.567, f32[1,8192]{1,0:T(1,128)} %bitcast.534, f32[1,8192]{1,0:T(1,128)} %bitcast.535, f32[1,8192]{1,0:T(1,128)} %bitcast.536, f32[1,8192]{1,0:T(1,128)} %bitcast.610, f32[1,8192]{1,0:T(1,128)} %bitcast.609, ...), dimensions={0} | concatenate | bytes 1572864 | tf_op jit(solution)/shard_map/stack | solution.py:102
  70.0 3.6 %stack.26 = f32[24,8192]{1,0:T(8,128)S(1)} concatenate(f32[1,8192]{1,0:T(1,128)S(1)} %bitcast.563, f32[1,8192]{1,0:T(1,128)S(1)} %bitcast.562, f32[1,8192]{1,0:T(1,128)S(1)} %bitcast.561, f32[1,8192]{1,0:T(1,128)S(1)} %bitcast.450, f32[1,8192]{1,0:T(1,128)S(1)} %bitcast.451, f32[1,8192]{1,0:T(1,128)S(1)} %bitcast.452, f32[1,8192]{1,0:T(1,128)} %bitcast.611, f32[1,8192]{1,0:T(1,128)} %bitcast.607, ...), dimensions={0} | concatenate | bytes 1572864 | tf_op jit(solution)/shard_map/stack | solution.py:102
  75.7 3.4 %stack.29 = f32[24,8192]{1,0:T(8,128)S(1)} concatenate(f32[1,8192]{1,0:T(1,128)S(1)} %bitcast.549, f32[1,8192]{1,0:T(1,128)S(1)} %bitcast.548, f32[1,8192]{1,0:T(1,128)S(1)} %bitcast.547, f32[1,8192]{1,0:T(1,128)S(1)} %bitcast.438, f32[1,8192]{1,0:T(1,128)S(1)} %bitcast.439, f32[1,8192]{1,0:T(1,128)S(1)} %bitcast.440, f32[1,8192]{1,0:T(1,128)} %bitcast.602, f32[1,8192]{1,0:T(1,128)} %bitcast.601, ...), dimensions={0} | concatenate | bytes 1572864 | tf_op jit(solution)/shard_map/stack | solution.py:102
  83.5 5.7 %collective-permute-start.6 = (f32[2,8,128]{2,1,0:T(8,128)S(1)}, f32[2,8,128]{2,1,0:T(8,128)S(1)}, u32[]{:S(2)}, u32[]{:S(2)}) collective-permute-start(f32[2,8,128]{2,1,0:T(8,128)S(1)} %get-tuple-element.212), channel_id=1, source_target_pairs={{0,16},{16,32},{32,48},{48,64},{64,80},{80,96},{96,112},{112,128},... | collective-permute-start | bytes 24584 | tf_op jit(solution)/shard_map/ppermute | solution.py:25
  90.5 9.6 %collective-permute-done.7 = f32[2,8,128]{2,1,0:T(8,128)S(1)} collective-permute-done((f32[2,8,128]{2,1,0:T(8,128)S(1)}, f32[2,8,128]{2,1,0:T(8,128)S(1)}, u32[]{:S(2)}, u32[]{:S(2)}) %collective-permute-start.7) | collective-permute-done | bytes 8224 | tf_op jit(solution)/shard_map/ppermute | solution.py:27
  100.1 1.9 %collective-permute-start.8 = (f32[12,2,128]{2,1,0:T(2,128)S(1)}, f32[12,2,128]{2,1,0:T(2,128)S(1)}, u32[]{:S(2)}, u32[]{:S(2)}) collective-permute-start(f32[12,2,128]{2,1,0:T(2,128)S(1)} %get-tuple-element.203), channel_id=1, source_target_pairs={{0,1},{1,2},{2,3},{3,4},{4,5},{5,6},{6,7},{7,8},{8,9},{9,10},{10,1... | collective-permute-start | bytes 36872 | tf_op jit(solution)/shard_map/ppermute | solution.py:25
  102.1 7.1 %collective-permute-start.9 = (f32[12,2,128]{2,1,0:T(2,128)S(1)}, f32[12,2,128]{2,1,0:T(2,128)S(1)}, u32[]{:S(2)}, u32[]{:S(2)}) collective-permute-start(f32[12,2,128]{2,1,0:T(2,128)S(1)} %get-tuple-element.204), channel_id=1, source_target_pairs={{1,0},{2,1},{3,2},{4,3},{5,4},{6,5},{7,6},{8,7},{9,8},{10,9},{11,1... | collective-permute-start | bytes 36872 | tf_op jit(solution)/shard_map/ppermute | solution.py:27
  112.6 1.9 %collective-permute-start.10 = (f32[63,64]{1,0:T(8,128)S(1)}, f32[63,64]{1,0:T(8,128)S(1)}, u32[]{:S(2)}, u32[]{:S(2)}) collective-permute-start(f32[63,64]{1,0:T(8,128)S(1)} %copy.121), channel_id=1, source_target_pairs={{0,1},{1,0},{2,3},{3,2},{4,5},{5,4},{6,7},{7,6},{8,9},{9,8},{10,11... | collective-permute-start | bytes 48392 | tf_op jit(solution)/shard_map/ppermute | solution.py:44
  114.5 3.9 %collective-permute-done.10 = f32[63,64]{1,0:T(8,128)S(1)} collective-permute-done((f32[63,64]{1,0:T(8,128)S(1)}, f32[63,64]{1,0:T(8,128)S(1)}, u32[]{:S(2)}, u32[]{:S(2)}) %collective-permute-start.10) | collective-permute-done | bytes 16160 | tf_op jit(solution)/shard_map/ppermute | solution.py:44
  118.4 1.9 collective-permute-start.11
  120.3 4.8 %collective-permute-done.11 = f32[63,64]{1,0:T(8,128)S(1)} collective-permute-done((f32[63,64]{1,0:T(8,128)S(1)}, f32[63,64]{1,0:T(8,128)S(1)}, u32[]{:S(2)}, u32[]{:S(2)}) %collective-permute-start.11) | collective-permute-done | bytes 16160 | tf_op jit(solution)/shard_map/ppermute | solution.py:44
  125.1 3.1 %collective-permute-start.12 = (f32[63,64]{1,0:T(8,128)S(1)}, f32[63,64]{1,0:T(8,128)S(1)}, u32[]{:S(2)}, u32[]{:S(2)}) collective-permute-start(f32[63,64]{1,0:T(8,128)S(1)} %add.1266), channel_id=1, source_target_pairs={{0,4},{1,5},{2,6},{3,7},{4,0},{5,1},{6,2},{7,3},{8,12},{9,13},{10,... | collective-permute-start | bytes 48392 | tf_op jit(solution)/shard_map/ppermute | solution.py:44
  128.2 2.7 %collective-permute-done.12 = f32[63,64]{1,0:T(8,128)S(1)} collective-permute-done((f32[63,64]{1,0:T(8,128)S(1)}, f32[63,64]{1,0:T(8,128)S(1)}, u32[]{:S(2)}, u32[]{:S(2)}) %collective-permute-start.12) | collective-permute-done | bytes 16160 | tf_op jit(solution)/shard_map/ppermute | solution.py:44
  130.9 4.0 %collective-permute-start.13 = (f32[63,64]{1,0:T(8,128)S(1)}, f32[63,64]{1,0:T(8,128)S(1)}, u32[]{:S(2)}, u32[]{:S(2)}) collective-permute-start(f32[63,64]{1,0:T(8,128)S(1)} %add.1267), channel_id=1, source_target_pairs={{0,8},{1,9},{2,10},{3,11},{4,12},{5,13},{6,14},{7,15},{8,0},{9,1},... | collective-permute-start | bytes 48392 | tf_op jit(solution)/shard_map/ppermute | solution.py:44
  134.8 3.3 %collective-permute-done.13 = f32[63,64]{1,0:T(8,128)S(1)} collective-permute-done((f32[63,64]{1,0:T(8,128)S(1)}, f32[63,64]{1,0:T(8,128)S(1)}, u32[]{:S(2)}, u32[]{:S(2)}) %collective-permute-start.13) | collective-permute-done | bytes 16160 | tf_op jit(solution)/shard_map/ppermute | solution.py:44
  138.2 2.8 %collective-permute-start.14 = (f32[63,64]{1,0:T(8,128)S(1)}, f32[63,64]{1,0:T(8,128)S(1)}, u32[]{:S(2)}, u32[]{:S(2)}) collective-permute-start(f32[63,64]{1,0:T(8,128)S(1)} %add.1268), channel_id=1, source_target_pairs={{0,16},{16,0},{32,48},{48,32},{64,80},{80,64},{96,112},{112,96},{1... | collective-permute-start | bytes 48392 | tf_op jit(solution)/shard_map/ppermute | solution.py:44
  141.9 9.7 %collective-permute-start.15 = (f32[63,64]{1,0:T(8,128)S(1)}, f32[63,64]{1,0:T(8,128)S(1)}, u32[]{:S(2)}, u32[]{:S(2)}) collective-permute-start(f32[63,64]{1,0:T(8,128)S(1)} %add.1269), channel_id=1, source_target_pairs={{0,32},{16,48},{32,0},{48,16},{64,96},{80,112},{96,64},{112,80},{1... | collective-permute-start | bytes 48392 | tf_op jit(solution)/shard_map/ppermute | solution.py:44
  151.6 2.0 %collective-permute-done.15 = f32[63,64]{1,0:T(8,128)S(1)} collective-permute-done((f32[63,64]{1,0:T(8,128)S(1)}, f32[63,64]{1,0:T(8,128)S(1)}, u32[]{:S(2)}, u32[]{:S(2)}) %collective-permute-start.15) | collective-permute-done | bytes 16160 | tf_op jit(solution)/shard_map/ppermute | solution.py:44
  153.6 7.8 %collective-permute-start.16 = (f32[63,64]{1,0:T(8,128)S(1)}, f32[63,64]{1,0:T(8,128)S(1)}, u32[]{:S(2)}, u32[]{:S(2)}) collective-permute-start(f32[63,64]{1,0:T(8,128)S(1)} %add.1270), channel_id=1, source_target_pairs={{0,64},{16,80},{32,96},{48,112},{64,0},{80,16},{96,32},{112,48},{1... | collective-permute-start | bytes 48392 | tf_op jit(solution)/shard_map/ppermute | solution.py:44
  163.3 6.4 %collective-permute-start.17 = (f32[63,64]{1,0:T(8,128)S(1)}, f32[63,64]{1,0:T(8,128)S(1)}, u32[]{:S(2)}, u32[]{:S(2)}) collective-permute-start(f32[63,64]{1,0:T(8,128)S(1)} %add.1271), channel_id=1, source_target_pairs={{0,128},{16,144},{32,160},{48,176},{64,192},{80,208},{96,224},{112... | collective-permute-start | bytes 48392 | tf_op jit(solution)/shard_map/ppermute | solution.py:44
  171.6 11.5 %collective-permute-start.18 = (f32[63,64]{1,0:T(8,128)S(1)}, f32[63,64]{1,0:T(8,128)S(1)}, u32[]{:S(2)}, u32[]{:S(2)}) collective-permute-start(f32[63,64]{1,0:T(8,128)S(1)} %add.1272), channel_id=1, source_target_pairs={{0,256},{16,272},{32,288},{48,304},{64,320},{80,336},{96,352},{112... | collective-permute-start | bytes 48392 | tf_op jit(solution)/shard_map/ppermute | solution.py:44
  183.1 2.0 %collective-permute-done.18 = f32[63,64]{1,0:T(8,128)S(1)} collective-permute-done((f32[63,64]{1,0:T(8,128)S(1)}, f32[63,64]{1,0:T(8,128)S(1)}, u32[]{:S(2)}, u32[]{:S(2)}) %collective-permute-start.18) | collective-permute-done | bytes 16160 | tf_op jit(solution)/shard_map/ppermute | solution.py:44
  (222 shorter events, 43.6 us)
Async XLA Ops:
  0.6 45.8 %copy-start = (f32[24,24]{1,0:T(8,128)S(1)}, f32[24,24]{1,0:T(8,128)}, u32[]{:S(2)}) copy-start(f32[24,24]{1,0:T(8,128)} %param.14) | copy-start | bytes 6916
  0.6 9.3 %copy-start.3 = (f32[8,8,128]{2,1,0:T(8,128)S(1)}, f32[8,8,128]{2,1,0:T(8,128)}, u32[]{:S(2)}) copy-start(f32[8,8,128]{2,1,0:T(8,128)} %param.9) | copy-start | bytes 98308
  1.4 9.2 %collective-permute-start.1 = (f32[2,8,128]{2,1,0:T(8,128)S(1)}, f32[2,8,128]{2,1,0:T(8,128)S(1)}, u32[]{:S(2)}, u32[]{:S(2)}) collective-permute-start(f32[2,8,128]{2,1,0:T(8,128)S(1)} %get-tuple-element.214), channel_id=1, source_target_pairs={{16,0},{32,16},{48,32},{64,48},{80,64},{96,80},{112,96},{128,112},... | collective-permute-start | bytes 24584 | tf_op jit(solution)/shard_map/ppermute | solution.py:27
  2.7 7.3 %collective-permute-start = (f32[2,8,128]{2,1,0:T(8,128)S(1)}, f32[2,8,128]{2,1,0:T(8,128)S(1)}, u32[]{:S(2)}, u32[]{:S(2)}) collective-permute-start(f32[2,8,128]{2,1,0:T(8,128)S(1)} %get-tuple-element.215), channel_id=1, source_target_pairs={{0,16},{16,32},{32,48},{48,64},{64,80},{80,96},{96,112},{112,128},... | collective-permute-start | bytes 24584 | tf_op jit(solution)/shard_map/ppermute | solution.py:25
  7.7 13.0 %collective-permute-start.4 = (f32[4,2,3,1,8,128]{5,4,3,2,1,0:T(8,128)S(1)}, f32[4,2,3,1,8,128]{5,4,3,2,1,0:T(8,128)S(1)}, u32[]{:S(2)}, u32[]{:S(2)}) collective-permute-start(f32[4,2,3,1,8,128]{5,4,3,2,1,0:T(8,128)S(1)} %slice.2424), channel_id=1, source_target_pairs={{16,0},{32,16},{48,32},{64,48},{80,64},{96,80},{112,96},{128,112},... | collective-permute-start | bytes 294920 | tf_op jit(solution)/shard_map/ppermute | solution.py:37
  10.6 8.7 %collective-permute-start.2 = (f32[12,2,128]{2,1,0:T(2,128)S(1)}, f32[12,2,128]{2,1,0:T(2,128)S(1)}, u32[]{:S(2)}, u32[]{:S(2)}) collective-permute-start(f32[12,2,128]{2,1,0:T(2,128)S(1)} %get-tuple-element.205), channel_id=1, source_target_pairs={{0,1},{1,2},{2,3},{3,4},{4,5},{5,6},{6,7},{7,8},{8,9},{9,10},{10,1... | collective-permute-start | bytes 36872 | tf_op jit(solution)/shard_map/ppermute | solution.py:25
  14.1 6.4 %collective-permute-start.3 = (f32[12,2,128]{2,1,0:T(2,128)S(1)}, f32[12,2,128]{2,1,0:T(2,128)S(1)}, u32[]{:S(2)}, u32[]{:S(2)}) collective-permute-start(f32[12,2,128]{2,1,0:T(2,128)S(1)} %get-tuple-element.206), channel_id=1, source_target_pairs={{1,0},{2,1},{3,2},{4,3},{5,4},{6,5},{7,6},{8,7},{9,8},{10,9},{11,1... | collective-permute-start | bytes 36872 | tf_op jit(solution)/shard_map/ppermute | solution.py:27
  20.9 10.1 %collective-permute-start.5 = (f32[4,2,3,9,1,128]{5,3,4,2,1,0:T(8,128)S(1)}, f32[4,2,3,9,1,128]{5,3,4,2,1,0:T(8,128)S(1)}, u32[]{:S(2)}, u32[]{:S(2)}) collective-permute-start(f32[4,2,3,9,1,128]{5,3,4,2,1,0:T(8,128)S(1)} %copy.116), channel_id=1, source_target_pairs={{1,0},{2,1},{3,2},{4,3},{5,4},{6,5},{7,6},{8,7},{9,8},{10,9},{11,1... | collective-permute-start | bytes 331784 | tf_op jit(solution)/shard_map/ppermute | solution.py:37
  40.6 8.5 %copy-start.4 = (f32[24,24]{1,0:T(8,128)S(1)}, f32[24,24]{1,0:T(8,128)}, u32[]{:S(2)}) copy-start(f32[24,24]{1,0:T(8,128)} %param.13) | copy-start | bytes 6916
  65.1 4.8 %copy-start.12 = (f32[1,1,1,8,8,128]{5,4,3,2,1,0:T(8,128)S(1)}, f32[1,1,1,8,8,128]{5,4,3,2,1,0:T(8,128)}, u32[]{:S(2)}) copy-start(f32[1,1,1,8,8,128]{5,4,3,2,1,0:T(8,128)} %get-tuple-element.19) | copy-start | bytes 98308
  65.1 4.8 %copy-start.13 = (f32[1,1,1,8,8,128]{5,4,3,2,1,0:T(8,128)S(1)}, f32[1,1,1,8,8,128]{5,4,3,2,1,0:T(8,128)}, u32[]{:S(2)}) copy-start(f32[1,1,1,8,8,128]{5,4,3,2,1,0:T(8,128)} %get-tuple-element.20) | copy-start | bytes 98308
  65.1 4.8 %copy-start.14 = (f32[1,1,1,8,8,128]{5,4,3,2,1,0:T(8,128)S(1)}, f32[1,1,1,8,8,128]{5,4,3,2,1,0:T(8,128)}, u32[]{:S(2)}) copy-start(f32[1,1,1,8,8,128]{5,4,3,2,1,0:T(8,128)} %get-tuple-element.21) | copy-start | bytes 98308
  65.1 4.8 %copy-start.15 = (f32[1,1,1,8,8,128]{5,4,3,2,1,0:T(8,128)S(1)}, f32[1,1,1,8,8,128]{5,4,3,2,1,0:T(8,128)}, u32[]{:S(2)}) copy-start(f32[1,1,1,8,8,128]{5,4,3,2,1,0:T(8,128)} %get-tuple-element.22) | copy-start | bytes 98308
  65.1 4.8 %copy-start.16 = (f32[1,1,1,8,8,128]{5,4,3,2,1,0:T(8,128)S(1)}, f32[1,1,1,8,8,128]{5,4,3,2,1,0:T(8,128)}, u32[]{:S(2)}) copy-start(f32[1,1,1,8,8,128]{5,4,3,2,1,0:T(8,128)} %get-tuple-element.23) | copy-start | bytes 98308
  65.1 4.8 %copy-start.17 = (f32[1,1,1,8,8,128]{5,4,3,2,1,0:T(8,128)S(1)}, f32[1,1,1,8,8,128]{5,4,3,2,1,0:T(8,128)}, u32[]{:S(2)}) copy-start(f32[1,1,1,8,8,128]{5,4,3,2,1,0:T(8,128)} %get-tuple-element.24) | copy-start | bytes 98308
  65.1 4.8 %copy-start.18 = (f32[1,1,1,8,8,128]{5,4,3,2,1,0:T(8,128)S(1)}, f32[1,1,1,8,8,128]{5,4,3,2,1,0:T(8,128)}, u32[]{:S(2)}) copy-start(f32[1,1,1,8,8,128]{5,4,3,2,1,0:T(8,128)} %get-tuple-element.25) | copy-start | bytes 98308
  82.2 26.9 %copy-start.56 = (f32[63,64]{0,1:T(8,128)S(1)}, f32[63,64]{0,1:T(8,128)}, u32[]{:S(2)}) copy-start(f32[63,64]{0,1:T(8,128)} %constant.25.clone.1) | copy-start | bytes 48388
  83.5 7.0 %collective-permute-start.6 = (f32[2,8,128]{2,1,0:T(8,128)S(1)}, f32[2,8,128]{2,1,0:T(8,128)S(1)}, u32[]{:S(2)}, u32[]{:S(2)}) collective-permute-start(f32[2,8,128]{2,1,0:T(8,128)S(1)} %get-tuple-element.212), channel_id=1, source_target_pairs={{0,16},{16,32},{32,48},{48,64},{64,80},{80,96},{96,112},{112,128},... | collective-permute-start | bytes 24584 | tf_op jit(solution)/shard_map/ppermute | solution.py:25
  89.2 10.9 %collective-permute-start.7 = (f32[2,8,128]{2,1,0:T(8,128)S(1)}, f32[2,8,128]{2,1,0:T(8,128)S(1)}, u32[]{:S(2)}, u32[]{:S(2)}) collective-permute-start(f32[2,8,128]{2,1,0:T(8,128)S(1)} %get-tuple-element.213), channel_id=1, source_target_pairs={{16,0},{32,16},{48,32},{64,48},{80,64},{96,80},{112,96},{128,112},... | collective-permute-start | bytes 24584 | tf_op jit(solution)/shard_map/ppermute | solution.py:27
  100.1 9.2 %collective-permute-start.8 = (f32[12,2,128]{2,1,0:T(2,128)S(1)}, f32[12,2,128]{2,1,0:T(2,128)S(1)}, u32[]{:S(2)}, u32[]{:S(2)}) collective-permute-start(f32[12,2,128]{2,1,0:T(2,128)S(1)} %get-tuple-element.203), channel_id=1, source_target_pairs={{0,1},{1,2},{2,3},{3,4},{4,5},{5,6},{6,7},{7,8},{8,9},{9,10},{10,1... | collective-permute-start | bytes 36872 | tf_op jit(solution)/shard_map/ppermute | solution.py:25
  102.1 8.5 %collective-permute-start.9 = (f32[12,2,128]{2,1,0:T(2,128)S(1)}, f32[12,2,128]{2,1,0:T(2,128)S(1)}, u32[]{:S(2)}, u32[]{:S(2)}) collective-permute-start(f32[12,2,128]{2,1,0:T(2,128)S(1)} %get-tuple-element.204), channel_id=1, source_target_pairs={{1,0},{2,1},{3,2},{4,3},{5,4},{6,5},{7,6},{8,7},{9,8},{10,9},{11,1... | collective-permute-start | bytes 36872 | tf_op jit(solution)/shard_map/ppermute | solution.py:27
  111.3 79.2 %copy-start.30 = (f32[8,8,128]{2,1,0:T(8,128)}, f32[8,8,128]{2,1,0:T(8,128)S(1)}, u32[]{:S(2)}) copy-start(f32[8,8,128]{2,1,0:T(8,128)S(1)} %get-tuple-element.6) | copy-start | bytes 98308
  111.3 74.7 %copy-start.59 = (f32[64]{0:T(128)S(1)}, f32[64]{0:T(128)}, u32[]{:S(2)}) copy-start(f32[64]{0:T(128)} %param.15) | copy-start | bytes 772
  112.6 5.8 %collective-permute-start.10 = (f32[63,64]{1,0:T(8,128)S(1)}, f32[63,64]{1,0:T(8,128)S(1)}, u32[]{:S(2)}, u32[]{:S(2)}) collective-permute-start(f32[63,64]{1,0:T(8,128)S(1)} %copy.121), channel_id=1, source_target_pairs={{0,1},{1,0},{2,3},{3,2},{4,5},{5,4},{6,7},{7,6},{8,9},{9,8},{10,11... | collective-permute-start | bytes 48392 | tf_op jit(solution)/shard_map/ppermute | solution.py:44
  118.4 6.7 %collective-permute-start.11 = (f32[63,64]{1,0:T(8,128)S(1)}, f32[63,64]{1,0:T(8,128)S(1)}, u32[]{:S(2)}, u32[]{:S(2)}) collective-permute-start(f32[63,64]{1,0:T(8,128)S(1)} %add.1265), channel_id=1, source_target_pairs={{0,2},{1,3},{2,0},{3,1},{4,6},{5,7},{6,4},{7,5},{8,10},{9,11},{10,... | collective-permute-start | bytes 48392 | tf_op jit(solution)/shard_map/ppermute | solution.py:44
  125.1 5.8 %collective-permute-start.12 = (f32[63,64]{1,0:T(8,128)S(1)}, f32[63,64]{1,0:T(8,128)S(1)}, u32[]{:S(2)}, u32[]{:S(2)}) collective-permute-start(f32[63,64]{1,0:T(8,128)S(1)} %add.1266), channel_id=1, source_target_pairs={{0,4},{1,5},{2,6},{3,7},{4,0},{5,1},{6,2},{7,3},{8,12},{9,13},{10,... | collective-permute-start | bytes 48392 | tf_op jit(solution)/shard_map/ppermute | solution.py:44
  130.9 7.3 %collective-permute-start.13 = (f32[63,64]{1,0:T(8,128)S(1)}, f32[63,64]{1,0:T(8,128)S(1)}, u32[]{:S(2)}, u32[]{:S(2)}) collective-permute-start(f32[63,64]{1,0:T(8,128)S(1)} %add.1267), channel_id=1, source_target_pairs={{0,8},{1,9},{2,10},{3,11},{4,12},{5,13},{6,14},{7,15},{8,0},{9,1},... | collective-permute-start | bytes 48392 | tf_op jit(solution)/shard_map/ppermute | solution.py:44
  138.2 3.7 %collective-permute-start.14 = (f32[63,64]{1,0:T(8,128)S(1)}, f32[63,64]{1,0:T(8,128)S(1)}, u32[]{:S(2)}, u32[]{:S(2)}) collective-permute-start(f32[63,64]{1,0:T(8,128)S(1)} %add.1268), channel_id=1, source_target_pairs={{0,16},{16,0},{32,48},{48,32},{64,80},{80,64},{96,112},{112,96},{1... | collective-permute-start | bytes 48392 | tf_op jit(solution)/shard_map/ppermute | solution.py:44
  141.9 11.7 %collective-permute-start.15 = (f32[63,64]{1,0:T(8,128)S(1)}, f32[63,64]{1,0:T(8,128)S(1)}, u32[]{:S(2)}, u32[]{:S(2)}) collective-permute-start(f32[63,64]{1,0:T(8,128)S(1)} %add.1269), channel_id=1, source_target_pairs={{0,32},{16,48},{32,0},{48,16},{64,96},{80,112},{96,64},{112,80},{1... | collective-permute-start | bytes 48392 | tf_op jit(solution)/shard_map/ppermute | solution.py:44
  153.6 9.7 %collective-permute-start.16 = (f32[63,64]{1,0:T(8,128)S(1)}, f32[63,64]{1,0:T(8,128)S(1)}, u32[]{:S(2)}, u32[]{:S(2)}) collective-permute-start(f32[63,64]{1,0:T(8,128)S(1)} %add.1270), channel_id=1, source_target_pairs={{0,64},{16,80},{32,96},{48,112},{64,0},{80,16},{96,32},{112,48},{1... | collective-permute-start | bytes 48392 | tf_op jit(solution)/shard_map/ppermute | solution.py:44
  163.3 8.3 %collective-permute-start.17 = (f32[63,64]{1,0:T(8,128)S(1)}, f32[63,64]{1,0:T(8,128)S(1)}, u32[]{:S(2)}, u32[]{:S(2)}) collective-permute-start(f32[63,64]{1,0:T(8,128)S(1)} %add.1271), channel_id=1, source_target_pairs={{0,128},{16,144},{32,160},{48,176},{64,192},{80,208},{96,224},{112... | collective-permute-start | bytes 48392 | tf_op jit(solution)/shard_map/ppermute | solution.py:44
  171.6 13.6 %collective-permute-start.18 = (f32[63,64]{1,0:T(8,128)S(1)}, f32[63,64]{1,0:T(8,128)S(1)}, u32[]{:S(2)}, u32[]{:S(2)}) collective-permute-start(f32[63,64]{1,0:T(8,128)S(1)} %add.1272), channel_id=1, source_target_pairs={{0,256},{16,272},{32,288},{48,304},{64,320},{80,336},{96,352},{112... | collective-permute-start | bytes 48392 | tf_op jit(solution)/shard_map/ppermute | solution.py:44
  (47 other events, 143.9 us)

commit v3 on v2

--- a/solution.py
+++ b/solution.py
@@ -4,6 +4,8 @@
 import jax.numpy as jnp
 from jax import lax
 from jax.sharding import PartitionSpec as P
+from jax.experimental import pallas as pl
+from jax.experimental.pallas import tpu as pltpu
 
 BISECT = 6
 REGIONS = 64
@@ -113,6 +115,70 @@
     )
 
 
+CORNERS = [(a, b, d) for a in (0, 1) for b in (0, 1) for d in (0, 1)]
+
+
+def energy_kernel(extended_ref, stiffness_ref, mass_ref, stiff_out, mass_out):
+    pair_count = extended_ref.shape[0]
+    cells_x, cells_y, cells_z = stiff_out.shape
+    lane = lax.broadcasted_iota(jnp.int32, (cells_y, cells_z), 1)
+    inside = lane < cells_z - 1
+
+    def node_view(pair, member, component, x, corner):
+        corner_x, corner_y, corner_z = corner
+        value = extended_ref[pair, member, component, x + corner_x, pl.ds(corner_y, cells_y), :]
+        if corner_z:
+            value = jnp.where(inside, pltpu.roll(value, cells_z - 1, 1), 0.0)
+        return value
+
+    def over_pairs(pair, energies):
+        stiff_sum, mass_sum, x = energies
+        adjoint = [
+            node_view(pair, 1, component, x, corner) for corner in CORNERS for component in range(3)
+        ]
+        for row in range(len(adjoint)):
+            state = node_view(pair, 0, row % 3, x, CORNERS[row // 3])
+            stiff_row = stiffness_ref[row, 0] * adjoint[0]
+            mass_row = mass_ref[row, 0] * adjoint[0]
+            for column in range(1, len(adjoint)):
+                stiff_row = stiff_row + stiffness_ref[row, column] * adjoint[column]
+                mass_row = mass_row + mass_ref[row, column] * adjoint[column]
+            stiff_sum = stiff_sum + state * stiff_row
+            mass_sum = mass_sum + state * mass_row
+        return stiff_sum, mass_sum, x
+
+    def over_x(x, carry):
+        zero = jnp.zeros((cells_y, cells_z), jnp.float32)
+        stiff_sum, mass_sum, _ = lax.fori_loop(0, pair_count, over_pairs, (zero, zero, x))
+        stiff_out[x] = stiff_sum
+        mass_out[x] = mass_sum
+        return carry
+
+    lax.fori_loop(0, cells_x, over_x, 0)
+
+
+def element_energies(extended, stiffness, mass_matrix):
+    pair_count = extended.shape[0]
+    cells = (extended.shape[3] - 1, extended.shape[4] - 1, extended.shape[5])
+    voxels = cells[0] * cells[1] * cells[2]
+    vmem = pl.BlockSpec(memory_space=pltpu.VMEM)
+    smem = pl.BlockSpec(memory_space=pltpu.SMEM)
+    return pl.pallas_call(
+        energy_kernel,
+        out_shape=(
+            jax.ShapeDtypeStruct(cells, jnp.float32),
+            jax.ShapeDtypeStruct(cells, jnp.float32),
+        ),
+        in_specs=[vmem, smem, smem],
+        out_specs=(vmem, vmem),
+        cost_estimate=pl.CostEstimate(
+            flops=pair_count * voxels * 2400,
+            bytes_accessed=extended.size * 4 + 2 * voxels * 4,
+            transcendentals=0,
+        ),
+    )(extended, stiffness, mass_matrix)
+
+
 def shards(design, passive, basis_pairs, supports, stiffness, mass_matrix, volume_fraction):
     block_shape = design.shape
     size_x, size_y, size_z = block_shape
@@ -137,8 +203,7 @@
     widened = jnp.concatenate([fields, rim_first], axis=3)
     rim_second = from_behind(widened[:, :, :, :, :1], "gy", -1)
     extended = jnp.concatenate([widened, rim_second], axis=4)
-    extended = jnp.pad(extended, ((0, 0), (0, 0), (0, 0), (0, 0), (0, 0), (0, 1)))
-    stiff_energy, mass_energy = element_terms(extended, stiffness, mass_matrix)
+    stiff_energy, mass_energy = element_energies(extended, stiffness, mass_matrix)
     raw_sensitivity = -(
         PENALTY_SCALE * physical * physical * stiff_energy - OMEGA_SQUARED * mass_energy
     )

time: 195 us -> 163 us (0.84)
  local copies, waits for them, and re-layouts: 45.7 us -> 5.5 us
  Pallas kernels: 0 us -> 19.8 us
  matrix products: 11.7 us -> 0 us
  starting transfers between devices: 86.2 us -> 91.5 us
  waiting for transfers between devices: 36.4 us -> 34 us
    another operation x8 -> x0, local copies, waits for them, and re-layouts: 30.8 us -> none  [element_terms(): vectors.append(jnp.stack(row_list))]
    pallas_call x0 -> x1, Pallas kernels: none -> 19.8 us  [element_energies(): pl.pallas_call(energy_kernel, out_shape=(jax.ShapeDtypeStruct(cells, jnp....]
    dot_general x8 -> x0, matrix products: 11.7 us -> none  [the longest x4 7.04 us: element_terms(): jnp.dot(mass_matrix, adjoint_rows, precision=lax.Precision.HIGHEST)]
    slice x10 -> x0, local copies, waits for them, and re-layouts: 8.27 us -> none  [the longest x9 8.25 us: element_terms(): extended[pair_index, member, component, corner_x:corner_x + cells_x, corn...]
    ppermute x9, starting transfers between devices: 49.1 us -> 54.7 us  [butterfly_sum(): lax.ppermute(value, axis, [(i, i ^ stride) for i in range(count)])]
    ppermute x4, waiting for transfers between devices: 12.1 us -> 7.65 us  [with_halo(): lax.ppermute(head, axis, [((i + 1) % count, i) for i in range(ends)])]
    concatenate x4 -> x1, other arithmetic: 2.28 us -> 0.06 us  [shards(): widened = jnp.concatenate([fields, rim_first], axis=3)]
  transfers between devices with their start and end apart: 19 -> 19, of which waited for: 13 -> 13; matrix products, arithmetic and copies ran while one was open for 3% -> 0% of each run, Pallas kernels for 0% -> 0%
where the time goes in v3:
time: 163 us; the launch traced here: 160 us
  starting transfers between devices  91.5 us (56%)
  waiting for transfers between devices  34 us (21%)
  Pallas kernels  19.8 us (12%)
  other arithmetic  8.43 us (5%)
  local copies, waits for them, and re-layouts  5.5 us (3%)
    ppermute x9, starting transfers between devices, butterfly_sum(): lax.ppermute(value, axis, [(i, i ^ stride) for i in range(count)])  54.7 us
    ppermute x9, waiting for transfers between devices, butterfly_sum(): lax.ppermute(value, axis, [(i, i ^ stride) for i in range(count)])  23.4 us
    pallas_call x1, Pallas kernels, element_energies(): pl.pallas_call(energy_kernel, out_shape=(jax.ShapeDtypeStruct(cells, jnp....  19.8 us
    ppermute x4, starting transfers between devices, with_halo(): lax.ppermute(head, axis, [((i + 1) % count, i) for i in range(ends)])  14.6 us
    ppermute x4, starting transfers between devices, with_halo(): lax.ppermute(tail, axis, [(i, (i + 1) % count) for i in range(ends)])  14.3 us
    ppermute x2, starting transfers between devices, from_behind(): lax.ppermute(value, axis, [(source, source + steps) for source in range(i...  7.91 us
    ppermute x4, waiting for transfers between devices, with_halo(): lax.ppermute(head, axis, [((i + 1) % count, i) for i in range(ends)])  7.65 us
    gather x6, local copies, waits for them, and re-layouts, bisect_round(): chosen = jnp.take_along_axis(volumes, heap_index[None, :], axis=0)[0]  4.85 us
  transfers between devices with their start and end apart: 19, of which 13 were waited for; matrix products, arithmetic and copies ran while one was open for 0% of the time, Pallas kernels for 0%

profile of v3, /device:TPU:6, one launch (start us, length us, event | category | flops | bytes accessed | tf_op | source)
XLA Modules:
  0.0 160.4 jit_solution(2030952881050923219)
XLA Ops:
  2.6 1.3 collective-permute-start.4
  3.9 3.0 %collective-permute-start = (f32[2,8,128]{2,1,0:T(8,128)S(1)}, f32[2,8,128]{2,1,0:T(8,128)S(1)}, u32[]{:S(2)}, u32[]{:S(2)}) collective-permute-start(f32[2,8,128]{2,1,0:T(8,128)S(1)} %get-tuple-element.27), channel_id=1, source_target_pairs={{0,16},{16,32},{32,48},{48,64},{64,80},{80,96},{96,112},{112,128},... | collective-permute-start | bytes 24584 | tf_op jit(solution)/shard_map/ppermute | solution.py:27
  7.0 1.3 collective-permute-start.1
  8.6 6.4 %collective-permute-done.1 = f32[2,8,128]{2,1,0:T(8,128)S(1)} collective-permute-done((f32[2,8,128]{2,1,0:T(8,128)S(1)}, f32[2,8,128]{2,1,0:T(8,128)S(1)}, u32[]{:S(2)}, u32[]{:S(2)}) %collective-permute-start.1) | collective-permute-done | bytes 8224 | tf_op jit(solution)/shard_map/ppermute | solution.py:29
  15.0 5.3 %collective-permute-start.3 = (f32[12,2,128]{2,1,0:T(2,128)S(1)}, f32[12,2,128]{2,1,0:T(2,128)S(1)}, u32[]{:S(2)}, u32[]{:S(2)}) collective-permute-start(f32[12,2,128]{2,1,0:T(2,128)S(1)} %get-tuple-element.18), channel_id=1, source_target_pairs={{1,0},{2,1},{3,2},{4,3},{5,4},{6,5},{7,6},{8,7},{9,8},{10,9},{11,1... | collective-permute-start | bytes 36872 | tf_op jit(solution)/shard_map/ppermute | solution.py:29
  20.3 1.9 %collective-permute-start.2 = (f32[12,2,128]{2,1,0:T(2,128)S(1)}, f32[12,2,128]{2,1,0:T(2,128)S(1)}, u32[]{:S(2)}, u32[]{:S(2)}) collective-permute-start(f32[12,2,128]{2,1,0:T(2,128)S(1)} %get-tuple-element.17), channel_id=1, source_target_pairs={{0,1},{1,2},{2,3},{3,4},{4,5},{5,6},{6,7},{7,8},{8,9},{9,10},{10,1... | collective-permute-start | bytes 36872 | tf_op jit(solution)/shard_map/ppermute | solution.py:27
  22.3 6.6 %collective-permute-start.5 = (f32[4,2,3,9,1,128]{5,4,3,2,1,0:T(1,128)S(1)}, f32[4,2,3,9,1,128]{5,4,3,2,1,0:T(1,128)S(1)}, u32[]{:S(2)}, u32[]{:S(2)}) collective-permute-start(f32[4,2,3,9,1,128]{5,4,3,2,1,0:T(1,128)S(1)} %pad_maximum_fusion.1), channel_id=1, source_target_pairs={{1,0},{2,1},{3,2},{4,3},{5,4},{6,5},{7,6},{8,7},{9,8},{10,9},{11,1... | collective-permute-start | bytes 331784 | tf_op jit(solution)/shard_map/ppermute | solution.py:39
  29.2 2.1 %collective-permute-done.5 = f32[4,2,3,9,1,128]{5,4,3,2,1,0:T(1,128)S(1)} collective-permute-done((f32[4,2,3,9,1,128]{5,4,3,2,1,0:T(1,128)S(1)}, f32[4,2,3,9,1,128]{5,4,3,2,1,0:T(1,128)S(1)}, u32[]{:S(2)}, u32[]{:S(2)}) %collective-permute-start.5) | collective-permute-done | bytes 110624 | tf_op jit(solution)/shard_map/ppermute | solution.py:39
  31.3 1.4 pad_maximum_fusion.extended_ref
  32.6 19.8 %shard_map.86 = (f32[8,8,128]{2,1,0:T(8,128)}, f32[8,8,128]{2,1,0:T(8,128)}) custom-call(f32[4,2,3,9,9,128]{5,4,3,2,1,0:T(8,128)} %pad_maximum_fusion.extended_ref, f32[24,24]{1,0:T(8,128)} %stiffness_ref.1, f32[24,24]{1,0:T(8,128)} %mass_ref.1), custom_call_target="tpu_custom_call" | custom-call | flops 78643200 | bytes 1060864 | tf_op jit(solution)/shard_map/pallas_call | solution.py:166
  52.4 2.0 %fusion.58 = (f32[8,8,128]{2,1,0:T(8,128)S(1)}, pred[8,8,128]{2,1,0:T(8,128)(4,1)S(1)}) fusion(f32[8,8,128]{2,1,0:T(8,128)} %get-tuple-element.5, f32[12,8,128]{2,1,0:T(8,128)S(1)} %get-tuple-element.31, f32[12,2,128]{2,1,0:T(2,128)S(1)} %collective-permute-done.3, f32[12,2,128]{2,1,0:T(2,128)S(1)} %collective-permute-done.2, ...), kind=kLoop, calls=%fused_computation.120 | loop fusion | flops 3186688 | bytes 5652480 | tf_op jit(solution)/shard_map/div | solution.py:211
  54.5 1.3 collective-permute-start.7
  55.8 7.4 %collective-permute-start.6 = (f32[2,8,128]{2,1,0:T(8,128)S(1)}, f32[2,8,128]{2,1,0:T(8,128)S(1)}, u32[]{:S(2)}, u32[]{:S(2)}) collective-permute-start(f32[2,8,128]{2,1,0:T(8,128)S(1)} %get-tuple-element.24), channel_id=1, source_target_pairs={{0,16},{16,32},{32,48},{48,64},{64,80},{80,96},{96,112},{112,128},... | collective-permute-start | bytes 24584 | tf_op jit(solution)/shard_map/ppermute | solution.py:27
  64.0 1.9 %collective-permute-start.8 = (f32[12,2,128]{2,1,0:T(2,128)S(1)}, f32[12,2,128]{2,1,0:T(2,128)S(1)}, u32[]{:S(2)}, u32[]{:S(2)}) collective-permute-start(f32[12,2,128]{2,1,0:T(2,128)S(1)} %get-tuple-element.15), channel_id=1, source_target_pairs={{0,1},{1,2},{2,3},{3,4},{4,5},{5,6},{6,7},{7,8},{8,9},{9,10},{10,1... | collective-permute-start | bytes 36872 | tf_op jit(solution)/shard_map/ppermute | solution.py:27
  65.9 6.7 %collective-permute-start.9 = (f32[12,2,128]{2,1,0:T(2,128)S(1)}, f32[12,2,128]{2,1,0:T(2,128)S(1)}, u32[]{:S(2)}, u32[]{:S(2)}) collective-permute-start(f32[12,2,128]{2,1,0:T(2,128)S(1)} %get-tuple-element.16), channel_id=1, source_target_pairs={{1,0},{2,1},{3,2},{4,3},{5,4},{6,5},{7,6},{8,7},{9,8},{10,9},{11,1... | collective-permute-start | bytes 36872 | tf_op jit(solution)/shard_map/ppermute | solution.py:29
  76.1 1.9 %collective-permute-start.10 = (f32[63,64]{1,0:T(8,128)S(1)}, f32[63,64]{1,0:T(8,128)S(1)}, u32[]{:S(2)}, u32[]{:S(2)}) collective-permute-start(f32[63,64]{1,0:T(8,128)S(1)} %copy.16), channel_id=1, source_target_pairs={{0,1},{1,0},{2,3},{3,2},{4,5},{5,4},{6,7},{7,6},{8,9},{9,8},{10,11... | collective-permute-start | bytes 48392 | tf_op jit(solution)/shard_map/ppermute | solution.py:46
  78.0 3.9 %collective-permute-done.10 = f32[63,64]{1,0:T(8,128)S(1)} collective-permute-done((f32[63,64]{1,0:T(8,128)S(1)}, f32[63,64]{1,0:T(8,128)S(1)}, u32[]{:S(2)}, u32[]{:S(2)}) %collective-permute-start.10) | collective-permute-done | bytes 16160 | tf_op jit(solution)/shard_map/ppermute | solution.py:46
  81.9 1.9 %collective-permute-start.11 = (f32[63,64]{1,0:T(8,128)S(1)}, f32[63,64]{1,0:T(8,128)S(1)}, u32[]{:S(2)}, u32[]{:S(2)}) collective-permute-start(f32[63,64]{1,0:T(8,128)S(1)} %add.1224), channel_id=1, source_target_pairs={{0,2},{1,3},{2,0},{3,1},{4,6},{5,7},{6,4},{7,5},{8,10},{9,11},{10,... | collective-permute-start | bytes 48392 | tf_op jit(solution)/shard_map/ppermute | solution.py:46
  83.8 4.8 %collective-permute-done.11 = f32[63,64]{1,0:T(8,128)S(1)} collective-permute-done((f32[63,64]{1,0:T(8,128)S(1)}, f32[63,64]{1,0:T(8,128)S(1)}, u32[]{:S(2)}, u32[]{:S(2)}) %collective-permute-start.11) | collective-permute-done | bytes 16160 | tf_op jit(solution)/shard_map/ppermute | solution.py:46
  88.6 3.1 %collective-permute-start.12 = (f32[63,64]{1,0:T(8,128)S(1)}, f32[63,64]{1,0:T(8,128)S(1)}, u32[]{:S(2)}, u32[]{:S(2)}) collective-permute-start(f32[63,64]{1,0:T(8,128)S(1)} %add.1225), channel_id=1, source_target_pairs={{0,4},{1,5},{2,6},{3,7},{4,0},{5,1},{6,2},{7,3},{8,12},{9,13},{10,... | collective-permute-start | bytes 48392 | tf_op jit(solution)/shard_map/ppermute | solution.py:46
  91.7 2.7 %collective-permute-done.12 = f32[63,64]{1,0:T(8,128)S(1)} collective-permute-done((f32[63,64]{1,0:T(8,128)S(1)}, f32[63,64]{1,0:T(8,128)S(1)}, u32[]{:S(2)}, u32[]{:S(2)}) %collective-permute-start.12) | collective-permute-done | bytes 16160 | tf_op jit(solution)/shard_map/ppermute | solution.py:46
  94.4 3.7 %collective-permute-start.13 = (f32[63,64]{1,0:T(8,128)S(1)}, f32[63,64]{1,0:T(8,128)S(1)}, u32[]{:S(2)}, u32[]{:S(2)}) collective-permute-start(f32[63,64]{1,0:T(8,128)S(1)} %add.1226), channel_id=1, source_target_pairs={{0,8},{1,9},{2,10},{3,11},{4,12},{5,13},{6,14},{7,15},{8,0},{9,1},... | collective-permute-start | bytes 48392 | tf_op jit(solution)/shard_map/ppermute | solution.py:46
  98.0 3.6 %collective-permute-done.13 = f32[63,64]{1,0:T(8,128)S(1)} collective-permute-done((f32[63,64]{1,0:T(8,128)S(1)}, f32[63,64]{1,0:T(8,128)S(1)}, u32[]{:S(2)}, u32[]{:S(2)}) %collective-permute-start.13) | collective-permute-done | bytes 16160 | tf_op jit(solution)/shard_map/ppermute | solution.py:46
  101.7 2.1 %collective-permute-start.14 = (f32[63,64]{1,0:T(8,128)S(1)}, f32[63,64]{1,0:T(8,128)S(1)}, u32[]{:S(2)}, u32[]{:S(2)}) collective-permute-start(f32[63,64]{1,0:T(8,128)S(1)} %add.1227), channel_id=1, source_target_pairs={{0,16},{16,0},{32,48},{48,32},{64,80},{80,64},{96,112},{112,96},{1... | collective-permute-start | bytes 48392 | tf_op jit(solution)/shard_map/ppermute | solution.py:46
  104.8 13.7 %collective-permute-start.15 = (f32[63,64]{1,0:T(8,128)S(1)}, f32[63,64]{1,0:T(8,128)S(1)}, u32[]{:S(2)}, u32[]{:S(2)}) collective-permute-start(f32[63,64]{1,0:T(8,128)S(1)} %add.1228), channel_id=1, source_target_pairs={{0,32},{16,48},{32,0},{48,16},{64,96},{80,112},{96,64},{112,80},{1... | collective-permute-start | bytes 48392 | tf_op jit(solution)/shard_map/ppermute | solution.py:46
  118.5 1.9 %collective-permute-done.15 = f32[63,64]{1,0:T(8,128)S(1)} collective-permute-done((f32[63,64]{1,0:T(8,128)S(1)}, f32[63,64]{1,0:T(8,128)S(1)}, u32[]{:S(2)}, u32[]{:S(2)}) %collective-permute-start.15) | collective-permute-done | bytes 16160 | tf_op jit(solution)/shard_map/ppermute | solution.py:46
  120.4 9.4 %collective-permute-start.16 = (f32[63,64]{1,0:T(8,128)S(1)}, f32[63,64]{1,0:T(8,128)S(1)}, u32[]{:S(2)}, u32[]{:S(2)}) collective-permute-start(f32[63,64]{1,0:T(8,128)S(1)} %add.1229), channel_id=1, source_target_pairs={{0,64},{16,80},{32,96},{48,112},{64,0},{80,16},{96,32},{112,48},{1... | collective-permute-start | bytes 48392 | tf_op jit(solution)/shard_map/ppermute | solution.py:46
  129.8 1.9 %collective-permute-done.16 = f32[63,64]{1,0:T(8,128)S(1)} collective-permute-done((f32[63,64]{1,0:T(8,128)S(1)}, f32[63,64]{1,0:T(8,128)S(1)}, u32[]{:S(2)}, u32[]{:S(2)}) %collective-permute-start.16) | collective-permute-done | bytes 16160 | tf_op jit(solution)/shard_map/ppermute | solution.py:46
  131.7 5.7 %collective-permute-start.17 = (f32[63,64]{1,0:T(8,128)S(1)}, f32[63,64]{1,0:T(8,128)S(1)}, u32[]{:S(2)}, u32[]{:S(2)}) collective-permute-start(f32[63,64]{1,0:T(8,128)S(1)} %add.1230), channel_id=1, source_target_pairs={{0,128},{16,144},{32,160},{48,176},{64,192},{80,208},{96,224},{112... | collective-permute-start | bytes 48392 | tf_op jit(solution)/shard_map/ppermute | solution.py:46
  137.4 1.9 %collective-permute-done.17 = f32[63,64]{1,0:T(8,128)S(1)} collective-permute-done((f32[63,64]{1,0:T(8,128)S(1)}, f32[63,64]{1,0:T(8,128)S(1)}, u32[]{:S(2)}, u32[]{:S(2)}) %collective-permute-start.17) | collective-permute-done | bytes 16160 | tf_op jit(solution)/shard_map/ppermute | solution.py:46
  139.3 13.1 %collective-permute-start.18 = (f32[63,64]{1,0:T(8,128)S(1)}, f32[63,64]{1,0:T(8,128)S(1)}, u32[]{:S(2)}, u32[]{:S(2)}) collective-permute-start(f32[63,64]{1,0:T(8,128)S(1)} %add.1231), channel_id=1, source_target_pairs={{0,256},{16,272},{32,288},{48,304},{64,320},{80,336},{96,352},{112... | collective-permute-start | bytes 48392 | tf_op jit(solution)/shard_map/ppermute | solution.py:46
  152.5 1.9 %collective-permute-done.18 = f32[63,64]{1,0:T(8,128)S(1)} collective-permute-done((f32[63,64]{1,0:T(8,128)S(1)}, f32[63,64]{1,0:T(8,128)S(1)}, u32[]{:S(2)}, u32[]{:S(2)}) %collective-permute-start.18) | collective-permute-done | bytes 16160 | tf_op jit(solution)/shard_map/ppermute | solution.py:46
  (83 shorter events, 13.6 us)
Async XLA Ops:
  0.6 3.3 %copy-start = (f32[8,8,128]{2,1,0:T(8,128)S(1)}, f32[8,8,128]{2,1,0:T(8,128)}, u32[]{:S(2)}) copy-start(f32[8,8,128]{2,1,0:T(8,128)} %param.9) | copy-start | bytes 98308
  2.6 19.6 %collective-permute-start.4 = (f32[4,2,3,1,8,128]{5,4,3,2,1,0:T(8,128)S(1)}, f32[4,2,3,1,8,128]{5,4,3,2,1,0:T(8,128)S(1)}, u32[]{:S(2)}, u32[]{:S(2)}) collective-permute-start(f32[4,2,3,1,8,128]{5,4,3,2,1,0:T(8,128)S(1)} %slice.1485), channel_id=1, source_target_pairs={{16,0},{32,16},{48,32},{64,48},{80,64},{96,80},{112,96},{128,112},... | collective-permute-start | bytes 294920 | tf_op jit(solution)/shard_map/ppermute | solution.py:39
  3.9 4.6 %collective-permute-start = (f32[2,8,128]{2,1,0:T(8,128)S(1)}, f32[2,8,128]{2,1,0:T(8,128)S(1)}, u32[]{:S(2)}, u32[]{:S(2)}) collective-permute-start(f32[2,8,128]{2,1,0:T(8,128)S(1)} %get-tuple-element.27), channel_id=1, source_target_pairs={{0,16},{16,32},{32,48},{48,64},{64,80},{80,96},{96,112},{112,128},... | collective-permute-start | bytes 24584 | tf_op jit(solution)/shard_map/ppermute | solution.py:27
  7.0 8.0 %collective-permute-start.1 = (f32[2,8,128]{2,1,0:T(8,128)S(1)}, f32[2,8,128]{2,1,0:T(8,128)S(1)}, u32[]{:S(2)}, u32[]{:S(2)}) collective-permute-start(f32[2,8,128]{2,1,0:T(8,128)S(1)} %get-tuple-element.26), channel_id=1, source_target_pairs={{16,0},{32,16},{48,32},{64,48},{80,64},{96,80},{112,96},{128,112},... | collective-permute-start | bytes 24584 | tf_op jit(solution)/shard_map/ppermute | solution.py:29
  15.0 14.0 %collective-permute-start.3 = (f32[12,2,128]{2,1,0:T(2,128)S(1)}, f32[12,2,128]{2,1,0:T(2,128)S(1)}, u32[]{:S(2)}, u32[]{:S(2)}) collective-permute-start(f32[12,2,128]{2,1,0:T(2,128)S(1)} %get-tuple-element.18), channel_id=1, source_target_pairs={{1,0},{2,1},{3,2},{4,3},{5,4},{6,5},{7,6},{8,7},{9,8},{10,9},{11,1... | collective-permute-start | bytes 36872 | tf_op jit(solution)/shard_map/ppermute | solution.py:29
  20.3 8.6 %collective-permute-start.2 = (f32[12,2,128]{2,1,0:T(2,128)S(1)}, f32[12,2,128]{2,1,0:T(2,128)S(1)}, u32[]{:S(2)}, u32[]{:S(2)}) collective-permute-start(f32[12,2,128]{2,1,0:T(2,128)S(1)} %get-tuple-element.17), channel_id=1, source_target_pairs={{0,1},{1,2},{2,3},{3,4},{4,5},{5,6},{6,7},{7,8},{8,9},{9,10},{10,1... | collective-permute-start | bytes 36872 | tf_op jit(solution)/shard_map/ppermute | solution.py:27
  22.3 8.9 %collective-permute-start.5 = (f32[4,2,3,9,1,128]{5,4,3,2,1,0:T(1,128)S(1)}, f32[4,2,3,9,1,128]{5,4,3,2,1,0:T(1,128)S(1)}, u32[]{:S(2)}, u32[]{:S(2)}) collective-permute-start(f32[4,2,3,9,1,128]{5,4,3,2,1,0:T(1,128)S(1)} %pad_maximum_fusion.1), channel_id=1, source_target_pairs={{1,0},{2,1},{3,2},{4,3},{5,4},{6,5},{7,6},{8,7},{9,8},{10,9},{11,1... | collective-permute-start | bytes 331784 | tf_op jit(solution)/shard_map/ppermute | solution.py:39
  29.2 23.3 %copy-start.2 = (s32[8,8,128]{2,1,0:T(8,128)S(1)}, s32[8,8,128]{2,1,0:T(8,128)}, u32[]{:S(2)}) copy-start(s32[8,8,128]{2,1,0:T(8,128)} %param.10) | copy-start | bytes 98308
  52.4 20.2 %copy-start.3 = (f32[63,64]{0,1:T(8,128)S(1)}, f32[63,64]{0,1:T(8,128)}, u32[]{:S(2)}) copy-start(f32[63,64]{0,1:T(8,128)} %constant.25.clone.1) | copy-start | bytes 48388
  54.5 8.7 %collective-permute-start.7 = (f32[2,8,128]{2,1,0:T(8,128)S(1)}, f32[2,8,128]{2,1,0:T(8,128)S(1)}, u32[]{:S(2)}, u32[]{:S(2)}) collective-permute-start(f32[2,8,128]{2,1,0:T(8,128)S(1)} %get-tuple-element.25), channel_id=1, source_target_pairs={{16,0},{32,16},{48,32},{64,48},{80,64},{96,80},{112,96},{128,112},... | collective-permute-start | bytes 24584 | tf_op jit(solution)/shard_map/ppermute | solution.py:29
  55.8 8.2 %collective-permute-start.6 = (f32[2,8,128]{2,1,0:T(8,128)S(1)}, f32[2,8,128]{2,1,0:T(8,128)S(1)}, u32[]{:S(2)}, u32[]{:S(2)}) collective-permute-start(f32[2,8,128]{2,1,0:T(8,128)S(1)} %get-tuple-element.24), channel_id=1, source_target_pairs={{0,16},{16,32},{32,48},{48,64},{64,80},{80,96},{96,112},{112,128},... | collective-permute-start | bytes 24584 | tf_op jit(solution)/shard_map/ppermute | solution.py:27
  64.0 8.8 %collective-permute-start.8 = (f32[12,2,128]{2,1,0:T(2,128)S(1)}, f32[12,2,128]{2,1,0:T(2,128)S(1)}, u32[]{:S(2)}, u32[]{:S(2)}) collective-permute-start(f32[12,2,128]{2,1,0:T(2,128)S(1)} %get-tuple-element.15), channel_id=1, source_target_pairs={{0,1},{1,2},{2,3},{3,4},{4,5},{5,6},{6,7},{7,8},{8,9},{9,10},{10,1... | collective-permute-start | bytes 36872 | tf_op jit(solution)/shard_map/ppermute | solution.py:27
  65.9 8.1 %collective-permute-start.9 = (f32[12,2,128]{2,1,0:T(2,128)S(1)}, f32[12,2,128]{2,1,0:T(2,128)S(1)}, u32[]{:S(2)}, u32[]{:S(2)}) collective-permute-start(f32[12,2,128]{2,1,0:T(2,128)S(1)} %get-tuple-element.16), channel_id=1, source_target_pairs={{1,0},{2,1},{3,2},{4,3},{5,4},{6,5},{7,6},{8,7},{9,8},{10,9},{11,1... | collective-permute-start | bytes 36872 | tf_op jit(solution)/shard_map/ppermute | solution.py:29
  74.8 84.9 %copy-start.1 = (f32[8,8,128]{2,1,0:T(8,128)}, f32[8,8,128]{2,1,0:T(8,128)S(1)}, u32[]{:S(2)}) copy-start(f32[8,8,128]{2,1,0:T(8,128)S(1)} %get-tuple-element.10) | copy-start | bytes 98308
  74.8 80.3 %copy-start.4 = (f32[64]{0:T(128)S(1)}, f32[64]{0:T(128)}, u32[]{:S(2)}) copy-start(f32[64]{0:T(128)} %param.15) | copy-start | bytes 772
  76.1 5.8 %collective-permute-start.10 = (f32[63,64]{1,0:T(8,128)S(1)}, f32[63,64]{1,0:T(8,128)S(1)}, u32[]{:S(2)}, u32[]{:S(2)}) collective-permute-start(f32[63,64]{1,0:T(8,128)S(1)} %copy.16), channel_id=1, source_target_pairs={{0,1},{1,0},{2,3},{3,2},{4,5},{5,4},{6,7},{7,6},{8,9},{9,8},{10,11... | collective-permute-start | bytes 48392 | tf_op jit(solution)/shard_map/ppermute | solution.py:46
  81.9 6.7 %collective-permute-start.11 = (f32[63,64]{1,0:T(8,128)S(1)}, f32[63,64]{1,0:T(8,128)S(1)}, u32[]{:S(2)}, u32[]{:S(2)}) collective-permute-start(f32[63,64]{1,0:T(8,128)S(1)} %add.1224), channel_id=1, source_target_pairs={{0,2},{1,3},{2,0},{3,1},{4,6},{5,7},{6,4},{7,5},{8,10},{9,11},{10,... | collective-permute-start | bytes 48392 | tf_op jit(solution)/shard_map/ppermute | solution.py:46
  88.6 5.8 %collective-permute-start.12 = (f32[63,64]{1,0:T(8,128)S(1)}, f32[63,64]{1,0:T(8,128)S(1)}, u32[]{:S(2)}, u32[]{:S(2)}) collective-permute-start(f32[63,64]{1,0:T(8,128)S(1)} %add.1225), channel_id=1, source_target_pairs={{0,4},{1,5},{2,6},{3,7},{4,0},{5,1},{6,2},{7,3},{8,12},{9,13},{10,... | collective-permute-start | bytes 48392 | tf_op jit(solution)/shard_map/ppermute | solution.py:46
  94.4 7.3 %collective-permute-start.13 = (f32[63,64]{1,0:T(8,128)S(1)}, f32[63,64]{1,0:T(8,128)S(1)}, u32[]{:S(2)}, u32[]{:S(2)}) collective-permute-start(f32[63,64]{1,0:T(8,128)S(1)} %add.1226), channel_id=1, source_target_pairs={{0,8},{1,9},{2,10},{3,11},{4,12},{5,13},{6,14},{7,15},{8,0},{9,1},... | collective-permute-start | bytes 48392 | tf_op jit(solution)/shard_map/ppermute | solution.py:46
  101.7 3.1 %collective-permute-start.14 = (f32[63,64]{1,0:T(8,128)S(1)}, f32[63,64]{1,0:T(8,128)S(1)}, u32[]{:S(2)}, u32[]{:S(2)}) collective-permute-start(f32[63,64]{1,0:T(8,128)S(1)} %add.1227), channel_id=1, source_target_pairs={{0,16},{16,0},{32,48},{48,32},{64,80},{80,64},{96,112},{112,96},{1... | collective-permute-start | bytes 48392 | tf_op jit(solution)/shard_map/ppermute | solution.py:46
  104.8 15.6 %collective-permute-start.15 = (f32[63,64]{1,0:T(8,128)S(1)}, f32[63,64]{1,0:T(8,128)S(1)}, u32[]{:S(2)}, u32[]{:S(2)}) collective-permute-start(f32[63,64]{1,0:T(8,128)S(1)} %add.1228), channel_id=1, source_target_pairs={{0,32},{16,48},{32,0},{48,16},{64,96},{80,112},{96,64},{112,80},{1... | collective-permute-start | bytes 48392 | tf_op jit(solution)/shard_map/ppermute | solution.py:46
  120.4 11.3 %collective-permute-start.16 = (f32[63,64]{1,0:T(8,128)S(1)}, f32[63,64]{1,0:T(8,128)S(1)}, u32[]{:S(2)}, u32[]{:S(2)}) collective-permute-start(f32[63,64]{1,0:T(8,128)S(1)} %add.1229), channel_id=1, source_target_pairs={{0,64},{16,80},{32,96},{48,112},{64,0},{80,16},{96,32},{112,48},{1... | collective-permute-start | bytes 48392 | tf_op jit(solution)/shard_map/ppermute | solution.py:46
  131.7 7.6 %collective-permute-start.17 = (f32[63,64]{1,0:T(8,128)S(1)}, f32[63,64]{1,0:T(8,128)S(1)}, u32[]{:S(2)}, u32[]{:S(2)}) collective-permute-start(f32[63,64]{1,0:T(8,128)S(1)} %add.1230), channel_id=1, source_target_pairs={{0,128},{16,144},{32,160},{48,176},{64,192},{80,208},{96,224},{112... | collective-permute-start | bytes 48392 | tf_op jit(solution)/shard_map/ppermute | solution.py:46
  139.3 15.0 %collective-permute-start.18 = (f32[63,64]{1,0:T(8,128)S(1)}, f32[63,64]{1,0:T(8,128)S(1)}, u32[]{:S(2)}, u32[]{:S(2)}) collective-permute-start(f32[63,64]{1,0:T(8,128)S(1)} %add.1231), channel_id=1, source_target_pairs={{0,256},{16,272},{32,288},{48,304},{64,320},{80,336},{96,352},{112... | collective-permute-start | bytes 48392 | tf_op jit(solution)/shard_map/ppermute | solution.py:46

commit v4 on v3

--- a/solution.py
+++ b/solution.py
@@ -31,6 +31,26 @@
             axis=dim,
         )
     return cells
+
+
+def front_exchange(cells, fields, width):
+    for axis, dim in (("gx", 0), ("gy", 1)):
+        count = lax.axis_size(axis)
+        ends = count - 1
+        field_dim = dim + 3
+        head = lax.slice_in_dim(cells, 0, width, axis=dim)
+        tail = lax.slice_in_dim(cells, cells.shape[dim] - width, cells.shape[dim], axis=dim)
+        rim = lax.slice_in_dim(fields, 0, 1, axis=field_dim)
+        lanes = cells.shape[-1]
+        packed = jnp.concatenate([head.reshape(-1, lanes), rim.reshape(-1, lanes)], axis=0)
+        packed = lax.ppermute(packed, axis, [((i + 1) % count, i) for i in range(ends)])
+        split = head.size // lanes
+        head = packed[:split].reshape(head.shape)
+        rim = packed[split:].reshape(rim.shape)
+        tail = lax.ppermute(tail, axis, [(i, (i + 1) % count) for i in range(ends)])
+        cells = jnp.concatenate([tail, cells, head], axis=dim)
+        fields = jnp.concatenate([fields, rim], axis=field_dim)
+    return cells, fields
 
 
 def from_behind(value, axis, steps):
@@ -195,14 +215,10 @@
     valid_z = jnp.pad(jnp.ones((size_z,), jnp.float32), 2)
     inside = valid_x[:, None, None] * valid_y[None, :, None] * valid_z[None, None, :]
     weight_sum = stencil(inside, block_shape)
-    design_wide = with_halo(design, (("gx", 0), ("gy", 1)), 2)
+    fields = basis_pairs * (1 - supports).astype(jnp.float32)
+    design_wide, extended = front_exchange(design, fields, 2)
     design_wide = jnp.pad(design_wide, ((0, 0), (0, 0), (2, 2)))
     physical = jnp.where(passive == 1, 1.0, stencil(design_wide, block_shape) / weight_sum)
-    fields = basis_pairs * (1 - supports).astype(jnp.float32)
-    rim_first = from_behind(fields[:, :, :, :1], "gx", -1)
-    widened = jnp.concatenate([fields, rim_first], axis=3)
-    rim_second = from_behind(widened[:, :, :, :, :1], "gy", -1)
-    extended = jnp.concatenate([widened, rim_second], axis=4)
     stiff_energy, mass_energy = element_energies(extended, stiffness, mass_matrix)
     raw_sensitivity = -(
         PENALTY_SCALE * physical * physical * stiff_energy - OMEGA_SQUARED * mass_energy
@@ -249,12 +265,13 @@
             jnp.sum(fields_of, axis=(1, 2)).reshape(len(midpoints), REGIONS, band_cells).sum(axis=2)
         )
         volumes = butterfly_sum(butterfly_sum(partial_volumes, "gy"), "gx")
+        heavier_all = volumes > target[None, :]
         position = jnp.zeros((REGIONS,), jnp.int32)
         for depth in range(levels):
             middle = jnp.sqrt(low_end * high_end)
-            heap_index = position + (2**depth - 1)
-            chosen = jnp.take_along_axis(volumes, heap_index[None, :], axis=0)[0]
-            heavier = chosen > target
+            nodes = lax.slice_in_dim(heavier_all, 2**depth - 1, 2 ** (depth + 1) - 1, axis=0)
+            slots = lax.broadcasted_iota(jnp.int32, nodes.shape, 0)
+            heavier = jnp.any(nodes & (slots == position[None, :]), axis=0)
             low_end = jnp.where(heavier, middle, low_end)
             high_end = jnp.where(heavier, high_end, middle)
             position = 2 * position + heavier.astype(jnp.int32)

time: 163 us -> 144 us (0.88)
  starting transfers between devices: 91.5 us -> 83.7 us
  waiting for transfers between devices: 34 us -> 26.4 us
  local copies, waits for them, and re-layouts: 5.5 us -> 0.96 us
    ppermute x4 -> x2, starting transfers between devices: 14.6 us -> 7.58 us  [with_halo(): lax.ppermute(head, axis, [((i + 1) % count, i) for i in range(ends)])]
    ppermute x4 -> x2, waiting for transfers between devices: 7.65 us -> 1.25 us  [with_halo(): lax.ppermute(head, axis, [((i + 1) % count, i) for i in range(ends)])]
    ppermute x4 -> x2, starting transfers between devices: 14.3 us -> 9.13 us  [with_halo(): lax.ppermute(tail, axis, [(i, (i + 1) % count) for i in range(ends)])]
    gather x6 -> x0, local copies, waits for them, and re-layouts: 4.85 us -> none  [bisect_round(): chosen = jnp.take_along_axis(volumes, heap_index[None, :], axis=0)[0]]
    ppermute x2 -> x4, starting transfers between devices: 7.91 us -> 12 us  [the longest x2 7.07 us: front_exchange(): lax.ppermute(packed, axis, [((i + 1) % count, i) for i in range(ends)])]
  transfers between devices with their start and end apart: 19 -> 17, of which waited for: 13 -> 13; matrix products, arithmetic and copies ran while one was open for 0% -> 1% of each run, Pallas kernels for 0% -> 14%
where the time goes in v4:
time: 144 us; the launch traced here: 142 us
  starting transfers between devices  83.7 us (58%)
  waiting for transfers between devices  26.4 us (18%)
  Pallas kernels  19.8 us (14%)
  other arithmetic  10 us (7%)
    ppermute x9, starting transfers between devices, butterfly_sum(): lax.ppermute(value, axis, [(i, i ^ stride) for i in range(count)])  54.9 us
    ppermute x9, waiting for transfers between devices, butterfly_sum(): lax.ppermute(value, axis, [(i, i ^ stride) for i in range(count)])  23.3 us
    pallas_call x1, Pallas kernels, element_energies(): pl.pallas_call(energy_kernel, out_shape=(jax.ShapeDtypeStruct(cells, jnp....  19.8 us
    ppermute x2, starting transfers between devices, with_halo(): lax.ppermute(tail, axis, [(i, (i + 1) % count) for i in range(ends)])  9.13 us
    ppermute x2, starting transfers between devices, with_halo(): lax.ppermute(head, axis, [((i + 1) % count, i) for i in range(ends)])  7.58 us
    ppermute x2, starting transfers between devices, front_exchange(): lax.ppermute(packed, axis, [((i + 1) % count, i) for i in range(ends)])  7.07 us
    ppermute x2, starting transfers between devices, front_exchange(): tail = lax.ppermute(tail, axis, [(i, (i + 1) % count) for i in range(ends)])  4.95 us
  transfers between devices with their start and end apart: 17, of which 13 were waited for; matrix products, arithmetic and copies ran while one was open for 1% of the time, Pallas kernels for 14%

profile of v4, /device:TPU:6, one launch (start us, length us, event | category | flops | bytes accessed | tf_op | source)
XLA Modules:
  0.0 141.9 jit_solution(2201492952962715299)
XLA Ops:
  1.4 1.2 broadcast_multiply_fusion
  2.7 1.3 collective-permute-start.1
  4.0 3.0 %collective-permute-start = (f32[2,8,128]{2,1,0:T(8,128)S(1)}, f32[2,8,128]{2,1,0:T(8,128)S(1)}, u32[]{:S(2)}, u32[]{:S(2)}) collective-permute-start(f32[2,8,128]{2,1,0:T(8,128)S(1)} %get-tuple-element.27), channel_id=1, source_target_pairs={{0,16},{16,32},{32,48},{48,64},{64,80},{80,96},{96,112},{112,128},... | collective-permute-start | bytes 24584 | tf_op jit(solution)/shard_map/ppermute | solution.py:50
  7.9 5.8 %collective-permute-start.3 = (f32[240,128]{1,0:T(8,128)S(1)}, f32[240,128]{1,0:T(8,128)S(1)}, u32[]{:S(2)}, u32[]{:S(2)}) collective-permute-start(f32[240,128]{1,0:T(8,128)S(1)} %pad_maximum_fusion.1), channel_id=1, source_target_pairs={{1,0},{2,1},{3,2},{4,3},{5,4},{6,5},{7,6},{8,7},{9,8},{10,9},{11,1... | collective-permute-start | bytes 368648 | tf_op jit(solution)/shard_map/ppermute | solution.py:46
  13.8 1.9 %collective-permute-start.2 = (f32[12,2,128]{2,1,0:T(2,128)S(1)}, f32[12,2,128]{2,1,0:T(2,128)S(1)}, u32[]{:S(2)}, u32[]{:S(2)}) collective-permute-start(f32[12,2,128]{2,1,0:T(2,128)S(1)} %get-tuple-element.20), channel_id=1, source_target_pairs={{0,1},{1,2},{2,3},{3,4},{4,5},{5,6},{6,7},{7,8},{8,9},{9,10},{10,1... | collective-permute-start | bytes 36872 | tf_op jit(solution)/shard_map/ppermute | solution.py:50
  16.2 1.4 pad_maximum_fusion.extended_ref
  17.5 19.8 %shard_map.86 = (f32[8,8,128]{2,1,0:T(8,128)}, f32[8,8,128]{2,1,0:T(8,128)}) custom-call(f32[4,2,3,9,9,128]{5,4,3,2,1,0:T(8,128)} %pad_maximum_fusion.extended_ref, f32[24,24]{1,0:T(8,128)} %stiffness_ref.1, f32[24,24]{1,0:T(8,128)} %mass_ref.1), custom_call_target="tpu_custom_call" | custom-call | flops 78643200 | bytes 1060864 | tf_op jit(solution)/shard_map/pallas_call | solution.py:186
  37.5 2.0 %fusion.82 = (f32[8,8,128]{2,1,0:T(8,128)S(1)}, pred[8,8,128]{2,1,0:T(8,128)(4,1)S(1)}) fusion(f32[8,8,128]{2,1,0:T(8,128)} %get-tuple-element.4, f32[12,10,128]{2,1,0:T(8,128)S(1)} %get-tuple-element.19, f32[12,12,132]{2,1,0:T(8,128)S(1)} %select_maximum_fusion.4, f32[2,8,128]{2,1,0:T(8,128)S(1)} %slice_bitcast_fusion, f32[8,8,128]{2,1,0:T(8,128)S(1)} %copy-done, ...), kind=kLoop, calls=%fused_computation.110 | loop fusion | flops 3039232 | bytes 6176768 | tf_op jit(solution)/shard_map/div | solution.py:227
  39.6 1.3 collective-permute-start.5
  40.9 6.7 %collective-permute-start.4 = (f32[2,8,128]{2,1,0:T(8,128)S(1)}, f32[2,8,128]{2,1,0:T(8,128)S(1)}, u32[]{:S(2)}, u32[]{:S(2)}) collective-permute-start(f32[2,8,128]{2,1,0:T(8,128)S(1)} %get-tuple-element.25), channel_id=1, source_target_pairs={{0,16},{16,32},{32,48},{48,64},{64,80},{80,96},{96,112},{112,128},... | collective-permute-start | bytes 24584 | tf_op jit(solution)/shard_map/ppermute | solution.py:27
  48.4 2.4 %collective-permute-start.6 = (f32[12,2,128]{2,1,0:T(2,128)S(1)}, f32[12,2,128]{2,1,0:T(2,128)S(1)}, u32[]{:S(2)}, u32[]{:S(2)}) collective-permute-start(f32[12,2,128]{2,1,0:T(2,128)S(1)} %get-tuple-element.16), channel_id=1, source_target_pairs={{0,1},{1,2},{2,3},{3,4},{4,5},{5,6},{6,7},{7,8},{8,9},{9,10},{10,1... | collective-permute-start | bytes 36872 | tf_op jit(solution)/shard_map/ppermute | solution.py:27
  50.8 6.3 %collective-permute-start.7 = (f32[12,2,128]{2,1,0:T(2,128)S(1)}, f32[12,2,128]{2,1,0:T(2,128)S(1)}, u32[]{:S(2)}, u32[]{:S(2)}) collective-permute-start(f32[12,2,128]{2,1,0:T(2,128)S(1)} %get-tuple-element.17), channel_id=1, source_target_pairs={{1,0},{2,1},{3,2},{4,3},{5,4},{6,5},{7,6},{8,7},{9,8},{10,9},{11,1... | collective-permute-start | bytes 36872 | tf_op jit(solution)/shard_map/ppermute | solution.py:29
  57.3 1.2 collective-permute-done.7
  59.3 0.9 fusion.4
  60.4 1.9 %collective-permute-start.8 = (f32[63,64]{0,1:T(8,128)S(1)}, f32[63,64]{0,1:T(8,128)S(1)}, u32[]{:S(2)}, u32[]{:S(2)}) collective-permute-start(f32[63,64]{0,1:T(8,128)S(1)} %reduce_sum.19), channel_id=1, source_target_pairs={{0,1},{1,0},{2,3},{3,2},{4,5},{5,4},{6,7},{7,6},{8,9},{9,8},{10,11... | collective-permute-start | bytes 48392 | tf_op jit(solution)/shard_map/ppermute | solution.py:66
  62.3 3.9 %collective-permute-done.8 = f32[63,64]{0,1:T(8,128)S(1)} collective-permute-done((f32[63,64]{0,1:T(8,128)S(1)}, f32[63,64]{0,1:T(8,128)S(1)}, u32[]{:S(2)}, u32[]{:S(2)}) %collective-permute-start.8) | collective-permute-done | bytes 16160 | tf_op jit(solution)/shard_map/ppermute | solution.py:66
  66.2 1.9 %collective-permute-start.9 = (f32[63,64]{0,1:T(8,128)S(1)}, f32[63,64]{0,1:T(8,128)S(1)}, u32[]{:S(2)}, u32[]{:S(2)}) collective-permute-start(f32[63,64]{0,1:T(8,128)S(1)} %add.1198), channel_id=1, source_target_pairs={{0,2},{1,3},{2,0},{3,1},{4,6},{5,7},{6,4},{7,5},{8,10},{9,11},{10,... | collective-permute-start | bytes 48392 | tf_op jit(solution)/shard_map/ppermute | solution.py:66
  68.1 4.8 %collective-permute-done.9 = f32[63,64]{0,1:T(8,128)S(1)} collective-permute-done((f32[63,64]{0,1:T(8,128)S(1)}, f32[63,64]{0,1:T(8,128)S(1)}, u32[]{:S(2)}, u32[]{:S(2)}) %collective-permute-start.9) | collective-permute-done | bytes 16160 | tf_op jit(solution)/shard_map/ppermute | solution.py:66
  72.9 3.1 %collective-permute-start.10 = (f32[63,64]{0,1:T(8,128)S(1)}, f32[63,64]{0,1:T(8,128)S(1)}, u32[]{:S(2)}, u32[]{:S(2)}) collective-permute-start(f32[63,64]{0,1:T(8,128)S(1)} %add.1199), channel_id=1, source_target_pairs={{0,4},{1,5},{2,6},{3,7},{4,0},{5,1},{6,2},{7,3},{8,12},{9,13},{10,... | collective-permute-start | bytes 48392 | tf_op jit(solution)/shard_map/ppermute | solution.py:66
  76.0 2.7 %collective-permute-done.10 = f32[63,64]{0,1:T(8,128)S(1)} collective-permute-done((f32[63,64]{0,1:T(8,128)S(1)}, f32[63,64]{0,1:T(8,128)S(1)}, u32[]{:S(2)}, u32[]{:S(2)}) %collective-permute-start.10) | collective-permute-done | bytes 16160 | tf_op jit(solution)/shard_map/ppermute | solution.py:66
  78.7 3.7 %collective-permute-start.11 = (f32[63,64]{0,1:T(8,128)S(1)}, f32[63,64]{0,1:T(8,128)S(1)}, u32[]{:S(2)}, u32[]{:S(2)}) collective-permute-start(f32[63,64]{0,1:T(8,128)S(1)} %add.1200), channel_id=1, source_target_pairs={{0,8},{1,9},{2,10},{3,11},{4,12},{5,13},{6,14},{7,15},{8,0},{9,1},... | collective-permute-start | bytes 48392 | tf_op jit(solution)/shard_map/ppermute | solution.py:66
  82.4 3.6 %collective-permute-done.11 = f32[63,64]{0,1:T(8,128)S(1)} collective-permute-done((f32[63,64]{0,1:T(8,128)S(1)}, f32[63,64]{0,1:T(8,128)S(1)}, u32[]{:S(2)}, u32[]{:S(2)}) %collective-permute-start.11) | collective-permute-done | bytes 16160 | tf_op jit(solution)/shard_map/ppermute | solution.py:66
  86.0 4.2 %collective-permute-start.12 = (f32[63,64]{0,1:T(8,128)S(1)}, f32[63,64]{0,1:T(8,128)S(1)}, u32[]{:S(2)}, u32[]{:S(2)}) collective-permute-start(f32[63,64]{0,1:T(8,128)S(1)} %add.1201), channel_id=1, source_target_pairs={{0,16},{16,0},{32,48},{48,32},{64,80},{80,64},{96,112},{112,96},{1... | collective-permute-start | bytes 48392 | tf_op jit(solution)/shard_map/ppermute | solution.py:66
  90.2 0.8 collective-permute-done.12
  91.1 13.8 %collective-permute-start.13 = (f32[63,64]{0,1:T(8,128)S(1)}, f32[63,64]{0,1:T(8,128)S(1)}, u32[]{:S(2)}, u32[]{:S(2)}) collective-permute-start(f32[63,64]{0,1:T(8,128)S(1)} %add.1202), channel_id=1, source_target_pairs={{0,32},{16,48},{32,0},{48,16},{64,96},{80,112},{96,64},{112,80},{1... | collective-permute-start | bytes 48392 | tf_op jit(solution)/shard_map/ppermute | solution.py:66
  104.9 1.9 %collective-permute-done.13 = f32[63,64]{0,1:T(8,128)S(1)} collective-permute-done((f32[63,64]{0,1:T(8,128)S(1)}, f32[63,64]{0,1:T(8,128)S(1)}, u32[]{:S(2)}, u32[]{:S(2)}) %collective-permute-start.13) | collective-permute-done | bytes 16160 | tf_op jit(solution)/shard_map/ppermute | solution.py:66
  106.8 8.5 %collective-permute-start.14 = (f32[63,64]{0,1:T(8,128)S(1)}, f32[63,64]{0,1:T(8,128)S(1)}, u32[]{:S(2)}, u32[]{:S(2)}) collective-permute-start(f32[63,64]{0,1:T(8,128)S(1)} %add.1203), channel_id=1, source_target_pairs={{0,64},{16,80},{32,96},{48,112},{64,0},{80,16},{96,32},{112,48},{1... | collective-permute-start | bytes 48392 | tf_op jit(solution)/shard_map/ppermute | solution.py:66
  115.3 1.9 %collective-permute-done.14 = f32[63,64]{0,1:T(8,128)S(1)} collective-permute-done((f32[63,64]{0,1:T(8,128)S(1)}, f32[63,64]{0,1:T(8,128)S(1)}, u32[]{:S(2)}, u32[]{:S(2)}) %collective-permute-start.14) | collective-permute-done | bytes 16160 | tf_op jit(solution)/shard_map/ppermute | solution.py:66
  117.2 6.2 %collective-permute-start.15 = (f32[63,64]{0,1:T(8,128)S(1)}, f32[63,64]{0,1:T(8,128)S(1)}, u32[]{:S(2)}, u32[]{:S(2)}) collective-permute-start(f32[63,64]{0,1:T(8,128)S(1)} %add.1204), channel_id=1, source_target_pairs={{0,128},{16,144},{32,160},{48,176},{64,192},{80,208},{96,224},{112... | collective-permute-start | bytes 48392 | tf_op jit(solution)/shard_map/ppermute | solution.py:66
  123.4 1.9 %collective-permute-done.15 = f32[63,64]{0,1:T(8,128)S(1)} collective-permute-done((f32[63,64]{0,1:T(8,128)S(1)}, f32[63,64]{0,1:T(8,128)S(1)}, u32[]{:S(2)}, u32[]{:S(2)}) %collective-permute-start.15) | collective-permute-done | bytes 16160 | tf_op jit(solution)/shard_map/ppermute | solution.py:66
  125.3 11.6 %collective-permute-start.16 = (f32[63,64]{0,1:T(8,128)S(1)}, f32[63,64]{0,1:T(8,128)S(1)}, u32[]{:S(2)}, u32[]{:S(2)}) collective-permute-start(f32[63,64]{0,1:T(8,128)S(1)} %add.1205), channel_id=1, source_target_pairs={{0,256},{16,272},{32,288},{48,304},{64,320},{80,336},{96,352},{112... | collective-permute-start | bytes 48392 | tf_op jit(solution)/shard_map/ppermute | solution.py:66
  136.9 1.9 %collective-permute-done.16 = f32[63,64]{0,1:T(8,128)S(1)} collective-permute-done((f32[63,64]{0,1:T(8,128)S(1)}, f32[63,64]{0,1:T(8,128)S(1)}, u32[]{:S(2)}, u32[]{:S(2)}) %collective-permute-start.16) | collective-permute-done | bytes 16160 | tf_op jit(solution)/shard_map/ppermute | solution.py:66
  (79 shorter events, 7.3 us)
Async XLA Ops:
  0.6 2.0 %copy-start = (f32[8,8,128]{2,1,0:T(8,128)S(1)}, f32[8,8,128]{2,1,0:T(8,128)}, u32[]{:S(2)}) copy-start(f32[8,8,128]{2,1,0:T(8,128)} %param.7) | copy-start | bytes 98308
  2.7 5.2 %collective-permute-start.1 = (f32[208,128]{1,0:T(8,128)S(1)}, f32[208,128]{1,0:T(8,128)S(1)}, u32[]{:S(2)}, u32[]{:S(2)}) collective-permute-start(f32[208,128]{1,0:T(8,128)S(1)} %pad_maximum_fusion.3), channel_id=1, source_target_pairs={{16,0},{32,16},{48,32},{64,48},{80,64},{96,80},{112,96},{128,112},... | collective-permute-start | bytes 319496 | tf_op jit(solution)/shard_map/ppermute | solution.py:46
  4.0 3.8 %collective-permute-start = (f32[2,8,128]{2,1,0:T(8,128)S(1)}, f32[2,8,128]{2,1,0:T(8,128)S(1)}, u32[]{:S(2)}, u32[]{:S(2)}) collective-permute-start(f32[2,8,128]{2,1,0:T(8,128)S(1)} %get-tuple-element.27), channel_id=1, source_target_pairs={{0,16},{16,32},{32,48},{48,64},{64,80},{80,96},{96,112},{112,128},... | collective-permute-start | bytes 24584 | tf_op jit(solution)/shard_map/ppermute | solution.py:50
  7.9 8.2 %collective-permute-start.3 = (f32[240,128]{1,0:T(8,128)S(1)}, f32[240,128]{1,0:T(8,128)S(1)}, u32[]{:S(2)}, u32[]{:S(2)}) collective-permute-start(f32[240,128]{1,0:T(8,128)S(1)} %pad_maximum_fusion.1), channel_id=1, source_target_pairs={{1,0},{2,1},{3,2},{4,3},{5,4},{6,5},{7,6},{8,7},{9,8},{10,9},{11,1... | collective-permute-start | bytes 368648 | tf_op jit(solution)/shard_map/ppermute | solution.py:46
  13.8 23.6 %collective-permute-start.2 = (f32[12,2,128]{2,1,0:T(2,128)S(1)}, f32[12,2,128]{2,1,0:T(2,128)S(1)}, u32[]{:S(2)}, u32[]{:S(2)}) collective-permute-start(f32[12,2,128]{2,1,0:T(2,128)S(1)} %get-tuple-element.20), channel_id=1, source_target_pairs={{0,1},{1,2},{2,3},{3,4},{4,5},{5,6},{6,7},{7,8},{8,9},{9,10},{10,1... | collective-permute-start | bytes 36872 | tf_op jit(solution)/shard_map/ppermute | solution.py:50
  17.5 20.0 %copy-start.2 = (s32[8,8,128]{2,1,0:T(8,128)S(1)}, s32[8,8,128]{2,1,0:T(8,128)}, u32[]{:S(2)}) copy-start(s32[8,8,128]{2,1,0:T(8,128)} %param.8) | copy-start | bytes 98308
  37.5 19.6 %copy-start.3 = (f32[63,64]{0,1:T(8,128)S(1)}, f32[63,64]{0,1:T(8,128)}, u32[]{:S(2)}) copy-start(f32[63,64]{0,1:T(8,128)} %constant.25.clone.1) | copy-start | bytes 48388
  39.6 8.0 %collective-permute-start.5 = (f32[2,8,128]{2,1,0:T(8,128)S(1)}, f32[2,8,128]{2,1,0:T(8,128)S(1)}, u32[]{:S(2)}, u32[]{:S(2)}) collective-permute-start(f32[2,8,128]{2,1,0:T(8,128)S(1)} %get-tuple-element.26), channel_id=1, source_target_pairs={{16,0},{32,16},{48,32},{64,48},{80,64},{96,80},{112,96},{128,112},... | collective-permute-start | bytes 24584 | tf_op jit(solution)/shard_map/ppermute | solution.py:29
  40.9 7.6 %collective-permute-start.4 = (f32[2,8,128]{2,1,0:T(8,128)S(1)}, f32[2,8,128]{2,1,0:T(8,128)S(1)}, u32[]{:S(2)}, u32[]{:S(2)}) collective-permute-start(f32[2,8,128]{2,1,0:T(8,128)S(1)} %get-tuple-element.25), channel_id=1, source_target_pairs={{0,16},{16,32},{32,48},{48,64},{64,80},{80,96},{96,112},{112,128},... | collective-permute-start | bytes 24584 | tf_op jit(solution)/shard_map/ppermute | solution.py:27
  48.4 8.8 %collective-permute-start.6 = (f32[12,2,128]{2,1,0:T(2,128)S(1)}, f32[12,2,128]{2,1,0:T(2,128)S(1)}, u32[]{:S(2)}, u32[]{:S(2)}) collective-permute-start(f32[12,2,128]{2,1,0:T(2,128)S(1)} %get-tuple-element.16), channel_id=1, source_target_pairs={{0,1},{1,2},{2,3},{3,4},{4,5},{5,6},{6,7},{7,8},{8,9},{9,10},{10,1... | collective-permute-start | bytes 36872 | tf_op jit(solution)/shard_map/ppermute | solution.py:27
  50.8 7.7 %collective-permute-start.7 = (f32[12,2,128]{2,1,0:T(2,128)S(1)}, f32[12,2,128]{2,1,0:T(2,128)S(1)}, u32[]{:S(2)}, u32[]{:S(2)}) collective-permute-start(f32[12,2,128]{2,1,0:T(2,128)S(1)} %get-tuple-element.17), channel_id=1, source_target_pairs={{1,0},{2,1},{3,2},{4,3},{5,4},{6,5},{7,6},{8,7},{9,8},{10,9},{11,1... | collective-permute-start | bytes 36872 | tf_op jit(solution)/shard_map/ppermute | solution.py:29
  58.7 78.2 %copy-start.4 = (f32[64]{0:T(128)S(1)}, f32[64]{0:T(128)}, u32[]{:S(2)}) copy-start(f32[64]{0:T(128)} %param.13) | copy-start | bytes 772
  59.3 82.7 %copy-start.1 = (f32[8,8,128]{2,1,0:T(8,128)}, f32[8,8,128]{2,1,0:T(8,128)S(1)}, u32[]{:S(2)}) copy-start(f32[8,8,128]{2,1,0:T(8,128)S(1)} %get-tuple-element.11) | copy-start | bytes 98308
  60.4 5.8 %collective-permute-start.8 = (f32[63,64]{0,1:T(8,128)S(1)}, f32[63,64]{0,1:T(8,128)S(1)}, u32[]{:S(2)}, u32[]{:S(2)}) collective-permute-start(f32[63,64]{0,1:T(8,128)S(1)} %reduce_sum.19), channel_id=1, source_target_pairs={{0,1},{1,0},{2,3},{3,2},{4,5},{5,4},{6,7},{7,6},{8,9},{9,8},{10,11... | collective-permute-start | bytes 48392 | tf_op jit(solution)/shard_map/ppermute | solution.py:66
  66.2 6.7 %collective-permute-start.9 = (f32[63,64]{0,1:T(8,128)S(1)}, f32[63,64]{0,1:T(8,128)S(1)}, u32[]{:S(2)}, u32[]{:S(2)}) collective-permute-start(f32[63,64]{0,1:T(8,128)S(1)} %add.1198), channel_id=1, source_target_pairs={{0,2},{1,3},{2,0},{3,1},{4,6},{5,7},{6,4},{7,5},{8,10},{9,11},{10,... | collective-permute-start | bytes 48392 | tf_op jit(solution)/shard_map/ppermute | solution.py:66
  72.9 5.8 %collective-permute-start.10 = (f32[63,64]{0,1:T(8,128)S(1)}, f32[63,64]{0,1:T(8,128)S(1)}, u32[]{:S(2)}, u32[]{:S(2)}) collective-permute-start(f32[63,64]{0,1:T(8,128)S(1)} %add.1199), channel_id=1, source_target_pairs={{0,4},{1,5},{2,6},{3,7},{4,0},{5,1},{6,2},{7,3},{8,12},{9,13},{10,... | collective-permute-start | bytes 48392 | tf_op jit(solution)/shard_map/ppermute | solution.py:66
  78.7 7.3 %collective-permute-start.11 = (f32[63,64]{0,1:T(8,128)S(1)}, f32[63,64]{0,1:T(8,128)S(1)}, u32[]{:S(2)}, u32[]{:S(2)}) collective-permute-start(f32[63,64]{0,1:T(8,128)S(1)} %add.1200), channel_id=1, source_target_pairs={{0,8},{1,9},{2,10},{3,11},{4,12},{5,13},{6,14},{7,15},{8,0},{9,1},... | collective-permute-start | bytes 48392 | tf_op jit(solution)/shard_map/ppermute | solution.py:66
  86.0 5.0 %collective-permute-start.12 = (f32[63,64]{0,1:T(8,128)S(1)}, f32[63,64]{0,1:T(8,128)S(1)}, u32[]{:S(2)}, u32[]{:S(2)}) collective-permute-start(f32[63,64]{0,1:T(8,128)S(1)} %add.1201), channel_id=1, source_target_pairs={{0,16},{16,0},{32,48},{48,32},{64,80},{80,64},{96,112},{112,96},{1... | collective-permute-start | bytes 48392 | tf_op jit(solution)/shard_map/ppermute | solution.py:66
  91.1 15.7 %collective-permute-start.13 = (f32[63,64]{0,1:T(8,128)S(1)}, f32[63,64]{0,1:T(8,128)S(1)}, u32[]{:S(2)}, u32[]{:S(2)}) collective-permute-start(f32[63,64]{0,1:T(8,128)S(1)} %add.1202), channel_id=1, source_target_pairs={{0,32},{16,48},{32,0},{48,16},{64,96},{80,112},{96,64},{112,80},{1... | collective-permute-start | bytes 48392 | tf_op jit(solution)/shard_map/ppermute | solution.py:66
  106.8 10.4 %collective-permute-start.14 = (f32[63,64]{0,1:T(8,128)S(1)}, f32[63,64]{0,1:T(8,128)S(1)}, u32[]{:S(2)}, u32[]{:S(2)}) collective-permute-start(f32[63,64]{0,1:T(8,128)S(1)} %add.1203), channel_id=1, source_target_pairs={{0,64},{16,80},{32,96},{48,112},{64,0},{80,16},{96,32},{112,48},{1... | collective-permute-start | bytes 48392 | tf_op jit(solution)/shard_map/ppermute | solution.py:66
  117.2 8.1 %collective-permute-start.15 = (f32[63,64]{0,1:T(8,128)S(1)}, f32[63,64]{0,1:T(8,128)S(1)}, u32[]{:S(2)}, u32[]{:S(2)}) collective-permute-start(f32[63,64]{0,1:T(8,128)S(1)} %add.1204), channel_id=1, source_target_pairs={{0,128},{16,144},{32,160},{48,176},{64,192},{80,208},{96,224},{112... | collective-permute-start | bytes 48392 | tf_op jit(solution)/shard_map/ppermute | solution.py:66
  125.3 13.5 %collective-permute-start.16 = (f32[63,64]{0,1:T(8,128)S(1)}, f32[63,64]{0,1:T(8,128)S(1)}, u32[]{:S(2)}, u32[]{:S(2)}) collective-permute-start(f32[63,64]{0,1:T(8,128)S(1)} %add.1205), channel_id=1, source_target_pairs={{0,256},{16,272},{32,288},{48,304},{64,320},{80,336},{96,352},{112... | collective-permute-start | bytes 48392 | tf_op jit(solution)/shard_map/ppermute | solution.py:66

commit v5 on v4

--- a/solution.py
+++ b/solution.py
@@ -177,26 +177,82 @@
     lax.fori_loop(0, cells_x, over_x, 0)
 
 
+def mxu_energy_kernel(extended_ref, coupling_ref, stiff_out, mass_out, adjoint_rows, products):
+    pair_count = extended_ref.shape[0]
+    cells_x, cells_y, cells_z = stiff_out.shape
+    dofs = 3 * len(CORNERS)
+    lane = lax.broadcasted_iota(jnp.int32, (cells_y, cells_z), 1)
+    inside = lane < cells_z - 1
+    stiff_out[...] = jnp.zeros(stiff_out.shape, jnp.float32)
+    mass_out[...] = jnp.zeros(mass_out.shape, jnp.float32)
+
+    def node_view(pair, member, row, x):
+        corner_x, corner_y, corner_z = CORNERS[row // 3]
+        value = extended_ref[pair, member, row % 3, x + corner_x, pl.ds(corner_y, cells_y), :]
+        if corner_z:
+            value = jnp.where(inside, pltpu.roll(value, cells_z - 1, 1), 0.0)
+        return value
+
+    def over_pairs(pair, carry):
+        def gather_x(x, inner):
+            columns = pl.ds(pl.multiple_of(x * cells_z, cells_z), cells_z)
+            for row in range(dofs):
+                adjoint_rows[pl.ds(row * cells_y, cells_y), columns] = node_view(pair, 1, row, x)
+            return inner
+
+        lax.fori_loop(0, cells_x, gather_x, 0)
+        products[...] = jnp.dot(
+            coupling_ref[...],
+            adjoint_rows[...],
+            precision=lax.Precision.HIGHEST,
+            preferred_element_type=jnp.float32,
+        )
+
+        def reduce_x(x, inner):
+            columns = pl.ds(pl.multiple_of(x * cells_z, cells_z), cells_z)
+            stiff_sum = stiff_out[x]
+            mass_sum = mass_out[x]
+            for row in range(dofs):
+                state = node_view(pair, 0, row, x)
+                stiff_sum = stiff_sum + state * products[pl.ds(row * cells_y, cells_y), columns]
+                mass_sum = mass_sum + state * products[pl.ds((dofs + row) * cells_y, cells_y), columns]
+            stiff_out[x] = stiff_sum
+            mass_out[x] = mass_sum
+            return inner
+
+        lax.fori_loop(0, cells_x, reduce_x, 0)
+        return carry
+
+    lax.fori_loop(0, pair_count, over_pairs, 0)
+
+
 def element_energies(extended, stiffness, mass_matrix):
     pair_count = extended.shape[0]
     cells = (extended.shape[3] - 1, extended.shape[4] - 1, extended.shape[5])
     voxels = cells[0] * cells[1] * cells[2]
+    dofs = stiffness.shape[0]
+    coupling = jnp.kron(
+        jnp.concatenate([stiffness, mass_matrix], axis=0), jnp.eye(cells[1], dtype=jnp.float32)
+    )
     vmem = pl.BlockSpec(memory_space=pltpu.VMEM)
-    smem = pl.BlockSpec(memory_space=pltpu.SMEM)
     return pl.pallas_call(
-        energy_kernel,
+        mxu_energy_kernel,
         out_shape=(
             jax.ShapeDtypeStruct(cells, jnp.float32),
             jax.ShapeDtypeStruct(cells, jnp.float32),
         ),
-        in_specs=[vmem, smem, smem],
+        in_specs=[vmem, vmem],
         out_specs=(vmem, vmem),
+        scratch_shapes=[
+            pltpu.VMEM((dofs * cells[1], cells[0] * cells[2]), jnp.float32),
+            pltpu.VMEM((2 * dofs * cells[1], cells[0] * cells[2]), jnp.float32),
+        ],
         cost_estimate=pl.CostEstimate(
-            flops=pair_count * voxels * 2400,
-            bytes_accessed=extended.size * 4 + 2 * voxels * 4,
+            flops=pair_count * (2 * coupling.size * cells[0] * cells[2] + 4 * dofs * voxels),
+            bytes_accessed=extended.size * 4 + coupling.size * 4 + 2 * voxels * 4,
             transcendentals=0,
         ),
-    )(extended, stiffness, mass_matrix)
+    )(extended, coupling)
 
 
 def shards(design, passive, basis_pairs, supports, stiffness, mass_matrix, volume_fraction):

time: 144 us -> 144 us (level)
  Pallas kernels: 19.8 us -> 13.4 us
  local copies, waits for them, and re-layouts: 0.96 us -> 6.65 us
  other arithmetic: 10 us -> 12.5 us
    pallas_call x1, Pallas kernels: 19.8 us -> 13.4 us  [element_energies(): pl.pallas_call(mxu_energy_kernel, out_shape=(jax.ShapeDtypeStruct(cells,...]
    mul x0 -> x2, local copies, waits for them, and re-layouts: none -> 4.89 us  [element_energies(): jnp.kron(jnp.concatenate([stiffness, mass_matrix], axis=0), jnp.eye(cells...]
    mul x0 -> x1, other arithmetic: none -> 2.5 us  [element_energies(): jnp.kron(jnp.concatenate([stiffness, mass_matrix], axis=0), jnp.eye(cells...]
    ppermute x9, starting transfers between devices: 54.9 us -> 53.5 us  [butterfly_sum(): lax.ppermute(value, axis, [(i, i ^ stride) for i in range(count)])]
  transfers between devices with their start and end apart: 17 -> 17, of which waited for: 13 -> 12; matrix products, arithmetic and copies ran while one was open for 1% -> 6% of each run, Pallas kernels for 14% -> 9%
where the time goes in v5:
time: 144 us; the launch traced here: 142 us
  starting transfers between devices  82.3 us (57%)
  waiting for transfers between devices  26 us (18%)
  Pallas kernels  13.4 us (9%)
  other arithmetic  12.5 us (9%)
  local copies, waits for them, and re-layouts  6.65 us (5%)
    ppermute x9, starting transfers between devices, butterfly_sum(): lax.ppermute(value, axis, [(i, i ^ stride) for i in range(count)])  53.5 us
    ppermute x9, waiting for transfers between devices, butterfly_sum(): lax.ppermute(value, axis, [(i, i ^ stride) for i in range(count)])  23.5 us
    pallas_call x1, Pallas kernels, element_energies(): pl.pallas_call(mxu_energy_kernel, out_shape=(jax.ShapeDtypeStruct(cells,...  13.4 us
    ppermute x2, starting transfers between devices, with_halo(): lax.ppermute(tail, axis, [(i, (i + 1) % count) for i in range(ends)])  8.69 us
    ppermute x2, starting transfers between devices, with_halo(): lax.ppermute(head, axis, [((i + 1) % count, i) for i in range(ends)])  8.09 us
    ppermute x2, starting transfers between devices, front_exchange(): lax.ppermute(packed, axis, [((i + 1) % count, i) for i in range(ends)])  7.07 us
    ppermute x2, starting transfers between devices, front_exchange(): tail = lax.ppermute(tail, axis, [(i, (i + 1) % count) for i in range(ends)])  4.95 us
    mul x2, local copies, waits for them, and re-layouts, element_energies(): jnp.kron(jnp.concatenate([stiffness, mass_matrix], axis=0), jnp.eye(cells...  4.89 us
  transfers between devices with their start and end apart: 17, of which 12 were waited for; matrix products, arithmetic and copies ran while one was open for 6% of the time, Pallas kernels for 9%

profile of v5, /device:TPU:6, one launch (start us, length us, event | category | flops | bytes accessed | tf_op | source)
XLA Modules:
  0.0 142.1 jit_solution(13093488506283533410)
XLA Ops:
  1.4 1.2 broadcast_multiply_fusion.1
  3.4 1.3 collective-permute-start.1
  4.7 3.0 %collective-permute-start = (f32[2,8,128]{2,1,0:T(8,128)S(1)}, f32[2,8,128]{2,1,0:T(8,128)S(1)}, u32[]{:S(2)}, u32[]{:S(2)}) collective-permute-start(f32[2,8,128]{2,1,0:T(8,128)S(1)} %get-tuple-element.27), channel_id=1, source_target_pairs={{0,16},{16,32},{32,48},{48,64},{64,80},{80,96},{96,112},{112,128},... | collective-permute-start | bytes 24584 | tf_op jit(solution)/shard_map/ppermute | solution.py:50
  7.8 2.5 %broadcast_multiply_fusion = f32[48,8,24,8]{1,0,3,2:T(8,128)} fusion(f32[8,8]{0,1:T(8,128)S(1)} %fusion.292, f32[48,24]{0,1:T(8,128)S(1)} %copy.26), kind=kLoop, calls=%fused_computation | loop fusion | flops 73728 | bytes 299776 | tf_op jit(solution)/shard_map/jit(kron)/mul | solution.py:234
  10.6 4.0 %mul.1113 = f32[384,192]{0,1:T(8,128)S(1)} reshape(f32[48,8,24,8]{1,0,3,2:T(8,128)} %broadcast_multiply_fusion) | data formatting | bytes 589824 | tf_op jit(solution)/shard_map/jit(kron)/mul | solution.py:234
  15.7 5.8 %collective-permute-start.3 = (f32[240,128]{1,0:T(8,128)S(1)}, f32[240,128]{1,0:T(8,128)S(1)}, u32[]{:S(2)}, u32[]{:S(2)}) collective-permute-start(f32[240,128]{1,0:T(8,128)S(1)} %pad_maximum_fusion.1), channel_id=1, source_target_pairs={{1,0},{2,1},{3,2},{4,3},{5,4},{6,5},{7,6},{8,7},{9,8},{10,9},{11,1... | collective-permute-start | bytes 368648 | tf_op jit(solution)/shard_map/ppermute | solution.py:46
  21.5 1.9 %collective-permute-start.2 = (f32[12,2,128]{2,1,0:T(2,128)S(1)}, f32[12,2,128]{2,1,0:T(2,128)S(1)}, u32[]{:S(2)}, u32[]{:S(2)}) collective-permute-start(f32[12,2,128]{2,1,0:T(2,128)S(1)} %get-tuple-element.20), channel_id=1, source_target_pairs={{0,1},{1,2},{2,3},{3,4},{4,5},{5,6},{6,7},{7,8},{8,9},{9,10},{10,1... | collective-permute-start | bytes 36872 | tf_op jit(solution)/shard_map/ppermute | solution.py:50
  23.9 1.4 pad_maximum_fusion.extended_ref
  25.2 13.4 %shard_map.86 = (f32[8,8,128]{2,1,0:T(8,128)}, f32[8,8,128]{2,1,0:T(8,128)}) custom-call(f32[4,2,3,9,9,128]{5,4,3,2,1,0:T(8,128)} %pad_maximum_fusion.extended_ref, f32[384,192]{1,0:T(8,128)} %copy.27.coupling_ref), custom_call_target="tpu_custom_call" | custom-call | flops 607125504 | bytes 1355776 | tf_op jit(solution)/shard_map/pallas_call | solution.py:238
  38.9 2.0 %fusion.82 = (f32[8,8,128]{2,1,0:T(8,128)S(1)}, pred[8,8,128]{2,1,0:T(8,128)(4,1)S(1)}) fusion(f32[8,8,128]{2,1,0:T(8,128)} %get-tuple-element.4, f32[12,10,128]{2,1,0:T(8,128)S(1)} %get-tuple-element.19, f32[12,12,132]{2,1,0:T(8,128)S(1)} %select_maximum_fusion.4, f32[2,8,128]{2,1,0:T(8,128)S(1)} %slice_bitcast_fusion, f32[8,8,128]{2,1,0:T(8,128)S(1)} %copy-done, ...), kind=kLoop, calls=%fused_computation.111 | loop fusion | flops 3039232 | bytes 6176768 | tf_op jit(solution)/shard_map/div | solution.py:283
  40.9 1.3 collective-permute-start.5
  42.2 6.8 %collective-permute-start.4 = (f32[2,8,128]{2,1,0:T(8,128)S(1)}, f32[2,8,128]{2,1,0:T(8,128)S(1)}, u32[]{:S(2)}, u32[]{:S(2)}) collective-permute-start(f32[2,8,128]{2,1,0:T(8,128)S(1)} %get-tuple-element.25), channel_id=1, source_target_pairs={{0,16},{16,32},{32,48},{48,64},{64,80},{80,96},{96,112},{112,128},... | collective-permute-start | bytes 24584 | tf_op jit(solution)/shard_map/ppermute | solution.py:27
  49.8 1.9 %collective-permute-start.6 = (f32[12,2,128]{2,1,0:T(2,128)S(1)}, f32[12,2,128]{2,1,0:T(2,128)S(1)}, u32[]{:S(2)}, u32[]{:S(2)}) collective-permute-start(f32[12,2,128]{2,1,0:T(2,128)S(1)} %get-tuple-element.16), channel_id=1, source_target_pairs={{0,1},{1,2},{2,3},{3,4},{4,5},{5,6},{6,7},{7,8},{8,9},{9,10},{10,1... | collective-permute-start | bytes 36872 | tf_op jit(solution)/shard_map/ppermute | solution.py:27
  51.8 6.8 %collective-permute-start.7 = (f32[12,2,128]{2,1,0:T(2,128)S(1)}, f32[12,2,128]{2,1,0:T(2,128)S(1)}, u32[]{:S(2)}, u32[]{:S(2)}) collective-permute-start(f32[12,2,128]{2,1,0:T(2,128)S(1)} %get-tuple-element.17), channel_id=1, source_target_pairs={{1,0},{2,1},{3,2},{4,3},{5,4},{6,5},{7,6},{8,7},{9,8},{10,9},{11,1... | collective-permute-start | bytes 36872 | tf_op jit(solution)/shard_map/ppermute | solution.py:29
  58.7 1.2 collective-permute-done.7
  61.9 1.9 %collective-permute-start.8 = (f32[63,64]{0,1:T(8,128)S(1)}, f32[63,64]{0,1:T(8,128)S(1)}, u32[]{:S(2)}, u32[]{:S(2)}) collective-permute-start(f32[63,64]{0,1:T(8,128)S(1)} %reduce_sum.19), channel_id=1, source_target_pairs={{0,1},{1,0},{2,3},{3,2},{4,5},{5,4},{6,7},{7,6},{8,9},{9,8},{10,11... | collective-permute-start | bytes 48392 | tf_op jit(solution)/shard_map/ppermute | solution.py:66
  63.8 3.9 %collective-permute-done.8 = f32[63,64]{0,1:T(8,128)S(1)} collective-permute-done((f32[63,64]{0,1:T(8,128)S(1)}, f32[63,64]{0,1:T(8,128)S(1)}, u32[]{:S(2)}, u32[]{:S(2)}) %collective-permute-start.8) | collective-permute-done | bytes 16160 | tf_op jit(solution)/shard_map/ppermute | solution.py:66
  67.7 1.9 %collective-permute-start.9 = (f32[63,64]{0,1:T(8,128)S(1)}, f32[63,64]{0,1:T(8,128)S(1)}, u32[]{:S(2)}, u32[]{:S(2)}) collective-permute-start(f32[63,64]{0,1:T(8,128)S(1)} %add.1198), channel_id=1, source_target_pairs={{0,2},{1,3},{2,0},{3,1},{4,6},{5,7},{6,4},{7,5},{8,10},{9,11},{10,... | collective-permute-start | bytes 48392 | tf_op jit(solution)/shard_map/ppermute | solution.py:66
  69.6 4.8 %collective-permute-done.9 = f32[63,64]{0,1:T(8,128)S(1)} collective-permute-done((f32[63,64]{0,1:T(8,128)S(1)}, f32[63,64]{0,1:T(8,128)S(1)}, u32[]{:S(2)}, u32[]{:S(2)}) %collective-permute-start.9) | collective-permute-done | bytes 16160 | tf_op jit(solution)/shard_map/ppermute | solution.py:66
  74.4 3.1 %collective-permute-start.10 = (f32[63,64]{0,1:T(8,128)S(1)}, f32[63,64]{0,1:T(8,128)S(1)}, u32[]{:S(2)}, u32[]{:S(2)}) collective-permute-start(f32[63,64]{0,1:T(8,128)S(1)} %add.1199), channel_id=1, source_target_pairs={{0,4},{1,5},{2,6},{3,7},{4,0},{5,1},{6,2},{7,3},{8,12},{9,13},{10,... | collective-permute-start | bytes 48392 | tf_op jit(solution)/shard_map/ppermute | solution.py:66
  77.5 2.7 %collective-permute-done.10 = f32[63,64]{0,1:T(8,128)S(1)} collective-permute-done((f32[63,64]{0,1:T(8,128)S(1)}, f32[63,64]{0,1:T(8,128)S(1)}, u32[]{:S(2)}, u32[]{:S(2)}) %collective-permute-start.10) | collective-permute-done | bytes 16160 | tf_op jit(solution)/shard_map/ppermute | solution.py:66
  80.2 3.6 %collective-permute-start.11 = (f32[63,64]{0,1:T(8,128)S(1)}, f32[63,64]{0,1:T(8,128)S(1)}, u32[]{:S(2)}, u32[]{:S(2)}) collective-permute-start(f32[63,64]{0,1:T(8,128)S(1)} %add.1200), channel_id=1, source_target_pairs={{0,8},{1,9},{2,10},{3,11},{4,12},{5,13},{6,14},{7,15},{8,0},{9,1},... | collective-permute-start | bytes 48392 | tf_op jit(solution)/shard_map/ppermute | solution.py:66
  83.8 3.7 %collective-permute-done.11 = f32[63,64]{0,1:T(8,128)S(1)} collective-permute-done((f32[63,64]{0,1:T(8,128)S(1)}, f32[63,64]{0,1:T(8,128)S(1)}, u32[]{:S(2)}, u32[]{:S(2)}) %collective-permute-start.11) | collective-permute-done | bytes 16160 | tf_op jit(solution)/shard_map/ppermute | solution.py:66
  87.5 2.1 %collective-permute-start.12 = (f32[63,64]{0,1:T(8,128)S(1)}, f32[63,64]{0,1:T(8,128)S(1)}, u32[]{:S(2)}, u32[]{:S(2)}) collective-permute-start(f32[63,64]{0,1:T(8,128)S(1)} %add.1201), channel_id=1, source_target_pairs={{0,16},{16,0},{32,48},{48,32},{64,80},{80,64},{96,112},{112,96},{1... | collective-permute-start | bytes 48392 | tf_op jit(solution)/shard_map/ppermute | solution.py:66
  90.6 13.6 %collective-permute-start.13 = (f32[63,64]{0,1:T(8,128)S(1)}, f32[63,64]{0,1:T(8,128)S(1)}, u32[]{:S(2)}, u32[]{:S(2)}) collective-permute-start(f32[63,64]{0,1:T(8,128)S(1)} %add.1202), channel_id=1, source_target_pairs={{0,32},{16,48},{32,0},{48,16},{64,96},{80,112},{96,64},{112,80},{1... | collective-permute-start | bytes 48392 | tf_op jit(solution)/shard_map/ppermute | solution.py:66
  104.2 1.9 %collective-permute-done.13 = f32[63,64]{0,1:T(8,128)S(1)} collective-permute-done((f32[63,64]{0,1:T(8,128)S(1)}, f32[63,64]{0,1:T(8,128)S(1)}, u32[]{:S(2)}, u32[]{:S(2)}) %collective-permute-start.13) | collective-permute-done | bytes 16160 | tf_op jit(solution)/shard_map/ppermute | solution.py:66
  106.1 8.9 %collective-permute-start.14 = (f32[63,64]{0,1:T(8,128)S(1)}, f32[63,64]{0,1:T(8,128)S(1)}, u32[]{:S(2)}, u32[]{:S(2)}) collective-permute-start(f32[63,64]{0,1:T(8,128)S(1)} %add.1203), channel_id=1, source_target_pairs={{0,64},{16,80},{32,96},{48,112},{64,0},{80,16},{96,32},{112,48},{1... | collective-permute-start | bytes 48392 | tf_op jit(solution)/shard_map/ppermute | solution.py:66
  115.0 1.9 %collective-permute-done.14 = f32[63,64]{0,1:T(8,128)S(1)} collective-permute-done((f32[63,64]{0,1:T(8,128)S(1)}, f32[63,64]{0,1:T(8,128)S(1)}, u32[]{:S(2)}, u32[]{:S(2)}) %collective-permute-start.14) | collective-permute-done | bytes 16160 | tf_op jit(solution)/shard_map/ppermute | solution.py:66
  116.9 6.2 %collective-permute-start.15 = (f32[63,64]{0,1:T(8,128)S(1)}, f32[63,64]{0,1:T(8,128)S(1)}, u32[]{:S(2)}, u32[]{:S(2)}) collective-permute-start(f32[63,64]{0,1:T(8,128)S(1)} %add.1204), channel_id=1, source_target_pairs={{0,128},{16,144},{32,160},{48,176},{64,192},{80,208},{96,224},{112... | collective-permute-start | bytes 48392 | tf_op jit(solution)/shard_map/ppermute | solution.py:66
  123.1 1.9 %collective-permute-done.15 = f32[63,64]{0,1:T(8,128)S(1)} collective-permute-done((f32[63,64]{0,1:T(8,128)S(1)}, f32[63,64]{0,1:T(8,128)S(1)}, u32[]{:S(2)}, u32[]{:S(2)}) %collective-permute-start.15) | collective-permute-done | bytes 16160 | tf_op jit(solution)/shard_map/ppermute | solution.py:66
  125.0 12.1 %collective-permute-start.16 = (f32[63,64]{0,1:T(8,128)S(1)}, f32[63,64]{0,1:T(8,128)S(1)}, u32[]{:S(2)}, u32[]{:S(2)}) collective-permute-start(f32[63,64]{0,1:T(8,128)S(1)} %add.1205), channel_id=1, source_target_pairs={{0,256},{16,272},{32,288},{48,304},{64,320},{80,336},{96,352},{112... | collective-permute-start | bytes 48392 | tf_op jit(solution)/shard_map/ppermute | solution.py:66
  137.1 1.9 %collective-permute-done.16 = f32[63,64]{0,1:T(8,128)S(1)} collective-permute-done((f32[63,64]{0,1:T(8,128)S(1)}, f32[63,64]{0,1:T(8,128)S(1)}, u32[]{:S(2)}, u32[]{:S(2)}) %collective-permute-start.16) | collective-permute-done | bytes 16160 | tf_op jit(solution)/shard_map/ppermute | solution.py:66
  (89 shorter events, 10.4 us)
Async XLA Ops:
  0.6 7.1 %copy-start.4 = (f32[24,24]{1,0:T(8,128)S(1)}, f32[24,24]{1,0:T(8,128)}, u32[]{:S(2)}) copy-start(f32[24,24]{1,0:T(8,128)} %param.12) | copy-start | bytes 6916
  0.6 7.1 %copy-start.5 = (f32[24,24]{1,0:T(8,128)S(1)}, f32[24,24]{1,0:T(8,128)}, u32[]{:S(2)}) copy-start(f32[24,24]{1,0:T(8,128)} %param.11) | copy-start | bytes 6916
  3.4 12.1 %collective-permute-start.1 = (f32[208,128]{1,0:T(8,128)S(1)}, f32[208,128]{1,0:T(8,128)S(1)}, u32[]{:S(2)}, u32[]{:S(2)}) collective-permute-start(f32[208,128]{1,0:T(8,128)S(1)} %pad_maximum_fusion.3), channel_id=1, source_target_pairs={{16,0},{32,16},{48,32},{64,48},{80,64},{96,80},{112,96},{128,112},... | collective-permute-start | bytes 319496 | tf_op jit(solution)/shard_map/ppermute | solution.py:46
  4.7 10.8 %collective-permute-start = (f32[2,8,128]{2,1,0:T(8,128)S(1)}, f32[2,8,128]{2,1,0:T(8,128)S(1)}, u32[]{:S(2)}, u32[]{:S(2)}) collective-permute-start(f32[2,8,128]{2,1,0:T(8,128)S(1)} %get-tuple-element.27), channel_id=1, source_target_pairs={{0,16},{16,32},{32,48},{48,64},{64,80},{80,96},{96,112},{112,128},... | collective-permute-start | bytes 24584 | tf_op jit(solution)/shard_map/ppermute | solution.py:50
  10.6 5.0 %copy-start = (f32[8,8,128]{2,1,0:T(8,128)S(1)}, f32[8,8,128]{2,1,0:T(8,128)}, u32[]{:S(2)}) copy-start(f32[8,8,128]{2,1,0:T(8,128)} %param.7) | copy-start | bytes 98308
  15.7 8.2 %collective-permute-start.3 = (f32[240,128]{1,0:T(8,128)S(1)}, f32[240,128]{1,0:T(8,128)S(1)}, u32[]{:S(2)}, u32[]{:S(2)}) collective-permute-start(f32[240,128]{1,0:T(8,128)S(1)} %pad_maximum_fusion.1), channel_id=1, source_target_pairs={{1,0},{2,1},{3,2},{4,3},{5,4},{6,5},{7,6},{8,7},{9,8},{10,9},{11,1... | collective-permute-start | bytes 368648 | tf_op jit(solution)/shard_map/ppermute | solution.py:46
  21.5 17.2 %collective-permute-start.2 = (f32[12,2,128]{2,1,0:T(2,128)S(1)}, f32[12,2,128]{2,1,0:T(2,128)S(1)}, u32[]{:S(2)}, u32[]{:S(2)}) collective-permute-start(f32[12,2,128]{2,1,0:T(2,128)S(1)} %get-tuple-element.20), channel_id=1, source_target_pairs={{0,1},{1,2},{2,3},{3,4},{4,5},{5,6},{6,7},{7,8},{8,9},{9,10},{10,1... | collective-permute-start | bytes 36872 | tf_op jit(solution)/shard_map/ppermute | solution.py:50
  25.2 13.7 %copy-start.2 = (s32[8,8,128]{2,1,0:T(8,128)S(1)}, s32[8,8,128]{2,1,0:T(8,128)}, u32[]{:S(2)}) copy-start(s32[8,8,128]{2,1,0:T(8,128)} %param.8) | copy-start | bytes 98308
  38.9 19.7 %copy-start.3 = (f32[63,64]{0,1:T(8,128)S(1)}, f32[63,64]{0,1:T(8,128)}, u32[]{:S(2)}) copy-start(f32[63,64]{0,1:T(8,128)} %constant.25.clone.1) | copy-start | bytes 48388
  40.9 8.1 %collective-permute-start.5 = (f32[2,8,128]{2,1,0:T(8,128)S(1)}, f32[2,8,128]{2,1,0:T(8,128)S(1)}, u32[]{:S(2)}, u32[]{:S(2)}) collective-permute-start(f32[2,8,128]{2,1,0:T(8,128)S(1)} %get-tuple-element.26), channel_id=1, source_target_pairs={{16,0},{32,16},{48,32},{64,48},{80,64},{96,80},{112,96},{128,112},... | collective-permute-start | bytes 24584 | tf_op jit(solution)/shard_map/ppermute | solution.py:29
  42.2 7.6 %collective-permute-start.4 = (f32[2,8,128]{2,1,0:T(8,128)S(1)}, f32[2,8,128]{2,1,0:T(8,128)S(1)}, u32[]{:S(2)}, u32[]{:S(2)}) collective-permute-start(f32[2,8,128]{2,1,0:T(8,128)S(1)} %get-tuple-element.25), channel_id=1, source_target_pairs={{0,16},{16,32},{32,48},{48,64},{64,80},{80,96},{96,112},{112,128},... | collective-permute-start | bytes 24584 | tf_op jit(solution)/shard_map/ppermute | solution.py:27
  49.8 8.9 %collective-permute-start.6 = (f32[12,2,128]{2,1,0:T(2,128)S(1)}, f32[12,2,128]{2,1,0:T(2,128)S(1)}, u32[]{:S(2)}, u32[]{:S(2)}) collective-permute-start(f32[12,2,128]{2,1,0:T(2,128)S(1)} %get-tuple-element.16), channel_id=1, source_target_pairs={{0,1},{1,2},{2,3},{3,4},{4,5},{5,6},{6,7},{7,8},{8,9},{9,10},{10,1... | collective-permute-start | bytes 36872 | tf_op jit(solution)/shard_map/ppermute | solution.py:27
  51.8 8.2 %collective-permute-start.7 = (f32[12,2,128]{2,1,0:T(2,128)S(1)}, f32[12,2,128]{2,1,0:T(2,128)S(1)}, u32[]{:S(2)}, u32[]{:S(2)}) collective-permute-start(f32[12,2,128]{2,1,0:T(2,128)S(1)} %get-tuple-element.17), channel_id=1, source_target_pairs={{1,0},{2,1},{3,2},{4,3},{5,4},{6,5},{7,6},{8,7},{9,8},{10,9},{11,1... | collective-permute-start | bytes 36872 | tf_op jit(solution)/shard_map/ppermute | solution.py:29
  60.1 76.9 %copy-start.6 = (f32[64]{0:T(128)S(1)}, f32[64]{0:T(128)}, u32[]{:S(2)}) copy-start(f32[64]{0:T(128)} %param.13) | copy-start | bytes 772
  60.7 81.4 %copy-start.1 = (f32[8,8,128]{2,1,0:T(8,128)}, f32[8,8,128]{2,1,0:T(8,128)S(1)}, u32[]{:S(2)}) copy-start(f32[8,8,128]{2,1,0:T(8,128)S(1)} %get-tuple-element.11) | copy-start | bytes 98308
  61.9 5.8 %collective-permute-start.8 = (f32[63,64]{0,1:T(8,128)S(1)}, f32[63,64]{0,1:T(8,128)S(1)}, u32[]{:S(2)}, u32[]{:S(2)}) collective-permute-start(f32[63,64]{0,1:T(8,128)S(1)} %reduce_sum.19), channel_id=1, source_target_pairs={{0,1},{1,0},{2,3},{3,2},{4,5},{5,4},{6,7},{7,6},{8,9},{9,8},{10,11... | collective-permute-start | bytes 48392 | tf_op jit(solution)/shard_map/ppermute | solution.py:66
  67.7 6.7 %collective-permute-start.9 = (f32[63,64]{0,1:T(8,128)S(1)}, f32[63,64]{0,1:T(8,128)S(1)}, u32[]{:S(2)}, u32[]{:S(2)}) collective-permute-start(f32[63,64]{0,1:T(8,128)S(1)} %add.1198), channel_id=1, source_target_pairs={{0,2},{1,3},{2,0},{3,1},{4,6},{5,7},{6,4},{7,5},{8,10},{9,11},{10,... | collective-permute-start | bytes 48392 | tf_op jit(solution)/shard_map/ppermute | solution.py:66
  74.4 5.8 %collective-permute-start.10 = (f32[63,64]{0,1:T(8,128)S(1)}, f32[63,64]{0,1:T(8,128)S(1)}, u32[]{:S(2)}, u32[]{:S(2)}) collective-permute-start(f32[63,64]{0,1:T(8,128)S(1)} %add.1199), channel_id=1, source_target_pairs={{0,4},{1,5},{2,6},{3,7},{4,0},{5,1},{6,2},{7,3},{8,12},{9,13},{10,... | collective-permute-start | bytes 48392 | tf_op jit(solution)/shard_map/ppermute | solution.py:66
  80.2 7.3 %collective-permute-start.11 = (f32[63,64]{0,1:T(8,128)S(1)}, f32[63,64]{0,1:T(8,128)S(1)}, u32[]{:S(2)}, u32[]{:S(2)}) collective-permute-start(f32[63,64]{0,1:T(8,128)S(1)} %add.1200), channel_id=1, source_target_pairs={{0,8},{1,9},{2,10},{3,11},{4,12},{5,13},{6,14},{7,15},{8,0},{9,1},... | collective-permute-start | bytes 48392 | tf_op jit(solution)/shard_map/ppermute | solution.py:66
  87.5 3.1 %collective-permute-start.12 = (f32[63,64]{0,1:T(8,128)S(1)}, f32[63,64]{0,1:T(8,128)S(1)}, u32[]{:S(2)}, u32[]{:S(2)}) collective-permute-start(f32[63,64]{0,1:T(8,128)S(1)} %add.1201), channel_id=1, source_target_pairs={{0,16},{16,0},{32,48},{48,32},{64,80},{80,64},{96,112},{112,96},{1... | collective-permute-start | bytes 48392 | tf_op jit(solution)/shard_map/ppermute | solution.py:66
  90.6 15.5 %collective-permute-start.13 = (f32[63,64]{0,1:T(8,128)S(1)}, f32[63,64]{0,1:T(8,128)S(1)}, u32[]{:S(2)}, u32[]{:S(2)}) collective-permute-start(f32[63,64]{0,1:T(8,128)S(1)} %add.1202), channel_id=1, source_target_pairs={{0,32},{16,48},{32,0},{48,16},{64,96},{80,112},{96,64},{112,80},{1... | collective-permute-start | bytes 48392 | tf_op jit(solution)/shard_map/ppermute | solution.py:66
  106.1 10.8 %collective-permute-start.14 = (f32[63,64]{0,1:T(8,128)S(1)}, f32[63,64]{0,1:T(8,128)S(1)}, u32[]{:S(2)}, u32[]{:S(2)}) collective-permute-start(f32[63,64]{0,1:T(8,128)S(1)} %add.1203), channel_id=1, source_target_pairs={{0,64},{16,80},{32,96},{48,112},{64,0},{80,16},{96,32},{112,48},{1... | collective-permute-start | bytes 48392 | tf_op jit(solution)/shard_map/ppermute | solution.py:66
  116.9 8.1 %collective-permute-start.15 = (f32[63,64]{0,1:T(8,128)S(1)}, f32[63,64]{0,1:T(8,128)S(1)}, u32[]{:S(2)}, u32[]{:S(2)}) collective-permute-start(f32[63,64]{0,1:T(8,128)S(1)} %add.1204), channel_id=1, source_target_pairs={{0,128},{16,144},{32,160},{48,176},{64,192},{80,208},{96,224},{112... | collective-permute-start | bytes 48392 | tf_op jit(solution)/shard_map/ppermute | solution.py:66
  125.0 14.0 %collective-permute-start.16 = (f32[63,64]{0,1:T(8,128)S(1)}, f32[63,64]{0,1:T(8,128)S(1)}, u32[]{:S(2)}, u32[]{:S(2)}) collective-permute-start(f32[63,64]{0,1:T(8,128)S(1)} %add.1205), channel_id=1, source_target_pairs={{0,256},{16,272},{32,288},{48,304},{64,320},{80,336},{96,352},{112... | collective-permute-start | bytes 48392 | tf_op jit(solution)/shard_map/ppermute | solution.py:66

commit v6 on v5

--- a/solution.py
+++ b/solution.py
@@ -177,10 +177,34 @@
     lax.fori_loop(0, cells_x, over_x, 0)
 
 
-def mxu_energy_kernel(extended_ref, coupling_ref, stiff_out, mass_out, adjoint_rows, products):
+def mxu_energy_kernel(
+    extended_ref, stiffness_ref, mass_ref, stiff_out, mass_out, coupling_ref, adjoint_rows, products
+):
     pair_count = extended_ref.shape[0]
     cells_x, cells_y, cells_z = stiff_out.shape
     dofs = 3 * len(CORNERS)
+    wide = dofs * cells_y
+    spread_rows = (
+        lax.broadcasted_iota(jnp.int32, (wide, dofs), 0) // cells_y
+        == lax.broadcasted_iota(jnp.int32, (wide, dofs), 1)
+    ).astype(jnp.float32)
+    spread_columns = (
+        lax.broadcasted_iota(jnp.int32, (dofs, wide), 0)
+        == lax.broadcasted_iota(jnp.int32, (dofs, wide), 1) // cells_y
+    ).astype(jnp.float32)
+    same_y = (
+        lax.broadcasted_iota(jnp.int32, (wide, wide), 0) % cells_y
+        == lax.broadcasted_iota(jnp.int32, (wide, wide), 1) % cells_y
+    )
+    for block, matrix_ref in enumerate((stiffness_ref, mass_ref)):
+        spread = jnp.dot(
+            matrix_ref[...], spread_columns, precision=lax.Precision.HIGHEST,
+            preferred_element_type=jnp.float32,
+        )
+        spread = jnp.dot(
+            spread_rows, spread, precision=lax.Precision.HIGHEST, preferred_element_type=jnp.float32
+        )
+        coupling_ref[pl.ds(block * wide, wide), :] = jnp.where(same_y, spread, 0.0)
     lane = lax.broadcasted_iota(jnp.int32, (cells_y, cells_z), 1)
     inside = lane < cells_z - 1
     stiff_out[...] = jnp.zeros(stiff_out.shape, jnp.float32)
@@ -231,9 +255,6 @@
     cells = (extended.shape[3] - 1, extended.shape[4] - 1, extended.shape[5])
     voxels = cells[0] * cells[1] * cells[2]
     dofs = stiffness.shape[0]
-    coupling = jnp.kron(
-        jnp.concatenate([stiffness, mass_matrix], axis=0), jnp.eye(cells[1], dtype=jnp.float32)
-    )
     vmem = pl.BlockSpec(memory_space=pltpu.VMEM)
     return pl.pallas_call(
         mxu_energy_kernel,
@@ -241,18 +262,19 @@
             jax.ShapeDtypeStruct(cells, jnp.float32),
             jax.ShapeDtypeStruct(cells, jnp.float32),
         ),
-        in_specs=[vmem, vmem],
+        in_specs=[vmem, vmem, vmem],
         out_specs=(vmem, vmem),
         scratch_shapes=[
+            pltpu.VMEM((2 * dofs * cells[1], dofs * cells[1]), jnp.float32),
             pltpu.VMEM((dofs * cells[1], cells[0] * cells[2]), jnp.float32),
             pltpu.VMEM((2 * dofs * cells[1], cells[0] * cells[2]), jnp.float32),
         ],
         cost_estimate=pl.CostEstimate(
-            flops=pair_count * (2 * coupling.size * cells[0] * cells[2] + 4 * dofs * voxels),
-            bytes_accessed=extended.size * 4 + coupling.size * 4 + 2 * voxels * 4,
+            flops=pair_count * (4 * (dofs * cells[1]) ** 2 * cells[0] * cells[2] + 4 * dofs * voxels),
+            bytes_accessed=extended.size * 4 + 2 * stiffness.size * 4 + 2 * voxels * 4,
             transcendentals=0,
         ),
-    )(extended, coupling)
+    )(extended, stiffness, mass_matrix)
 
 
 def shards(design, passive, basis_pairs, supports, stiffness, mass_matrix, volume_fraction):

time: 144 us -> 138 us (0.958)
  local copies, waits for them, and re-layouts: 6.65 us -> 0.96 us
  other arithmetic: 12.5 us -> 10 us
    mul x2 -> x0, local copies, waits for them, and re-layouts: 4.89 us -> none  [element_energies(): jnp.kron(jnp.concatenate([stiffness, mass_matrix], axis=0), jnp.eye(cells...]
    mul x1 -> x0, other arithmetic: 2.5 us -> none  [element_energies(): jnp.kron(jnp.concatenate([stiffness, mass_matrix], axis=0), jnp.eye(cells...]
    ppermute x9, starting transfers between devices: 53.5 us -> 54.9 us  [butterfly_sum(): lax.ppermute(value, axis, [(i, i ^ stride) for i in range(count)])]
  transfers between devices with their start and end apart: 17 -> 17, of which waited for: 12 -> 13; matrix products, arithmetic and copies ran while one was open for 6% -> 1% of each run, Pallas kernels for 9% -> 10%
where the time goes in v6:
time: 138 us; the launch traced here: 136 us
  starting transfers between devices  83.6 us (61%)
  waiting for transfers between devices  26.4 us (19%)
  Pallas kernels  14.1 us (10%)
  other arithmetic  10 us (7%)
    ppermute x9, starting transfers between devices, butterfly_sum(): lax.ppermute(value, axis, [(i, i ^ stride) for i in range(count)])  54.9 us
    ppermute x9, waiting for transfers between devices, butterfly_sum(): lax.ppermute(value, axis, [(i, i ^ stride) for i in range(count)])  23.3 us
    pallas_call x1, Pallas kernels, element_energies(): pl.pallas_call(mxu_energy_kernel, out_shape=(jax.ShapeDtypeStruct(cells,...  14.1 us
    ppermute x2, starting transfers between devices, with_halo(): lax.ppermute(tail, axis, [(i, (i + 1) % count) for i in range(ends)])  9.13 us
    ppermute x2, starting transfers between devices, with_halo(): lax.ppermute(head, axis, [((i + 1) % count, i) for i in range(ends)])  7.58 us
    ppermute x2, starting transfers between devices, front_exchange(): lax.ppermute(packed, axis, [((i + 1) % count, i) for i in range(ends)])  7.07 us
    ppermute x2, starting transfers between devices, front_exchange(): tail = lax.ppermute(tail, axis, [(i, (i + 1) % count) for i in range(ends)])  4.95 us
  transfers between devices with their start and end apart: 17, of which 13 were waited for; matrix products, arithmetic and copies ran while one was open for 1% of the time, Pallas kernels for 10%

profile of v6, /device:TPU:6, one launch (start us, length us, event | category | flops | bytes accessed | tf_op | source)
XLA Modules:
  0.0 136.3 jit_solution(4870247800715075951)
XLA Ops:
  1.4 1.2 broadcast_multiply_fusion
  2.7 1.3 collective-permute-start.1
  4.0 3.0 %collective-permute-start = (f32[2,8,128]{2,1,0:T(8,128)S(1)}, f32[2,8,128]{2,1,0:T(8,128)S(1)}, u32[]{:S(2)}, u32[]{:S(2)}) collective-permute-start(f32[2,8,128]{2,1,0:T(8,128)S(1)} %get-tuple-element.27), channel_id=1, source_target_pairs={{0,16},{16,32},{32,48},{48,64},{64,80},{80,96},{96,112},{112,128},... | collective-permute-start | bytes 24584 | tf_op jit(solution)/shard_map/ppermute | solution.py:50
  7.9 5.8 %collective-permute-start.3 = (f32[240,128]{1,0:T(8,128)S(1)}, f32[240,128]{1,0:T(8,128)S(1)}, u32[]{:S(2)}, u32[]{:S(2)}) collective-permute-start(f32[240,128]{1,0:T(8,128)S(1)} %pad_maximum_fusion.1), channel_id=1, source_target_pairs={{1,0},{2,1},{3,2},{4,3},{5,4},{6,5},{7,6},{8,7},{9,8},{10,9},{11,1... | collective-permute-start | bytes 368648 | tf_op jit(solution)/shard_map/ppermute | solution.py:46
  13.8 1.9 %collective-permute-start.2 = (f32[12,2,128]{2,1,0:T(2,128)S(1)}, f32[12,2,128]{2,1,0:T(2,128)S(1)}, u32[]{:S(2)}, u32[]{:S(2)}) collective-permute-start(f32[12,2,128]{2,1,0:T(2,128)S(1)} %get-tuple-element.20), channel_id=1, source_target_pairs={{0,1},{1,2},{2,3},{3,4},{4,5},{5,6},{6,7},{7,8},{8,9},{9,10},{10,1... | collective-permute-start | bytes 36872 | tf_op jit(solution)/shard_map/ppermute | solution.py:50
  16.2 1.4 pad_maximum_fusion.extended_ref
  17.5 14.1 %shard_map.86 = (f32[8,8,128]{2,1,0:T(8,128)}, f32[8,8,128]{2,1,0:T(8,128)}) custom-call(f32[4,2,3,9,9,128]{5,4,3,2,1,0:T(8,128)} %pad_maximum_fusion.extended_ref, f32[24,24]{1,0:T(8,128)} %stiffness_ref.1, f32[24,24]{1,0:T(8,128)} %mass_ref.1), custom_call_target="tpu_custom_call" | custom-call | flops 607125504 | bytes 1065472 | tf_op jit(solution)/shard_map/pallas_call | solution.py:259
  31.9 2.0 %fusion.82 = (f32[8,8,128]{2,1,0:T(8,128)S(1)}, pred[8,8,128]{2,1,0:T(8,128)(4,1)S(1)}) fusion(f32[8,8,128]{2,1,0:T(8,128)} %get-tuple-element.4, f32[12,10,128]{2,1,0:T(8,128)S(1)} %get-tuple-element.19, f32[12,12,132]{2,1,0:T(8,128)S(1)} %select_maximum_fusion.4, f32[2,8,128]{2,1,0:T(8,128)S(1)} %slice_bitcast_fusion, f32[8,8,128]{2,1,0:T(8,128)S(1)} %copy-done, ...), kind=kLoop, calls=%fused_computation.110 | loop fusion | flops 3039232 | bytes 6176768 | tf_op jit(solution)/shard_map/div | solution.py:305
  33.9 1.3 collective-permute-start.5
  35.2 6.7 %collective-permute-start.4 = (f32[2,8,128]{2,1,0:T(8,128)S(1)}, f32[2,8,128]{2,1,0:T(8,128)S(1)}, u32[]{:S(2)}, u32[]{:S(2)}) collective-permute-start(f32[2,8,128]{2,1,0:T(8,128)S(1)} %get-tuple-element.25), channel_id=1, source_target_pairs={{0,16},{16,32},{32,48},{48,64},{64,80},{80,96},{96,112},{112,128},... | collective-permute-start | bytes 24584 | tf_op jit(solution)/shard_map/ppermute | solution.py:27
  42.8 2.4 %collective-permute-start.6 = (f32[12,2,128]{2,1,0:T(2,128)S(1)}, f32[12,2,128]{2,1,0:T(2,128)S(1)}, u32[]{:S(2)}, u32[]{:S(2)}) collective-permute-start(f32[12,2,128]{2,1,0:T(2,128)S(1)} %get-tuple-element.16), channel_id=1, source_target_pairs={{0,1},{1,2},{2,3},{3,4},{4,5},{5,6},{6,7},{7,8},{8,9},{9,10},{10,1... | collective-permute-start | bytes 36872 | tf_op jit(solution)/shard_map/ppermute | solution.py:27
  45.2 6.3 %collective-permute-start.7 = (f32[12,2,128]{2,1,0:T(2,128)S(1)}, f32[12,2,128]{2,1,0:T(2,128)S(1)}, u32[]{:S(2)}, u32[]{:S(2)}) collective-permute-start(f32[12,2,128]{2,1,0:T(2,128)S(1)} %get-tuple-element.17), channel_id=1, source_target_pairs={{1,0},{2,1},{3,2},{4,3},{5,4},{6,5},{7,6},{8,7},{9,8},{10,9},{11,1... | collective-permute-start | bytes 36872 | tf_op jit(solution)/shard_map/ppermute | solution.py:29
  51.6 1.2 collective-permute-done.7
  53.6 0.9 fusion.4
  54.8 1.9 %collective-permute-start.8 = (f32[63,64]{0,1:T(8,128)S(1)}, f32[63,64]{0,1:T(8,128)S(1)}, u32[]{:S(2)}, u32[]{:S(2)}) collective-permute-start(f32[63,64]{0,1:T(8,128)S(1)} %reduce_sum.19), channel_id=1, source_target_pairs={{0,1},{1,0},{2,3},{3,2},{4,5},{5,4},{6,7},{7,6},{8,9},{9,8},{10,11... | collective-permute-start | bytes 48392 | tf_op jit(solution)/shard_map/ppermute | solution.py:66
  56.7 3.9 %collective-permute-done.8 = f32[63,64]{0,1:T(8,128)S(1)} collective-permute-done((f32[63,64]{0,1:T(8,128)S(1)}, f32[63,64]{0,1:T(8,128)S(1)}, u32[]{:S(2)}, u32[]{:S(2)}) %collective-permute-start.8) | collective-permute-done | bytes 16160 | tf_op jit(solution)/shard_map/ppermute | solution.py:66
  60.6 1.9 %collective-permute-start.9 = (f32[63,64]{0,1:T(8,128)S(1)}, f32[63,64]{0,1:T(8,128)S(1)}, u32[]{:S(2)}, u32[]{:S(2)}) collective-permute-start(f32[63,64]{0,1:T(8,128)S(1)} %add.1198), channel_id=1, source_target_pairs={{0,2},{1,3},{2,0},{3,1},{4,6},{5,7},{6,4},{7,5},{8,10},{9,11},{10,... | collective-permute-start | bytes 48392 | tf_op jit(solution)/shard_map/ppermute | solution.py:66
  62.5 4.8 %collective-permute-done.9 = f32[63,64]{0,1:T(8,128)S(1)} collective-permute-done((f32[63,64]{0,1:T(8,128)S(1)}, f32[63,64]{0,1:T(8,128)S(1)}, u32[]{:S(2)}, u32[]{:S(2)}) %collective-permute-start.9) | collective-permute-done | bytes 16160 | tf_op jit(solution)/shard_map/ppermute | solution.py:66
  67.3 3.1 %collective-permute-start.10 = (f32[63,64]{0,1:T(8,128)S(1)}, f32[63,64]{0,1:T(8,128)S(1)}, u32[]{:S(2)}, u32[]{:S(2)}) collective-permute-start(f32[63,64]{0,1:T(8,128)S(1)} %add.1199), channel_id=1, source_target_pairs={{0,4},{1,5},{2,6},{3,7},{4,0},{5,1},{6,2},{7,3},{8,12},{9,13},{10,... | collective-permute-start | bytes 48392 | tf_op jit(solution)/shard_map/ppermute | solution.py:66
  70.4 2.7 %collective-permute-done.10 = f32[63,64]{0,1:T(8,128)S(1)} collective-permute-done((f32[63,64]{0,1:T(8,128)S(1)}, f32[63,64]{0,1:T(8,128)S(1)}, u32[]{:S(2)}, u32[]{:S(2)}) %collective-permute-start.10) | collective-permute-done | bytes 16160 | tf_op jit(solution)/shard_map/ppermute | solution.py:66
  73.1 3.7 %collective-permute-start.11 = (f32[63,64]{0,1:T(8,128)S(1)}, f32[63,64]{0,1:T(8,128)S(1)}, u32[]{:S(2)}, u32[]{:S(2)}) collective-permute-start(f32[63,64]{0,1:T(8,128)S(1)} %add.1200), channel_id=1, source_target_pairs={{0,8},{1,9},{2,10},{3,11},{4,12},{5,13},{6,14},{7,15},{8,0},{9,1},... | collective-permute-start | bytes 48392 | tf_op jit(solution)/shard_map/ppermute | solution.py:66
  76.8 3.6 %collective-permute-done.11 = f32[63,64]{0,1:T(8,128)S(1)} collective-permute-done((f32[63,64]{0,1:T(8,128)S(1)}, f32[63,64]{0,1:T(8,128)S(1)}, u32[]{:S(2)}, u32[]{:S(2)}) %collective-permute-start.11) | collective-permute-done | bytes 16160 | tf_op jit(solution)/shard_map/ppermute | solution.py:66
  80.4 4.2 %collective-permute-start.12 = (f32[63,64]{0,1:T(8,128)S(1)}, f32[63,64]{0,1:T(8,128)S(1)}, u32[]{:S(2)}, u32[]{:S(2)}) collective-permute-start(f32[63,64]{0,1:T(8,128)S(1)} %add.1201), channel_id=1, source_target_pairs={{0,16},{16,0},{32,48},{48,32},{64,80},{80,64},{96,112},{112,96},{1... | collective-permute-start | bytes 48392 | tf_op jit(solution)/shard_map/ppermute | solution.py:66
  84.6 0.8 collective-permute-done.12
  85.4 13.8 %collective-permute-start.13 = (f32[63,64]{0,1:T(8,128)S(1)}, f32[63,64]{0,1:T(8,128)S(1)}, u32[]{:S(2)}, u32[]{:S(2)}) collective-permute-start(f32[63,64]{0,1:T(8,128)S(1)} %add.1202), channel_id=1, source_target_pairs={{0,32},{16,48},{32,0},{48,16},{64,96},{80,112},{96,64},{112,80},{1... | collective-permute-start | bytes 48392 | tf_op jit(solution)/shard_map/ppermute | solution.py:66
  99.2 1.9 %collective-permute-done.13 = f32[63,64]{0,1:T(8,128)S(1)} collective-permute-done((f32[63,64]{0,1:T(8,128)S(1)}, f32[63,64]{0,1:T(8,128)S(1)}, u32[]{:S(2)}, u32[]{:S(2)}) %collective-permute-start.13) | collective-permute-done | bytes 16160 | tf_op jit(solution)/shard_map/ppermute | solution.py:66
  101.1 8.5 %collective-permute-start.14 = (f32[63,64]{0,1:T(8,128)S(1)}, f32[63,64]{0,1:T(8,128)S(1)}, u32[]{:S(2)}, u32[]{:S(2)}) collective-permute-start(f32[63,64]{0,1:T(8,128)S(1)} %add.1203), channel_id=1, source_target_pairs={{0,64},{16,80},{32,96},{48,112},{64,0},{80,16},{96,32},{112,48},{1... | collective-permute-start | bytes 48392 | tf_op jit(solution)/shard_map/ppermute | solution.py:66
  109.7 1.9 %collective-permute-done.14 = f32[63,64]{0,1:T(8,128)S(1)} collective-permute-done((f32[63,64]{0,1:T(8,128)S(1)}, f32[63,64]{0,1:T(8,128)S(1)}, u32[]{:S(2)}, u32[]{:S(2)}) %collective-permute-start.14) | collective-permute-done | bytes 16160 | tf_op jit(solution)/shard_map/ppermute | solution.py:66
  111.5 6.2 %collective-permute-start.15 = (f32[63,64]{0,1:T(8,128)S(1)}, f32[63,64]{0,1:T(8,128)S(1)}, u32[]{:S(2)}, u32[]{:S(2)}) collective-permute-start(f32[63,64]{0,1:T(8,128)S(1)} %add.1204), channel_id=1, source_target_pairs={{0,128},{16,144},{32,160},{48,176},{64,192},{80,208},{96,224},{112... | collective-permute-start | bytes 48392 | tf_op jit(solution)/shard_map/ppermute | solution.py:66
  117.7 1.9 %collective-permute-done.15 = f32[63,64]{0,1:T(8,128)S(1)} collective-permute-done((f32[63,64]{0,1:T(8,128)S(1)}, f32[63,64]{0,1:T(8,128)S(1)}, u32[]{:S(2)}, u32[]{:S(2)}) %collective-permute-start.15) | collective-permute-done | bytes 16160 | tf_op jit(solution)/shard_map/ppermute | solution.py:66
  119.6 11.6 %collective-permute-start.16 = (f32[63,64]{0,1:T(8,128)S(1)}, f32[63,64]{0,1:T(8,128)S(1)}, u32[]{:S(2)}, u32[]{:S(2)}) collective-permute-start(f32[63,64]{0,1:T(8,128)S(1)} %add.1205), channel_id=1, source_target_pairs={{0,256},{16,272},{32,288},{48,304},{64,320},{80,336},{96,352},{112... | collective-permute-start | bytes 48392 | tf_op jit(solution)/shard_map/ppermute | solution.py:66
  131.3 1.9 %collective-permute-done.16 = f32[63,64]{0,1:T(8,128)S(1)} collective-permute-done((f32[63,64]{0,1:T(8,128)S(1)}, f32[63,64]{0,1:T(8,128)S(1)}, u32[]{:S(2)}, u32[]{:S(2)}) %collective-permute-start.16) | collective-permute-done | bytes 16160 | tf_op jit(solution)/shard_map/ppermute | solution.py:66
  (79 shorter events, 7.3 us)
Async XLA Ops:
  0.6 2.0 %copy-start = (f32[8,8,128]{2,1,0:T(8,128)S(1)}, f32[8,8,128]{2,1,0:T(8,128)}, u32[]{:S(2)}) copy-start(f32[8,8,128]{2,1,0:T(8,128)} %param.7) | copy-start | bytes 98308
  2.7 5.2 %collective-permute-start.1 = (f32[208,128]{1,0:T(8,128)S(1)}, f32[208,128]{1,0:T(8,128)S(1)}, u32[]{:S(2)}, u32[]{:S(2)}) collective-permute-start(f32[208,128]{1,0:T(8,128)S(1)} %pad_maximum_fusion.3), channel_id=1, source_target_pairs={{16,0},{32,16},{48,32},{64,48},{80,64},{96,80},{112,96},{128,112},... | collective-permute-start | bytes 319496 | tf_op jit(solution)/shard_map/ppermute | solution.py:46
  4.0 3.8 %collective-permute-start = (f32[2,8,128]{2,1,0:T(8,128)S(1)}, f32[2,8,128]{2,1,0:T(8,128)S(1)}, u32[]{:S(2)}, u32[]{:S(2)}) collective-permute-start(f32[2,8,128]{2,1,0:T(8,128)S(1)} %get-tuple-element.27), channel_id=1, source_target_pairs={{0,16},{16,32},{32,48},{48,64},{64,80},{80,96},{96,112},{112,128},... | collective-permute-start | bytes 24584 | tf_op jit(solution)/shard_map/ppermute | solution.py:50
  7.9 8.2 %collective-permute-start.3 = (f32[240,128]{1,0:T(8,128)S(1)}, f32[240,128]{1,0:T(8,128)S(1)}, u32[]{:S(2)}, u32[]{:S(2)}) collective-permute-start(f32[240,128]{1,0:T(8,128)S(1)} %pad_maximum_fusion.1), channel_id=1, source_target_pairs={{1,0},{2,1},{3,2},{4,3},{5,4},{6,5},{7,6},{8,7},{9,8},{10,9},{11,1... | collective-permute-start | bytes 368648 | tf_op jit(solution)/shard_map/ppermute | solution.py:46
  13.8 17.9 %collective-permute-start.2 = (f32[12,2,128]{2,1,0:T(2,128)S(1)}, f32[12,2,128]{2,1,0:T(2,128)S(1)}, u32[]{:S(2)}, u32[]{:S(2)}) collective-permute-start(f32[12,2,128]{2,1,0:T(2,128)S(1)} %get-tuple-element.20), channel_id=1, source_target_pairs={{0,1},{1,2},{2,3},{3,4},{4,5},{5,6},{6,7},{7,8},{8,9},{9,10},{10,1... | collective-permute-start | bytes 36872 | tf_op jit(solution)/shard_map/ppermute | solution.py:50
  17.5 14.4 %copy-start.2 = (s32[8,8,128]{2,1,0:T(8,128)S(1)}, s32[8,8,128]{2,1,0:T(8,128)}, u32[]{:S(2)}) copy-start(s32[8,8,128]{2,1,0:T(8,128)} %param.8) | copy-start | bytes 98308
  31.9 19.6 %copy-start.3 = (f32[63,64]{0,1:T(8,128)S(1)}, f32[63,64]{0,1:T(8,128)}, u32[]{:S(2)}) copy-start(f32[63,64]{0,1:T(8,128)} %constant.25.clone.1) | copy-start | bytes 48388
  33.9 8.0 %collective-permute-start.5 = (f32[2,8,128]{2,1,0:T(8,128)S(1)}, f32[2,8,128]{2,1,0:T(8,128)S(1)}, u32[]{:S(2)}, u32[]{:S(2)}) collective-permute-start(f32[2,8,128]{2,1,0:T(8,128)S(1)} %get-tuple-element.26), channel_id=1, source_target_pairs={{16,0},{32,16},{48,32},{64,48},{80,64},{96,80},{112,96},{128,112},... | collective-permute-start | bytes 24584 | tf_op jit(solution)/shard_map/ppermute | solution.py:29
  35.2 7.6 %collective-permute-start.4 = (f32[2,8,128]{2,1,0:T(8,128)S(1)}, f32[2,8,128]{2,1,0:T(8,128)S(1)}, u32[]{:S(2)}, u32[]{:S(2)}) collective-permute-start(f32[2,8,128]{2,1,0:T(8,128)S(1)} %get-tuple-element.25), channel_id=1, source_target_pairs={{0,16},{16,32},{32,48},{48,64},{64,80},{80,96},{96,112},{112,128},... | collective-permute-start | bytes 24584 | tf_op jit(solution)/shard_map/ppermute | solution.py:27
  42.8 8.8 %collective-permute-start.6 = (f32[12,2,128]{2,1,0:T(2,128)S(1)}, f32[12,2,128]{2,1,0:T(2,128)S(1)}, u32[]{:S(2)}, u32[]{:S(2)}) collective-permute-start(f32[12,2,128]{2,1,0:T(2,128)S(1)} %get-tuple-element.16), channel_id=1, source_target_pairs={{0,1},{1,2},{2,3},{3,4},{4,5},{5,6},{6,7},{7,8},{8,9},{9,10},{10,1... | collective-permute-start | bytes 36872 | tf_op jit(solution)/shard_map/ppermute | solution.py:27
  45.2 7.7 %collective-permute-start.7 = (f32[12,2,128]{2,1,0:T(2,128)S(1)}, f32[12,2,128]{2,1,0:T(2,128)S(1)}, u32[]{:S(2)}, u32[]{:S(2)}) collective-permute-start(f32[12,2,128]{2,1,0:T(2,128)S(1)} %get-tuple-element.17), channel_id=1, source_target_pairs={{1,0},{2,1},{3,2},{4,3},{5,4},{6,5},{7,6},{8,7},{9,8},{10,9},{11,1... | collective-permute-start | bytes 36872 | tf_op jit(solution)/shard_map/ppermute | solution.py:29
  53.1 78.2 %copy-start.4 = (f32[64]{0:T(128)S(1)}, f32[64]{0:T(128)}, u32[]{:S(2)}) copy-start(f32[64]{0:T(128)} %param.13) | copy-start | bytes 772
  53.6 82.7 %copy-start.1 = (f32[8,8,128]{2,1,0:T(8,128)}, f32[8,8,128]{2,1,0:T(8,128)S(1)}, u32[]{:S(2)}) copy-start(f32[8,8,128]{2,1,0:T(8,128)S(1)} %get-tuple-element.11) | copy-start | bytes 98308
  54.8 5.8 %collective-permute-start.8 = (f32[63,64]{0,1:T(8,128)S(1)}, f32[63,64]{0,1:T(8,128)S(1)}, u32[]{:S(2)}, u32[]{:S(2)}) collective-permute-start(f32[63,64]{0,1:T(8,128)S(1)} %reduce_sum.19), channel_id=1, source_target_pairs={{0,1},{1,0},{2,3},{3,2},{4,5},{5,4},{6,7},{7,6},{8,9},{9,8},{10,11... | collective-permute-start | bytes 48392 | tf_op jit(solution)/shard_map/ppermute | solution.py:66
  60.6 6.7 %collective-permute-start.9 = (f32[63,64]{0,1:T(8,128)S(1)}, f32[63,64]{0,1:T(8,128)S(1)}, u32[]{:S(2)}, u32[]{:S(2)}) collective-permute-start(f32[63,64]{0,1:T(8,128)S(1)} %add.1198), channel_id=1, source_target_pairs={{0,2},{1,3},{2,0},{3,1},{4,6},{5,7},{6,4},{7,5},{8,10},{9,11},{10,... | collective-permute-start | bytes 48392 | tf_op jit(solution)/shard_map/ppermute | solution.py:66
  67.3 5.8 %collective-permute-start.10 = (f32[63,64]{0,1:T(8,128)S(1)}, f32[63,64]{0,1:T(8,128)S(1)}, u32[]{:S(2)}, u32[]{:S(2)}) collective-permute-start(f32[63,64]{0,1:T(8,128)S(1)} %add.1199), channel_id=1, source_target_pairs={{0,4},{1,5},{2,6},{3,7},{4,0},{5,1},{6,2},{7,3},{8,12},{9,13},{10,... | collective-permute-start | bytes 48392 | tf_op jit(solution)/shard_map/ppermute | solution.py:66
  73.1 7.3 %collective-permute-start.11 = (f32[63,64]{0,1:T(8,128)S(1)}, f32[63,64]{0,1:T(8,128)S(1)}, u32[]{:S(2)}, u32[]{:S(2)}) collective-permute-start(f32[63,64]{0,1:T(8,128)S(1)} %add.1200), channel_id=1, source_target_pairs={{0,8},{1,9},{2,10},{3,11},{4,12},{5,13},{6,14},{7,15},{8,0},{9,1},... | collective-permute-start | bytes 48392 | tf_op jit(solution)/shard_map/ppermute | solution.py:66
  80.4 5.0 %collective-permute-start.12 = (f32[63,64]{0,1:T(8,128)S(1)}, f32[63,64]{0,1:T(8,128)S(1)}, u32[]{:S(2)}, u32[]{:S(2)}) collective-permute-start(f32[63,64]{0,1:T(8,128)S(1)} %add.1201), channel_id=1, source_target_pairs={{0,16},{16,0},{32,48},{48,32},{64,80},{80,64},{96,112},{112,96},{1... | collective-permute-start | bytes 48392 | tf_op jit(solution)/shard_map/ppermute | solution.py:66
  85.4 15.7 %collective-permute-start.13 = (f32[63,64]{0,1:T(8,128)S(1)}, f32[63,64]{0,1:T(8,128)S(1)}, u32[]{:S(2)}, u32[]{:S(2)}) collective-permute-start(f32[63,64]{0,1:T(8,128)S(1)} %add.1202), channel_id=1, source_target_pairs={{0,32},{16,48},{32,0},{48,16},{64,96},{80,112},{96,64},{112,80},{1... | collective-permute-start | bytes 48392 | tf_op jit(solution)/shard_map/ppermute | solution.py:66
  101.1 10.4 %collective-permute-start.14 = (f32[63,64]{0,1:T(8,128)S(1)}, f32[63,64]{0,1:T(8,128)S(1)}, u32[]{:S(2)}, u32[]{:S(2)}) collective-permute-start(f32[63,64]{0,1:T(8,128)S(1)} %add.1203), channel_id=1, source_target_pairs={{0,64},{16,80},{32,96},{48,112},{64,0},{80,16},{96,32},{112,48},{1... | collective-permute-start | bytes 48392 | tf_op jit(solution)/shard_map/ppermute | solution.py:66
  111.5 8.1 %collective-permute-start.15 = (f32[63,64]{0,1:T(8,128)S(1)}, f32[63,64]{0,1:T(8,128)S(1)}, u32[]{:S(2)}, u32[]{:S(2)}) collective-permute-start(f32[63,64]{0,1:T(8,128)S(1)} %add.1204), channel_id=1, source_target_pairs={{0,128},{16,144},{32,160},{48,176},{64,192},{80,208},{96,224},{112... | collective-permute-start | bytes 48392 | tf_op jit(solution)/shard_map/ppermute | solution.py:66
  119.6 13.5 %collective-permute-start.16 = (f32[63,64]{0,1:T(8,128)S(1)}, f32[63,64]{0,1:T(8,128)S(1)}, u32[]{:S(2)}, u32[]{:S(2)}) collective-permute-start(f32[63,64]{0,1:T(8,128)S(1)} %add.1205), channel_id=1, source_target_pairs={{0,256},{16,272},{32,288},{48,304},{64,320},{80,336},{96,352},{112... | collective-permute-start | bytes 48392 | tf_op jit(solution)/shard_map/ppermute | solution.py:66

commit v7 on v6

--- a/solution.py
+++ b/solution.py
@@ -1,3 +1,4 @@
+import functools
 import math
 
 import jax
@@ -34,7 +35,8 @@
 
 
 def front_exchange(cells, fields, width):
-    for axis, dim in (("gx", 0), ("gy", 1)):
+    stages = []
+    for axis, dim in (("gy", 1), ("gx", 0)):
         count = lax.axis_size(axis)
         ends = count - 1
         field_dim = dim + 3
@@ -50,7 +52,8 @@
         tail = lax.ppermute(tail, axis, [(i, (i + 1) % count) for i in range(ends)])
         cells = jnp.concatenate([tail, cells, head], axis=dim)
         fields = jnp.concatenate([fields, rim], axis=field_dim)
-    return cells, fields
+        stages.append(fields)
+    return cells, stages[0], stages[1]
 
 
 def from_behind(value, axis, steps):
@@ -178,10 +181,11 @@
 
 
 def mxu_energy_kernel(
-    extended_ref, stiffness_ref, mass_ref, stiff_out, mass_out, coupling_ref, adjoint_rows, products
+    slices, extended_ref, stiffness_ref, mass_ref, stiff_out, mass_out, coupling_ref, adjoint_rows,
+    products,
 ):
     pair_count = extended_ref.shape[0]
-    cells_x, cells_y, cells_z = stiff_out.shape
+    _, cells_y, cells_z = stiff_out.shape
     dofs = 3 * len(CORNERS)
     wide = dofs * cells_y
     spread_rows = (
@@ -218,46 +222,39 @@
         return value
 
     def over_pairs(pair, carry):
-        def gather_x(x, inner):
-            columns = pl.ds(pl.multiple_of(x * cells_z, cells_z), cells_z)
+        for place, x in enumerate(slices):
+            columns = pl.ds(place * cells_z, cells_z)
             for row in range(dofs):
                 adjoint_rows[pl.ds(row * cells_y, cells_y), columns] = node_view(pair, 1, row, x)
-            return inner
-
-        lax.fori_loop(0, cells_x, gather_x, 0)
         products[...] = jnp.dot(
             coupling_ref[...],
             adjoint_rows[...],
             precision=lax.Precision.HIGHEST,
             preferred_element_type=jnp.float32,
         )
-
-        def reduce_x(x, inner):
-            columns = pl.ds(pl.multiple_of(x * cells_z, cells_z), cells_z)
-            stiff_sum = stiff_out[x]
-            mass_sum = mass_out[x]
+        for place, x in enumerate(slices):
+            columns = pl.ds(place * cells_z, cells_z)
+            stiff_sum = stiff_out[place]
+            mass_sum = mass_out[place]
             for row in range(dofs):
                 state = node_view(pair, 0, row, x)
                 stiff_sum = stiff_sum + state * products[pl.ds(row * cells_y, cells_y), columns]
                 mass_sum = mass_sum + state * products[pl.ds((dofs + row) * cells_y, cells_y), columns]
-            stiff_out[x] = stiff_sum
-            mass_out[x] = mass_sum
-            return inner
-
-        lax.fori_loop(0, cells_x, reduce_x, 0)
+            stiff_out[place] = stiff_sum
+            mass_out[place] = mass_sum
         return carry
 
     lax.fori_loop(0, pair_count, over_pairs, 0)
 
 
-def element_energies(extended, stiffness, mass_matrix):
+def element_energies(extended, stiffness, mass_matrix, slices):
     pair_count = extended.shape[0]
-    cells = (extended.shape[3] - 1, extended.shape[4] - 1, extended.shape[5])
+    cells = (len(slices), extended.shape[4] - 1, extended.shape[5])
     voxels = cells[0] * cells[1] * cells[2]
     dofs = stiffness.shape[0]
     vmem = pl.BlockSpec(memory_space=pltpu.VMEM)
     return pl.pallas_call(
-        mxu_energy_kernel,
+        functools.partial(mxu_energy_kernel, slices),
         out_shape=(
             jax.ShapeDtypeStruct(cells, jnp.float32),
             jax.ShapeDtypeStruct(cells, jnp.float32),
@@ -294,15 +291,41 @@
     inside = valid_x[:, None, None] * valid_y[None, :, None] * valid_z[None, None, :]
     weight_sum = stencil(inside, block_shape)
     fields = basis_pairs * (1 - supports).astype(jnp.float32)
-    design_wide, extended = front_exchange(design, fields, 2)
+    design_wide, widened, extended = front_exchange(design, fields, 2)
     design_wide = jnp.pad(design_wide, ((0, 0), (0, 0), (2, 2)))
     physical = jnp.where(passive == 1, 1.0, stencil(design_wide, block_shape) / weight_sum)
-    stiff_energy, mass_energy = element_energies(extended, stiffness, mass_matrix)
-    raw_sensitivity = -(
-        PENALTY_SCALE * physical * physical * stiff_energy - OMEGA_SQUARED * mass_energy
+    last = size_x - 1
+    early = (0, 1, last - 1)
+    middle_slices = tuple(range(2, last - 1))
+    parts = [
+        element_energies(widened, stiffness, mass_matrix, early),
+        element_energies(extended, stiffness, mass_matrix, (last,)),
+        element_energies(widened, stiffness, mass_matrix, middle_slices),
+    ]
+
+    def scaled_raw(stiff_rows, mass_rows, first, end):
+        physical_rows = physical[first:end]
+        raw_rows = -(
+            PENALTY_SCALE * physical_rows * physical_rows * stiff_rows - OMEGA_SQUARED * mass_rows
+        )
+        raw_rows = jnp.where(passive[first:end] == 1, 0.0, raw_rows)
+        return raw_rows / weight_sum[first:end]
+
+    (early_stiff, early_mass), (last_stiff, last_mass), (middle_stiff, middle_mass) = parts
+    head_rows = scaled_raw(early_stiff[:2], early_mass[:2], 0, 2)
+    tail_rows = scaled_raw(
+        jnp.concatenate([early_stiff[2:], last_stiff], axis=0),
+        jnp.concatenate([early_mass[2:], last_mass], axis=0),
+        last - 1,
+        last + 1,
     )
-    raw_sensitivity = jnp.where(passive == 1, 0.0, raw_sensitivity)
-    scaled_wide = with_halo(raw_sensitivity / weight_sum, (("gx", 0), ("gy", 1)), 2)
+    middle_rows = scaled_raw(middle_stiff, middle_mass, 2, last - 1)
+    count_x = lax.axis_size("gx")
+    head_x = lax.ppermute(head_rows, "gx", [(i + 1, i) for i in range(count_x - 1)])
+    tail_x = lax.ppermute(tail_rows, "gx", [(i, i + 1) for i in range(count_x - 1)])
+    scaled = jnp.concatenate([head_rows, middle_rows, tail_rows], axis=0)
+    scaled_wide = jnp.concatenate([tail_x, scaled, head_x], axis=0)
+    scaled_wide = with_halo(scaled_wide, (("gy", 1),), 2)
     scaled_wide = jnp.pad(scaled_wide, ((0, 0), (0, 0), (2, 2)))
     sensitivity = stencil(scaled_wide, block_shape)
     benefit = jnp.maximum(-sensitivity, 0.0)

time: 138 us -> 138 us (level)
  starting transfers between devices: 83.6 us -> 71.9 us
  waiting for transfers between devices: 26.4 us -> 31.9 us
  Pallas kernels: 14.1 us -> 17.2 us
  local copies, waits for them, and re-layouts: 0.96 us -> 2.42 us
    ppermute x9, starting transfers between devices: 54.9 us -> 44.6 us  [butterfly_sum(): lax.ppermute(value, axis, [(i, i ^ stride) for i in range(count)])]
    ppermute x2 -> x1, starting transfers between devices: 9.13 us -> 1.92 us  [with_halo(): lax.ppermute(tail, axis, [(i, (i + 1) % count) for i in range(ends)])]
    ppermute x0 -> x2, starting transfers between devices: none -> 6.76 us  [the longest x1 5.47 us: shards(): lax.ppermute(tail_rows, 'gx', [(i, i + 1) for i in range(count_x - 1)])]
    ppermute x2, waiting for transfers between devices: 0.54 us -> 5.95 us  [front_exchange(): tail = lax.ppermute(tail, axis, [(i, (i + 1) % count) for i in range(ends)])]
    pallas_call x1 -> x3, Pallas kernels: 14.1 us -> 17.2 us  [element_energies(): pl.pallas_call(functools.partial(mxu_energy_kernel, slices), out_shape=(j...]
    div x1, other arithmetic: 2 us -> 0.01 us  [scaled_raw(): return raw_rows / weight_sum[first:end]]
    ppermute x2 -> x1, starting transfers between devices: 7.58 us -> 6.62 us  [with_halo(): lax.ppermute(head, axis, [((i + 1) % count, i) for i in range(ends)])]
  transfers between devices with their start and end apart: 17 -> 17, of which waited for: 13 -> 13; matrix products, arithmetic and copies ran while one was open for 1% -> 4% of each run, Pallas kernels for 10% -> 13%
where the time goes in v7:
time: 138 us; the launch traced here: 136 us
  starting transfers between devices  71.9 us (52%)
  waiting for transfers between devices  31.9 us (23%)
  Pallas kernels  17.2 us (12%)
  other arithmetic  11.2 us (8%)
  local copies, waits for them, and re-layouts  2.42 us (2%)
    ppermute x9, starting transfers between devices, butterfly_sum(): lax.ppermute(value, axis, [(i, i ^ stride) for i in range(count)])  44.6 us
    ppermute x9, waiting for transfers between devices, butterfly_sum(): lax.ppermute(value, axis, [(i, i ^ stride) for i in range(count)])  23.6 us
    pallas_call x3, Pallas kernels, element_energies(): pl.pallas_call(functools.partial(mxu_energy_kernel, slices), out_shape=(j...  17.2 us
    ppermute x2, starting transfers between devices, front_exchange(): lax.ppermute(packed, axis, [((i + 1) % count, i) for i in range(ends)])  7.07 us
    ppermute x1, starting transfers between devices, with_halo(): lax.ppermute(head, axis, [((i + 1) % count, i) for i in range(ends)])  6.62 us
    ppermute x2, waiting for transfers between devices, front_exchange(): tail = lax.ppermute(tail, axis, [(i, (i + 1) % count) for i in range(ends)])  5.95 us
    ppermute x1, starting transfers between devices, shards(): lax.ppermute(tail_rows, 'gx', [(i, i + 1) for i in range(count_x - 1)])  5.47 us
    ppermute x2, starting transfers between devices, front_exchange(): tail = lax.ppermute(tail, axis, [(i, (i + 1) % count) for i in range(ends)])  4.95 us
  transfers between devices with their start and end apart: 17, of which 13 were waited for; matrix products, arithmetic and copies ran while one was open for 4% of the time, Pallas kernels for 13%

profile of v7, /device:TPU:6, one launch (start us, length us, event | category | flops | bytes accessed | tf_op | source)
XLA Modules:
  0.0 135.8 jit_solution(15067296147463554161)
XLA Ops:
  2.7 5.8 %collective-permute-start.1 = (f32[208,128]{1,0:T(8,128)S(1)}, f32[208,128]{1,0:T(8,128)S(1)}, u32[]{:S(2)}, u32[]{:S(2)}) collective-permute-start(f32[208,128]{1,0:T(8,128)S(1)} %pad_maximum_fusion.3), channel_id=1, source_target_pairs={{1,0},{2,1},{3,2},{4,3},{5,4},{6,5},{7,6},{8,7},{9,8},{10,9},{11,1... | collective-permute-start | bytes 319496 | tf_op jit(solution)/shard_map/ppermute | solution.py:48
  8.5 1.9 %collective-permute-start = (f32[8,2,128]{2,1,0:T(2,128)S(1)}, f32[8,2,128]{2,1,0:T(2,128)S(1)}, u32[]{:S(2)}, u32[]{:S(2)}) collective-permute-start(f32[8,2,128]{2,1,0:T(2,128)S(1)} %get-tuple-element.35), channel_id=1, source_target_pairs={{0,1},{1,2},{2,3},{3,4},{4,5},{5,6},{6,7},{7,8},{8,9},{9,10},{10,1... | collective-permute-start | bytes 24584 | tf_op jit(solution)/shard_map/ppermute | solution.py:52
  10.8 5.9 %collective-permute-done = f32[8,2,128]{2,1,0:T(2,128)S(1)} collective-permute-done((f32[8,2,128]{2,1,0:T(2,128)S(1)}, f32[8,2,128]{2,1,0:T(2,128)S(1)}, u32[]{:S(2)}, u32[]{:S(2)}) %collective-permute-start) | collective-permute-done | bytes 8224 | tf_op jit(solution)/shard_map/ppermute | solution.py:52
  16.8 1.3 collective-permute-start.3
  18.1 3.0 %collective-permute-start.2 = (f32[2,12,128]{2,1,0:T(8,128)S(1)}, f32[2,12,128]{2,1,0:T(8,128)S(1)}, u32[]{:S(2)}, u32[]{:S(2)}) collective-permute-start(f32[2,12,128]{2,1,0:T(8,128)S(1)} %get-tuple-element.31), channel_id=1, source_target_pairs={{0,16},{16,32},{32,48},{48,64},{64,80},{80,96},{96,112},{112,128},... | collective-permute-start | bytes 36872 | tf_op jit(solution)/shard_map/ppermute | solution.py:52
  21.2 1.3 pad_maximum_fusion.extended_ref
  22.5 6.1 %shard_map.86 = (f32[3,8,128]{2,1,0:T(8,128)}, f32[3,8,128]{2,1,0:T(8,128)}) custom-call(f32[4,2,3,8,9,128]{5,4,3,2,1,0:T(8,128)} %pad_maximum_fusion.extended_ref, f32[24,24]{1,0:T(8,128)} %stiffness_ref.5, f32[24,24]{1,0:T(8,128)} %mass_ref.5), custom_call_target="tpu_custom_call" | custom-call | flops 227672064 | bytes 913920 | tf_op jit(solution)/shard_map/pallas_call | solution.py:256
  30.0 1.3 pad_maximum_fusion.1.extended_ref
  31.3 4.9 %shard_map.87 = (f32[1,8,128]{2,1,0:T(8,128)}, f32[1,8,128]{2,1,0:T(8,128)}) custom-call(f32[4,2,3,9,9,128]{5,4,3,2,1,0:T(8,128)} %pad_maximum_fusion.1.extended_ref, f32[24,24]{1,0:T(8,128)} %stiffness_ref.5, f32[24,24]{1,0:T(8,128)} %mass_ref.5), custom_call_target="tpu_custom_call" | custom-call | flops 75890688 | bytes 1008128 | tf_op jit(solution)/shard_map/pallas_call | solution.py:256
  37.8 5.5 %collective-permute-start.4 = (f32[2,8,128]{2,1,0:T(8,128)S(1)}, f32[2,8,128]{2,1,0:T(8,128)S(1)}, u32[]{:S(2)}, u32[]{:S(2)}) collective-permute-start(f32[2,8,128]{2,1,0:T(8,128)S(1)} %fusion.340), channel_id=1, source_target_pairs={{0,16},{16,32},{32,48},{48,64},{64,80},{80,96},{96,112},{112,128},... | collective-permute-start | bytes 24584 | tf_op jit(solution)/shard_map/ppermute | solution.py:325
  43.2 6.1 %shard_map.88 = (f32[4,8,128]{2,1,0:T(8,128)}, f32[4,8,128]{2,1,0:T(8,128)}) custom-call(f32[4,2,3,8,9,128]{5,4,3,2,1,0:T(8,128)} %pad_maximum_fusion.extended_ref, f32[24,24]{1,0:T(8,128)} %stiffness_ref.5, f32[24,24]{1,0:T(8,128)} %mass_ref.5), custom_call_target="tpu_custom_call" | custom-call | flops 303562752 | bytes 922112 | tf_op jit(solution)/shard_map/pallas_call | solution.py:256
  49.4 1.3 collective-permute-start.5
  52.5 1.9 %collective-permute-start.6 = (f32[12,2,128]{2,1,0:T(2,128)S(1)}, f32[12,2,128]{2,1,0:T(2,128)S(1)}, u32[]{:S(2)}, u32[]{:S(2)}) collective-permute-start(f32[12,2,128]{2,1,0:T(2,128)S(1)} %get-tuple-element.27), channel_id=1, source_target_pairs={{0,1},{1,2},{2,3},{3,4},{4,5},{5,6},{6,7},{7,8},{8,9},{9,10},{10,1... | collective-permute-start | bytes 36872 | tf_op jit(solution)/shard_map/ppermute | solution.py:28
  54.4 6.6 %collective-permute-start.7 = (f32[12,2,128]{2,1,0:T(2,128)S(1)}, f32[12,2,128]{2,1,0:T(2,128)S(1)}, u32[]{:S(2)}, u32[]{:S(2)}) collective-permute-start(f32[12,2,128]{2,1,0:T(2,128)S(1)} %get-tuple-element.28), channel_id=1, source_target_pairs={{1,0},{2,1},{3,2},{4,3},{5,4},{6,5},{7,6},{8,7},{9,8},{10,9},{11,1... | collective-permute-start | bytes 36872 | tf_op jit(solution)/shard_map/ppermute | solution.py:30
  61.2 1.2 collective-permute-done.7
  64.3 1.9 %collective-permute-start.8 = (f32[63,64]{0,1:T(8,128)S(1)}, f32[63,64]{0,1:T(8,128)S(1)}, u32[]{:S(2)}, u32[]{:S(2)}) collective-permute-start(f32[63,64]{0,1:T(8,128)S(1)} %reduce_sum.19), channel_id=1, source_target_pairs={{0,1},{1,0},{2,3},{3,2},{4,5},{5,4},{6,7},{7,6},{8,9},{9,8},{10,11... | collective-permute-start | bytes 48392 | tf_op jit(solution)/shard_map/ppermute | solution.py:69
  66.3 3.9 %collective-permute-done.8 = f32[63,64]{0,1:T(8,128)S(1)} collective-permute-done((f32[63,64]{0,1:T(8,128)S(1)}, f32[63,64]{0,1:T(8,128)S(1)}, u32[]{:S(2)}, u32[]{:S(2)}) %collective-permute-start.8) | collective-permute-done | bytes 16160 | tf_op jit(solution)/shard_map/ppermute | solution.py:69
  70.1 1.9 %collective-permute-start.9 = (f32[63,64]{0,1:T(8,128)S(1)}, f32[63,64]{0,1:T(8,128)S(1)}, u32[]{:S(2)}, u32[]{:S(2)}) collective-permute-start(f32[63,64]{0,1:T(8,128)S(1)} %add.1198), channel_id=1, source_target_pairs={{0,2},{1,3},{2,0},{3,1},{4,6},{5,7},{6,4},{7,5},{8,10},{9,11},{10,... | collective-permute-start | bytes 48392 | tf_op jit(solution)/shard_map/ppermute | solution.py:69
  72.1 4.8 %collective-permute-done.9 = f32[63,64]{0,1:T(8,128)S(1)} collective-permute-done((f32[63,64]{0,1:T(8,128)S(1)}, f32[63,64]{0,1:T(8,128)S(1)}, u32[]{:S(2)}, u32[]{:S(2)}) %collective-permute-start.9) | collective-permute-done | bytes 16160 | tf_op jit(solution)/shard_map/ppermute | solution.py:69
  76.8 3.1 %collective-permute-start.10 = (f32[63,64]{0,1:T(8,128)S(1)}, f32[63,64]{0,1:T(8,128)S(1)}, u32[]{:S(2)}, u32[]{:S(2)}) collective-permute-start(f32[63,64]{0,1:T(8,128)S(1)} %add.1199), channel_id=1, source_target_pairs={{0,4},{1,5},{2,6},{3,7},{4,0},{5,1},{6,2},{7,3},{8,12},{9,13},{10,... | collective-permute-start | bytes 48392 | tf_op jit(solution)/shard_map/ppermute | solution.py:69
  79.9 2.7 %collective-permute-done.10 = f32[63,64]{0,1:T(8,128)S(1)} collective-permute-done((f32[63,64]{0,1:T(8,128)S(1)}, f32[63,64]{0,1:T(8,128)S(1)}, u32[]{:S(2)}, u32[]{:S(2)}) %collective-permute-start.10) | collective-permute-done | bytes 16160 | tf_op jit(solution)/shard_map/ppermute | solution.py:69
  82.6 3.6 %collective-permute-start.11 = (f32[63,64]{0,1:T(8,128)S(1)}, f32[63,64]{0,1:T(8,128)S(1)}, u32[]{:S(2)}, u32[]{:S(2)}) collective-permute-start(f32[63,64]{0,1:T(8,128)S(1)} %add.1200), channel_id=1, source_target_pairs={{0,8},{1,9},{2,10},{3,11},{4,12},{5,13},{6,14},{7,15},{8,0},{9,1},... | collective-permute-start | bytes 48392 | tf_op jit(solution)/shard_map/ppermute | solution.py:69
  86.3 3.6 %collective-permute-done.11 = f32[63,64]{0,1:T(8,128)S(1)} collective-permute-done((f32[63,64]{0,1:T(8,128)S(1)}, f32[63,64]{0,1:T(8,128)S(1)}, u32[]{:S(2)}, u32[]{:S(2)}) %collective-permute-start.11) | collective-permute-done | bytes 16160 | tf_op jit(solution)/shard_map/ppermute | solution.py:69
  90.0 2.1 %collective-permute-start.12 = (f32[63,64]{0,1:T(8,128)S(1)}, f32[63,64]{0,1:T(8,128)S(1)}, u32[]{:S(2)}, u32[]{:S(2)}) collective-permute-start(f32[63,64]{0,1:T(8,128)S(1)} %add.1201), channel_id=1, source_target_pairs={{0,16},{16,0},{32,48},{48,32},{64,80},{80,64},{96,112},{112,96},{1... | collective-permute-start | bytes 48392 | tf_op jit(solution)/shard_map/ppermute | solution.py:69
  93.1 7.8 %collective-permute-start.13 = (f32[63,64]{0,1:T(8,128)S(1)}, f32[63,64]{0,1:T(8,128)S(1)}, u32[]{:S(2)}, u32[]{:S(2)}) collective-permute-start(f32[63,64]{0,1:T(8,128)S(1)} %add.1202), channel_id=1, source_target_pairs={{0,32},{16,48},{32,0},{48,16},{64,96},{80,112},{96,64},{112,80},{1... | collective-permute-start | bytes 48392 | tf_op jit(solution)/shard_map/ppermute | solution.py:69
  100.9 1.9 %collective-permute-done.13 = f32[63,64]{0,1:T(8,128)S(1)} collective-permute-done((f32[63,64]{0,1:T(8,128)S(1)}, f32[63,64]{0,1:T(8,128)S(1)}, u32[]{:S(2)}, u32[]{:S(2)}) %collective-permute-start.13) | collective-permute-done | bytes 16160 | tf_op jit(solution)/shard_map/ppermute | solution.py:69
  102.8 7.6 %collective-permute-start.14 = (f32[63,64]{0,1:T(8,128)S(1)}, f32[63,64]{0,1:T(8,128)S(1)}, u32[]{:S(2)}, u32[]{:S(2)}) collective-permute-start(f32[63,64]{0,1:T(8,128)S(1)} %add.1203), channel_id=1, source_target_pairs={{0,64},{16,80},{32,96},{48,112},{64,0},{80,16},{96,32},{112,48},{1... | collective-permute-start | bytes 48392 | tf_op jit(solution)/shard_map/ppermute | solution.py:69
  110.4 1.9 %collective-permute-done.14 = f32[63,64]{0,1:T(8,128)S(1)} collective-permute-done((f32[63,64]{0,1:T(8,128)S(1)}, f32[63,64]{0,1:T(8,128)S(1)}, u32[]{:S(2)}, u32[]{:S(2)}) %collective-permute-start.14) | collective-permute-done | bytes 16160 | tf_op jit(solution)/shard_map/ppermute | solution.py:69
  112.3 6.1 %collective-permute-start.15 = (f32[63,64]{0,1:T(8,128)S(1)}, f32[63,64]{0,1:T(8,128)S(1)}, u32[]{:S(2)}, u32[]{:S(2)}) collective-permute-start(f32[63,64]{0,1:T(8,128)S(1)} %add.1204), channel_id=1, source_target_pairs={{0,128},{16,144},{32,160},{48,176},{64,192},{80,208},{96,224},{112... | collective-permute-start | bytes 48392 | tf_op jit(solution)/shard_map/ppermute | solution.py:69
  118.3 1.9 %collective-permute-done.15 = f32[63,64]{0,1:T(8,128)S(1)} collective-permute-done((f32[63,64]{0,1:T(8,128)S(1)}, f32[63,64]{0,1:T(8,128)S(1)}, u32[]{:S(2)}, u32[]{:S(2)}) %collective-permute-start.15) | collective-permute-done | bytes 16160 | tf_op jit(solution)/shard_map/ppermute | solution.py:69
  120.2 10.5 %collective-permute-start.16 = (f32[63,64]{0,1:T(8,128)S(1)}, f32[63,64]{0,1:T(8,128)S(1)}, u32[]{:S(2)}, u32[]{:S(2)}) collective-permute-start(f32[63,64]{0,1:T(8,128)S(1)} %add.1205), channel_id=1, source_target_pairs={{0,256},{16,272},{32,288},{48,304},{64,320},{80,336},{96,352},{112... | collective-permute-start | bytes 48392 | tf_op jit(solution)/shard_map/ppermute | solution.py:69
  130.7 2.0 %collective-permute-done.16 = f32[63,64]{0,1:T(8,128)S(1)} collective-permute-done((f32[63,64]{0,1:T(8,128)S(1)}, f32[63,64]{0,1:T(8,128)S(1)}, u32[]{:S(2)}, u32[]{:S(2)}) %collective-permute-start.16) | collective-permute-done | bytes 16160 | tf_op jit(solution)/shard_map/ppermute | solution.py:69
  (99 shorter events, 13.1 us)
Async XLA Ops:
  0.6 2.0 %copy-start = (f32[8,8,128]{2,1,0:T(8,128)S(1)}, f32[8,8,128]{2,1,0:T(8,128)}, u32[]{:S(2)}) copy-start(f32[8,8,128]{2,1,0:T(8,128)} %param.7) | copy-start | bytes 98308
  2.7 8.1 %collective-permute-start.1 = (f32[208,128]{1,0:T(8,128)S(1)}, f32[208,128]{1,0:T(8,128)S(1)}, u32[]{:S(2)}, u32[]{:S(2)}) collective-permute-start(f32[208,128]{1,0:T(8,128)S(1)} %pad_maximum_fusion.3), channel_id=1, source_target_pairs={{1,0},{2,1},{3,2},{4,3},{5,4},{6,5},{7,6},{8,7},{9,8},{10,9},{11,1... | collective-permute-start | bytes 319496 | tf_op jit(solution)/shard_map/ppermute | solution.py:48
  8.5 8.2 %collective-permute-start = (f32[8,2,128]{2,1,0:T(2,128)S(1)}, f32[8,2,128]{2,1,0:T(2,128)S(1)}, u32[]{:S(2)}, u32[]{:S(2)}) collective-permute-start(f32[8,2,128]{2,1,0:T(2,128)S(1)} %get-tuple-element.35), channel_id=1, source_target_pairs={{0,1},{1,2},{2,3},{3,4},{4,5},{5,6},{6,7},{7,8},{8,9},{9,10},{10,1... | collective-permute-start | bytes 24584 | tf_op jit(solution)/shard_map/ppermute | solution.py:52
  16.8 13.1 %collective-permute-start.3 = (f32[240,128]{1,0:T(8,128)S(1)}, f32[240,128]{1,0:T(8,128)S(1)}, u32[]{:S(2)}, u32[]{:S(2)}) collective-permute-start(f32[240,128]{1,0:T(8,128)S(1)} %pad_maximum_fusion.2), channel_id=1, source_target_pairs={{16,0},{32,16},{48,32},{64,48},{80,64},{96,80},{112,96},{128,112},... | collective-permute-start | bytes 368648 | tf_op jit(solution)/shard_map/ppermute | solution.py:48
  18.1 18.1 %collective-permute-start.2 = (f32[2,12,128]{2,1,0:T(8,128)S(1)}, f32[2,12,128]{2,1,0:T(8,128)S(1)}, u32[]{:S(2)}, u32[]{:S(2)}) collective-permute-start(f32[2,12,128]{2,1,0:T(8,128)S(1)} %get-tuple-element.31), channel_id=1, source_target_pairs={{0,16},{16,32},{32,48},{48,64},{64,80},{80,96},{96,112},{112,128},... | collective-permute-start | bytes 36872 | tf_op jit(solution)/shard_map/ppermute | solution.py:52
  31.3 5.1 %copy-start.1 = (s32[8,8,128]{2,1,0:T(8,128)S(1)}, s32[8,8,128]{2,1,0:T(8,128)}, u32[]{:S(2)}) copy-start(s32[8,8,128]{2,1,0:T(8,128)} %param.8) | copy-start | bytes 98308
  36.4 1.3 copy-start.6
  36.5 1.3 copy-start.7
  36.5 12.9 %copy-start.4 = (f32[3,8,128]{2,1,0:T(8,128)S(1)}, f32[3,8,128]{2,1,0:T(8,128)}, u32[]{:S(2)}) copy-start(f32[3,8,128]{2,1,0:T(8,128)} %get-tuple-element.8) | copy-start | bytes 36868
  36.5 12.9 %copy-start.5 = (f32[3,8,128]{2,1,0:T(8,128)S(1)}, f32[3,8,128]{2,1,0:T(8,128)}, u32[]{:S(2)}) copy-start(f32[3,8,128]{2,1,0:T(8,128)} %get-tuple-element.10) | copy-start | bytes 36868
  37.7 23.4 %copy-start.3 = (f32[63,64]{0,1:T(8,128)S(1)}, f32[63,64]{0,1:T(8,128)}, u32[]{:S(2)}) copy-start(f32[63,64]{0,1:T(8,128)} %constant.21.clone.1) | copy-start | bytes 48388
  37.8 11.6 %collective-permute-start.4 = (f32[2,8,128]{2,1,0:T(8,128)S(1)}, f32[2,8,128]{2,1,0:T(8,128)S(1)}, u32[]{:S(2)}, u32[]{:S(2)}) collective-permute-start(f32[2,8,128]{2,1,0:T(8,128)S(1)} %fusion.340), channel_id=1, source_target_pairs={{0,16},{16,32},{32,48},{48,64},{64,80},{80,96},{96,112},{112,128},... | collective-permute-start | bytes 24584 | tf_op jit(solution)/shard_map/ppermute | solution.py:325
  49.4 3.1 %collective-permute-start.5 = (f32[2,8,128]{2,1,0:T(8,128)S(1)}, f32[2,8,128]{2,1,0:T(8,128)S(1)}, u32[]{:S(2)}, u32[]{:S(2)}) collective-permute-start(f32[2,8,128]{2,1,0:T(8,128)S(1)} %get-tuple-element.23), channel_id=1, source_target_pairs={{16,0},{32,16},{48,32},{64,48},{80,64},{96,80},{112,96},{128,112},... | collective-permute-start | bytes 24584 | tf_op jit(solution)/shard_map/ppermute | solution.py:324
  52.5 8.7 %collective-permute-start.6 = (f32[12,2,128]{2,1,0:T(2,128)S(1)}, f32[12,2,128]{2,1,0:T(2,128)S(1)}, u32[]{:S(2)}, u32[]{:S(2)}) collective-permute-start(f32[12,2,128]{2,1,0:T(2,128)S(1)} %get-tuple-element.27), channel_id=1, source_target_pairs={{0,1},{1,2},{2,3},{3,4},{4,5},{5,6},{6,7},{7,8},{8,9},{9,10},{10,1... | collective-permute-start | bytes 36872 | tf_op jit(solution)/shard_map/ppermute | solution.py:28
  54.4 8.0 %collective-permute-start.7 = (f32[12,2,128]{2,1,0:T(2,128)S(1)}, f32[12,2,128]{2,1,0:T(2,128)S(1)}, u32[]{:S(2)}, u32[]{:S(2)}) collective-permute-start(f32[12,2,128]{2,1,0:T(2,128)S(1)} %get-tuple-element.28), channel_id=1, source_target_pairs={{1,0},{2,1},{3,2},{4,3},{5,4},{6,5},{7,6},{8,7},{9,8},{10,9},{11,1... | collective-permute-start | bytes 36872 | tf_op jit(solution)/shard_map/ppermute | solution.py:30
  62.6 68.1 %copy-start.8 = (f32[64]{0:T(128)S(1)}, f32[64]{0:T(128)}, u32[]{:S(2)}) copy-start(f32[64]{0:T(128)} %param.13) | copy-start | bytes 772
  63.2 72.6 %copy-start.2 = (f32[8,8,128]{2,1,0:T(8,128)}, f32[8,8,128]{2,1,0:T(8,128)S(1)}, u32[]{:S(2)}) copy-start(f32[8,8,128]{2,1,0:T(8,128)S(1)} %get-tuple-element.19) | copy-start | bytes 98308
  64.3 5.8 %collective-permute-start.8 = (f32[63,64]{0,1:T(8,128)S(1)}, f32[63,64]{0,1:T(8,128)S(1)}, u32[]{:S(2)}, u32[]{:S(2)}) collective-permute-start(f32[63,64]{0,1:T(8,128)S(1)} %reduce_sum.19), channel_id=1, source_target_pairs={{0,1},{1,0},{2,3},{3,2},{4,5},{5,4},{6,7},{7,6},{8,9},{9,8},{10,11... | collective-permute-start | bytes 48392 | tf_op jit(solution)/shard_map/ppermute | solution.py:69
  70.1 6.7 %collective-permute-start.9 = (f32[63,64]{0,1:T(8,128)S(1)}, f32[63,64]{0,1:T(8,128)S(1)}, u32[]{:S(2)}, u32[]{:S(2)}) collective-permute-start(f32[63,64]{0,1:T(8,128)S(1)} %add.1198), channel_id=1, source_target_pairs={{0,2},{1,3},{2,0},{3,1},{4,6},{5,7},{6,4},{7,5},{8,10},{9,11},{10,... | collective-permute-start | bytes 48392 | tf_op jit(solution)/shard_map/ppermute | solution.py:69
  76.8 5.8 %collective-permute-start.10 = (f32[63,64]{0,1:T(8,128)S(1)}, f32[63,64]{0,1:T(8,128)S(1)}, u32[]{:S(2)}, u32[]{:S(2)}) collective-permute-start(f32[63,64]{0,1:T(8,128)S(1)} %add.1199), channel_id=1, source_target_pairs={{0,4},{1,5},{2,6},{3,7},{4,0},{5,1},{6,2},{7,3},{8,12},{9,13},{10,... | collective-permute-start | bytes 48392 | tf_op jit(solution)/shard_map/ppermute | solution.py:69
  82.6 7.3 %collective-permute-start.11 = (f32[63,64]{0,1:T(8,128)S(1)}, f32[63,64]{0,1:T(8,128)S(1)}, u32[]{:S(2)}, u32[]{:S(2)}) collective-permute-start(f32[63,64]{0,1:T(8,128)S(1)} %add.1200), channel_id=1, source_target_pairs={{0,8},{1,9},{2,10},{3,11},{4,12},{5,13},{6,14},{7,15},{8,0},{9,1},... | collective-permute-start | bytes 48392 | tf_op jit(solution)/shard_map/ppermute | solution.py:69
  90.0 3.1 %collective-permute-start.12 = (f32[63,64]{0,1:T(8,128)S(1)}, f32[63,64]{0,1:T(8,128)S(1)}, u32[]{:S(2)}, u32[]{:S(2)}) collective-permute-start(f32[63,64]{0,1:T(8,128)S(1)} %add.1201), channel_id=1, source_target_pairs={{0,16},{16,0},{32,48},{48,32},{64,80},{80,64},{96,112},{112,96},{1... | collective-permute-start | bytes 48392 | tf_op jit(solution)/shard_map/ppermute | solution.py:69
  93.1 9.7 %collective-permute-start.13 = (f32[63,64]{0,1:T(8,128)S(1)}, f32[63,64]{0,1:T(8,128)S(1)}, u32[]{:S(2)}, u32[]{:S(2)}) collective-permute-start(f32[63,64]{0,1:T(8,128)S(1)} %add.1202), channel_id=1, source_target_pairs={{0,32},{16,48},{32,0},{48,16},{64,96},{80,112},{96,64},{112,80},{1... | collective-permute-start | bytes 48392 | tf_op jit(solution)/shard_map/ppermute | solution.py:69
  102.8 9.5 %collective-permute-start.14 = (f32[63,64]{0,1:T(8,128)S(1)}, f32[63,64]{0,1:T(8,128)S(1)}, u32[]{:S(2)}, u32[]{:S(2)}) collective-permute-start(f32[63,64]{0,1:T(8,128)S(1)} %add.1203), channel_id=1, source_target_pairs={{0,64},{16,80},{32,96},{48,112},{64,0},{80,16},{96,32},{112,48},{1... | collective-permute-start | bytes 48392 | tf_op jit(solution)/shard_map/ppermute | solution.py:69
  112.3 8.0 %collective-permute-start.15 = (f32[63,64]{0,1:T(8,128)S(1)}, f32[63,64]{0,1:T(8,128)S(1)}, u32[]{:S(2)}, u32[]{:S(2)}) collective-permute-start(f32[63,64]{0,1:T(8,128)S(1)} %add.1204), channel_id=1, source_target_pairs={{0,128},{16,144},{32,160},{48,176},{64,192},{80,208},{96,224},{112... | collective-permute-start | bytes 48392 | tf_op jit(solution)/shard_map/ppermute | solution.py:69
  120.2 12.5 %collective-permute-start.16 = (f32[63,64]{0,1:T(8,128)S(1)}, f32[63,64]{0,1:T(8,128)S(1)}, u32[]{:S(2)}, u32[]{:S(2)}) collective-permute-start(f32[63,64]{0,1:T(8,128)S(1)} %add.1205), channel_id=1, source_target_pairs={{0,256},{16,272},{32,288},{48,304},{64,320},{80,336},{96,352},{112... | collective-permute-start | bytes 48392 | tf_op jit(solution)/shard_map/ppermute | solution.py:69

commit v8 on v6

--- a/solution.py
+++ b/solution.py
@@ -342,7 +342,12 @@
         partial_volumes = (
             jnp.sum(fields_of, axis=(1, 2)).reshape(len(midpoints), REGIONS, band_cells).sum(axis=2)
         )
-        volumes = butterfly_sum(butterfly_sum(partial_volumes, "gy"), "gx")
+        lanes = 128
+        flat = partial_volumes.reshape(-1)
+        spare = -flat.size % lanes
+        dense = jnp.pad(flat, (0, spare)).reshape(-1, lanes)
+        dense = butterfly_sum(butterfly_sum(dense, "gy"), "gx")
+        volumes = dense.reshape(-1)[: flat.size].reshape(partial_volumes.shape)
         heavier_all = volumes > target[None, :]
         position = jnp.zeros((REGIONS,), jnp.int32)
         for depth in range(levels):

time: 138 us -> 135 us (0.978)
  other arithmetic: 10 us -> 8.45 us
  waiting for transfers between devices: 26.4 us -> 25 us
    ppermute x9, waiting for transfers between devices: 23.3 us -> 21.9 us  [butterfly_sum(): lax.ppermute(value, axis, [(i, i ^ stride) for i in range(count)])]
  transfers between devices with their start and end apart: 17 -> 17, of which waited for: 13 -> 13; matrix products, arithmetic and copies ran while one was open for 1% -> 1% of each run, Pallas kernels for 10% -> 11%
where the time goes in v8:
time: 135 us; the launch traced here: 133 us
  starting transfers between devices  83.6 us (62%)
  waiting for transfers between devices  25 us (19%)
  Pallas kernels  14.1 us (10%)
  other arithmetic  8.45 us (6%)
    ppermute x9, starting transfers between devices, butterfly_sum(): lax.ppermute(value, axis, [(i, i ^ stride) for i in range(count)])  54.9 us
    ppermute x9, waiting for transfers between devices, butterfly_sum(): lax.ppermute(value, axis, [(i, i ^ stride) for i in range(count)])  21.9 us
    pallas_call x1, Pallas kernels, element_energies(): pl.pallas_call(mxu_energy_kernel, out_shape=(jax.ShapeDtypeStruct(cells,...  14.1 us
    ppermute x2, starting transfers between devices, with_halo(): lax.ppermute(tail, axis, [(i, (i + 1) % count) for i in range(ends)])  9.13 us
    ppermute x2, starting transfers between devices, with_halo(): lax.ppermute(head, axis, [((i + 1) % count, i) for i in range(ends)])  7.58 us
    ppermute x2, starting transfers between devices, front_exchange(): lax.ppermute(packed, axis, [((i + 1) % count, i) for i in range(ends)])  7.07 us
    ppermute x2, starting transfers between devices, front_exchange(): tail = lax.ppermute(tail, axis, [(i, (i + 1) % count) for i in range(ends)])  4.95 us
  transfers between devices with their start and end apart: 17, of which 13 were waited for; matrix products, arithmetic and copies ran while one was open for 1% of the time, Pallas kernels for 11%

profile of v8, /device:TPU:6, one launch (start us, length us, event | category | flops | bytes accessed | tf_op | source)
XLA Modules:
  0.0 133.0 jit_solution(1157069917822578853)
XLA Ops:
  1.4 1.2 broadcast_multiply_fusion
  2.7 1.3 collective-permute-start.1
  4.0 3.0 %collective-permute-start = (f32[2,8,128]{2,1,0:T(8,128)S(1)}, f32[2,8,128]{2,1,0:T(8,128)S(1)}, u32[]{:S(2)}, u32[]{:S(2)}) collective-permute-start(f32[2,8,128]{2,1,0:T(8,128)S(1)} %get-tuple-element.23), channel_id=1, source_target_pairs={{0,16},{16,32},{32,48},{48,64},{64,80},{80,96},{96,112},{112,128},... | collective-permute-start | bytes 24584 | tf_op jit(solution)/shard_map/ppermute | solution.py:50
  7.9 5.8 %collective-permute-start.3 = (f32[240,128]{1,0:T(8,128)S(1)}, f32[240,128]{1,0:T(8,128)S(1)}, u32[]{:S(2)}, u32[]{:S(2)}) collective-permute-start(f32[240,128]{1,0:T(8,128)S(1)} %pad_maximum_fusion.1), channel_id=1, source_target_pairs={{1,0},{2,1},{3,2},{4,3},{5,4},{6,5},{7,6},{8,7},{9,8},{10,9},{11,1... | collective-permute-start | bytes 368648 | tf_op jit(solution)/shard_map/ppermute | solution.py:46
  13.8 1.9 %collective-permute-start.2 = (f32[12,2,128]{2,1,0:T(2,128)S(1)}, f32[12,2,128]{2,1,0:T(2,128)S(1)}, u32[]{:S(2)}, u32[]{:S(2)}) collective-permute-start(f32[12,2,128]{2,1,0:T(2,128)S(1)} %get-tuple-element.16), channel_id=1, source_target_pairs={{0,1},{1,2},{2,3},{3,4},{4,5},{5,6},{6,7},{7,8},{8,9},{9,10},{10,1... | collective-permute-start | bytes 36872 | tf_op jit(solution)/shard_map/ppermute | solution.py:50
  16.2 1.4 %pad_maximum_fusion.extended_ref = f32[4,2,3,9,9,128]{5,4,3,2,1,0:T(8,128)} fusion(f32[4,2,3,9,1,128]{5,4,3,2,1,0:T(1,128)S(1)} %bitcast.65, f32[4,2,3,1,8,128]{5,4,3,2,1,0:T(8,128)S(1)} %bitcast.64, f32[4,2,3,8,8,128]{5,4,3,2,1,0:T(8,128)S(1)} %broadcast_multiply_fusion), kind=kLoop, calls=%fused_computation.6 | loop fusion | flops 497664 | bytes 1990656 | tf_op jit(solution)/shard_map/concatenate | solution.py:52
  17.5 14.1 %shard_map.86 = (f32[8,8,128]{2,1,0:T(8,128)}, f32[8,8,128]{2,1,0:T(8,128)}) custom-call(f32[4,2,3,9,9,128]{5,4,3,2,1,0:T(8,128)} %pad_maximum_fusion.extended_ref, f32[24,24]{1,0:T(8,128)} %stiffness_ref.1, f32[24,24]{1,0:T(8,128)} %mass_ref.1), custom_call_target="tpu_custom_call" | custom-call | flops 607125504 | bytes 1065472 | tf_op jit(solution)/shard_map/pallas_call | solution.py:259
  31.9 2.0 %fusion.82 = (f32[8,8,128]{2,1,0:T(8,128)S(1)}, pred[8,8,128]{2,1,0:T(8,128)(4,1)S(1)}) fusion(f32[8,8,128]{2,1,0:T(8,128)} %get-tuple-element.4, f32[12,10,128]{2,1,0:T(8,128)S(1)} %get-tuple-element.15, f32[12,12,132]{2,1,0:T(8,128)S(1)} %select_maximum_fusion.4, f32[2,8,128]{2,1,0:T(8,128)S(1)} %slice_bitcast_fusion, f32[8,8,128]{2,1,0:T(8,128)S(1)} %copy-done, ...), kind=kLoop, calls=%fused_computation.110 | loop fusion | flops 3039232 | bytes 6176768 | tf_op jit(solution)/shard_map/div | solution.py:305
  33.9 1.3 collective-permute-start.5
  35.2 6.7 %collective-permute-start.4 = (f32[2,8,128]{2,1,0:T(8,128)S(1)}, f32[2,8,128]{2,1,0:T(8,128)S(1)}, u32[]{:S(2)}, u32[]{:S(2)}) collective-permute-start(f32[2,8,128]{2,1,0:T(8,128)S(1)} %get-tuple-element.21), channel_id=1, source_target_pairs={{0,16},{16,32},{32,48},{48,64},{64,80},{80,96},{96,112},{112,128},... | collective-permute-start | bytes 24584 | tf_op jit(solution)/shard_map/ppermute | solution.py:27
  42.8 2.4 %collective-permute-start.6 = (f32[12,2,128]{2,1,0:T(2,128)S(1)}, f32[12,2,128]{2,1,0:T(2,128)S(1)}, u32[]{:S(2)}, u32[]{:S(2)}) collective-permute-start(f32[12,2,128]{2,1,0:T(2,128)S(1)} %get-tuple-element.12), channel_id=1, source_target_pairs={{0,1},{1,2},{2,3},{3,4},{4,5},{5,6},{6,7},{7,8},{8,9},{9,10},{10,1... | collective-permute-start | bytes 36872 | tf_op jit(solution)/shard_map/ppermute | solution.py:27
  45.2 6.3 %collective-permute-start.7 = (f32[12,2,128]{2,1,0:T(2,128)S(1)}, f32[12,2,128]{2,1,0:T(2,128)S(1)}, u32[]{:S(2)}, u32[]{:S(2)}) collective-permute-start(f32[12,2,128]{2,1,0:T(2,128)S(1)} %get-tuple-element.13), channel_id=1, source_target_pairs={{1,0},{2,1},{3,2},{4,3},{5,4},{6,5},{7,6},{8,7},{9,8},{10,9},{11,1... | collective-permute-start | bytes 36872 | tf_op jit(solution)/shard_map/ppermute | solution.py:29
  51.6 1.2 collective-permute-done.7
  53.6 0.9 fusion.4
  54.9 1.9 %collective-permute-start.8 = (f32[32,128]{1,0:T(8,128)S(1)}, f32[32,128]{1,0:T(8,128)S(1)}, u32[]{:S(2)}, u32[]{:S(2)}) collective-permute-start(f32[32,128]{1,0:T(8,128)S(1)} %pad_bitcast_fusion), channel_id=1, source_target_pairs={{0,1},{1,0},{2,3},{3,2},{4,5},{5,4},{6,7},{7,6},{8,9},{9,8},{10,11... | collective-permute-start | bytes 49160 | tf_op jit(solution)/shard_map/ppermute | solution.py:66
  56.9 3.7 %collective-permute-done.8 = f32[32,128]{1,0:T(8,128)S(1)} collective-permute-done((f32[32,128]{1,0:T(8,128)S(1)}, f32[32,128]{1,0:T(8,128)S(1)}, u32[]{:S(2)}, u32[]{:S(2)}) %collective-permute-start.8) | collective-permute-done | bytes 16416 | tf_op jit(solution)/shard_map/ppermute | solution.py:66
  60.6 1.9 %collective-permute-start.9 = (f32[32,128]{1,0:T(8,128)S(1)}, f32[32,128]{1,0:T(8,128)S(1)}, u32[]{:S(2)}, u32[]{:S(2)}) collective-permute-start(f32[32,128]{1,0:T(8,128)S(1)} %fusion.293), channel_id=1, source_target_pairs={{0,2},{1,3},{2,0},{3,1},{4,6},{5,7},{6,4},{7,5},{8,10},{9,11},{10,... | collective-permute-start | bytes 49160 | tf_op jit(solution)/shard_map/ppermute | solution.py:66
  62.5 4.6 %collective-permute-done.9 = f32[32,128]{1,0:T(8,128)S(1)} collective-permute-done((f32[32,128]{1,0:T(8,128)S(1)}, f32[32,128]{1,0:T(8,128)S(1)}, u32[]{:S(2)}, u32[]{:S(2)}) %collective-permute-start.9) | collective-permute-done | bytes 16416 | tf_op jit(solution)/shard_map/ppermute | solution.py:66
  67.1 3.1 %collective-permute-start.10 = (f32[32,128]{1,0:T(8,128)S(1)}, f32[32,128]{1,0:T(8,128)S(1)}, u32[]{:S(2)}, u32[]{:S(2)}) collective-permute-start(f32[32,128]{1,0:T(8,128)S(1)} %fusion.297), channel_id=1, source_target_pairs={{0,4},{1,5},{2,6},{3,7},{4,0},{5,1},{6,2},{7,3},{8,12},{9,13},{10,... | collective-permute-start | bytes 49160 | tf_op jit(solution)/shard_map/ppermute | solution.py:66
  70.2 2.5 %collective-permute-done.10 = f32[32,128]{1,0:T(8,128)S(1)} collective-permute-done((f32[32,128]{1,0:T(8,128)S(1)}, f32[32,128]{1,0:T(8,128)S(1)}, u32[]{:S(2)}, u32[]{:S(2)}) %collective-permute-start.10) | collective-permute-done | bytes 16416 | tf_op jit(solution)/shard_map/ppermute | solution.py:66
  72.7 3.7 %collective-permute-start.11 = (f32[32,128]{1,0:T(8,128)S(1)}, f32[32,128]{1,0:T(8,128)S(1)}, u32[]{:S(2)}, u32[]{:S(2)}) collective-permute-start(f32[32,128]{1,0:T(8,128)S(1)} %add.1202), channel_id=1, source_target_pairs={{0,8},{1,9},{2,10},{3,11},{4,12},{5,13},{6,14},{7,15},{8,0},{9,1},... | collective-permute-start | bytes 49160 | tf_op jit(solution)/shard_map/ppermute | solution.py:66
  76.4 3.5 %collective-permute-done.11 = f32[32,128]{1,0:T(8,128)S(1)} collective-permute-done((f32[32,128]{1,0:T(8,128)S(1)}, f32[32,128]{1,0:T(8,128)S(1)}, u32[]{:S(2)}, u32[]{:S(2)}) %collective-permute-start.11) | collective-permute-done | bytes 16416 | tf_op jit(solution)/shard_map/ppermute | solution.py:66
  79.9 3.8 %collective-permute-start.12 = (f32[32,128]{1,0:T(8,128)S(1)}, f32[32,128]{1,0:T(8,128)S(1)}, u32[]{:S(2)}, u32[]{:S(2)}) collective-permute-start(f32[32,128]{1,0:T(8,128)S(1)} %add.1203), channel_id=1, source_target_pairs={{0,16},{16,0},{32,48},{48,32},{64,80},{80,64},{96,112},{112,96},{1... | collective-permute-start | bytes 49160 | tf_op jit(solution)/shard_map/ppermute | solution.py:66
  83.7 0.8 collective-permute-done.12
  84.5 13.9 %collective-permute-start.13 = (f32[32,128]{1,0:T(8,128)S(1)}, f32[32,128]{1,0:T(8,128)S(1)}, u32[]{:S(2)}, u32[]{:S(2)}) collective-permute-start(f32[32,128]{1,0:T(8,128)S(1)} %add.1204), channel_id=1, source_target_pairs={{0,32},{16,48},{32,0},{48,16},{64,96},{80,112},{96,64},{112,80},{1... | collective-permute-start | bytes 49160 | tf_op jit(solution)/shard_map/ppermute | solution.py:66
  98.4 1.7 %collective-permute-done.13 = f32[32,128]{1,0:T(8,128)S(1)} collective-permute-done((f32[32,128]{1,0:T(8,128)S(1)}, f32[32,128]{1,0:T(8,128)S(1)}, u32[]{:S(2)}, u32[]{:S(2)}) %collective-permute-start.13) | collective-permute-done | bytes 16416 | tf_op jit(solution)/shard_map/ppermute | solution.py:66
  100.1 8.8 %collective-permute-start.14 = (f32[32,128]{1,0:T(8,128)S(1)}, f32[32,128]{1,0:T(8,128)S(1)}, u32[]{:S(2)}, u32[]{:S(2)}) collective-permute-start(f32[32,128]{1,0:T(8,128)S(1)} %add.1205), channel_id=1, source_target_pairs={{0,64},{16,80},{32,96},{48,112},{64,0},{80,16},{96,32},{112,48},{1... | collective-permute-start | bytes 49160 | tf_op jit(solution)/shard_map/ppermute | solution.py:66
  108.9 1.7 %collective-permute-done.14 = f32[32,128]{1,0:T(8,128)S(1)} collective-permute-done((f32[32,128]{1,0:T(8,128)S(1)}, f32[32,128]{1,0:T(8,128)S(1)}, u32[]{:S(2)}, u32[]{:S(2)}) %collective-permute-start.14) | collective-permute-done | bytes 16416 | tf_op jit(solution)/shard_map/ppermute | solution.py:66
  110.6 6.1 %collective-permute-start.15 = (f32[32,128]{1,0:T(8,128)S(1)}, f32[32,128]{1,0:T(8,128)S(1)}, u32[]{:S(2)}, u32[]{:S(2)}) collective-permute-start(f32[32,128]{1,0:T(8,128)S(1)} %add.1206), channel_id=1, source_target_pairs={{0,128},{16,144},{32,160},{48,176},{64,192},{80,208},{96,224},{112... | collective-permute-start | bytes 49160 | tf_op jit(solution)/shard_map/ppermute | solution.py:66
  116.7 1.7 %collective-permute-done.15 = f32[32,128]{1,0:T(8,128)S(1)} collective-permute-done((f32[32,128]{1,0:T(8,128)S(1)}, f32[32,128]{1,0:T(8,128)S(1)}, u32[]{:S(2)}, u32[]{:S(2)}) %collective-permute-start.15) | collective-permute-done | bytes 16416 | tf_op jit(solution)/shard_map/ppermute | solution.py:66
  118.4 11.7 %collective-permute-start.16 = (f32[32,128]{1,0:T(8,128)S(1)}, f32[32,128]{1,0:T(8,128)S(1)}, u32[]{:S(2)}, u32[]{:S(2)}) collective-permute-start(f32[32,128]{1,0:T(8,128)S(1)} %add.1207), channel_id=1, source_target_pairs={{0,256},{16,272},{32,288},{48,304},{64,320},{80,336},{96,352},{112... | collective-permute-start | bytes 49160 | tf_op jit(solution)/shard_map/ppermute | solution.py:66
  130.1 1.7 %collective-permute-done.16 = f32[32,128]{1,0:T(8,128)S(1)} collective-permute-done((f32[32,128]{1,0:T(8,128)S(1)}, f32[32,128]{1,0:T(8,128)S(1)}, u32[]{:S(2)}, u32[]{:S(2)}) %collective-permute-start.16) | collective-permute-done | bytes 16416 | tf_op jit(solution)/shard_map/ppermute | solution.py:66
  (75 shorter events, 5.6 us)
Async XLA Ops:
  0.6 2.0 %copy-start = (f32[8,8,128]{2,1,0:T(8,128)S(1)}, f32[8,8,128]{2,1,0:T(8,128)}, u32[]{:S(2)}) copy-start(f32[8,8,128]{2,1,0:T(8,128)} %param.7) | copy-start | bytes 98308
  2.7 5.2 %collective-permute-start.1 = (f32[208,128]{1,0:T(8,128)S(1)}, f32[208,128]{1,0:T(8,128)S(1)}, u32[]{:S(2)}, u32[]{:S(2)}) collective-permute-start(f32[208,128]{1,0:T(8,128)S(1)} %pad_maximum_fusion.3), channel_id=1, source_target_pairs={{16,0},{32,16},{48,32},{64,48},{80,64},{96,80},{112,96},{128,112},... | collective-permute-start | bytes 319496 | tf_op jit(solution)/shard_map/ppermute | solution.py:46
  4.0 3.8 %collective-permute-start = (f32[2,8,128]{2,1,0:T(8,128)S(1)}, f32[2,8,128]{2,1,0:T(8,128)S(1)}, u32[]{:S(2)}, u32[]{:S(2)}) collective-permute-start(f32[2,8,128]{2,1,0:T(8,128)S(1)} %get-tuple-element.23), channel_id=1, source_target_pairs={{0,16},{16,32},{32,48},{48,64},{64,80},{80,96},{96,112},{112,128},... | collective-permute-start | bytes 24584 | tf_op jit(solution)/shard_map/ppermute | solution.py:50
  7.9 8.2 %collective-permute-start.3 = (f32[240,128]{1,0:T(8,128)S(1)}, f32[240,128]{1,0:T(8,128)S(1)}, u32[]{:S(2)}, u32[]{:S(2)}) collective-permute-start(f32[240,128]{1,0:T(8,128)S(1)} %pad_maximum_fusion.1), channel_id=1, source_target_pairs={{1,0},{2,1},{3,2},{4,3},{5,4},{6,5},{7,6},{8,7},{9,8},{10,9},{11,1... | collective-permute-start | bytes 368648 | tf_op jit(solution)/shard_map/ppermute | solution.py:46
  13.8 17.9 %collective-permute-start.2 = (f32[12,2,128]{2,1,0:T(2,128)S(1)}, f32[12,2,128]{2,1,0:T(2,128)S(1)}, u32[]{:S(2)}, u32[]{:S(2)}) collective-permute-start(f32[12,2,128]{2,1,0:T(2,128)S(1)} %get-tuple-element.16), channel_id=1, source_target_pairs={{0,1},{1,2},{2,3},{3,4},{4,5},{5,6},{6,7},{7,8},{8,9},{9,10},{10,1... | collective-permute-start | bytes 36872 | tf_op jit(solution)/shard_map/ppermute | solution.py:50
  17.5 14.4 %copy-start.2 = (s32[8,8,128]{2,1,0:T(8,128)S(1)}, s32[8,8,128]{2,1,0:T(8,128)}, u32[]{:S(2)}) copy-start(s32[8,8,128]{2,1,0:T(8,128)} %param.8) | copy-start | bytes 98308
  31.9 19.6 %copy-start.3 = (f32[63,64]{0,1:T(8,128)S(1)}, f32[63,64]{0,1:T(8,128)}, u32[]{:S(2)}) copy-start(f32[63,64]{0,1:T(8,128)} %constant.25.clone.1) | copy-start | bytes 48388
  33.9 8.0 %collective-permute-start.5 = (f32[2,8,128]{2,1,0:T(8,128)S(1)}, f32[2,8,128]{2,1,0:T(8,128)S(1)}, u32[]{:S(2)}, u32[]{:S(2)}) collective-permute-start(f32[2,8,128]{2,1,0:T(8,128)S(1)} %get-tuple-element.22), channel_id=1, source_target_pairs={{16,0},{32,16},{48,32},{64,48},{80,64},{96,80},{112,96},{128,112},... | collective-permute-start | bytes 24584 | tf_op jit(solution)/shard_map/ppermute | solution.py:29
  35.2 7.6 %collective-permute-start.4 = (f32[2,8,128]{2,1,0:T(8,128)S(1)}, f32[2,8,128]{2,1,0:T(8,128)S(1)}, u32[]{:S(2)}, u32[]{:S(2)}) collective-permute-start(f32[2,8,128]{2,1,0:T(8,128)S(1)} %get-tuple-element.21), channel_id=1, source_target_pairs={{0,16},{16,32},{32,48},{48,64},{64,80},{80,96},{96,112},{112,128},... | collective-permute-start | bytes 24584 | tf_op jit(solution)/shard_map/ppermute | solution.py:27
  42.8 8.8 %collective-permute-start.6 = (f32[12,2,128]{2,1,0:T(2,128)S(1)}, f32[12,2,128]{2,1,0:T(2,128)S(1)}, u32[]{:S(2)}, u32[]{:S(2)}) collective-permute-start(f32[12,2,128]{2,1,0:T(2,128)S(1)} %get-tuple-element.12), channel_id=1, source_target_pairs={{0,1},{1,2},{2,3},{3,4},{4,5},{5,6},{6,7},{7,8},{8,9},{9,10},{10,1... | collective-permute-start | bytes 36872 | tf_op jit(solution)/shard_map/ppermute | solution.py:27
  45.2 7.7 %collective-permute-start.7 = (f32[12,2,128]{2,1,0:T(2,128)S(1)}, f32[12,2,128]{2,1,0:T(2,128)S(1)}, u32[]{:S(2)}, u32[]{:S(2)}) collective-permute-start(f32[12,2,128]{2,1,0:T(2,128)S(1)} %get-tuple-element.13), channel_id=1, source_target_pairs={{1,0},{2,1},{3,2},{4,3},{5,4},{6,5},{7,6},{8,7},{9,8},{10,9},{11,1... | collective-permute-start | bytes 36872 | tf_op jit(solution)/shard_map/ppermute | solution.py:29
  53.1 77.1 %copy-start.4 = (f32[64]{0:T(128)S(1)}, f32[64]{0:T(128)}, u32[]{:S(2)}) copy-start(f32[64]{0:T(128)} %param.13) | copy-start | bytes 772
  53.6 79.4 %copy-start.1 = (f32[8,8,128]{2,1,0:T(8,128)}, f32[8,8,128]{2,1,0:T(8,128)S(1)}, u32[]{:S(2)}) copy-start(f32[8,8,128]{2,1,0:T(8,128)S(1)} %get-tuple-element.7) | copy-start | bytes 98308
  54.9 5.6 %collective-permute-start.8 = (f32[32,128]{1,0:T(8,128)S(1)}, f32[32,128]{1,0:T(8,128)S(1)}, u32[]{:S(2)}, u32[]{:S(2)}) collective-permute-start(f32[32,128]{1,0:T(8,128)S(1)} %pad_bitcast_fusion), channel_id=1, source_target_pairs={{0,1},{1,0},{2,3},{3,2},{4,5},{5,4},{6,7},{7,6},{8,9},{9,8},{10,11... | collective-permute-start | bytes 49160 | tf_op jit(solution)/shard_map/ppermute | solution.py:66
  60.6 6.5 %collective-permute-start.9 = (f32[32,128]{1,0:T(8,128)S(1)}, f32[32,128]{1,0:T(8,128)S(1)}, u32[]{:S(2)}, u32[]{:S(2)}) collective-permute-start(f32[32,128]{1,0:T(8,128)S(1)} %fusion.293), channel_id=1, source_target_pairs={{0,2},{1,3},{2,0},{3,1},{4,6},{5,7},{6,4},{7,5},{8,10},{9,11},{10,... | collective-permute-start | bytes 49160 | tf_op jit(solution)/shard_map/ppermute | solution.py:66
  67.1 5.6 %collective-permute-start.10 = (f32[32,128]{1,0:T(8,128)S(1)}, f32[32,128]{1,0:T(8,128)S(1)}, u32[]{:S(2)}, u32[]{:S(2)}) collective-permute-start(f32[32,128]{1,0:T(8,128)S(1)} %fusion.297), channel_id=1, source_target_pairs={{0,4},{1,5},{2,6},{3,7},{4,0},{5,1},{6,2},{7,3},{8,12},{9,13},{10,... | collective-permute-start | bytes 49160 | tf_op jit(solution)/shard_map/ppermute | solution.py:66
  72.7 7.1 %collective-permute-start.11 = (f32[32,128]{1,0:T(8,128)S(1)}, f32[32,128]{1,0:T(8,128)S(1)}, u32[]{:S(2)}, u32[]{:S(2)}) collective-permute-start(f32[32,128]{1,0:T(8,128)S(1)} %add.1202), channel_id=1, source_target_pairs={{0,8},{1,9},{2,10},{3,11},{4,12},{5,13},{6,14},{7,15},{8,0},{9,1},... | collective-permute-start | bytes 49160 | tf_op jit(solution)/shard_map/ppermute | solution.py:66
  79.9 4.6 %collective-permute-start.12 = (f32[32,128]{1,0:T(8,128)S(1)}, f32[32,128]{1,0:T(8,128)S(1)}, u32[]{:S(2)}, u32[]{:S(2)}) collective-permute-start(f32[32,128]{1,0:T(8,128)S(1)} %add.1203), channel_id=1, source_target_pairs={{0,16},{16,0},{32,48},{48,32},{64,80},{80,64},{96,112},{112,96},{1... | collective-permute-start | bytes 49160 | tf_op jit(solution)/shard_map/ppermute | solution.py:66
  84.5 15.6 %collective-permute-start.13 = (f32[32,128]{1,0:T(8,128)S(1)}, f32[32,128]{1,0:T(8,128)S(1)}, u32[]{:S(2)}, u32[]{:S(2)}) collective-permute-start(f32[32,128]{1,0:T(8,128)S(1)} %add.1204), channel_id=1, source_target_pairs={{0,32},{16,48},{32,0},{48,16},{64,96},{80,112},{96,64},{112,80},{1... | collective-permute-start | bytes 49160 | tf_op jit(solution)/shard_map/ppermute | solution.py:66
  100.1 10.5 %collective-permute-start.14 = (f32[32,128]{1,0:T(8,128)S(1)}, f32[32,128]{1,0:T(8,128)S(1)}, u32[]{:S(2)}, u32[]{:S(2)}) collective-permute-start(f32[32,128]{1,0:T(8,128)S(1)} %add.1205), channel_id=1, source_target_pairs={{0,64},{16,80},{32,96},{48,112},{64,0},{80,16},{96,32},{112,48},{1... | collective-permute-start | bytes 49160 | tf_op jit(solution)/shard_map/ppermute | solution.py:66
  110.6 7.8 %collective-permute-start.15 = (f32[32,128]{1,0:T(8,128)S(1)}, f32[32,128]{1,0:T(8,128)S(1)}, u32[]{:S(2)}, u32[]{:S(2)}) collective-permute-start(f32[32,128]{1,0:T(8,128)S(1)} %add.1206), channel_id=1, source_target_pairs={{0,128},{16,144},{32,160},{48,176},{64,192},{80,208},{96,224},{112... | collective-permute-start | bytes 49160 | tf_op jit(solution)/shard_map/ppermute | solution.py:66
  118.4 13.4 %collective-permute-start.16 = (f32[32,128]{1,0:T(8,128)S(1)}, f32[32,128]{1,0:T(8,128)S(1)}, u32[]{:S(2)}, u32[]{:S(2)}) collective-permute-start(f32[32,128]{1,0:T(8,128)S(1)} %add.1207), channel_id=1, source_target_pairs={{0,256},{16,272},{32,288},{48,304},{64,320},{80,336},{96,352},{112... | collective-permute-start | bytes 49160 | tf_op jit(solution)/shard_map/ppermute | solution.py:66

commit v9 on v8

--- a/solution.py
+++ b/solution.py
@@ -228,7 +228,7 @@
         products[...] = jnp.dot(
             coupling_ref[...],
             adjoint_rows[...],
-            precision=lax.Precision.HIGHEST,
+            precision=lax.Precision.HIGH,
             preferred_element_type=jnp.float32,
         )
 

time: 135 us -> 133 us (0.985)
  Pallas kernels: 14.1 us -> 11.6 us
    pallas_call x1, Pallas kernels: 14.1 us -> 11.6 us  [element_energies(): pl.pallas_call(mxu_energy_kernel, out_shape=(jax.ShapeDtypeStruct(cells,...]
  transfers between devices with their start and end apart: 17 -> 17, of which waited for: 13 -> 13; matrix products, arithmetic and copies ran while one was open for 1% -> 1% of each run, Pallas kernels for 11% -> 9%
where the time goes in v9:
time: 133 us; the launch traced here: 131 us
  starting transfers between devices  83.6 us (63%)
  waiting for transfers between devices  25 us (19%)
  Pallas kernels  11.6 us (9%)
  other arithmetic  8.45 us (6%)
    ppermute x9, starting transfers between devices, butterfly_sum(): lax.ppermute(value, axis, [(i, i ^ stride) for i in range(count)])  54.9 us
    ppermute x9, waiting for transfers between devices, butterfly_sum(): lax.ppermute(value, axis, [(i, i ^ stride) for i in range(count)])  21.9 us
    pallas_call x1, Pallas kernels, element_energies(): pl.pallas_call(mxu_energy_kernel, out_shape=(jax.ShapeDtypeStruct(cells,...  11.6 us
    ppermute x2, starting transfers between devices, with_halo(): lax.ppermute(tail, axis, [(i, (i + 1) % count) for i in range(ends)])  9.13 us
    ppermute x2, starting transfers between devices, with_halo(): lax.ppermute(head, axis, [((i + 1) % count, i) for i in range(ends)])  7.58 us
    ppermute x2, starting transfers between devices, front_exchange(): lax.ppermute(packed, axis, [((i + 1) % count, i) for i in range(ends)])  7.07 us
    ppermute x2, starting transfers between devices, front_exchange(): tail = lax.ppermute(tail, axis, [(i, (i + 1) % count) for i in range(ends)])  4.95 us
  transfers between devices with their start and end apart: 17, of which 13 were waited for; matrix products, arithmetic and copies ran while one was open for 1% of the time, Pallas kernels for 9%

profile of v9, /device:TPU:6, one launch (start us, length us, event | category | flops | bytes accessed | tf_op | source)
XLA Modules:
  0.0 130.5 jit_solution(4601937510329589859)
XLA Ops:
  1.4 1.2 broadcast_multiply_fusion
  2.7 1.3 collective-permute-start.1
  4.0 3.0 %collective-permute-start = (f32[2,8,128]{2,1,0:T(8,128)S(1)}, f32[2,8,128]{2,1,0:T(8,128)S(1)}, u32[]{:S(2)}, u32[]{:S(2)}) collective-permute-start(f32[2,8,128]{2,1,0:T(8,128)S(1)} %get-tuple-element.23), channel_id=1, source_target_pairs={{0,16},{16,32},{32,48},{48,64},{64,80},{80,96},{96,112},{112,128},... | collective-permute-start | bytes 24584 | tf_op jit(solution)/shard_map/ppermute | solution.py:50
  7.9 5.8 %collective-permute-start.3 = (f32[240,128]{1,0:T(8,128)S(1)}, f32[240,128]{1,0:T(8,128)S(1)}, u32[]{:S(2)}, u32[]{:S(2)}) collective-permute-start(f32[240,128]{1,0:T(8,128)S(1)} %pad_maximum_fusion.1), channel_id=1, source_target_pairs={{1,0},{2,1},{3,2},{4,3},{5,4},{6,5},{7,6},{8,7},{9,8},{10,9},{11,1... | collective-permute-start | bytes 368648 | tf_op jit(solution)/shard_map/ppermute | solution.py:46
  13.8 1.9 %collective-permute-start.2 = (f32[12,2,128]{2,1,0:T(2,128)S(1)}, f32[12,2,128]{2,1,0:T(2,128)S(1)}, u32[]{:S(2)}, u32[]{:S(2)}) collective-permute-start(f32[12,2,128]{2,1,0:T(2,128)S(1)} %get-tuple-element.16), channel_id=1, source_target_pairs={{0,1},{1,2},{2,3},{3,4},{4,5},{5,6},{6,7},{7,8},{8,9},{9,10},{10,1... | collective-permute-start | bytes 36872 | tf_op jit(solution)/shard_map/ppermute | solution.py:50
  16.2 1.4 %pad_maximum_fusion.extended_ref = f32[4,2,3,9,9,128]{5,4,3,2,1,0:T(8,128)} fusion(f32[4,2,3,9,1,128]{5,4,3,2,1,0:T(1,128)S(1)} %bitcast.65, f32[4,2,3,1,8,128]{5,4,3,2,1,0:T(8,128)S(1)} %bitcast.64, f32[4,2,3,8,8,128]{5,4,3,2,1,0:T(8,128)S(1)} %broadcast_multiply_fusion), kind=kLoop, calls=%fused_computation.6 | loop fusion | flops 497664 | bytes 1990656 | tf_op jit(solution)/shard_map/concatenate | solution.py:52
  17.5 11.6 %shard_map.86 = (f32[8,8,128]{2,1,0:T(8,128)}, f32[8,8,128]{2,1,0:T(8,128)}) custom-call(f32[4,2,3,9,9,128]{5,4,3,2,1,0:T(8,128)} %pad_maximum_fusion.extended_ref, f32[24,24]{1,0:T(8,128)} %stiffness_ref.1, f32[24,24]{1,0:T(8,128)} %mass_ref.1), custom_call_target="tpu_custom_call" | custom-call | flops 607125504 | bytes 1065472 | tf_op jit(solution)/shard_map/pallas_call | solution.py:259
  29.4 2.0 %fusion.82 = (f32[8,8,128]{2,1,0:T(8,128)S(1)}, pred[8,8,128]{2,1,0:T(8,128)(4,1)S(1)}) fusion(f32[8,8,128]{2,1,0:T(8,128)} %get-tuple-element.4, f32[12,10,128]{2,1,0:T(8,128)S(1)} %get-tuple-element.15, f32[12,12,132]{2,1,0:T(8,128)S(1)} %select_maximum_fusion.4, f32[2,8,128]{2,1,0:T(8,128)S(1)} %slice_bitcast_fusion, f32[8,8,128]{2,1,0:T(8,128)S(1)} %copy-done, ...), kind=kLoop, calls=%fused_computation.110 | loop fusion | flops 3039232 | bytes 6176768 | tf_op jit(solution)/shard_map/div | solution.py:305
  31.4 1.3 collective-permute-start.5
  32.7 6.7 %collective-permute-start.4 = (f32[2,8,128]{2,1,0:T(8,128)S(1)}, f32[2,8,128]{2,1,0:T(8,128)S(1)}, u32[]{:S(2)}, u32[]{:S(2)}) collective-permute-start(f32[2,8,128]{2,1,0:T(8,128)S(1)} %get-tuple-element.21), channel_id=1, source_target_pairs={{0,16},{16,32},{32,48},{48,64},{64,80},{80,96},{96,112},{112,128},... | collective-permute-start | bytes 24584 | tf_op jit(solution)/shard_map/ppermute | solution.py:27
  40.3 2.4 %collective-permute-start.6 = (f32[12,2,128]{2,1,0:T(2,128)S(1)}, f32[12,2,128]{2,1,0:T(2,128)S(1)}, u32[]{:S(2)}, u32[]{:S(2)}) collective-permute-start(f32[12,2,128]{2,1,0:T(2,128)S(1)} %get-tuple-element.12), channel_id=1, source_target_pairs={{0,1},{1,2},{2,3},{3,4},{4,5},{5,6},{6,7},{7,8},{8,9},{9,10},{10,1... | collective-permute-start | bytes 36872 | tf_op jit(solution)/shard_map/ppermute | solution.py:27
  42.7 6.3 %collective-permute-start.7 = (f32[12,2,128]{2,1,0:T(2,128)S(1)}, f32[12,2,128]{2,1,0:T(2,128)S(1)}, u32[]{:S(2)}, u32[]{:S(2)}) collective-permute-start(f32[12,2,128]{2,1,0:T(2,128)S(1)} %get-tuple-element.13), channel_id=1, source_target_pairs={{1,0},{2,1},{3,2},{4,3},{5,4},{6,5},{7,6},{8,7},{9,8},{10,9},{11,1... | collective-permute-start | bytes 36872 | tf_op jit(solution)/shard_map/ppermute | solution.py:29
  49.1 1.2 collective-permute-done.7
  51.1 0.9 fusion.4
  52.4 1.9 %collective-permute-start.8 = (f32[32,128]{1,0:T(8,128)S(1)}, f32[32,128]{1,0:T(8,128)S(1)}, u32[]{:S(2)}, u32[]{:S(2)}) collective-permute-start(f32[32,128]{1,0:T(8,128)S(1)} %pad_bitcast_fusion), channel_id=1, source_target_pairs={{0,1},{1,0},{2,3},{3,2},{4,5},{5,4},{6,7},{7,6},{8,9},{9,8},{10,11... | collective-permute-start | bytes 49160 | tf_op jit(solution)/shard_map/ppermute | solution.py:66
  54.4 3.7 %collective-permute-done.8 = f32[32,128]{1,0:T(8,128)S(1)} collective-permute-done((f32[32,128]{1,0:T(8,128)S(1)}, f32[32,128]{1,0:T(8,128)S(1)}, u32[]{:S(2)}, u32[]{:S(2)}) %collective-permute-start.8) | collective-permute-done | bytes 16416 | tf_op jit(solution)/shard_map/ppermute | solution.py:66
  58.1 1.9 %collective-permute-start.9 = (f32[32,128]{1,0:T(8,128)S(1)}, f32[32,128]{1,0:T(8,128)S(1)}, u32[]{:S(2)}, u32[]{:S(2)}) collective-permute-start(f32[32,128]{1,0:T(8,128)S(1)} %fusion.293), channel_id=1, source_target_pairs={{0,2},{1,3},{2,0},{3,1},{4,6},{5,7},{6,4},{7,5},{8,10},{9,11},{10,... | collective-permute-start | bytes 49160 | tf_op jit(solution)/shard_map/ppermute | solution.py:66
  60.0 4.6 %collective-permute-done.9 = f32[32,128]{1,0:T(8,128)S(1)} collective-permute-done((f32[32,128]{1,0:T(8,128)S(1)}, f32[32,128]{1,0:T(8,128)S(1)}, u32[]{:S(2)}, u32[]{:S(2)}) %collective-permute-start.9) | collective-permute-done | bytes 16416 | tf_op jit(solution)/shard_map/ppermute | solution.py:66
  64.6 3.1 %collective-permute-start.10 = (f32[32,128]{1,0:T(8,128)S(1)}, f32[32,128]{1,0:T(8,128)S(1)}, u32[]{:S(2)}, u32[]{:S(2)}) collective-permute-start(f32[32,128]{1,0:T(8,128)S(1)} %fusion.297), channel_id=1, source_target_pairs={{0,4},{1,5},{2,6},{3,7},{4,0},{5,1},{6,2},{7,3},{8,12},{9,13},{10,... | collective-permute-start | bytes 49160 | tf_op jit(solution)/shard_map/ppermute | solution.py:66
  67.7 2.5 %collective-permute-done.10 = f32[32,128]{1,0:T(8,128)S(1)} collective-permute-done((f32[32,128]{1,0:T(8,128)S(1)}, f32[32,128]{1,0:T(8,128)S(1)}, u32[]{:S(2)}, u32[]{:S(2)}) %collective-permute-start.10) | collective-permute-done | bytes 16416 | tf_op jit(solution)/shard_map/ppermute | solution.py:66
  70.2 3.7 %collective-permute-start.11 = (f32[32,128]{1,0:T(8,128)S(1)}, f32[32,128]{1,0:T(8,128)S(1)}, u32[]{:S(2)}, u32[]{:S(2)}) collective-permute-start(f32[32,128]{1,0:T(8,128)S(1)} %add.1202), channel_id=1, source_target_pairs={{0,8},{1,9},{2,10},{3,11},{4,12},{5,13},{6,14},{7,15},{8,0},{9,1},... | collective-permute-start | bytes 49160 | tf_op jit(solution)/shard_map/ppermute | solution.py:66
  73.9 3.5 %collective-permute-done.11 = f32[32,128]{1,0:T(8,128)S(1)} collective-permute-done((f32[32,128]{1,0:T(8,128)S(1)}, f32[32,128]{1,0:T(8,128)S(1)}, u32[]{:S(2)}, u32[]{:S(2)}) %collective-permute-start.11) | collective-permute-done | bytes 16416 | tf_op jit(solution)/shard_map/ppermute | solution.py:66
  77.3 3.8 %collective-permute-start.12 = (f32[32,128]{1,0:T(8,128)S(1)}, f32[32,128]{1,0:T(8,128)S(1)}, u32[]{:S(2)}, u32[]{:S(2)}) collective-permute-start(f32[32,128]{1,0:T(8,128)S(1)} %add.1203), channel_id=1, source_target_pairs={{0,16},{16,0},{32,48},{48,32},{64,80},{80,64},{96,112},{112,96},{1... | collective-permute-start | bytes 49160 | tf_op jit(solution)/shard_map/ppermute | solution.py:66
  81.2 0.8 collective-permute-done.12
  82.0 13.9 %collective-permute-start.13 = (f32[32,128]{1,0:T(8,128)S(1)}, f32[32,128]{1,0:T(8,128)S(1)}, u32[]{:S(2)}, u32[]{:S(2)}) collective-permute-start(f32[32,128]{1,0:T(8,128)S(1)} %add.1204), channel_id=1, source_target_pairs={{0,32},{16,48},{32,0},{48,16},{64,96},{80,112},{96,64},{112,80},{1... | collective-permute-start | bytes 49160 | tf_op jit(solution)/shard_map/ppermute | solution.py:66
  95.9 1.7 %collective-permute-done.13 = f32[32,128]{1,0:T(8,128)S(1)} collective-permute-done((f32[32,128]{1,0:T(8,128)S(1)}, f32[32,128]{1,0:T(8,128)S(1)}, u32[]{:S(2)}, u32[]{:S(2)}) %collective-permute-start.13) | collective-permute-done | bytes 16416 | tf_op jit(solution)/shard_map/ppermute | solution.py:66
  97.6 8.8 %collective-permute-start.14 = (f32[32,128]{1,0:T(8,128)S(1)}, f32[32,128]{1,0:T(8,128)S(1)}, u32[]{:S(2)}, u32[]{:S(2)}) collective-permute-start(f32[32,128]{1,0:T(8,128)S(1)} %add.1205), channel_id=1, source_target_pairs={{0,64},{16,80},{32,96},{48,112},{64,0},{80,16},{96,32},{112,48},{1... | collective-permute-start | bytes 49160 | tf_op jit(solution)/shard_map/ppermute | solution.py:66
  106.4 1.7 %collective-permute-done.14 = f32[32,128]{1,0:T(8,128)S(1)} collective-permute-done((f32[32,128]{1,0:T(8,128)S(1)}, f32[32,128]{1,0:T(8,128)S(1)}, u32[]{:S(2)}, u32[]{:S(2)}) %collective-permute-start.14) | collective-permute-done | bytes 16416 | tf_op jit(solution)/shard_map/ppermute | solution.py:66
  108.1 6.1 %collective-permute-start.15 = (f32[32,128]{1,0:T(8,128)S(1)}, f32[32,128]{1,0:T(8,128)S(1)}, u32[]{:S(2)}, u32[]{:S(2)}) collective-permute-start(f32[32,128]{1,0:T(8,128)S(1)} %add.1206), channel_id=1, source_target_pairs={{0,128},{16,144},{32,160},{48,176},{64,192},{80,208},{96,224},{112... | collective-permute-start | bytes 49160 | tf_op jit(solution)/shard_map/ppermute | solution.py:66
  114.2 1.7 %collective-permute-done.15 = f32[32,128]{1,0:T(8,128)S(1)} collective-permute-done((f32[32,128]{1,0:T(8,128)S(1)}, f32[32,128]{1,0:T(8,128)S(1)}, u32[]{:S(2)}, u32[]{:S(2)}) %collective-permute-start.15) | collective-permute-done | bytes 16416 | tf_op jit(solution)/shard_map/ppermute | solution.py:66
  115.9 11.7 %collective-permute-start.16 = (f32[32,128]{1,0:T(8,128)S(1)}, f32[32,128]{1,0:T(8,128)S(1)}, u32[]{:S(2)}, u32[]{:S(2)}) collective-permute-start(f32[32,128]{1,0:T(8,128)S(1)} %add.1207), channel_id=1, source_target_pairs={{0,256},{16,272},{32,288},{48,304},{64,320},{80,336},{96,352},{112... | collective-permute-start | bytes 49160 | tf_op jit(solution)/shard_map/ppermute | solution.py:66
  127.6 1.7 %collective-permute-done.16 = f32[32,128]{1,0:T(8,128)S(1)} collective-permute-done((f32[32,128]{1,0:T(8,128)S(1)}, f32[32,128]{1,0:T(8,128)S(1)}, u32[]{:S(2)}, u32[]{:S(2)}) %collective-permute-start.16) | collective-permute-done | bytes 16416 | tf_op jit(solution)/shard_map/ppermute | solution.py:66
  (75 shorter events, 5.6 us)
Async XLA Ops:
  0.6 2.0 %copy-start = (f32[8,8,128]{2,1,0:T(8,128)S(1)}, f32[8,8,128]{2,1,0:T(8,128)}, u32[]{:S(2)}) copy-start(f32[8,8,128]{2,1,0:T(8,128)} %param.7) | copy-start | bytes 98308
  2.7 5.2 %collective-permute-start.1 = (f32[208,128]{1,0:T(8,128)S(1)}, f32[208,128]{1,0:T(8,128)S(1)}, u32[]{:S(2)}, u32[]{:S(2)}) collective-permute-start(f32[208,128]{1,0:T(8,128)S(1)} %pad_maximum_fusion.3), channel_id=1, source_target_pairs={{16,0},{32,16},{48,32},{64,48},{80,64},{96,80},{112,96},{128,112},... | collective-permute-start | bytes 319496 | tf_op jit(solution)/shard_map/ppermute | solution.py:46
  4.0 3.8 %collective-permute-start = (f32[2,8,128]{2,1,0:T(8,128)S(1)}, f32[2,8,128]{2,1,0:T(8,128)S(1)}, u32[]{:S(2)}, u32[]{:S(2)}) collective-permute-start(f32[2,8,128]{2,1,0:T(8,128)S(1)} %get-tuple-element.23), channel_id=1, source_target_pairs={{0,16},{16,32},{32,48},{48,64},{64,80},{80,96},{96,112},{112,128},... | collective-permute-start | bytes 24584 | tf_op jit(solution)/shard_map/ppermute | solution.py:50
  7.9 8.2 %collective-permute-start.3 = (f32[240,128]{1,0:T(8,128)S(1)}, f32[240,128]{1,0:T(8,128)S(1)}, u32[]{:S(2)}, u32[]{:S(2)}) collective-permute-start(f32[240,128]{1,0:T(8,128)S(1)} %pad_maximum_fusion.1), channel_id=1, source_target_pairs={{1,0},{2,1},{3,2},{4,3},{5,4},{6,5},{7,6},{8,7},{9,8},{10,9},{11,1... | collective-permute-start | bytes 368648 | tf_op jit(solution)/shard_map/ppermute | solution.py:46
  13.8 15.4 %collective-permute-start.2 = (f32[12,2,128]{2,1,0:T(2,128)S(1)}, f32[12,2,128]{2,1,0:T(2,128)S(1)}, u32[]{:S(2)}, u32[]{:S(2)}) collective-permute-start(f32[12,2,128]{2,1,0:T(2,128)S(1)} %get-tuple-element.16), channel_id=1, source_target_pairs={{0,1},{1,2},{2,3},{3,4},{4,5},{5,6},{6,7},{7,8},{8,9},{9,10},{10,1... | collective-permute-start | bytes 36872 | tf_op jit(solution)/shard_map/ppermute | solution.py:50
  17.5 11.9 %copy-start.2 = (s32[8,8,128]{2,1,0:T(8,128)S(1)}, s32[8,8,128]{2,1,0:T(8,128)}, u32[]{:S(2)}) copy-start(s32[8,8,128]{2,1,0:T(8,128)} %param.8) | copy-start | bytes 98308
  29.4 19.6 %copy-start.3 = (f32[63,64]{0,1:T(8,128)S(1)}, f32[63,64]{0,1:T(8,128)}, u32[]{:S(2)}) copy-start(f32[63,64]{0,1:T(8,128)} %constant.25.clone.1) | copy-start | bytes 48388
  31.4 8.1 %collective-permute-start.5 = (f32[2,8,128]{2,1,0:T(8,128)S(1)}, f32[2,8,128]{2,1,0:T(8,128)S(1)}, u32[]{:S(2)}, u32[]{:S(2)}) collective-permute-start(f32[2,8,128]{2,1,0:T(8,128)S(1)} %get-tuple-element.22), channel_id=1, source_target_pairs={{16,0},{32,16},{48,32},{64,48},{80,64},{96,80},{112,96},{128,112},... | collective-permute-start | bytes 24584 | tf_op jit(solution)/shard_map/ppermute | solution.py:29
  32.7 7.6 %collective-permute-start.4 = (f32[2,8,128]{2,1,0:T(8,128)S(1)}, f32[2,8,128]{2,1,0:T(8,128)S(1)}, u32[]{:S(2)}, u32[]{:S(2)}) collective-permute-start(f32[2,8,128]{2,1,0:T(8,128)S(1)} %get-tuple-element.21), channel_id=1, source_target_pairs={{0,16},{16,32},{32,48},{48,64},{64,80},{80,96},{96,112},{112,128},... | collective-permute-start | bytes 24584 | tf_op jit(solution)/shard_map/ppermute | solution.py:27
  40.3 8.8 %collective-permute-start.6 = (f32[12,2,128]{2,1,0:T(2,128)S(1)}, f32[12,2,128]{2,1,0:T(2,128)S(1)}, u32[]{:S(2)}, u32[]{:S(2)}) collective-permute-start(f32[12,2,128]{2,1,0:T(2,128)S(1)} %get-tuple-element.12), channel_id=1, source_target_pairs={{0,1},{1,2},{2,3},{3,4},{4,5},{5,6},{6,7},{7,8},{8,9},{9,10},{10,1... | collective-permute-start | bytes 36872 | tf_op jit(solution)/shard_map/ppermute | solution.py:27
  42.7 7.7 %collective-permute-start.7 = (f32[12,2,128]{2,1,0:T(2,128)S(1)}, f32[12,2,128]{2,1,0:T(2,128)S(1)}, u32[]{:S(2)}, u32[]{:S(2)}) collective-permute-start(f32[12,2,128]{2,1,0:T(2,128)S(1)} %get-tuple-element.13), channel_id=1, source_target_pairs={{1,0},{2,1},{3,2},{4,3},{5,4},{6,5},{7,6},{8,7},{9,8},{10,9},{11,1... | collective-permute-start | bytes 36872 | tf_op jit(solution)/shard_map/ppermute | solution.py:29
  50.6 77.1 %copy-start.4 = (f32[64]{0:T(128)S(1)}, f32[64]{0:T(128)}, u32[]{:S(2)}) copy-start(f32[64]{0:T(128)} %param.13) | copy-start | bytes 772
  51.1 79.4 %copy-start.1 = (f32[8,8,128]{2,1,0:T(8,128)}, f32[8,8,128]{2,1,0:T(8,128)S(1)}, u32[]{:S(2)}) copy-start(f32[8,8,128]{2,1,0:T(8,128)S(1)} %get-tuple-element.7) | copy-start | bytes 98308
  52.4 5.6 %collective-permute-start.8 = (f32[32,128]{1,0:T(8,128)S(1)}, f32[32,128]{1,0:T(8,128)S(1)}, u32[]{:S(2)}, u32[]{:S(2)}) collective-permute-start(f32[32,128]{1,0:T(8,128)S(1)} %pad_bitcast_fusion), channel_id=1, source_target_pairs={{0,1},{1,0},{2,3},{3,2},{4,5},{5,4},{6,7},{7,6},{8,9},{9,8},{10,11... | collective-permute-start | bytes 49160 | tf_op jit(solution)/shard_map/ppermute | solution.py:66
  58.1 6.5 %collective-permute-start.9 = (f32[32,128]{1,0:T(8,128)S(1)}, f32[32,128]{1,0:T(8,128)S(1)}, u32[]{:S(2)}, u32[]{:S(2)}) collective-permute-start(f32[32,128]{1,0:T(8,128)S(1)} %fusion.293), channel_id=1, source_target_pairs={{0,2},{1,3},{2,0},{3,1},{4,6},{5,7},{6,4},{7,5},{8,10},{9,11},{10,... | collective-permute-start | bytes 49160 | tf_op jit(solution)/shard_map/ppermute | solution.py:66
  64.6 5.6 %collective-permute-start.10 = (f32[32,128]{1,0:T(8,128)S(1)}, f32[32,128]{1,0:T(8,128)S(1)}, u32[]{:S(2)}, u32[]{:S(2)}) collective-permute-start(f32[32,128]{1,0:T(8,128)S(1)} %fusion.297), channel_id=1, source_target_pairs={{0,4},{1,5},{2,6},{3,7},{4,0},{5,1},{6,2},{7,3},{8,12},{9,13},{10,... | collective-permute-start | bytes 49160 | tf_op jit(solution)/shard_map/ppermute | solution.py:66
  70.2 7.1 %collective-permute-start.11 = (f32[32,128]{1,0:T(8,128)S(1)}, f32[32,128]{1,0:T(8,128)S(1)}, u32[]{:S(2)}, u32[]{:S(2)}) collective-permute-start(f32[32,128]{1,0:T(8,128)S(1)} %add.1202), channel_id=1, source_target_pairs={{0,8},{1,9},{2,10},{3,11},{4,12},{5,13},{6,14},{7,15},{8,0},{9,1},... | collective-permute-start | bytes 49160 | tf_op jit(solution)/shard_map/ppermute | solution.py:66
  77.3 4.6 %collective-permute-start.12 = (f32[32,128]{1,0:T(8,128)S(1)}, f32[32,128]{1,0:T(8,128)S(1)}, u32[]{:S(2)}, u32[]{:S(2)}) collective-permute-start(f32[32,128]{1,0:T(8,128)S(1)} %add.1203), channel_id=1, source_target_pairs={{0,16},{16,0},{32,48},{48,32},{64,80},{80,64},{96,112},{112,96},{1... | collective-permute-start | bytes 49160 | tf_op jit(solution)/shard_map/ppermute | solution.py:66
  82.0 15.6 %collective-permute-start.13 = (f32[32,128]{1,0:T(8,128)S(1)}, f32[32,128]{1,0:T(8,128)S(1)}, u32[]{:S(2)}, u32[]{:S(2)}) collective-permute-start(f32[32,128]{1,0:T(8,128)S(1)} %add.1204), channel_id=1, source_target_pairs={{0,32},{16,48},{32,0},{48,16},{64,96},{80,112},{96,64},{112,80},{1... | collective-permute-start | bytes 49160 | tf_op jit(solution)/shard_map/ppermute | solution.py:66
  97.6 10.5 %collective-permute-start.14 = (f32[32,128]{1,0:T(8,128)S(1)}, f32[32,128]{1,0:T(8,128)S(1)}, u32[]{:S(2)}, u32[]{:S(2)}) collective-permute-start(f32[32,128]{1,0:T(8,128)S(1)} %add.1205), channel_id=1, source_target_pairs={{0,64},{16,80},{32,96},{48,112},{64,0},{80,16},{96,32},{112,48},{1... | collective-permute-start | bytes 49160 | tf_op jit(solution)/shard_map/ppermute | solution.py:66
  108.1 7.8 %collective-permute-start.15 = (f32[32,128]{1,0:T(8,128)S(1)}, f32[32,128]{1,0:T(8,128)S(1)}, u32[]{:S(2)}, u32[]{:S(2)}) collective-permute-start(f32[32,128]{1,0:T(8,128)S(1)} %add.1206), channel_id=1, source_target_pairs={{0,128},{16,144},{32,160},{48,176},{64,192},{80,208},{96,224},{112... | collective-permute-start | bytes 49160 | tf_op jit(solution)/shard_map/ppermute | solution.py:66
  115.9 13.4 %collective-permute-start.16 = (f32[32,128]{1,0:T(8,128)S(1)}, f32[32,128]{1,0:T(8,128)S(1)}, u32[]{:S(2)}, u32[]{:S(2)}) collective-permute-start(f32[32,128]{1,0:T(8,128)S(1)} %add.1207), channel_id=1, source_target_pairs={{0,256},{16,272},{32,288},{48,304},{64,320},{80,336},{96,352},{112... | collective-permute-start | bytes 49160 | tf_op jit(solution)/shard_map/ppermute | solution.py:66

commit v10 on v9

--- a/solution.py
+++ b/solution.py
@@ -178,7 +178,8 @@
 
 
 def mxu_energy_kernel(
-    extended_ref, stiffness_ref, mass_ref, stiff_out, mass_out, coupling_ref, adjoint_rows, products
+    extended_ref, stiffness_ref, mass_ref, stiff_out, mass_out, coupling_ref, state_rows,
+    adjoint_rows, products,
 ):
     pair_count = extended_ref.shape[0]
     cells_x, cells_y, cells_z = stiff_out.shape
@@ -209,42 +210,45 @@
     inside = lane < cells_z - 1
     stiff_out[...] = jnp.zeros(stiff_out.shape, jnp.float32)
     mass_out[...] = jnp.zeros(mass_out.shape, jnp.float32)
-
-    def node_view(pair, member, row, x):
-        corner_x, corner_y, corner_z = CORNERS[row // 3]
-        value = extended_ref[pair, member, row % 3, x + corner_x, pl.ds(corner_y, cells_y), :]
-        if corner_z:
-            value = jnp.where(inside, pltpu.roll(value, cells_z - 1, 1), 0.0)
-        return value
+    member_rows = (state_rows, adjoint_rows)
 
     def over_pairs(pair, carry):
-        def gather_x(x, inner):
-            columns = pl.ds(pl.multiple_of(x * cells_z, cells_z), cells_z)
-            for row in range(dofs):
-                adjoint_rows[pl.ds(row * cells_y, cells_y), columns] = node_view(pair, 1, row, x)
-            return inner
-
-        lax.fori_loop(0, cells_x, gather_x, 0)
+        for node_x in range(cells_x + 1):
+            for member in range(2):
+                for component in range(3):
+                    for corner_y in (0, 1):
+                        base = extended_ref[
+                            pair, member, component, node_x, pl.ds(corner_y, cells_y), :
+                        ]
+                        for corner_z in (0, 1):
+                            value = base
+                            if corner_z:
+                                value = jnp.where(inside, pltpu.roll(base, cells_z - 1, 1), 0.0)
+                            for corner_x in (0, 1):
+                                x = node_x - corner_x
+                                if 0 <= x < cells_x:
+                                    corner = CORNERS.index((corner_x, corner_y, corner_z))
+                                    row = 3 * corner + component
+                                    member_rows[member][
+                                        pl.ds(row * cells_y, cells_y), pl.ds(x * cells_z, cells_z)
+                                    ] = value
         products[...] = jnp.dot(
             coupling_ref[...],
             adjoint_rows[...],
             precision=lax.Precision.HIGH,
             preferred_element_type=jnp.float32,
         )
-
-        def reduce_x(x, inner):
-            columns = pl.ds(pl.multiple_of(x * cells_z, cells_z), cells_z)
-            stiff_sum = stiff_out[x]
-            mass_sum = mass_out[x]
-            for row in range(dofs):
-                state = node_view(pair, 0, row, x)
-                stiff_sum = stiff_sum + state * products[pl.ds(row * cells_y, cells_y), columns]
-                mass_sum = mass_sum + state * products[pl.ds((dofs + row) * cells_y, cells_y), columns]
-            stiff_out[x] = stiff_sum
-            mass_out[x] = mass_sum
-            return inner
-
-        lax.fori_loop(0, cells_x, reduce_x, 0)
+        state = state_rows[...].reshape(dofs, cells_y, cells_x * cells_z)
+        stiff_sum = jnp.sum(
+            state * products[pl.ds(0, wide), :].reshape(dofs, cells_y, cells_x * cells_z), axis=0
+        )
+        mass_sum = jnp.sum(
+            state * products[pl.ds(wide, wide), :].reshape(dofs, cells_y, cells_x * cells_z), axis=0
+        )
+        for x in range(cells_x):
+            columns = slice(x * cells_z, (x + 1) * cells_z)
+            stiff_out[x] = stiff_out[x] + stiff_sum[:, columns]
+            mass_out[x] = mass_out[x] + mass_sum[:, columns]
         return carry
 
     lax.fori_loop(0, pair_count, over_pairs, 0)
@@ -266,6 +270,7 @@
         out_specs=(vmem, vmem),
         scratch_shapes=[
             pltpu.VMEM((2 * dofs * cells[1], dofs * cells[1]), jnp.float32),
+            pltpu.VMEM((dofs * cells[1], cells[0] * cells[2]), jnp.float32),
             pltpu.VMEM((dofs * cells[1], cells[0] * cells[2]), jnp.float32),
             pltpu.VMEM((2 * dofs * cells[1], cells[0] * cells[2]), jnp.float32),
         ],

time: 133 us -> 127 us (0.955)
  Pallas kernels: 11.6 us -> 6.22 us
    pallas_call x1, Pallas kernels: 11.6 us -> 6.22 us  [element_energies(): pl.pallas_call(mxu_energy_kernel, out_shape=(jax.ShapeDtypeStruct(cells,...]
  transfers between devices with their start and end apart: 17 -> 17, of which waited for: 13 -> 13; matrix products, arithmetic and copies ran while one was open for 1% -> 1% of each run, Pallas kernels for 9% -> 5%
where the time goes in v10:
time: 127 us; the launch traced here: 125 us
  starting transfers between devices  83.6 us (66%)
  waiting for transfers between devices  25 us (20%)
  other arithmetic  8.45 us (7%)
  Pallas kernels  6.22 us (5%)
    ppermute x9, starting transfers between devices, butterfly_sum(): lax.ppermute(value, axis, [(i, i ^ stride) for i in range(count)])  54.9 us
    ppermute x9, waiting for transfers between devices, butterfly_sum(): lax.ppermute(value, axis, [(i, i ^ stride) for i in range(count)])  21.9 us
    ppermute x2, starting transfers between devices, with_halo(): lax.ppermute(tail, axis, [(i, (i + 1) % count) for i in range(ends)])  9.13 us
    ppermute x2, starting transfers between devices, with_halo(): lax.ppermute(head, axis, [((i + 1) % count, i) for i in range(ends)])  7.58 us
    ppermute x2, starting transfers between devices, front_exchange(): lax.ppermute(packed, axis, [((i + 1) % count, i) for i in range(ends)])  7.07 us
    pallas_call x1, Pallas kernels, element_energies(): pl.pallas_call(mxu_energy_kernel, out_shape=(jax.ShapeDtypeStruct(cells,...  6.22 us
    ppermute x2, starting transfers between devices, front_exchange(): tail = lax.ppermute(tail, axis, [(i, (i + 1) % count) for i in range(ends)])  4.95 us
  transfers between devices with their start and end apart: 17, of which 13 were waited for; matrix products, arithmetic and copies ran while one was open for 1% of the time, Pallas kernels for 5%

profile of v10, /device:TPU:6, one launch (start us, length us, event | category | flops | bytes accessed | tf_op | source)
XLA Modules:
  0.0 125.1 jit_solution(10927535536778678042)
XLA Ops:
  1.4 1.2 broadcast_multiply_fusion
  2.7 1.3 %collective-permute-start.1 = (f32[208,128]{1,0:T(8,128)S(1)}, f32[208,128]{1,0:T(8,128)S(1)}, u32[]{:S(2)}, u32[]{:S(2)}) collective-permute-start(f32[208,128]{1,0:T(8,128)S(1)} %pad_maximum_fusion.3), channel_id=1, source_target_pairs={{16,0},{32,16},{48,32},{64,48},{80,64},{96,80},{112,96},{128,112},... | collective-permute-start | bytes 319496 | tf_op jit(solution)/shard_map/ppermute | solution.py:46
  4.0 3.0 %collective-permute-start = (f32[2,8,128]{2,1,0:T(8,128)S(1)}, f32[2,8,128]{2,1,0:T(8,128)S(1)}, u32[]{:S(2)}, u32[]{:S(2)}) collective-permute-start(f32[2,8,128]{2,1,0:T(8,128)S(1)} %get-tuple-element.23), channel_id=1, source_target_pairs={{0,16},{16,32},{32,48},{48,64},{64,80},{80,96},{96,112},{112,128},... | collective-permute-start | bytes 24584 | tf_op jit(solution)/shard_map/ppermute | solution.py:50
  7.9 5.8 %collective-permute-start.3 = (f32[240,128]{1,0:T(8,128)S(1)}, f32[240,128]{1,0:T(8,128)S(1)}, u32[]{:S(2)}, u32[]{:S(2)}) collective-permute-start(f32[240,128]{1,0:T(8,128)S(1)} %pad_maximum_fusion.1), channel_id=1, source_target_pairs={{1,0},{2,1},{3,2},{4,3},{5,4},{6,5},{7,6},{8,7},{9,8},{10,9},{11,1... | collective-permute-start | bytes 368648 | tf_op jit(solution)/shard_map/ppermute | solution.py:46
  13.8 1.9 %collective-permute-start.2 = (f32[12,2,128]{2,1,0:T(2,128)S(1)}, f32[12,2,128]{2,1,0:T(2,128)S(1)}, u32[]{:S(2)}, u32[]{:S(2)}) collective-permute-start(f32[12,2,128]{2,1,0:T(2,128)S(1)} %get-tuple-element.16), channel_id=1, source_target_pairs={{0,1},{1,2},{2,3},{3,4},{4,5},{5,6},{6,7},{7,8},{8,9},{9,10},{10,1... | collective-permute-start | bytes 36872 | tf_op jit(solution)/shard_map/ppermute | solution.py:50
  16.2 1.4 %pad_maximum_fusion.extended_ref = f32[4,2,3,9,9,128]{5,4,3,2,1,0:T(8,128)} fusion(f32[4,2,3,9,1,128]{5,4,3,2,1,0:T(1,128)S(1)} %bitcast.65, f32[4,2,3,1,8,128]{5,4,3,2,1,0:T(8,128)S(1)} %bitcast.64, f32[4,2,3,8,8,128]{5,4,3,2,1,0:T(8,128)S(1)} %broadcast_multiply_fusion), kind=kLoop, calls=%fused_computation.6 | loop fusion | flops 497664 | bytes 1990656 | tf_op jit(solution)/shard_map/concatenate | solution.py:52
  17.5 6.2 %shard_map.86 = (f32[8,8,128]{2,1,0:T(8,128)}, f32[8,8,128]{2,1,0:T(8,128)}) custom-call(f32[4,2,3,9,9,128]{5,4,3,2,1,0:T(8,128)} %pad_maximum_fusion.extended_ref, f32[24,24]{1,0:T(8,128)} %stiffness_ref.1, f32[24,24]{1,0:T(8,128)} %mass_ref.1), custom_call_target="tpu_custom_call" | custom-call | flops 607125504 | bytes 1065472 | tf_op jit(solution)/shard_map/pallas_call | solution.py:263
  24.0 2.0 %fusion.82 = (f32[8,8,128]{2,1,0:T(8,128)S(1)}, pred[8,8,128]{2,1,0:T(8,128)(4,1)S(1)}) fusion(f32[8,8,128]{2,1,0:T(8,128)} %get-tuple-element.4, f32[12,10,128]{2,1,0:T(8,128)S(1)} %get-tuple-element.15, f32[12,12,132]{2,1,0:T(8,128)S(1)} %select_maximum_fusion.4, f32[2,8,128]{2,1,0:T(8,128)S(1)} %slice_bitcast_fusion, f32[8,8,128]{2,1,0:T(8,128)S(1)} %copy-done, ...), kind=kLoop, calls=%fused_computation.110 | loop fusion | flops 3039232 | bytes 6176768 | tf_op jit(solution)/shard_map/div | solution.py:310
  26.0 1.3 %collective-permute-start.5 = (f32[2,8,128]{2,1,0:T(8,128)S(1)}, f32[2,8,128]{2,1,0:T(8,128)S(1)}, u32[]{:S(2)}, u32[]{:S(2)}) collective-permute-start(f32[2,8,128]{2,1,0:T(8,128)S(1)} %get-tuple-element.22), channel_id=1, source_target_pairs={{16,0},{32,16},{48,32},{64,48},{80,64},{96,80},{112,96},{128,112},... | collective-permute-start | bytes 24584 | tf_op jit(solution)/shard_map/ppermute | solution.py:29
  27.3 6.7 %collective-permute-start.4 = (f32[2,8,128]{2,1,0:T(8,128)S(1)}, f32[2,8,128]{2,1,0:T(8,128)S(1)}, u32[]{:S(2)}, u32[]{:S(2)}) collective-permute-start(f32[2,8,128]{2,1,0:T(8,128)S(1)} %get-tuple-element.21), channel_id=1, source_target_pairs={{0,16},{16,32},{32,48},{48,64},{64,80},{80,96},{96,112},{112,128},... | collective-permute-start | bytes 24584 | tf_op jit(solution)/shard_map/ppermute | solution.py:27
  34.9 2.4 %collective-permute-start.6 = (f32[12,2,128]{2,1,0:T(2,128)S(1)}, f32[12,2,128]{2,1,0:T(2,128)S(1)}, u32[]{:S(2)}, u32[]{:S(2)}) collective-permute-start(f32[12,2,128]{2,1,0:T(2,128)S(1)} %get-tuple-element.12), channel_id=1, source_target_pairs={{0,1},{1,2},{2,3},{3,4},{4,5},{5,6},{6,7},{7,8},{8,9},{9,10},{10,1... | collective-permute-start | bytes 36872 | tf_op jit(solution)/shard_map/ppermute | solution.py:27
  37.3 6.3 %collective-permute-start.7 = (f32[12,2,128]{2,1,0:T(2,128)S(1)}, f32[12,2,128]{2,1,0:T(2,128)S(1)}, u32[]{:S(2)}, u32[]{:S(2)}) collective-permute-start(f32[12,2,128]{2,1,0:T(2,128)S(1)} %get-tuple-element.13), channel_id=1, source_target_pairs={{1,0},{2,1},{3,2},{4,3},{5,4},{6,5},{7,6},{8,7},{9,8},{10,9},{11,1... | collective-permute-start | bytes 36872 | tf_op jit(solution)/shard_map/ppermute | solution.py:29
  43.7 1.2 collective-permute-done.7
  45.7 0.9 fusion.4
  47.0 1.9 %collective-permute-start.8 = (f32[32,128]{1,0:T(8,128)S(1)}, f32[32,128]{1,0:T(8,128)S(1)}, u32[]{:S(2)}, u32[]{:S(2)}) collective-permute-start(f32[32,128]{1,0:T(8,128)S(1)} %pad_bitcast_fusion), channel_id=1, source_target_pairs={{0,1},{1,0},{2,3},{3,2},{4,5},{5,4},{6,7},{7,6},{8,9},{9,8},{10,11... | collective-permute-start | bytes 49160 | tf_op jit(solution)/shard_map/ppermute | solution.py:66
  48.9 3.7 %collective-permute-done.8 = f32[32,128]{1,0:T(8,128)S(1)} collective-permute-done((f32[32,128]{1,0:T(8,128)S(1)}, f32[32,128]{1,0:T(8,128)S(1)}, u32[]{:S(2)}, u32[]{:S(2)}) %collective-permute-start.8) | collective-permute-done | bytes 16416 | tf_op jit(solution)/shard_map/ppermute | solution.py:66
  52.6 1.9 %collective-permute-start.9 = (f32[32,128]{1,0:T(8,128)S(1)}, f32[32,128]{1,0:T(8,128)S(1)}, u32[]{:S(2)}, u32[]{:S(2)}) collective-permute-start(f32[32,128]{1,0:T(8,128)S(1)} %fusion.293), channel_id=1, source_target_pairs={{0,2},{1,3},{2,0},{3,1},{4,6},{5,7},{6,4},{7,5},{8,10},{9,11},{10,... | collective-permute-start | bytes 49160 | tf_op jit(solution)/shard_map/ppermute | solution.py:66
  54.6 4.6 %collective-permute-done.9 = f32[32,128]{1,0:T(8,128)S(1)} collective-permute-done((f32[32,128]{1,0:T(8,128)S(1)}, f32[32,128]{1,0:T(8,128)S(1)}, u32[]{:S(2)}, u32[]{:S(2)}) %collective-permute-start.9) | collective-permute-done | bytes 16416 | tf_op jit(solution)/shard_map/ppermute | solution.py:66
  59.2 3.1 %collective-permute-start.10 = (f32[32,128]{1,0:T(8,128)S(1)}, f32[32,128]{1,0:T(8,128)S(1)}, u32[]{:S(2)}, u32[]{:S(2)}) collective-permute-start(f32[32,128]{1,0:T(8,128)S(1)} %fusion.297), channel_id=1, source_target_pairs={{0,4},{1,5},{2,6},{3,7},{4,0},{5,1},{6,2},{7,3},{8,12},{9,13},{10,... | collective-permute-start | bytes 49160 | tf_op jit(solution)/shard_map/ppermute | solution.py:66
  62.3 2.5 %collective-permute-done.10 = f32[32,128]{1,0:T(8,128)S(1)} collective-permute-done((f32[32,128]{1,0:T(8,128)S(1)}, f32[32,128]{1,0:T(8,128)S(1)}, u32[]{:S(2)}, u32[]{:S(2)}) %collective-permute-start.10) | collective-permute-done | bytes 16416 | tf_op jit(solution)/shard_map/ppermute | solution.py:66
  64.8 3.7 %collective-permute-start.11 = (f32[32,128]{1,0:T(8,128)S(1)}, f32[32,128]{1,0:T(8,128)S(1)}, u32[]{:S(2)}, u32[]{:S(2)}) collective-permute-start(f32[32,128]{1,0:T(8,128)S(1)} %add.1202), channel_id=1, source_target_pairs={{0,8},{1,9},{2,10},{3,11},{4,12},{5,13},{6,14},{7,15},{8,0},{9,1},... | collective-permute-start | bytes 49160 | tf_op jit(solution)/shard_map/ppermute | solution.py:66
  68.5 3.5 %collective-permute-done.11 = f32[32,128]{1,0:T(8,128)S(1)} collective-permute-done((f32[32,128]{1,0:T(8,128)S(1)}, f32[32,128]{1,0:T(8,128)S(1)}, u32[]{:S(2)}, u32[]{:S(2)}) %collective-permute-start.11) | collective-permute-done | bytes 16416 | tf_op jit(solution)/shard_map/ppermute | solution.py:66
  71.9 3.8 %collective-permute-start.12 = (f32[32,128]{1,0:T(8,128)S(1)}, f32[32,128]{1,0:T(8,128)S(1)}, u32[]{:S(2)}, u32[]{:S(2)}) collective-permute-start(f32[32,128]{1,0:T(8,128)S(1)} %add.1203), channel_id=1, source_target_pairs={{0,16},{16,0},{32,48},{48,32},{64,80},{80,64},{96,112},{112,96},{1... | collective-permute-start | bytes 49160 | tf_op jit(solution)/shard_map/ppermute | solution.py:66
  75.8 0.8 collective-permute-done.12
  76.6 13.9 %collective-permute-start.13 = (f32[32,128]{1,0:T(8,128)S(1)}, f32[32,128]{1,0:T(8,128)S(1)}, u32[]{:S(2)}, u32[]{:S(2)}) collective-permute-start(f32[32,128]{1,0:T(8,128)S(1)} %add.1204), channel_id=1, source_target_pairs={{0,32},{16,48},{32,0},{48,16},{64,96},{80,112},{96,64},{112,80},{1... | collective-permute-start | bytes 49160 | tf_op jit(solution)/shard_map/ppermute | solution.py:66
  90.5 1.7 %collective-permute-done.13 = f32[32,128]{1,0:T(8,128)S(1)} collective-permute-done((f32[32,128]{1,0:T(8,128)S(1)}, f32[32,128]{1,0:T(8,128)S(1)}, u32[]{:S(2)}, u32[]{:S(2)}) %collective-permute-start.13) | collective-permute-done | bytes 16416 | tf_op jit(solution)/shard_map/ppermute | solution.py:66
  92.2 8.8 %collective-permute-start.14 = (f32[32,128]{1,0:T(8,128)S(1)}, f32[32,128]{1,0:T(8,128)S(1)}, u32[]{:S(2)}, u32[]{:S(2)}) collective-permute-start(f32[32,128]{1,0:T(8,128)S(1)} %add.1205), channel_id=1, source_target_pairs={{0,64},{16,80},{32,96},{48,112},{64,0},{80,16},{96,32},{112,48},{1... | collective-permute-start | bytes 49160 | tf_op jit(solution)/shard_map/ppermute | solution.py:66
  101.0 1.7 %collective-permute-done.14 = f32[32,128]{1,0:T(8,128)S(1)} collective-permute-done((f32[32,128]{1,0:T(8,128)S(1)}, f32[32,128]{1,0:T(8,128)S(1)}, u32[]{:S(2)}, u32[]{:S(2)}) %collective-permute-start.14) | collective-permute-done | bytes 16416 | tf_op jit(solution)/shard_map/ppermute | solution.py:66
  102.7 6.1 %collective-permute-start.15 = (f32[32,128]{1,0:T(8,128)S(1)}, f32[32,128]{1,0:T(8,128)S(1)}, u32[]{:S(2)}, u32[]{:S(2)}) collective-permute-start(f32[32,128]{1,0:T(8,128)S(1)} %add.1206), channel_id=1, source_target_pairs={{0,128},{16,144},{32,160},{48,176},{64,192},{80,208},{96,224},{112... | collective-permute-start | bytes 49160 | tf_op jit(solution)/shard_map/ppermute | solution.py:66
  108.8 1.7 %collective-permute-done.15 = f32[32,128]{1,0:T(8,128)S(1)} collective-permute-done((f32[32,128]{1,0:T(8,128)S(1)}, f32[32,128]{1,0:T(8,128)S(1)}, u32[]{:S(2)}, u32[]{:S(2)}) %collective-permute-start.15) | collective-permute-done | bytes 16416 | tf_op jit(solution)/shard_map/ppermute | solution.py:66
  110.5 11.7 %collective-permute-start.16 = (f32[32,128]{1,0:T(8,128)S(1)}, f32[32,128]{1,0:T(8,128)S(1)}, u32[]{:S(2)}, u32[]{:S(2)}) collective-permute-start(f32[32,128]{1,0:T(8,128)S(1)} %add.1207), channel_id=1, source_target_pairs={{0,256},{16,272},{32,288},{48,304},{64,320},{80,336},{96,352},{112... | collective-permute-start | bytes 49160 | tf_op jit(solution)/shard_map/ppermute | solution.py:66
  122.2 1.7 %collective-permute-done.16 = f32[32,128]{1,0:T(8,128)S(1)} collective-permute-done((f32[32,128]{1,0:T(8,128)S(1)}, f32[32,128]{1,0:T(8,128)S(1)}, u32[]{:S(2)}, u32[]{:S(2)}) %collective-permute-start.16) | collective-permute-done | bytes 16416 | tf_op jit(solution)/shard_map/ppermute | solution.py:66
  (75 shorter events, 5.6 us)
Async XLA Ops:
  0.6 2.0 %copy-start = (f32[8,8,128]{2,1,0:T(8,128)S(1)}, f32[8,8,128]{2,1,0:T(8,128)}, u32[]{:S(2)}) copy-start(f32[8,8,128]{2,1,0:T(8,128)} %param.7) | copy-start | bytes 98308
  2.7 5.2 %collective-permute-start.1 = (f32[208,128]{1,0:T(8,128)S(1)}, f32[208,128]{1,0:T(8,128)S(1)}, u32[]{:S(2)}, u32[]{:S(2)}) collective-permute-start(f32[208,128]{1,0:T(8,128)S(1)} %pad_maximum_fusion.3), channel_id=1, source_target_pairs={{16,0},{32,16},{48,32},{64,48},{80,64},{96,80},{112,96},{128,112},... | collective-permute-start | bytes 319496 | tf_op jit(solution)/shard_map/ppermute | solution.py:46
  4.0 3.8 %collective-permute-start = (f32[2,8,128]{2,1,0:T(8,128)S(1)}, f32[2,8,128]{2,1,0:T(8,128)S(1)}, u32[]{:S(2)}, u32[]{:S(2)}) collective-permute-start(f32[2,8,128]{2,1,0:T(8,128)S(1)} %get-tuple-element.23), channel_id=1, source_target_pairs={{0,16},{16,32},{32,48},{48,64},{64,80},{80,96},{96,112},{112,128},... | collective-permute-start | bytes 24584 | tf_op jit(solution)/shard_map/ppermute | solution.py:50
  7.9 8.2 %collective-permute-start.3 = (f32[240,128]{1,0:T(8,128)S(1)}, f32[240,128]{1,0:T(8,128)S(1)}, u32[]{:S(2)}, u32[]{:S(2)}) collective-permute-start(f32[240,128]{1,0:T(8,128)S(1)} %pad_maximum_fusion.1), channel_id=1, source_target_pairs={{1,0},{2,1},{3,2},{4,3},{5,4},{6,5},{7,6},{8,7},{9,8},{10,9},{11,1... | collective-permute-start | bytes 368648 | tf_op jit(solution)/shard_map/ppermute | solution.py:46
  13.8 10.0 %collective-permute-start.2 = (f32[12,2,128]{2,1,0:T(2,128)S(1)}, f32[12,2,128]{2,1,0:T(2,128)S(1)}, u32[]{:S(2)}, u32[]{:S(2)}) collective-permute-start(f32[12,2,128]{2,1,0:T(2,128)S(1)} %get-tuple-element.16), channel_id=1, source_target_pairs={{0,1},{1,2},{2,3},{3,4},{4,5},{5,6},{6,7},{7,8},{8,9},{9,10},{10,1... | collective-permute-start | bytes 36872 | tf_op jit(solution)/shard_map/ppermute | solution.py:50
  17.5 6.4 %copy-start.2 = (s32[8,8,128]{2,1,0:T(8,128)S(1)}, s32[8,8,128]{2,1,0:T(8,128)}, u32[]{:S(2)}) copy-start(s32[8,8,128]{2,1,0:T(8,128)} %param.8) | copy-start | bytes 98308
  24.0 19.6 %copy-start.3 = (f32[63,64]{0,1:T(8,128)S(1)}, f32[63,64]{0,1:T(8,128)}, u32[]{:S(2)}) copy-start(f32[63,64]{0,1:T(8,128)} %constant.25.clone.1) | copy-start | bytes 48388
  26.0 8.0 %collective-permute-start.5 = (f32[2,8,128]{2,1,0:T(8,128)S(1)}, f32[2,8,128]{2,1,0:T(8,128)S(1)}, u32[]{:S(2)}, u32[]{:S(2)}) collective-permute-start(f32[2,8,128]{2,1,0:T(8,128)S(1)} %get-tuple-element.22), channel_id=1, source_target_pairs={{16,0},{32,16},{48,32},{64,48},{80,64},{96,80},{112,96},{128,112},... | collective-permute-start | bytes 24584 | tf_op jit(solution)/shard_map/ppermute | solution.py:29
  27.3 7.6 %collective-permute-start.4 = (f32[2,8,128]{2,1,0:T(8,128)S(1)}, f32[2,8,128]{2,1,0:T(8,128)S(1)}, u32[]{:S(2)}, u32[]{:S(2)}) collective-permute-start(f32[2,8,128]{2,1,0:T(8,128)S(1)} %get-tuple-element.21), channel_id=1, source_target_pairs={{0,16},{16,32},{32,48},{48,64},{64,80},{80,96},{96,112},{112,128},... | collective-permute-start | bytes 24584 | tf_op jit(solution)/shard_map/ppermute | solution.py:27
  34.9 8.8 %collective-permute-start.6 = (f32[12,2,128]{2,1,0:T(2,128)S(1)}, f32[12,2,128]{2,1,0:T(2,128)S(1)}, u32[]{:S(2)}, u32[]{:S(2)}) collective-permute-start(f32[12,2,128]{2,1,0:T(2,128)S(1)} %get-tuple-element.12), channel_id=1, source_target_pairs={{0,1},{1,2},{2,3},{3,4},{4,5},{5,6},{6,7},{7,8},{8,9},{9,10},{10,1... | collective-permute-start | bytes 36872 | tf_op jit(solution)/shard_map/ppermute | solution.py:27
  37.3 7.7 %collective-permute-start.7 = (f32[12,2,128]{2,1,0:T(2,128)S(1)}, f32[12,2,128]{2,1,0:T(2,128)S(1)}, u32[]{:S(2)}, u32[]{:S(2)}) collective-permute-start(f32[12,2,128]{2,1,0:T(2,128)S(1)} %get-tuple-element.13), channel_id=1, source_target_pairs={{1,0},{2,1},{3,2},{4,3},{5,4},{6,5},{7,6},{8,7},{9,8},{10,9},{11,1... | collective-permute-start | bytes 36872 | tf_op jit(solution)/shard_map/ppermute | solution.py:29
  45.1 77.1 %copy-start.4 = (f32[64]{0:T(128)S(1)}, f32[64]{0:T(128)}, u32[]{:S(2)}) copy-start(f32[64]{0:T(128)} %param.13) | copy-start | bytes 772
  45.7 79.4 %copy-start.1 = (f32[8,8,128]{2,1,0:T(8,128)}, f32[8,8,128]{2,1,0:T(8,128)S(1)}, u32[]{:S(2)}) copy-start(f32[8,8,128]{2,1,0:T(8,128)S(1)} %get-tuple-element.7) | copy-start | bytes 98308
  47.0 5.6 %collective-permute-start.8 = (f32[32,128]{1,0:T(8,128)S(1)}, f32[32,128]{1,0:T(8,128)S(1)}, u32[]{:S(2)}, u32[]{:S(2)}) collective-permute-start(f32[32,128]{1,0:T(8,128)S(1)} %pad_bitcast_fusion), channel_id=1, source_target_pairs={{0,1},{1,0},{2,3},{3,2},{4,5},{5,4},{6,7},{7,6},{8,9},{9,8},{10,11... | collective-permute-start | bytes 49160 | tf_op jit(solution)/shard_map/ppermute | solution.py:66
  52.6 6.5 %collective-permute-start.9 = (f32[32,128]{1,0:T(8,128)S(1)}, f32[32,128]{1,0:T(8,128)S(1)}, u32[]{:S(2)}, u32[]{:S(2)}) collective-permute-start(f32[32,128]{1,0:T(8,128)S(1)} %fusion.293), channel_id=1, source_target_pairs={{0,2},{1,3},{2,0},{3,1},{4,6},{5,7},{6,4},{7,5},{8,10},{9,11},{10,... | collective-permute-start | bytes 49160 | tf_op jit(solution)/shard_map/ppermute | solution.py:66
  59.2 5.6 %collective-permute-start.10 = (f32[32,128]{1,0:T(8,128)S(1)}, f32[32,128]{1,0:T(8,128)S(1)}, u32[]{:S(2)}, u32[]{:S(2)}) collective-permute-start(f32[32,128]{1,0:T(8,128)S(1)} %fusion.297), channel_id=1, source_target_pairs={{0,4},{1,5},{2,6},{3,7},{4,0},{5,1},{6,2},{7,3},{8,12},{9,13},{10,... | collective-permute-start | bytes 49160 | tf_op jit(solution)/shard_map/ppermute | solution.py:66
  64.8 7.1 %collective-permute-start.11 = (f32[32,128]{1,0:T(8,128)S(1)}, f32[32,128]{1,0:T(8,128)S(1)}, u32[]{:S(2)}, u32[]{:S(2)}) collective-permute-start(f32[32,128]{1,0:T(8,128)S(1)} %add.1202), channel_id=1, source_target_pairs={{0,8},{1,9},{2,10},{3,11},{4,12},{5,13},{6,14},{7,15},{8,0},{9,1},... | collective-permute-start | bytes 49160 | tf_op jit(solution)/shard_map/ppermute | solution.py:66
  71.9 4.6 %collective-permute-start.12 = (f32[32,128]{1,0:T(8,128)S(1)}, f32[32,128]{1,0:T(8,128)S(1)}, u32[]{:S(2)}, u32[]{:S(2)}) collective-permute-start(f32[32,128]{1,0:T(8,128)S(1)} %add.1203), channel_id=1, source_target_pairs={{0,16},{16,0},{32,48},{48,32},{64,80},{80,64},{96,112},{112,96},{1... | collective-permute-start | bytes 49160 | tf_op jit(solution)/shard_map/ppermute | solution.py:66
  76.6 15.6 %collective-permute-start.13 = (f32[32,128]{1,0:T(8,128)S(1)}, f32[32,128]{1,0:T(8,128)S(1)}, u32[]{:S(2)}, u32[]{:S(2)}) collective-permute-start(f32[32,128]{1,0:T(8,128)S(1)} %add.1204), channel_id=1, source_target_pairs={{0,32},{16,48},{32,0},{48,16},{64,96},{80,112},{96,64},{112,80},{1... | collective-permute-start | bytes 49160 | tf_op jit(solution)/shard_map/ppermute | solution.py:66
  92.2 10.5 %collective-permute-start.14 = (f32[32,128]{1,0:T(8,128)S(1)}, f32[32,128]{1,0:T(8,128)S(1)}, u32[]{:S(2)}, u32[]{:S(2)}) collective-permute-start(f32[32,128]{1,0:T(8,128)S(1)} %add.1205), channel_id=1, source_target_pairs={{0,64},{16,80},{32,96},{48,112},{64,0},{80,16},{96,32},{112,48},{1... | collective-permute-start | bytes 49160 | tf_op jit(solution)/shard_map/ppermute | solution.py:66
  102.7 7.8 %collective-permute-start.15 = (f32[32,128]{1,0:T(8,128)S(1)}, f32[32,128]{1,0:T(8,128)S(1)}, u32[]{:S(2)}, u32[]{:S(2)}) collective-permute-start(f32[32,128]{1,0:T(8,128)S(1)} %add.1206), channel_id=1, source_target_pairs={{0,128},{16,144},{32,160},{48,176},{64,192},{80,208},{96,224},{112... | collective-permute-start | bytes 49160 | tf_op jit(solution)/shard_map/ppermute | solution.py:66
  110.5 13.4 %collective-permute-start.16 = (f32[32,128]{1,0:T(8,128)S(1)}, f32[32,128]{1,0:T(8,128)S(1)}, u32[]{:S(2)}, u32[]{:S(2)}) collective-permute-start(f32[32,128]{1,0:T(8,128)S(1)} %add.1207), channel_id=1, source_target_pairs={{0,256},{16,272},{32,288},{48,304},{64,320},{80,336},{96,352},{112... | collective-permute-start | bytes 49160 | tf_op jit(solution)/shard_map/ppermute | solution.py:66

commit v11 on v10

--- a/solution.py
+++ b/solution.py
@@ -33,24 +33,29 @@
     return cells
 
 
-def front_exchange(cells, fields, width):
+def front_exchange(cells, basis_pairs, supports, width):
+    open_nodes = (1 - supports).astype(jnp.float32)
+    rim = basis_pairs[:, :, :, :1] * open_nodes[:1]
+    rims = []
     for axis, dim in (("gx", 0), ("gy", 1)):
         count = lax.axis_size(axis)
         ends = count - 1
-        field_dim = dim + 3
         head = lax.slice_in_dim(cells, 0, width, axis=dim)
         tail = lax.slice_in_dim(cells, cells.shape[dim] - width, cells.shape[dim], axis=dim)
-        rim = lax.slice_in_dim(fields, 0, 1, axis=field_dim)
         lanes = cells.shape[-1]
         packed = jnp.concatenate([head.reshape(-1, lanes), rim.reshape(-1, lanes)], axis=0)
         packed = lax.ppermute(packed, axis, [((i + 1) % count, i) for i in range(ends)])
         split = head.size // lanes
         head = packed[:split].reshape(head.shape)
-        rim = packed[split:].reshape(rim.shape)
+        received = packed[split:].reshape(rim.shape)
         tail = lax.ppermute(tail, axis, [(i, (i + 1) % count) for i in range(ends)])
         cells = jnp.concatenate([tail, cells, head], axis=dim)
-        fields = jnp.concatenate([fields, rim], axis=field_dim)
-    return cells, fields
+        rims.append(received)
+        if axis == "gx":
+            rim = jnp.concatenate(
+                [basis_pairs[:, :, :, :, :1] * open_nodes[:, :1], received[:, :, :, :, :1]], axis=3
+            )
+    return cells, rims
 
 
 def from_behind(value, axis, steps):
@@ -143,6 +148,7 @@
     cells_x, cells_y, cells_z = stiff_out.shape
     lane = lax.broadcasted_iota(jnp.int32, (cells_y, cells_z), 1)
     inside = lane < cells_z - 1
+    last_row = lax.broadcasted_iota(jnp.int32, (cells_y, cells_z), 0) == cells_y - 1
 
     def node_view(pair, member, component, x, corner):
         corner_x, corner_y, corner_z = corner
@@ -178,10 +184,10 @@
 
 
 def mxu_energy_kernel(
-    extended_ref, stiffness_ref, mass_ref, stiff_out, mass_out, coupling_ref, state_rows,
-    adjoint_rows, products,
+    fields_ref, rim_x_ref, rim_y_ref, stiffness_ref, mass_ref, stiff_out, mass_out, coupling_ref,
+    state_rows, adjoint_rows, products,
 ):
-    pair_count = extended_ref.shape[0]
+    pair_count = fields_ref.shape[0]
     cells_x, cells_y, cells_z = stiff_out.shape
     dofs = 3 * len(CORNERS)
     wide = dofs * cells_y
@@ -208,6 +214,7 @@
         coupling_ref[pl.ds(block * wide, wide), :] = jnp.where(same_y, spread, 0.0)
     lane = lax.broadcasted_iota(jnp.int32, (cells_y, cells_z), 1)
     inside = lane < cells_z - 1
+    last_row = lax.broadcasted_iota(jnp.int32, (cells_y, cells_z), 0) == cells_y - 1
     stiff_out[...] = jnp.zeros(stiff_out.shape, jnp.float32)
     mass_out[...] = jnp.zeros(mass_out.shape, jnp.float32)
     member_rows = (state_rows, adjoint_rows)
@@ -216,10 +223,17 @@
         for node_x in range(cells_x + 1):
             for member in range(2):
                 for component in range(3):
+                    if node_x < cells_x:
+                        tile = fields_ref[pair, member, component, node_x]
+                    else:
+                        tile = rim_x_ref[pair, member, component, 0]
                     for corner_y in (0, 1):
-                        base = extended_ref[
-                            pair, member, component, node_x, pl.ds(corner_y, cells_y), :
-                        ]
+                        base = tile
+                        if corner_y:
+                            below = jnp.broadcast_to(
+                                rim_y_ref[pair, member, component, node_x], (cells_y, cells_z)
+                            )
+                            base = jnp.where(last_row, below, pltpu.roll(tile, cells_y - 1, 0))
                         for corner_z in (0, 1):
                             value = base
                             if corner_z:
@@ -254,9 +268,9 @@
     lax.fori_loop(0, pair_count, over_pairs, 0)
 
 
-def element_energies(extended, stiffness, mass_matrix):
-    pair_count = extended.shape[0]
-    cells = (extended.shape[3] - 1, extended.shape[4] - 1, extended.shape[5])
+def element_energies(fields, rim_x, rim_y, stiffness, mass_matrix):
+    pair_count = fields.shape[0]
+    cells = fields.shape[3:]
     voxels = cells[0] * cells[1] * cells[2]
     dofs = stiffness.shape[0]
     vmem = pl.BlockSpec(memory_space=pltpu.VMEM)
@@ -266,7 +280,7 @@
             jax.ShapeDtypeStruct(cells, jnp.float32),
             jax.ShapeDtypeStruct(cells, jnp.float32),
         ),
-        in_specs=[vmem, vmem, vmem],
+        in_specs=[vmem, vmem, vmem, vmem, vmem],
         out_specs=(vmem, vmem),
         scratch_shapes=[
             pltpu.VMEM((2 * dofs * cells[1], dofs * cells[1]), jnp.float32),
@@ -276,10 +290,10 @@
         ],
         cost_estimate=pl.CostEstimate(
             flops=pair_count * (4 * (dofs * cells[1]) ** 2 * cells[0] * cells[2] + 4 * dofs * voxels),
-            bytes_accessed=extended.size * 4 + 2 * stiffness.size * 4 + 2 * voxels * 4,
+            bytes_accessed=(fields.size + rim_x.size + rim_y.size) * 4 + 2 * stiffness.size * 4 + 2 * voxels * 4,
             transcendentals=0,
         ),
-    )(extended, stiffness, mass_matrix)
+    )(fields, rim_x, rim_y, stiffness, mass_matrix)
 
 
 def shards(design, passive, basis_pairs, supports, stiffness, mass_matrix, volume_fraction):
@@ -299,10 +313,10 @@
     inside = valid_x[:, None, None] * valid_y[None, :, None] * valid_z[None, None, :]
     weight_sum = stencil(inside, block_shape)
     fields = basis_pairs * (1 - supports).astype(jnp.float32)
-    design_wide, extended = front_exchange(design, fields, 2)
+    design_wide, (rim_x, rim_y) = front_exchange(design, basis_pairs, supports, 2)
     design_wide = jnp.pad(design_wide, ((0, 0), (0, 0), (2, 2)))
     physical = jnp.where(passive == 1, 1.0, stencil(design_wide, block_shape) / weight_sum)
-    stiff_energy, mass_energy = element_energies(extended, stiffness, mass_matrix)
+    stiff_energy, mass_energy = element_energies(fields, rim_x, rim_y, stiffness, mass_matrix)
     raw_sensitivity = -(
         PENALTY_SCALE * physical * physical * stiff_energy - OMEGA_SQUARED * mass_energy
     )

time: 127 us -> 128 us (level)
  local copies, waits for them, and re-layouts: 0.82 us -> 2.53 us
  starting transfers between devices: 83.6 us -> 82.3 us
    ppermute x9, starting transfers between devices: 54.9 us -> 53.4 us  [butterfly_sum(): lax.ppermute(value, axis, [(i, i ^ stride) for i in range(count)])]
    concatenate x2 -> x1, other arithmetic: 1.41 us -> 0.02 us  [front_exchange(): jnp.concatenate([basis_pairs[:, :, :, :, :1] * open_nodes[:, :1], receive...]
  transfers between devices with their start and end apart: 17 -> 17, of which waited for: 13 -> 12; matrix products, arithmetic and copies ran while one was open for 1% -> 3% of each run, Pallas kernels for 5% -> 5%
where the time goes in v11:
time: 128 us; the launch traced here: 125 us
  starting transfers between devices  82.3 us (64%)
  waiting for transfers between devices  24.7 us (19%)
  other arithmetic  8.9 us (7%)
  Pallas kernels  5.92 us (5%)
  local copies, waits for them, and re-layouts  2.53 us (2%)
    ppermute x9, starting transfers between devices, butterfly_sum(): lax.ppermute(value, axis, [(i, i ^ stride) for i in range(count)])  53.4 us
    ppermute x9, waiting for transfers between devices, butterfly_sum(): lax.ppermute(value, axis, [(i, i ^ stride) for i in range(count)])  22.1 us
    ppermute x2, starting transfers between devices, with_halo(): lax.ppermute(tail, axis, [(i, (i + 1) % count) for i in range(ends)])  8.65 us
    ppermute x2, starting transfers between devices, with_halo(): lax.ppermute(head, axis, [((i + 1) % count, i) for i in range(ends)])  8.09 us
    ppermute x2, starting transfers between devices, front_exchange(): lax.ppermute(packed, axis, [((i + 1) % count, i) for i in range(ends)])  7.07 us
    pallas_call x1, Pallas kernels, element_energies(): pl.pallas_call(mxu_energy_kernel, out_shape=(jax.ShapeDtypeStruct(cells,...  5.92 us
    ppermute x2, starting transfers between devices, front_exchange(): tail = lax.ppermute(tail, axis, [(i, (i + 1) % count) for i in range(ends)])  5.08 us
  transfers between devices with their start and end apart: 17, of which 12 were waited for; matrix products, arithmetic and copies ran while one was open for 3% of the time, Pallas kernels for 5%

profile of v11, /device:TPU:6, one launch (start us, length us, event | category | flops | bytes accessed | tf_op | source)
XLA Modules:
  0.0 125.4 jit_solution(6160807864482514200)
XLA Ops:
  2.1 0.9 slice_multiply_fusion
  3.0 1.3 %collective-permute-start.1 = (f32[208,128]{1,0:T(8,128)S(1)}, f32[208,128]{1,0:T(8,128)S(1)}, u32[]{:S(2)}, u32[]{:S(2)}) collective-permute-start(f32[208,128]{1,0:T(8,128)S(1)} %pad_maximum_fusion.2), channel_id=1, source_target_pairs={{16,0},{32,16},{48,32},{64,48},{80,64},{96,80},{112,96},{128,112},... | collective-permute-start | bytes 319496 | tf_op jit(solution)/shard_map/ppermute | solution.py:47
  4.3 3.2 %collective-permute-start = (f32[2,8,128]{2,1,0:T(8,128)S(1)}, f32[2,8,128]{2,1,0:T(8,128)S(1)}, u32[]{:S(2)}, u32[]{:S(2)}) collective-permute-start(f32[2,8,128]{2,1,0:T(8,128)S(1)} %get-tuple-element.23), channel_id=1, source_target_pairs={{0,16},{16,32},{32,48},{48,64},{64,80},{80,96},{96,112},{112,128},... | collective-permute-start | bytes 24584 | tf_op jit(solution)/shard_map/ppermute | solution.py:51
  7.5 2.1 %broadcast_multiply_fusion.fields_ref = f32[4,2,3,8,8,128]{5,4,3,2,1,0:T(8,128)} fusion(f32[4,2,3,8,8,128]{5,4,3,2,1,0:T(8,128)} %param.9, f32[8,8,128]{2,1,0:T(8,128)S(1)} %subtract_convert_fusion), kind=kLoop, calls=%fused_computation.6 | loop fusion | flops 196608 | bytes 1605632 | tf_op jit(solution)/shard_map/mul | solution.py:315
  10.4 5.8 %collective-permute-start.3 = (f32[240,128]{1,0:T(8,128)S(1)}, f32[240,128]{1,0:T(8,128)S(1)}, u32[]{:S(2)}, u32[]{:S(2)}) collective-permute-start(f32[240,128]{1,0:T(8,128)S(1)} %pad_maximum_fusion.1), channel_id=1, source_target_pairs={{1,0},{2,1},{3,2},{4,3},{5,4},{6,5},{7,6},{8,7},{9,8},{10,9},{11,1... | collective-permute-start | bytes 368648 | tf_op jit(solution)/shard_map/ppermute | solution.py:47
  16.2 1.9 %collective-permute-start.2 = (f32[12,2,128]{2,1,0:T(2,128)S(1)}, f32[12,2,128]{2,1,0:T(2,128)S(1)}, u32[]{:S(2)}, u32[]{:S(2)}) collective-permute-start(f32[12,2,128]{2,1,0:T(2,128)S(1)} %get-tuple-element.16), channel_id=1, source_target_pairs={{0,1},{1,2},{2,3},{3,4},{4,5},{5,6},{6,7},{7,8},{8,9},{9,10},{10,1... | collective-permute-start | bytes 36872 | tf_op jit(solution)/shard_map/ppermute | solution.py:51
  19.3 5.9 %shard_map.86 = (f32[8,8,128]{2,1,0:T(8,128)}, f32[8,8,128]{2,1,0:T(8,128)}) custom-call(f32[4,2,3,8,8,128]{5,4,3,2,1,0:T(8,128)} %broadcast_multiply_fusion.fields_ref, f32[4,2,3,1,8,128]{5,4,3,2,1,0:T(8,128)} %bitcast.75, f32[4,2,3,9,1,128]{5,4,3,2,1,0:T(1,128)} %bitcast.78, f32[24,24]{1,0:T(8,128)} %stiffness_ref.1, f32[24,24]{1,0:T(8,128)} %mass_ref.1), custom_call_target="tpu_custom_call" | custom-call | flops 607125504 | bytes 1065472 | tf_op jit(solution)/shard_map/pallas_call | solution.py:277
  25.5 2.0 %fusion.82 = (f32[8,8,128]{2,1,0:T(8,128)S(1)}, pred[8,8,128]{2,1,0:T(8,128)(4,1)S(1)}) fusion(f32[8,8,128]{2,1,0:T(8,128)} %get-tuple-element.4, f32[12,10,128]{2,1,0:T(8,128)S(1)} %get-tuple-element.15, f32[12,12,132]{2,1,0:T(8,128)S(1)} %select_maximum_fusion.4, f32[2,8,128]{2,1,0:T(8,128)S(1)} %slice_bitcast_fusion.1, f32[8,8,128]{2,1,0:T(8,128)S(1)} %copy-done, ...), kind=kLoop, calls=%fused_computation.111 | loop fusion | flops 3039232 | bytes 6176768 | tf_op jit(solution)/shard_map/div | solution.py:324
  27.5 1.3 %collective-permute-start.5 = (f32[2,8,128]{2,1,0:T(8,128)S(1)}, f32[2,8,128]{2,1,0:T(8,128)S(1)}, u32[]{:S(2)}, u32[]{:S(2)}) collective-permute-start(f32[2,8,128]{2,1,0:T(8,128)S(1)} %get-tuple-element.22), channel_id=1, source_target_pairs={{16,0},{32,16},{48,32},{64,48},{80,64},{96,80},{112,96},{128,112},... | collective-permute-start | bytes 24584 | tf_op jit(solution)/shard_map/ppermute | solution.py:29
  28.8 6.7 %collective-permute-start.4 = (f32[2,8,128]{2,1,0:T(8,128)S(1)}, f32[2,8,128]{2,1,0:T(8,128)S(1)}, u32[]{:S(2)}, u32[]{:S(2)}) collective-permute-start(f32[2,8,128]{2,1,0:T(8,128)S(1)} %get-tuple-element.21), channel_id=1, source_target_pairs={{0,16},{16,32},{32,48},{48,64},{64,80},{80,96},{96,112},{112,128},... | collective-permute-start | bytes 24584 | tf_op jit(solution)/shard_map/ppermute | solution.py:27
  36.4 1.9 %collective-permute-start.6 = (f32[12,2,128]{2,1,0:T(2,128)S(1)}, f32[12,2,128]{2,1,0:T(2,128)S(1)}, u32[]{:S(2)}, u32[]{:S(2)}) collective-permute-start(f32[12,2,128]{2,1,0:T(2,128)S(1)} %get-tuple-element.12), channel_id=1, source_target_pairs={{0,1},{1,2},{2,3},{3,4},{4,5},{5,6},{6,7},{7,8},{8,9},{9,10},{10,1... | collective-permute-start | bytes 36872 | tf_op jit(solution)/shard_map/ppermute | solution.py:27
  38.3 6.8 %collective-permute-start.7 = (f32[12,2,128]{2,1,0:T(2,128)S(1)}, f32[12,2,128]{2,1,0:T(2,128)S(1)}, u32[]{:S(2)}, u32[]{:S(2)}) collective-permute-start(f32[12,2,128]{2,1,0:T(2,128)S(1)} %get-tuple-element.13), channel_id=1, source_target_pairs={{1,0},{2,1},{3,2},{4,3},{5,4},{6,5},{7,6},{8,7},{9,8},{10,9},{11,1... | collective-permute-start | bytes 36872 | tf_op jit(solution)/shard_map/ppermute | solution.py:29
  45.2 1.2 collective-permute-done.7
  47.2 0.9 fusion.4
  48.6 1.9 %collective-permute-start.8 = (f32[32,128]{1,0:T(8,128)S(1)}, f32[32,128]{1,0:T(8,128)S(1)}, u32[]{:S(2)}, u32[]{:S(2)}) collective-permute-start(f32[32,128]{1,0:T(8,128)S(1)} %pad_bitcast_fusion), channel_id=1, source_target_pairs={{0,1},{1,0},{2,3},{3,2},{4,5},{5,4},{6,7},{7,6},{8,9},{9,8},{10,11... | collective-permute-start | bytes 49160 | tf_op jit(solution)/shard_map/ppermute | solution.py:71
  50.5 3.7 %collective-permute-done.8 = f32[32,128]{1,0:T(8,128)S(1)} collective-permute-done((f32[32,128]{1,0:T(8,128)S(1)}, f32[32,128]{1,0:T(8,128)S(1)}, u32[]{:S(2)}, u32[]{:S(2)}) %collective-permute-start.8) | collective-permute-done | bytes 16416 | tf_op jit(solution)/shard_map/ppermute | solution.py:71
  54.2 1.9 %collective-permute-start.9 = (f32[32,128]{1,0:T(8,128)S(1)}, f32[32,128]{1,0:T(8,128)S(1)}, u32[]{:S(2)}, u32[]{:S(2)}) collective-permute-start(f32[32,128]{1,0:T(8,128)S(1)} %fusion.293), channel_id=1, source_target_pairs={{0,2},{1,3},{2,0},{3,1},{4,6},{5,7},{6,4},{7,5},{8,10},{9,11},{10,... | collective-permute-start | bytes 49160 | tf_op jit(solution)/shard_map/ppermute | solution.py:71
  56.1 4.6 %collective-permute-done.9 = f32[32,128]{1,0:T(8,128)S(1)} collective-permute-done((f32[32,128]{1,0:T(8,128)S(1)}, f32[32,128]{1,0:T(8,128)S(1)}, u32[]{:S(2)}, u32[]{:S(2)}) %collective-permute-start.9) | collective-permute-done | bytes 16416 | tf_op jit(solution)/shard_map/ppermute | solution.py:71
  60.7 3.1 %collective-permute-start.10 = (f32[32,128]{1,0:T(8,128)S(1)}, f32[32,128]{1,0:T(8,128)S(1)}, u32[]{:S(2)}, u32[]{:S(2)}) collective-permute-start(f32[32,128]{1,0:T(8,128)S(1)} %fusion.297), channel_id=1, source_target_pairs={{0,4},{1,5},{2,6},{3,7},{4,0},{5,1},{6,2},{7,3},{8,12},{9,13},{10,... | collective-permute-start | bytes 49160 | tf_op jit(solution)/shard_map/ppermute | solution.py:71
  63.8 2.5 %collective-permute-done.10 = f32[32,128]{1,0:T(8,128)S(1)} collective-permute-done((f32[32,128]{1,0:T(8,128)S(1)}, f32[32,128]{1,0:T(8,128)S(1)}, u32[]{:S(2)}, u32[]{:S(2)}) %collective-permute-start.10) | collective-permute-done | bytes 16416 | tf_op jit(solution)/shard_map/ppermute | solution.py:71
  66.3 3.6 %collective-permute-start.11 = (f32[32,128]{1,0:T(8,128)S(1)}, f32[32,128]{1,0:T(8,128)S(1)}, u32[]{:S(2)}, u32[]{:S(2)}) collective-permute-start(f32[32,128]{1,0:T(8,128)S(1)} %add.1202), channel_id=1, source_target_pairs={{0,8},{1,9},{2,10},{3,11},{4,12},{5,13},{6,14},{7,15},{8,0},{9,1},... | collective-permute-start | bytes 49160 | tf_op jit(solution)/shard_map/ppermute | solution.py:71
  70.0 3.5 %collective-permute-done.11 = f32[32,128]{1,0:T(8,128)S(1)} collective-permute-done((f32[32,128]{1,0:T(8,128)S(1)}, f32[32,128]{1,0:T(8,128)S(1)}, u32[]{:S(2)}, u32[]{:S(2)}) %collective-permute-start.11) | collective-permute-done | bytes 16416 | tf_op jit(solution)/shard_map/ppermute | solution.py:71
  73.5 2.1 %collective-permute-start.12 = (f32[32,128]{1,0:T(8,128)S(1)}, f32[32,128]{1,0:T(8,128)S(1)}, u32[]{:S(2)}, u32[]{:S(2)}) collective-permute-start(f32[32,128]{1,0:T(8,128)S(1)} %add.1203), channel_id=1, source_target_pairs={{0,16},{16,0},{32,48},{48,32},{64,80},{80,64},{96,112},{112,96},{1... | collective-permute-start | bytes 49160 | tf_op jit(solution)/shard_map/ppermute | solution.py:71
  75.5 1.0 collective-permute-done.12
  76.5 13.7 %collective-permute-start.13 = (f32[32,128]{1,0:T(8,128)S(1)}, f32[32,128]{1,0:T(8,128)S(1)}, u32[]{:S(2)}, u32[]{:S(2)}) collective-permute-start(f32[32,128]{1,0:T(8,128)S(1)} %add.1204), channel_id=1, source_target_pairs={{0,32},{16,48},{32,0},{48,16},{64,96},{80,112},{96,64},{112,80},{1... | collective-permute-start | bytes 49160 | tf_op jit(solution)/shard_map/ppermute | solution.py:71
  90.2 1.7 %collective-permute-done.13 = f32[32,128]{1,0:T(8,128)S(1)} collective-permute-done((f32[32,128]{1,0:T(8,128)S(1)}, f32[32,128]{1,0:T(8,128)S(1)}, u32[]{:S(2)}, u32[]{:S(2)}) %collective-permute-start.13) | collective-permute-done | bytes 16416 | tf_op jit(solution)/shard_map/ppermute | solution.py:71
  91.9 8.9 %collective-permute-start.14 = (f32[32,128]{1,0:T(8,128)S(1)}, f32[32,128]{1,0:T(8,128)S(1)}, u32[]{:S(2)}, u32[]{:S(2)}) collective-permute-start(f32[32,128]{1,0:T(8,128)S(1)} %add.1205), channel_id=1, source_target_pairs={{0,64},{16,80},{32,96},{48,112},{64,0},{80,16},{96,32},{112,48},{1... | collective-permute-start | bytes 49160 | tf_op jit(solution)/shard_map/ppermute | solution.py:71
  100.9 1.7 %collective-permute-done.14 = f32[32,128]{1,0:T(8,128)S(1)} collective-permute-done((f32[32,128]{1,0:T(8,128)S(1)}, f32[32,128]{1,0:T(8,128)S(1)}, u32[]{:S(2)}, u32[]{:S(2)}) %collective-permute-start.14) | collective-permute-done | bytes 16416 | tf_op jit(solution)/shard_map/ppermute | solution.py:71
  102.6 6.1 %collective-permute-start.15 = (f32[32,128]{1,0:T(8,128)S(1)}, f32[32,128]{1,0:T(8,128)S(1)}, u32[]{:S(2)}, u32[]{:S(2)}) collective-permute-start(f32[32,128]{1,0:T(8,128)S(1)} %add.1206), channel_id=1, source_target_pairs={{0,128},{16,144},{32,160},{48,176},{64,192},{80,208},{96,224},{112... | collective-permute-start | bytes 49160 | tf_op jit(solution)/shard_map/ppermute | solution.py:71
  108.7 1.7 %collective-permute-done.15 = f32[32,128]{1,0:T(8,128)S(1)} collective-permute-done((f32[32,128]{1,0:T(8,128)S(1)}, f32[32,128]{1,0:T(8,128)S(1)}, u32[]{:S(2)}, u32[]{:S(2)}) %collective-permute-start.15) | collective-permute-done | bytes 16416 | tf_op jit(solution)/shard_map/ppermute | solution.py:71
  110.4 12.1 %collective-permute-start.16 = (f32[32,128]{1,0:T(8,128)S(1)}, f32[32,128]{1,0:T(8,128)S(1)}, u32[]{:S(2)}, u32[]{:S(2)}) collective-permute-start(f32[32,128]{1,0:T(8,128)S(1)} %add.1207), channel_id=1, source_target_pairs={{0,256},{16,272},{32,288},{48,304},{64,320},{80,336},{96,352},{112... | collective-permute-start | bytes 49160 | tf_op jit(solution)/shard_map/ppermute | solution.py:71
  122.5 1.7 %collective-permute-done.16 = f32[32,128]{1,0:T(8,128)S(1)} collective-permute-done((f32[32,128]{1,0:T(8,128)S(1)}, f32[32,128]{1,0:T(8,128)S(1)}, u32[]{:S(2)}, u32[]{:S(2)}) %collective-permute-start.16) | collective-permute-done | bytes 16416 | tf_op jit(solution)/shard_map/ppermute | solution.py:71
  (83 shorter events, 6.8 us)
Async XLA Ops:
  3.0 6.9 %collective-permute-start.1 = (f32[208,128]{1,0:T(8,128)S(1)}, f32[208,128]{1,0:T(8,128)S(1)}, u32[]{:S(2)}, u32[]{:S(2)}) collective-permute-start(f32[208,128]{1,0:T(8,128)S(1)} %pad_maximum_fusion.2), channel_id=1, source_target_pairs={{16,0},{32,16},{48,32},{64,48},{80,64},{96,80},{112,96},{128,112},... | collective-permute-start | bytes 319496 | tf_op jit(solution)/shard_map/ppermute | solution.py:47
  4.3 5.6 %slice-start = ((f32[4,2,3,8,8,128]{5,4,3,2,1,0:T(8,128)}), f32[4,2,3,8,1,128]{5,4,3,2,1,0:T(1,128)S(1)}, s32[]{:S(2)}) async-start(f32[4,2,3,8,8,128]{5,4,3,2,1,0:T(8,128)} %param.9), calls=%async_computation | async-start | bytes 196608 | tf_op jit(solution)/shard_map/slice | solution.py:56
  4.3 5.6 %collective-permute-start = (f32[2,8,128]{2,1,0:T(8,128)S(1)}, f32[2,8,128]{2,1,0:T(8,128)S(1)}, u32[]{:S(2)}, u32[]{:S(2)}) collective-permute-start(f32[2,8,128]{2,1,0:T(8,128)S(1)} %get-tuple-element.23), channel_id=1, source_target_pairs={{0,16},{16,32},{32,48},{48,64},{64,80},{80,96},{96,112},{112,128},... | collective-permute-start | bytes 24584 | tf_op jit(solution)/shard_map/ppermute | solution.py:51
  9.6 0.8 copy-start
  10.0 9.4 %copy-start.2 = (f32[192,128]{1,0:T(8,128)}, f32[192,128]{1,0:T(8,128)S(1)}, u32[]{:S(2)}) copy-start(f32[192,128]{1,0:T(8,128)S(1)} %slice.1322) | copy-start | bytes 294916
  10.4 8.2 %collective-permute-start.3 = (f32[240,128]{1,0:T(8,128)S(1)}, f32[240,128]{1,0:T(8,128)S(1)}, u32[]{:S(2)}, u32[]{:S(2)}) collective-permute-start(f32[240,128]{1,0:T(8,128)S(1)} %pad_maximum_fusion.1), channel_id=1, source_target_pairs={{1,0},{2,1},{3,2},{4,3},{5,4},{6,5},{7,6},{8,7},{9,8},{10,9},{11,1... | collective-permute-start | bytes 368648 | tf_op jit(solution)/shard_map/ppermute | solution.py:47
  16.2 9.0 %collective-permute-start.2 = (f32[12,2,128]{2,1,0:T(2,128)S(1)}, f32[12,2,128]{2,1,0:T(2,128)S(1)}, u32[]{:S(2)}, u32[]{:S(2)}) collective-permute-start(f32[12,2,128]{2,1,0:T(2,128)S(1)} %get-tuple-element.16), channel_id=1, source_target_pairs={{0,1},{1,2},{2,3},{3,4},{4,5},{5,6},{6,7},{7,8},{8,9},{9,10},{10,1... | collective-permute-start | bytes 36872 | tf_op jit(solution)/shard_map/ppermute | solution.py:51
  19.3 6.1 %copy-start.3 = (s32[8,8,128]{2,1,0:T(8,128)S(1)}, s32[8,8,128]{2,1,0:T(8,128)}, u32[]{:S(2)}) copy-start(s32[8,8,128]{2,1,0:T(8,128)} %param.8) | copy-start | bytes 98308
  25.5 19.6 %copy-start.4 = (f32[63,64]{0,1:T(8,128)S(1)}, f32[63,64]{0,1:T(8,128)}, u32[]{:S(2)}) copy-start(f32[63,64]{0,1:T(8,128)} %constant.25.clone.1) | copy-start | bytes 48388
  27.5 8.0 %collective-permute-start.5 = (f32[2,8,128]{2,1,0:T(8,128)S(1)}, f32[2,8,128]{2,1,0:T(8,128)S(1)}, u32[]{:S(2)}, u32[]{:S(2)}) collective-permute-start(f32[2,8,128]{2,1,0:T(8,128)S(1)} %get-tuple-element.22), channel_id=1, source_target_pairs={{16,0},{32,16},{48,32},{64,48},{80,64},{96,80},{112,96},{128,112},... | collective-permute-start | bytes 24584 | tf_op jit(solution)/shard_map/ppermute | solution.py:29
  28.8 7.5 %collective-permute-start.4 = (f32[2,8,128]{2,1,0:T(8,128)S(1)}, f32[2,8,128]{2,1,0:T(8,128)S(1)}, u32[]{:S(2)}, u32[]{:S(2)}) collective-permute-start(f32[2,8,128]{2,1,0:T(8,128)S(1)} %get-tuple-element.21), channel_id=1, source_target_pairs={{0,16},{16,32},{32,48},{48,64},{64,80},{80,96},{96,112},{112,128},... | collective-permute-start | bytes 24584 | tf_op jit(solution)/shard_map/ppermute | solution.py:27
  36.4 8.9 %collective-permute-start.6 = (f32[12,2,128]{2,1,0:T(2,128)S(1)}, f32[12,2,128]{2,1,0:T(2,128)S(1)}, u32[]{:S(2)}, u32[]{:S(2)}) collective-permute-start(f32[12,2,128]{2,1,0:T(2,128)S(1)} %get-tuple-element.12), channel_id=1, source_target_pairs={{0,1},{1,2},{2,3},{3,4},{4,5},{5,6},{6,7},{7,8},{8,9},{9,10},{10,1... | collective-permute-start | bytes 36872 | tf_op jit(solution)/shard_map/ppermute | solution.py:27
  38.3 8.2 %collective-permute-start.7 = (f32[12,2,128]{2,1,0:T(2,128)S(1)}, f32[12,2,128]{2,1,0:T(2,128)S(1)}, u32[]{:S(2)}, u32[]{:S(2)}) collective-permute-start(f32[12,2,128]{2,1,0:T(2,128)S(1)} %get-tuple-element.13), channel_id=1, source_target_pairs={{1,0},{2,1},{3,2},{4,3},{5,4},{6,5},{7,6},{8,7},{9,8},{10,9},{11,1... | collective-permute-start | bytes 36872 | tf_op jit(solution)/shard_map/ppermute | solution.py:29
  47.2 77.5 %copy-start.1 = (f32[8,8,128]{2,1,0:T(8,128)}, f32[8,8,128]{2,1,0:T(8,128)S(1)}, u32[]{:S(2)}) copy-start(f32[8,8,128]{2,1,0:T(8,128)S(1)} %get-tuple-element.7) | copy-start | bytes 98308
  47.2 75.2 %copy-start.5 = (f32[64]{0:T(128)S(1)}, f32[64]{0:T(128)}, u32[]{:S(2)}) copy-start(f32[64]{0:T(128)} %param.13) | copy-start | bytes 772
  48.6 5.6 %collective-permute-start.8 = (f32[32,128]{1,0:T(8,128)S(1)}, f32[32,128]{1,0:T(8,128)S(1)}, u32[]{:S(2)}, u32[]{:S(2)}) collective-permute-start(f32[32,128]{1,0:T(8,128)S(1)} %pad_bitcast_fusion), channel_id=1, source_target_pairs={{0,1},{1,0},{2,3},{3,2},{4,5},{5,4},{6,7},{7,6},{8,9},{9,8},{10,11... | collective-permute-start | bytes 49160 | tf_op jit(solution)/shard_map/ppermute | solution.py:71
  54.2 6.5 %collective-permute-start.9 = (f32[32,128]{1,0:T(8,128)S(1)}, f32[32,128]{1,0:T(8,128)S(1)}, u32[]{:S(2)}, u32[]{:S(2)}) collective-permute-start(f32[32,128]{1,0:T(8,128)S(1)} %fusion.293), channel_id=1, source_target_pairs={{0,2},{1,3},{2,0},{3,1},{4,6},{5,7},{6,4},{7,5},{8,10},{9,11},{10,... | collective-permute-start | bytes 49160 | tf_op jit(solution)/shard_map/ppermute | solution.py:71
  60.7 5.6 %collective-permute-start.10 = (f32[32,128]{1,0:T(8,128)S(1)}, f32[32,128]{1,0:T(8,128)S(1)}, u32[]{:S(2)}, u32[]{:S(2)}) collective-permute-start(f32[32,128]{1,0:T(8,128)S(1)} %fusion.297), channel_id=1, source_target_pairs={{0,4},{1,5},{2,6},{3,7},{4,0},{5,1},{6,2},{7,3},{8,12},{9,13},{10,... | collective-permute-start | bytes 49160 | tf_op jit(solution)/shard_map/ppermute | solution.py:71
  66.3 7.1 %collective-permute-start.11 = (f32[32,128]{1,0:T(8,128)S(1)}, f32[32,128]{1,0:T(8,128)S(1)}, u32[]{:S(2)}, u32[]{:S(2)}) collective-permute-start(f32[32,128]{1,0:T(8,128)S(1)} %add.1202), channel_id=1, source_target_pairs={{0,8},{1,9},{2,10},{3,11},{4,12},{5,13},{6,14},{7,15},{8,0},{9,1},... | collective-permute-start | bytes 49160 | tf_op jit(solution)/shard_map/ppermute | solution.py:71
  73.5 3.1 %collective-permute-start.12 = (f32[32,128]{1,0:T(8,128)S(1)}, f32[32,128]{1,0:T(8,128)S(1)}, u32[]{:S(2)}, u32[]{:S(2)}) collective-permute-start(f32[32,128]{1,0:T(8,128)S(1)} %add.1203), channel_id=1, source_target_pairs={{0,16},{16,0},{32,48},{48,32},{64,80},{80,64},{96,112},{112,96},{1... | collective-permute-start | bytes 49160 | tf_op jit(solution)/shard_map/ppermute | solution.py:71
  76.5 15.4 %collective-permute-start.13 = (f32[32,128]{1,0:T(8,128)S(1)}, f32[32,128]{1,0:T(8,128)S(1)}, u32[]{:S(2)}, u32[]{:S(2)}) collective-permute-start(f32[32,128]{1,0:T(8,128)S(1)} %add.1204), channel_id=1, source_target_pairs={{0,32},{16,48},{32,0},{48,16},{64,96},{80,112},{96,64},{112,80},{1... | collective-permute-start | bytes 49160 | tf_op jit(solution)/shard_map/ppermute | solution.py:71
  91.9 10.7 %collective-permute-start.14 = (f32[32,128]{1,0:T(8,128)S(1)}, f32[32,128]{1,0:T(8,128)S(1)}, u32[]{:S(2)}, u32[]{:S(2)}) collective-permute-start(f32[32,128]{1,0:T(8,128)S(1)} %add.1205), channel_id=1, source_target_pairs={{0,64},{16,80},{32,96},{48,112},{64,0},{80,16},{96,32},{112,48},{1... | collective-permute-start | bytes 49160 | tf_op jit(solution)/shard_map/ppermute | solution.py:71
  102.6 7.8 %collective-permute-start.15 = (f32[32,128]{1,0:T(8,128)S(1)}, f32[32,128]{1,0:T(8,128)S(1)}, u32[]{:S(2)}, u32[]{:S(2)}) collective-permute-start(f32[32,128]{1,0:T(8,128)S(1)} %add.1206), channel_id=1, source_target_pairs={{0,128},{16,144},{32,160},{48,176},{64,192},{80,208},{96,224},{112... | collective-permute-start | bytes 49160 | tf_op jit(solution)/shard_map/ppermute | solution.py:71
  110.4 13.8 %collective-permute-start.16 = (f32[32,128]{1,0:T(8,128)S(1)}, f32[32,128]{1,0:T(8,128)S(1)}, u32[]{:S(2)}, u32[]{:S(2)}) collective-permute-start(f32[32,128]{1,0:T(8,128)S(1)} %add.1207), channel_id=1, source_target_pairs={{0,256},{16,272},{32,288},{48,304},{64,320},{80,336},{96,352},{112... | collective-permute-start | bytes 49160 | tf_op jit(solution)/shard_map/ppermute | solution.py:71

commit v12 on v11

--- a/solution.py
+++ b/solution.py
@@ -1,3 +1,4 @@
+import functools
 import math
 
 import jax
@@ -183,12 +184,18 @@
     lax.fori_loop(0, cells_x, over_x, 0)
 
 
-def mxu_energy_kernel(
-    fields_ref, rim_x_ref, rim_y_ref, stiffness_ref, mass_ref, stiff_out, mass_out, coupling_ref,
-    state_rows, adjoint_rows, products,
-):
+def mxu_energy_kernel(slices, scaled, *refs):
+    if scaled:
+        (fields_ref, rim_x_ref, rim_y_ref, stiffness_ref, mass_ref, physical_ref, passive_ref,
+         weight_ref, stiff_out, mass_out, scaled_out, coupling_ref, state_rows, adjoint_rows,
+         products) = refs
+    else:
+        (fields_ref, rim_x_ref, rim_y_ref, stiffness_ref, mass_ref, stiff_out, mass_out,
+         coupling_ref, state_rows, adjoint_rows, products) = refs
     pair_count = fields_ref.shape[0]
-    cells_x, cells_y, cells_z = stiff_out.shape
+    cells_x = fields_ref.shape[3]
+    _, cells_y, cells_z = stiff_out.shape
+    columns_of = len(slices) * cells_z
     dofs = 3 * len(CORNERS)
     wide = dofs * cells_y
     spread_rows = (
@@ -220,7 +227,7 @@
     member_rows = (state_rows, adjoint_rows)
 
     def over_pairs(pair, carry):
-        for node_x in range(cells_x + 1):
+        for node_x in sorted(set(slices) | {x + 1 for x in slices}):
             for member in range(2):
                 for component in range(3):
                     if node_x < cells_x:
@@ -240,11 +247,12 @@
                                 value = jnp.where(inside, pltpu.roll(base, cells_z - 1, 1), 0.0)
                             for corner_x in (0, 1):
                                 x = node_x - corner_x
-                                if 0 <= x < cells_x:
+                                if x in slices:
+                                    place = slices.index(x)
                                     corner = CORNERS.index((corner_x, corner_y, corner_z))
                                     row = 3 * corner + component
                                     member_rows[member][
-                                        pl.ds(row * cells_y, cells_y), pl.ds(x * cells_z, cells_z)
+                                        pl.ds(row * cells_y, cells_y), pl.ds(place * cells_z, cells_z)
                                     ] = value
         products[...] = jnp.dot(
             coupling_ref[...],
@@ -252,36 +260,41 @@
             precision=lax.Precision.HIGH,
             preferred_element_type=jnp.float32,
         )
-        state = state_rows[...].reshape(dofs, cells_y, cells_x * cells_z)
+        state = state_rows[...].reshape(dofs, cells_y, columns_of)
         stiff_sum = jnp.sum(
-            state * products[pl.ds(0, wide), :].reshape(dofs, cells_y, cells_x * cells_z), axis=0
+            state * products[pl.ds(0, wide), :].reshape(dofs, cells_y, columns_of), axis=0
         )
         mass_sum = jnp.sum(
-            state * products[pl.ds(wide, wide), :].reshape(dofs, cells_y, cells_x * cells_z), axis=0
-        )
-        for x in range(cells_x):
-            columns = slice(x * cells_z, (x + 1) * cells_z)
-            stiff_out[x] = stiff_out[x] + stiff_sum[:, columns]
-            mass_out[x] = mass_out[x] + mass_sum[:, columns]
+            state * products[pl.ds(wide, wide), :].reshape(dofs, cells_y, columns_of), axis=0
+        )
+        for place in range(len(slices)):
+            columns = slice(place * cells_z, (place + 1) * cells_z)
+            stiff_out[place] = stiff_out[place] + stiff_sum[:, columns]
+            mass_out[place] = mass_out[place] + mass_sum[:, columns]
         return carry
 
     lax.fori_loop(0, pair_count, over_pairs, 0)
-
-
-def element_energies(fields, rim_x, rim_y, stiffness, mass_matrix):
+    if scaled:
+        physical_rows = physical_ref[...]
+        raw_rows = -(
+            PENALTY_SCALE * physical_rows * physical_rows * stiff_out[...]
+            - OMEGA_SQUARED * mass_out[...]
+        )
+        raw_rows = jnp.where(passive_ref[...] == 1, 0.0, raw_rows)
+        scaled_out[...] = raw_rows / weight_ref[...]
+
+
+def element_energies(fields, rim_x, rim_y, stiffness, mass_matrix, slices, scaling=()):
     pair_count = fields.shape[0]
-    cells = fields.shape[3:]
+    cells = (len(slices),) + fields.shape[4:]
     voxels = cells[0] * cells[1] * cells[2]
     dofs = stiffness.shape[0]
     vmem = pl.BlockSpec(memory_space=pltpu.VMEM)
     return pl.pallas_call(
-        mxu_energy_kernel,
-        out_shape=(
-            jax.ShapeDtypeStruct(cells, jnp.float32),
-            jax.ShapeDtypeStruct(cells, jnp.float32),
-        ),
-        in_specs=[vmem, vmem, vmem, vmem, vmem],
-        out_specs=(vmem, vmem),
+        functools.partial(mxu_energy_kernel, slices, bool(scaling)),
+        out_shape=(jax.ShapeDtypeStruct(cells, jnp.float32),) * (3 if scaling else 2),
+        in_specs=[vmem] * (5 + len(scaling)),
+        out_specs=(vmem,) * (3 if scaling else 2),
         scratch_shapes=[
             pltpu.VMEM((2 * dofs * cells[1], dofs * cells[1]), jnp.float32),
             pltpu.VMEM((dofs * cells[1], cells[0] * cells[2]), jnp.float32),
@@ -290,10 +303,11 @@
         ],
         cost_estimate=pl.CostEstimate(
             flops=pair_count * (4 * (dofs * cells[1]) ** 2 * cells[0] * cells[2] + 4 * dofs * voxels),
-            bytes_accessed=(fields.size + rim_x.size + rim_y.size) * 4 + 2 * stiffness.size * 4 + 2 * voxels * 4,
+            bytes_accessed=(fields.size + rim_x.size + rim_y.size) * 4 * cells[0] // fields.shape[3]
+            + 2 * stiffness.size * 4 + 2 * voxels * 4,
             transcendentals=0,
         ),
-    )(fields, rim_x, rim_y, stiffness, mass_matrix)
+    )(fields, rim_x, rim_y, stiffness, mass_matrix, *scaling)
 
 
 def shards(design, passive, basis_pairs, supports, stiffness, mass_matrix, volume_fraction):
@@ -316,12 +330,35 @@
     design_wide, (rim_x, rim_y) = front_exchange(design, basis_pairs, supports, 2)
     design_wide = jnp.pad(design_wide, ((0, 0), (0, 0), (2, 2)))
     physical = jnp.where(passive == 1, 1.0, stencil(design_wide, block_shape) / weight_sum)
-    stiff_energy, mass_energy = element_energies(fields, rim_x, rim_y, stiffness, mass_matrix)
-    raw_sensitivity = -(
-        PENALTY_SCALE * physical * physical * stiff_energy - OMEGA_SQUARED * mass_energy
-    )
-    raw_sensitivity = jnp.where(passive == 1, 0.0, raw_sensitivity)
-    scaled_wide = with_halo(raw_sensitivity / weight_sum, (("gx", 0), ("gy", 1)), 2)
+    last = size_x - 1
+    rim_slices = (0, 1, last - 1, last)
+    inner_slices = tuple(range(2, last - 1))
+    rim_scaling = tuple(
+        jnp.concatenate([array[:2], array[last - 1 :]], axis=0) for array in (physical, passive, weight_sum)
+    )
+    _, _, rim_rows = element_energies(
+        fields, rim_x, rim_y, stiffness, mass_matrix, rim_slices, rim_scaling
+    )
+    inner_stiff, inner_mass = element_energies(
+        fields, rim_x, rim_y, stiffness, mass_matrix, inner_slices
+    )
+
+    def scaled_raw(stiff_rows, mass_rows, first, end):
+        physical_rows = physical[first:end]
+        raw_rows = -(
+            PENALTY_SCALE * physical_rows * physical_rows * stiff_rows - OMEGA_SQUARED * mass_rows
+        )
+        raw_rows = jnp.where(passive[first:end] == 1, 0.0, raw_rows)
+        return raw_rows / weight_sum[first:end]
+
+    head_rows = rim_rows[:2]
+    tail_rows = rim_rows[2:]
+    inner_rows = scaled_raw(inner_stiff, inner_mass, 2, last - 1)
+    count_x = lax.axis_size("gx")
+    head_x = lax.ppermute(head_rows, "gx", [(i + 1, i) for i in range(count_x - 1)])
+    tail_x = lax.ppermute(tail_rows, "gx", [(i, i + 1) for i in range(count_x - 1)])
+    scaled_wide = jnp.concatenate([tail_x, head_rows, inner_rows, tail_rows, head_x], axis=0)
+    scaled_wide = with_halo(scaled_wide, (("gy", 1),), 2)
     scaled_wide = jnp.pad(scaled_wide, ((0, 0), (0, 0), (2, 2)))
     sensitivity = stencil(scaled_wide, block_shape)
     benefit = jnp.maximum(-sensitivity, 0.0)

time: 128 us -> 137 us (1.070)
  waiting for transfers between devices: 24.7 us -> 36.1 us
  starting transfers between devices: 82.3 us -> 74.2 us
  Pallas kernels: 5.92 us -> 9.46 us
  other arithmetic: 8.9 us -> 10.7 us
    ppermute x2 -> x1, starting transfers between devices: 8.65 us -> 1.92 us  [with_halo(): lax.ppermute(tail, axis, [(i, (i + 1) % count) for i in range(ends)])]
    ppermute x0 -> x2, starting transfers between devices: none -> 6.72 us  [the longest x1 5.43 us: shards(): lax.ppermute(tail_rows, 'gx', [(i, i + 1) for i in range(count_x - 1)])]
    ppermute x0 -> x2, waiting for transfers between devices: none -> 6.65 us  [the longest x1 6.65 us: shards(): lax.ppermute(head_rows, 'gx', [(i + 1, i) for i in range(count_x - 1)])]
    ppermute x9, starting transfers between devices: 53.4 us -> 46.9 us  [butterfly_sum(): lax.ppermute(value, axis, [(i, i ^ stride) for i in range(count)])]
    ppermute x2, waiting for transfers between devices: 0.01 us -> 5.86 us  [front_exchange(): tail = lax.ppermute(tail, axis, [(i, (i + 1) % count) for i in range(ends)])]
    pallas_call x1 -> x2, Pallas kernels: 5.92 us -> 9.46 us  [element_energies(): pl.pallas_call(functools.partial(mxu_energy_kernel, slices, bool(scaling)...]
    div x1 -> x0, other arithmetic: 2 us -> none  [shards(): raw_sensitivity / weight_sum]
    concatenate x0 -> x3, other arithmetic: none -> 1.82 us  [shards(): jnp.concatenate([array[:2], array[last - 1:]], axis=0)]
  transfers between devices with their start and end apart: 17 -> 17, of which waited for: 12 -> 13; matrix products, arithmetic and copies ran while one was open for 3% -> 2% of each run, Pallas kernels for 5% -> 4%
where the time goes in v12:
time: 137 us; the launch traced here: 135 us
  starting transfers between devices  74.2 us (54%)
  waiting for transfers between devices  36.1 us (26%)
  other arithmetic  10.7 us (8%)
  Pallas kernels  9.46 us (7%)
  local copies, waits for them, and re-layouts  2.98 us (2%)
    ppermute x9, starting transfers between devices, butterfly_sum(): lax.ppermute(value, axis, [(i, i ^ stride) for i in range(count)])  46.9 us
    ppermute x9, waiting for transfers between devices, butterfly_sum(): lax.ppermute(value, axis, [(i, i ^ stride) for i in range(count)])  21.9 us
    pallas_call x2, Pallas kernels, element_energies(): pl.pallas_call(functools.partial(mxu_energy_kernel, slices, bool(scaling)...  9.46 us
    ppermute x2, starting transfers between devices, front_exchange(): lax.ppermute(packed, axis, [((i + 1) % count, i) for i in range(ends)])  7.07 us
    ppermute x1, waiting for transfers between devices, shards(): lax.ppermute(head_rows, 'gx', [(i + 1, i) for i in range(count_x - 1)])  6.65 us
    ppermute x1, starting transfers between devices, with_halo(): lax.ppermute(head, axis, [((i + 1) % count, i) for i in range(ends)])  6.62 us
    ppermute x2, waiting for transfers between devices, front_exchange(): tail = lax.ppermute(tail, axis, [(i, (i + 1) % count) for i in range(ends)])  5.86 us
    ppermute x1, starting transfers between devices, shards(): lax.ppermute(tail_rows, 'gx', [(i, i + 1) for i in range(count_x - 1)])  5.43 us
  transfers between devices with their start and end apart: 17, of which 13 were waited for; matrix products, arithmetic and copies ran while one was open for 2% of the time, Pallas kernels for 4%

profile of v12, /device:TPU:6, one launch (start us, length us, event | category | flops | bytes accessed | tf_op | source)
XLA Modules:
  0.0 134.6 jit_solution(16110024518499903266)
XLA Ops:
  3.0 1.3 collective-permute-start
  4.3 3.0 %collective-permute-start.1 = (f32[2,8,128]{2,1,0:T(8,128)S(1)}, f32[2,8,128]{2,1,0:T(8,128)S(1)}, u32[]{:S(2)}, u32[]{:S(2)}) collective-permute-start(f32[2,8,128]{2,1,0:T(8,128)S(1)} %get-tuple-element.30), channel_id=1, source_target_pairs={{0,16},{16,32},{32,48},{48,64},{64,80},{80,96},{96,112},{112,128},... | collective-permute-start | bytes 24584 | tf_op jit(solution)/shard_map/ppermute | solution.py:52
  7.4 2.2 %broadcast_multiply_fusion.refs_0_ = f32[4,2,3,8,8,128]{5,4,3,2,1,0:T(8,128)} fusion(f32[4,2,3,8,8,128]{5,4,3,2,1,0:T(8,128)} %param.9, f32[8,8,128]{2,1,0:T(8,128)S(1)} %subtract_convert_fusion), kind=kLoop, calls=%fused_computation.24 | loop fusion | flops 196608 | bytes 1605632 | tf_op jit(solution)/shard_map/mul | solution.py:329
  10.6 5.8 %collective-permute-start.2 = (f32[240,128]{1,0:T(8,128)S(1)}, f32[240,128]{1,0:T(8,128)S(1)}, u32[]{:S(2)}, u32[]{:S(2)}) collective-permute-start(f32[240,128]{1,0:T(8,128)S(1)} %pad_maximum_fusion.1), channel_id=1, source_target_pairs={{1,0},{2,1},{3,2},{4,3},{5,4},{6,5},{7,6},{8,7},{9,8},{10,9},{11,1... | collective-permute-start | bytes 368648 | tf_op jit(solution)/shard_map/ppermute | solution.py:48
  16.4 1.9 %collective-permute-start.3 = (f32[12,2,128]{2,1,0:T(2,128)S(1)}, f32[12,2,128]{2,1,0:T(2,128)S(1)}, u32[]{:S(2)}, u32[]{:S(2)}) collective-permute-start(f32[12,2,128]{2,1,0:T(2,128)S(1)} %get-tuple-element.19), channel_id=1, source_target_pairs={{0,1},{1,2},{2,3},{3,4},{4,5},{5,6},{6,7},{7,8},{8,9},{9,10},{10,1... | collective-permute-start | bytes 36872 | tf_op jit(solution)/shard_map/ppermute | solution.py:52
  18.8 5.9 %collective-permute-done.3 = f32[12,2,128]{2,1,0:T(2,128)S(1)} collective-permute-done((f32[12,2,128]{2,1,0:T(2,128)S(1)}, f32[12,2,128]{2,1,0:T(2,128)S(1)}, u32[]{:S(2)}, u32[]{:S(2)}) %collective-permute-start.3) | collective-permute-done | bytes 12320 | tf_op jit(solution)/shard_map/ppermute | solution.py:52
  24.9 1.2 fusion.248
  28.0 4.7 %shard_map.86 = (f32[4,8,128]{2,1,0:T(8,128)}, f32[4,8,128]{2,1,0:T(8,128)}, f32[4,8,128]{2,1,0:T(8,128)}) custom-call(f32[4,2,3,8,8,128]{5,4,3,2,1,0:T(8,128)} %broadcast_multiply_fusion.refs_0_, f32[4,2,3,1,8,128]{5,4,3,2,1,0:T(8,128)} %bitcast.75, f32[4,2,3,9,1,128]{5,4,3,2,1,0:T(1,128)} %bitcast.79, f32[24,24]{1,0:T(8,128)} %refs_3_.3, ...), custom_call_target="tpu_custom_call" | custom-call | flops 303562752 | bytes 535040 | tf_op jit(solution)/shard_map/pallas_call | solution.py:293
  33.5 5.4 %collective-permute-start.4 = (f32[2,8,128]{2,1,0:T(8,128)S(1)}, f32[2,8,128]{2,1,0:T(8,128)S(1)}, u32[]{:S(2)}, u32[]{:S(2)}) collective-permute-start(f32[2,8,128]{2,1,0:T(8,128)S(1)} %slice.1244), channel_id=1, source_target_pairs={{0,16},{16,32},{32,48},{48,64},{64,80},{80,96},{96,112},{112,128},... | collective-permute-start | bytes 24584 | tf_op jit(solution)/shard_map/ppermute | solution.py:359
  39.0 4.7 %shard_map.87 = (f32[4,8,128]{2,1,0:T(8,128)}, f32[4,8,128]{2,1,0:T(8,128)}) custom-call(f32[4,2,3,8,8,128]{5,4,3,2,1,0:T(8,128)} %broadcast_multiply_fusion.refs_0_, f32[4,2,3,1,8,128]{5,4,3,2,1,0:T(8,128)} %bitcast.76, f32[4,2,3,9,1,128]{5,4,3,2,1,0:T(1,128)} %bitcast.80, f32[24,24]{1,0:T(8,128)} %refs_3_.3, f32[24,24]{1,0:T(8,128)} %refs_4_.3), custom_call_target="tpu_custom_call" | custom-call | flops 303562752 | bytes 535040 | tf_op jit(solution)/shard_map/pallas_call | solution.py:293
  44.5 1.3 collective-permute-start.5
  45.8 6.6 %collective-permute-done.5 = f32[2,8,128]{2,1,0:T(8,128)S(1)} collective-permute-done((f32[2,8,128]{2,1,0:T(8,128)S(1)}, f32[2,8,128]{2,1,0:T(8,128)S(1)}, u32[]{:S(2)}, u32[]{:S(2)}) %collective-permute-start.5) | collective-permute-done | bytes 8224 | tf_op jit(solution)/shard_map/ppermute | solution.py:358
  52.4 1.9 %collective-permute-start.6 = (f32[12,2,128]{2,1,0:T(2,128)S(1)}, f32[12,2,128]{2,1,0:T(2,128)S(1)}, u32[]{:S(2)}, u32[]{:S(2)}) collective-permute-start(f32[12,2,128]{2,1,0:T(2,128)S(1)} %get-tuple-element.15), channel_id=1, source_target_pairs={{0,1},{1,2},{2,3},{3,4},{4,5},{5,6},{6,7},{7,8},{8,9},{9,10},{10,1... | collective-permute-start | bytes 36872 | tf_op jit(solution)/shard_map/ppermute | solution.py:28
  54.4 6.6 %collective-permute-start.7 = (f32[12,2,128]{2,1,0:T(2,128)S(1)}, f32[12,2,128]{2,1,0:T(2,128)S(1)}, u32[]{:S(2)}, u32[]{:S(2)}) collective-permute-start(f32[12,2,128]{2,1,0:T(2,128)S(1)} %get-tuple-element.16), channel_id=1, source_target_pairs={{1,0},{2,1},{3,2},{4,3},{5,4},{6,5},{7,6},{8,7},{9,8},{10,9},{11,1... | collective-permute-start | bytes 36872 | tf_op jit(solution)/shard_map/ppermute | solution.py:30
  61.1 1.2 collective-permute-done.7
  64.4 1.9 %collective-permute-start.8 = (f32[32,128]{1,0:T(8,128)S(1)}, f32[32,128]{1,0:T(8,128)S(1)}, u32[]{:S(2)}, u32[]{:S(2)}) collective-permute-start(f32[32,128]{1,0:T(8,128)S(1)} %pad_bitcast_fusion), channel_id=1, source_target_pairs={{0,1},{1,0},{2,3},{3,2},{4,5},{5,4},{6,7},{7,6},{8,9},{9,8},{10,11... | collective-permute-start | bytes 49160 | tf_op jit(solution)/shard_map/ppermute | solution.py:72
  66.4 3.7 %collective-permute-done.8 = f32[32,128]{1,0:T(8,128)S(1)} collective-permute-done((f32[32,128]{1,0:T(8,128)S(1)}, f32[32,128]{1,0:T(8,128)S(1)}, u32[]{:S(2)}, u32[]{:S(2)}) %collective-permute-start.8) | collective-permute-done | bytes 16416 | tf_op jit(solution)/shard_map/ppermute | solution.py:72
  70.1 1.9 %collective-permute-start.9 = (f32[32,128]{1,0:T(8,128)S(1)}, f32[32,128]{1,0:T(8,128)S(1)}, u32[]{:S(2)}, u32[]{:S(2)}) collective-permute-start(f32[32,128]{1,0:T(8,128)S(1)} %fusion.331), channel_id=1, source_target_pairs={{0,2},{1,3},{2,0},{3,1},{4,6},{5,7},{6,4},{7,5},{8,10},{9,11},{10,... | collective-permute-start | bytes 49160 | tf_op jit(solution)/shard_map/ppermute | solution.py:72
  72.0 4.6 %collective-permute-done.9 = f32[32,128]{1,0:T(8,128)S(1)} collective-permute-done((f32[32,128]{1,0:T(8,128)S(1)}, f32[32,128]{1,0:T(8,128)S(1)}, u32[]{:S(2)}, u32[]{:S(2)}) %collective-permute-start.9) | collective-permute-done | bytes 16416 | tf_op jit(solution)/shard_map/ppermute | solution.py:72
  76.6 3.1 %collective-permute-start.10 = (f32[32,128]{1,0:T(8,128)S(1)}, f32[32,128]{1,0:T(8,128)S(1)}, u32[]{:S(2)}, u32[]{:S(2)}) collective-permute-start(f32[32,128]{1,0:T(8,128)S(1)} %fusion.341), channel_id=1, source_target_pairs={{0,4},{1,5},{2,6},{3,7},{4,0},{5,1},{6,2},{7,3},{8,12},{9,13},{10,... | collective-permute-start | bytes 49160 | tf_op jit(solution)/shard_map/ppermute | solution.py:72
  79.7 2.5 %collective-permute-done.10 = f32[32,128]{1,0:T(8,128)S(1)} collective-permute-done((f32[32,128]{1,0:T(8,128)S(1)}, f32[32,128]{1,0:T(8,128)S(1)}, u32[]{:S(2)}, u32[]{:S(2)}) %collective-permute-start.10) | collective-permute-done | bytes 16416 | tf_op jit(solution)/shard_map/ppermute | solution.py:72
  82.2 3.7 %collective-permute-start.11 = (f32[32,128]{1,0:T(8,128)S(1)}, f32[32,128]{1,0:T(8,128)S(1)}, u32[]{:S(2)}, u32[]{:S(2)}) collective-permute-start(f32[32,128]{1,0:T(8,128)S(1)} %add.1202), channel_id=1, source_target_pairs={{0,8},{1,9},{2,10},{3,11},{4,12},{5,13},{6,14},{7,15},{8,0},{9,1},... | collective-permute-start | bytes 49160 | tf_op jit(solution)/shard_map/ppermute | solution.py:72
  85.9 3.5 %collective-permute-done.11 = f32[32,128]{1,0:T(8,128)S(1)} collective-permute-done((f32[32,128]{1,0:T(8,128)S(1)}, f32[32,128]{1,0:T(8,128)S(1)}, u32[]{:S(2)}, u32[]{:S(2)}) %collective-permute-start.11) | collective-permute-done | bytes 16416 | tf_op jit(solution)/shard_map/ppermute | solution.py:72
  89.4 2.5 %collective-permute-start.12 = (f32[32,128]{1,0:T(8,128)S(1)}, f32[32,128]{1,0:T(8,128)S(1)}, u32[]{:S(2)}, u32[]{:S(2)}) collective-permute-start(f32[32,128]{1,0:T(8,128)S(1)} %add.1203), channel_id=1, source_target_pairs={{0,16},{16,0},{32,48},{48,32},{64,80},{80,64},{96,112},{112,96},{1... | collective-permute-start | bytes 49160 | tf_op jit(solution)/shard_map/ppermute | solution.py:72
  92.7 7.9 %collective-permute-start.13 = (f32[32,128]{1,0:T(8,128)S(1)}, f32[32,128]{1,0:T(8,128)S(1)}, u32[]{:S(2)}, u32[]{:S(2)}) collective-permute-start(f32[32,128]{1,0:T(8,128)S(1)} %add.1204), channel_id=1, source_target_pairs={{0,32},{16,48},{32,0},{48,16},{64,96},{80,112},{96,64},{112,80},{1... | collective-permute-start | bytes 49160 | tf_op jit(solution)/shard_map/ppermute | solution.py:72
  100.6 1.7 %collective-permute-done.13 = f32[32,128]{1,0:T(8,128)S(1)} collective-permute-done((f32[32,128]{1,0:T(8,128)S(1)}, f32[32,128]{1,0:T(8,128)S(1)}, u32[]{:S(2)}, u32[]{:S(2)}) %collective-permute-start.13) | collective-permute-done | bytes 16416 | tf_op jit(solution)/shard_map/ppermute | solution.py:72
  102.3 8.2 %collective-permute-start.14 = (f32[32,128]{1,0:T(8,128)S(1)}, f32[32,128]{1,0:T(8,128)S(1)}, u32[]{:S(2)}, u32[]{:S(2)}) collective-permute-start(f32[32,128]{1,0:T(8,128)S(1)} %add.1205), channel_id=1, source_target_pairs={{0,64},{16,80},{32,96},{48,112},{64,0},{80,16},{96,32},{112,48},{1... | collective-permute-start | bytes 49160 | tf_op jit(solution)/shard_map/ppermute | solution.py:72
  110.5 1.7 %collective-permute-done.14 = f32[32,128]{1,0:T(8,128)S(1)} collective-permute-done((f32[32,128]{1,0:T(8,128)S(1)}, f32[32,128]{1,0:T(8,128)S(1)}, u32[]{:S(2)}, u32[]{:S(2)}) %collective-permute-start.14) | collective-permute-done | bytes 16416 | tf_op jit(solution)/shard_map/ppermute | solution.py:72
  112.2 6.1 %collective-permute-start.15 = (f32[32,128]{1,0:T(8,128)S(1)}, f32[32,128]{1,0:T(8,128)S(1)}, u32[]{:S(2)}, u32[]{:S(2)}) collective-permute-start(f32[32,128]{1,0:T(8,128)S(1)} %add.1206), channel_id=1, source_target_pairs={{0,128},{16,144},{32,160},{48,176},{64,192},{80,208},{96,224},{112... | collective-permute-start | bytes 49160 | tf_op jit(solution)/shard_map/ppermute | solution.py:72
  118.3 1.7 %collective-permute-done.15 = f32[32,128]{1,0:T(8,128)S(1)} collective-permute-done((f32[32,128]{1,0:T(8,128)S(1)}, f32[32,128]{1,0:T(8,128)S(1)}, u32[]{:S(2)}, u32[]{:S(2)}) %collective-permute-start.15) | collective-permute-done | bytes 16416 | tf_op jit(solution)/shard_map/ppermute | solution.py:72
  120.0 11.6 %collective-permute-start.16 = (f32[32,128]{1,0:T(8,128)S(1)}, f32[32,128]{1,0:T(8,128)S(1)}, u32[]{:S(2)}, u32[]{:S(2)}) collective-permute-start(f32[32,128]{1,0:T(8,128)S(1)} %add.1207), channel_id=1, source_target_pairs={{0,256},{16,272},{32,288},{48,304},{64,320},{80,336},{96,352},{112... | collective-permute-start | bytes 49160 | tf_op jit(solution)/shard_map/ppermute | solution.py:72
  131.7 1.7 %collective-permute-done.16 = f32[32,128]{1,0:T(8,128)S(1)} collective-permute-done((f32[32,128]{1,0:T(8,128)S(1)}, f32[32,128]{1,0:T(8,128)S(1)}, u32[]{:S(2)}, u32[]{:S(2)}) %collective-permute-start.16) | collective-permute-done | bytes 16416 | tf_op jit(solution)/shard_map/ppermute | solution.py:72
  (96 shorter events, 11.6 us)
Async XLA Ops:
  3.0 7.5 %collective-permute-start = (f32[208,128]{1,0:T(8,128)S(1)}, f32[208,128]{1,0:T(8,128)S(1)}, u32[]{:S(2)}, u32[]{:S(2)}) collective-permute-start(f32[208,128]{1,0:T(8,128)S(1)} %pad_maximum_fusion.2), channel_id=1, source_target_pairs={{16,0},{32,16},{48,32},{64,48},{80,64},{96,80},{112,96},{128,112},... | collective-permute-start | bytes 319496 | tf_op jit(solution)/shard_map/ppermute | solution.py:48
  4.3 6.2 %collective-permute-start.1 = (f32[2,8,128]{2,1,0:T(8,128)S(1)}, f32[2,8,128]{2,1,0:T(8,128)S(1)}, u32[]{:S(2)}, u32[]{:S(2)}) collective-permute-start(f32[2,8,128]{2,1,0:T(8,128)S(1)} %get-tuple-element.30), channel_id=1, source_target_pairs={{0,16},{16,32},{32,48},{48,64},{64,80},{80,96},{96,112},{112,128},... | collective-permute-start | bytes 24584 | tf_op jit(solution)/shard_map/ppermute | solution.py:52
  7.4 2.2 %copy-start.1 = (s32[8,8,128]{2,1,0:T(8,128)S(1)}, s32[8,8,128]{2,1,0:T(8,128)}, u32[]{:S(2)}) copy-start(s32[8,8,128]{2,1,0:T(8,128)} %param.8) | copy-start | bytes 98308
  7.4 2.2 %slice-start = ((f32[4,2,3,8,8,128]{5,4,3,2,1,0:T(8,128)}), f32[4,2,3,8,1,128]{5,4,3,2,1,0:T(1,128)S(1)}, s32[]{:S(2)}) async-start(f32[4,2,3,8,8,128]{5,4,3,2,1,0:T(8,128)} %param.9), calls=%async_computation | async-start | bytes 196608 | tf_op jit(solution)/shard_map/slice | solution.py:57
  9.6 1.0 copy-start
  10.5 14.4 %copy-start.3 = (f32[192,128]{1,0:T(8,128)}, f32[192,128]{1,0:T(8,128)S(1)}, u32[]{:S(2)}) copy-start(f32[192,128]{1,0:T(8,128)S(1)} %slice.1350) | copy-start | bytes 294916
  10.6 8.2 %collective-permute-start.2 = (f32[240,128]{1,0:T(8,128)S(1)}, f32[240,128]{1,0:T(8,128)S(1)}, u32[]{:S(2)}, u32[]{:S(2)}) collective-permute-start(f32[240,128]{1,0:T(8,128)S(1)} %pad_maximum_fusion.1), channel_id=1, source_target_pairs={{1,0},{2,1},{3,2},{4,3},{5,4},{6,5},{7,6},{8,7},{9,8},{10,9},{11,1... | collective-permute-start | bytes 368648 | tf_op jit(solution)/shard_map/ppermute | solution.py:48
  16.4 8.3 %collective-permute-start.3 = (f32[12,2,128]{2,1,0:T(2,128)S(1)}, f32[12,2,128]{2,1,0:T(2,128)S(1)}, u32[]{:S(2)}, u32[]{:S(2)}) collective-permute-start(f32[12,2,128]{2,1,0:T(2,128)S(1)} %get-tuple-element.19), channel_id=1, source_target_pairs={{0,1},{1,2},{2,3},{3,4},{4,5},{5,6},{6,7},{7,8},{8,9},{9,10},{10,1... | collective-permute-start | bytes 36872 | tf_op jit(solution)/shard_map/ppermute | solution.py:52
  32.7 10.9 %copy-start.4 = (f32[4,8,128]{2,1,0:T(8,128)S(1)}, f32[4,8,128]{2,1,0:T(8,128)}, u32[]{:S(2)}) copy-start(f32[4,8,128]{2,1,0:T(8,128)} %get-tuple-element.5) | copy-start | bytes 49156
  32.7 28.2 %copy-start.5 = (f32[63,64]{0,1:T(8,128)S(1)}, f32[63,64]{0,1:T(8,128)}, u32[]{:S(2)}) copy-start(f32[63,64]{0,1:T(8,128)} %constant.24.clone.1) | copy-start | bytes 48388
  33.5 10.2 %collective-permute-start.4 = (f32[2,8,128]{2,1,0:T(8,128)S(1)}, f32[2,8,128]{2,1,0:T(8,128)S(1)}, u32[]{:S(2)}, u32[]{:S(2)}) collective-permute-start(f32[2,8,128]{2,1,0:T(8,128)S(1)} %slice.1244), channel_id=1, source_target_pairs={{0,16},{16,32},{32,48},{48,64},{64,80},{80,96},{96,112},{112,128},... | collective-permute-start | bytes 24584 | tf_op jit(solution)/shard_map/ppermute | solution.py:359
  44.5 7.9 %collective-permute-start.5 = (f32[2,8,128]{2,1,0:T(8,128)S(1)}, f32[2,8,128]{2,1,0:T(8,128)S(1)}, u32[]{:S(2)}, u32[]{:S(2)}) collective-permute-start(f32[2,8,128]{2,1,0:T(8,128)S(1)} %get-tuple-element.32), channel_id=1, source_target_pairs={{16,0},{32,16},{48,32},{64,48},{80,64},{96,80},{112,96},{128,112},... | collective-permute-start | bytes 24584 | tf_op jit(solution)/shard_map/ppermute | solution.py:358
  52.4 8.7 %collective-permute-start.6 = (f32[12,2,128]{2,1,0:T(2,128)S(1)}, f32[12,2,128]{2,1,0:T(2,128)S(1)}, u32[]{:S(2)}, u32[]{:S(2)}) collective-permute-start(f32[12,2,128]{2,1,0:T(2,128)S(1)} %get-tuple-element.15), channel_id=1, source_target_pairs={{0,1},{1,2},{2,3},{3,4},{4,5},{5,6},{6,7},{7,8},{8,9},{9,10},{10,1... | collective-permute-start | bytes 36872 | tf_op jit(solution)/shard_map/ppermute | solution.py:28
  54.4 8.0 %collective-permute-start.7 = (f32[12,2,128]{2,1,0:T(2,128)S(1)}, f32[12,2,128]{2,1,0:T(2,128)S(1)}, u32[]{:S(2)}, u32[]{:S(2)}) collective-permute-start(f32[12,2,128]{2,1,0:T(2,128)S(1)} %get-tuple-element.16), channel_id=1, source_target_pairs={{1,0},{2,1},{3,2},{4,3},{5,4},{6,5},{7,6},{8,7},{9,8},{10,9},{11,1... | collective-permute-start | bytes 36872 | tf_op jit(solution)/shard_map/ppermute | solution.py:30
  63.1 70.8 %copy-start.2 = (f32[8,8,128]{2,1,0:T(8,128)}, f32[8,8,128]{2,1,0:T(8,128)S(1)}, u32[]{:S(2)}) copy-start(f32[8,8,128]{2,1,0:T(8,128)S(1)} %get-tuple-element.9) | copy-start | bytes 98308
  63.1 68.6 %copy-start.6 = (f32[64]{0:T(128)S(1)}, f32[64]{0:T(128)}, u32[]{:S(2)}) copy-start(f32[64]{0:T(128)} %param.13) | copy-start | bytes 772
  64.4 5.6 %collective-permute-start.8 = (f32[32,128]{1,0:T(8,128)S(1)}, f32[32,128]{1,0:T(8,128)S(1)}, u32[]{:S(2)}, u32[]{:S(2)}) collective-permute-start(f32[32,128]{1,0:T(8,128)S(1)} %pad_bitcast_fusion), channel_id=1, source_target_pairs={{0,1},{1,0},{2,3},{3,2},{4,5},{5,4},{6,7},{7,6},{8,9},{9,8},{10,11... | collective-permute-start | bytes 49160 | tf_op jit(solution)/shard_map/ppermute | solution.py:72
  70.1 6.5 %collective-permute-start.9 = (f32[32,128]{1,0:T(8,128)S(1)}, f32[32,128]{1,0:T(8,128)S(1)}, u32[]{:S(2)}, u32[]{:S(2)}) collective-permute-start(f32[32,128]{1,0:T(8,128)S(1)} %fusion.331), channel_id=1, source_target_pairs={{0,2},{1,3},{2,0},{3,1},{4,6},{5,7},{6,4},{7,5},{8,10},{9,11},{10,... | collective-permute-start | bytes 49160 | tf_op jit(solution)/shard_map/ppermute | solution.py:72
  76.6 5.6 %collective-permute-start.10 = (f32[32,128]{1,0:T(8,128)S(1)}, f32[32,128]{1,0:T(8,128)S(1)}, u32[]{:S(2)}, u32[]{:S(2)}) collective-permute-start(f32[32,128]{1,0:T(8,128)S(1)} %fusion.341), channel_id=1, source_target_pairs={{0,4},{1,5},{2,6},{3,7},{4,0},{5,1},{6,2},{7,3},{8,12},{9,13},{10,... | collective-permute-start | bytes 49160 | tf_op jit(solution)/shard_map/ppermute | solution.py:72
  82.2 7.1 %collective-permute-start.11 = (f32[32,128]{1,0:T(8,128)S(1)}, f32[32,128]{1,0:T(8,128)S(1)}, u32[]{:S(2)}, u32[]{:S(2)}) collective-permute-start(f32[32,128]{1,0:T(8,128)S(1)} %add.1202), channel_id=1, source_target_pairs={{0,8},{1,9},{2,10},{3,11},{4,12},{5,13},{6,14},{7,15},{8,0},{9,1},... | collective-permute-start | bytes 49160 | tf_op jit(solution)/shard_map/ppermute | solution.py:72
  89.4 3.3 %collective-permute-start.12 = (f32[32,128]{1,0:T(8,128)S(1)}, f32[32,128]{1,0:T(8,128)S(1)}, u32[]{:S(2)}, u32[]{:S(2)}) collective-permute-start(f32[32,128]{1,0:T(8,128)S(1)} %add.1203), channel_id=1, source_target_pairs={{0,16},{16,0},{32,48},{48,32},{64,80},{80,64},{96,112},{112,96},{1... | collective-permute-start | bytes 49160 | tf_op jit(solution)/shard_map/ppermute | solution.py:72
  92.7 9.6 %collective-permute-start.13 = (f32[32,128]{1,0:T(8,128)S(1)}, f32[32,128]{1,0:T(8,128)S(1)}, u32[]{:S(2)}, u32[]{:S(2)}) collective-permute-start(f32[32,128]{1,0:T(8,128)S(1)} %add.1204), channel_id=1, source_target_pairs={{0,32},{16,48},{32,0},{48,16},{64,96},{80,112},{96,64},{112,80},{1... | collective-permute-start | bytes 49160 | tf_op jit(solution)/shard_map/ppermute | solution.py:72
  102.3 9.9 %collective-permute-start.14 = (f32[32,128]{1,0:T(8,128)S(1)}, f32[32,128]{1,0:T(8,128)S(1)}, u32[]{:S(2)}, u32[]{:S(2)}) collective-permute-start(f32[32,128]{1,0:T(8,128)S(1)} %add.1205), channel_id=1, source_target_pairs={{0,64},{16,80},{32,96},{48,112},{64,0},{80,16},{96,32},{112,48},{1... | collective-permute-start | bytes 49160 | tf_op jit(solution)/shard_map/ppermute | solution.py:72
  112.2 7.8 %collective-permute-start.15 = (f32[32,128]{1,0:T(8,128)S(1)}, f32[32,128]{1,0:T(8,128)S(1)}, u32[]{:S(2)}, u32[]{:S(2)}) collective-permute-start(f32[32,128]{1,0:T(8,128)S(1)} %add.1206), channel_id=1, source_target_pairs={{0,128},{16,144},{32,160},{48,176},{64,192},{80,208},{96,224},{112... | collective-permute-start | bytes 49160 | tf_op jit(solution)/shard_map/ppermute | solution.py:72
  120.0 13.4 %collective-permute-start.16 = (f32[32,128]{1,0:T(8,128)S(1)}, f32[32,128]{1,0:T(8,128)S(1)}, u32[]{:S(2)}, u32[]{:S(2)}) collective-permute-start(f32[32,128]{1,0:T(8,128)S(1)} %add.1207), channel_id=1, source_target_pairs={{0,256},{16,272},{32,288},{48,304},{64,320},{80,336},{96,352},{112... | collective-permute-start | bytes 49160 | tf_op jit(solution)/shard_map/ppermute | solution.py:72

commit v13 on v11

--- a/solution.py
+++ b/solution.py
@@ -365,7 +365,7 @@
         flat = partial_volumes.reshape(-1)
         spare = -flat.size % lanes
         dense = jnp.pad(flat, (0, spare)).reshape(-1, lanes)
-        dense = butterfly_sum(butterfly_sum(dense, "gy"), "gx")
+        dense = butterfly_sum(butterfly_sum(dense, "gx"), "gy")
         volumes = dense.reshape(-1)[: flat.size].reshape(partial_volumes.shape)
         heavier_all = volumes > target[None, :]
         position = jnp.zeros((REGIONS,), jnp.int32)

time: 128 us -> 128 us (level)
  no operation moved by 1% of the time
where the time goes in v13:
time: 128 us; the launch traced here: 125 us
  starting transfers between devices  82.6 us (65%)
  waiting for transfers between devices  24.5 us (19%)
  other arithmetic  8.9 us (7%)
  Pallas kernels  5.92 us (5%)
  local copies, waits for them, and re-layouts  2.53 us (2%)
    ppermute x9, starting transfers between devices, butterfly_sum(): lax.ppermute(value, axis, [(i, i ^ stride) for i in range(count)])  53.7 us
    ppermute x9, waiting for transfers between devices, butterfly_sum(): lax.ppermute(value, axis, [(i, i ^ stride) for i in range(count)])  21.9 us
    ppermute x2, starting transfers between devices, with_halo(): lax.ppermute(tail, axis, [(i, (i + 1) % count) for i in range(ends)])  8.65 us
    ppermute x2, starting transfers between devices, with_halo(): lax.ppermute(head, axis, [((i + 1) % count, i) for i in range(ends)])  8.09 us
    ppermute x2, starting transfers between devices, front_exchange(): lax.ppermute(packed, axis, [((i + 1) % count, i) for i in range(ends)])  7.07 us
    pallas_call x1, Pallas kernels, element_energies(): pl.pallas_call(mxu_energy_kernel, out_shape=(jax.ShapeDtypeStruct(cells,...  5.92 us
    ppermute x2, starting transfers between devices, front_exchange(): tail = lax.ppermute(tail, axis, [(i, (i + 1) % count) for i in range(ends)])  5.08 us
  transfers between devices with their start and end apart: 17, of which 12 were waited for; matrix products, arithmetic and copies ran while one was open for 3% of the time, Pallas kernels for 5%

profile of v13, /device:TPU:6, one launch (start us, length us, event | category | flops | bytes accessed | tf_op | source)
XLA Modules:
  0.0 125.5 jit_solution(13790391452082480945)
XLA Ops:
  2.1 0.9 slice_multiply_fusion
  3.0 1.3 %collective-permute-start.1 = (f32[208,128]{1,0:T(8,128)S(1)}, f32[208,128]{1,0:T(8,128)S(1)}, u32[]{:S(2)}, u32[]{:S(2)}) collective-permute-start(f32[208,128]{1,0:T(8,128)S(1)} %pad_maximum_fusion.2), channel_id=1, source_target_pairs={{16,0},{32,16},{48,32},{64,48},{80,64},{96,80},{112,96},{128,112},... | collective-permute-start | bytes 319496 | tf_op jit(solution)/shard_map/ppermute | solution.py:47
  4.3 3.2 %collective-permute-start = (f32[2,8,128]{2,1,0:T(8,128)S(1)}, f32[2,8,128]{2,1,0:T(8,128)S(1)}, u32[]{:S(2)}, u32[]{:S(2)}) collective-permute-start(f32[2,8,128]{2,1,0:T(8,128)S(1)} %get-tuple-element.23), channel_id=1, source_target_pairs={{0,16},{16,32},{32,48},{48,64},{64,80},{80,96},{96,112},{112,128},... | collective-permute-start | bytes 24584 | tf_op jit(solution)/shard_map/ppermute | solution.py:51
  7.5 2.1 %broadcast_multiply_fusion.fields_ref = f32[4,2,3,8,8,128]{5,4,3,2,1,0:T(8,128)} fusion(f32[4,2,3,8,8,128]{5,4,3,2,1,0:T(8,128)} %param.9, f32[8,8,128]{2,1,0:T(8,128)S(1)} %subtract_convert_fusion), kind=kLoop, calls=%fused_computation.6 | loop fusion | flops 196608 | bytes 1605632 | tf_op jit(solution)/shard_map/mul | solution.py:315
  10.4 5.8 %collective-permute-start.3 = (f32[240,128]{1,0:T(8,128)S(1)}, f32[240,128]{1,0:T(8,128)S(1)}, u32[]{:S(2)}, u32[]{:S(2)}) collective-permute-start(f32[240,128]{1,0:T(8,128)S(1)} %pad_maximum_fusion.1), channel_id=1, source_target_pairs={{1,0},{2,1},{3,2},{4,3},{5,4},{6,5},{7,6},{8,7},{9,8},{10,9},{11,1... | collective-permute-start | bytes 368648 | tf_op jit(solution)/shard_map/ppermute | solution.py:47
  16.2 1.9 %collective-permute-start.2 = (f32[12,2,128]{2,1,0:T(2,128)S(1)}, f32[12,2,128]{2,1,0:T(2,128)S(1)}, u32[]{:S(2)}, u32[]{:S(2)}) collective-permute-start(f32[12,2,128]{2,1,0:T(2,128)S(1)} %get-tuple-element.16), channel_id=1, source_target_pairs={{0,1},{1,2},{2,3},{3,4},{4,5},{5,6},{6,7},{7,8},{8,9},{9,10},{10,1... | collective-permute-start | bytes 36872 | tf_op jit(solution)/shard_map/ppermute | solution.py:51
  19.3 5.9 %shard_map.86 = (f32[8,8,128]{2,1,0:T(8,128)}, f32[8,8,128]{2,1,0:T(8,128)}) custom-call(f32[4,2,3,8,8,128]{5,4,3,2,1,0:T(8,128)} %broadcast_multiply_fusion.fields_ref, f32[4,2,3,1,8,128]{5,4,3,2,1,0:T(8,128)} %bitcast.75, f32[4,2,3,9,1,128]{5,4,3,2,1,0:T(1,128)} %bitcast.78, f32[24,24]{1,0:T(8,128)} %stiffness_ref.1, f32[24,24]{1,0:T(8,128)} %mass_ref.1), custom_call_target="tpu_custom_call" | custom-call | flops 607125504 | bytes 1065472 | tf_op jit(solution)/shard_map/pallas_call | solution.py:277
  25.5 2.0 %fusion.82 = (f32[8,8,128]{2,1,0:T(8,128)S(1)}, pred[8,8,128]{2,1,0:T(8,128)(4,1)S(1)}) fusion(f32[8,8,128]{2,1,0:T(8,128)} %get-tuple-element.4, f32[12,10,128]{2,1,0:T(8,128)S(1)} %get-tuple-element.15, f32[12,12,132]{2,1,0:T(8,128)S(1)} %select_maximum_fusion.4, f32[2,8,128]{2,1,0:T(8,128)S(1)} %slice_bitcast_fusion.1, f32[8,8,128]{2,1,0:T(8,128)S(1)} %copy-done, ...), kind=kLoop, calls=%fused_computation.111 | loop fusion | flops 3039232 | bytes 6176768 | tf_op jit(solution)/shard_map/div | solution.py:324
  27.5 1.3 %collective-permute-start.5 = (f32[2,8,128]{2,1,0:T(8,128)S(1)}, f32[2,8,128]{2,1,0:T(8,128)S(1)}, u32[]{:S(2)}, u32[]{:S(2)}) collective-permute-start(f32[2,8,128]{2,1,0:T(8,128)S(1)} %get-tuple-element.22), channel_id=1, source_target_pairs={{16,0},{32,16},{48,32},{64,48},{80,64},{96,80},{112,96},{128,112},... | collective-permute-start | bytes 24584 | tf_op jit(solution)/shard_map/ppermute | solution.py:29
  28.8 6.7 %collective-permute-start.4 = (f32[2,8,128]{2,1,0:T(8,128)S(1)}, f32[2,8,128]{2,1,0:T(8,128)S(1)}, u32[]{:S(2)}, u32[]{:S(2)}) collective-permute-start(f32[2,8,128]{2,1,0:T(8,128)S(1)} %get-tuple-element.21), channel_id=1, source_target_pairs={{0,16},{16,32},{32,48},{48,64},{64,80},{80,96},{96,112},{112,128},... | collective-permute-start | bytes 24584 | tf_op jit(solution)/shard_map/ppermute | solution.py:27
  36.4 1.9 %collective-permute-start.6 = (f32[12,2,128]{2,1,0:T(2,128)S(1)}, f32[12,2,128]{2,1,0:T(2,128)S(1)}, u32[]{:S(2)}, u32[]{:S(2)}) collective-permute-start(f32[12,2,128]{2,1,0:T(2,128)S(1)} %get-tuple-element.12), channel_id=1, source_target_pairs={{0,1},{1,2},{2,3},{3,4},{4,5},{5,6},{6,7},{7,8},{8,9},{9,10},{10,1... | collective-permute-start | bytes 36872 | tf_op jit(solution)/shard_map/ppermute | solution.py:27
  38.3 6.8 %collective-permute-start.7 = (f32[12,2,128]{2,1,0:T(2,128)S(1)}, f32[12,2,128]{2,1,0:T(2,128)S(1)}, u32[]{:S(2)}, u32[]{:S(2)}) collective-permute-start(f32[12,2,128]{2,1,0:T(2,128)S(1)} %get-tuple-element.13), channel_id=1, source_target_pairs={{1,0},{2,1},{3,2},{4,3},{5,4},{6,5},{7,6},{8,7},{9,8},{10,9},{11,1... | collective-permute-start | bytes 36872 | tf_op jit(solution)/shard_map/ppermute | solution.py:29
  45.2 1.2 collective-permute-done.7
  47.2 0.9 fusion.4
  48.6 6.7 %collective-permute-start.8 = (f32[32,128]{1,0:T(8,128)S(1)}, f32[32,128]{1,0:T(8,128)S(1)}, u32[]{:S(2)}, u32[]{:S(2)}) collective-permute-start(f32[32,128]{1,0:T(8,128)S(1)} %pad_bitcast_fusion), channel_id=1, source_target_pairs={{0,16},{16,0},{32,48},{48,32},{64,80},{80,64},{96,112},{112,96},{1... | collective-permute-start | bytes 49160 | tf_op jit(solution)/shard_map/ppermute | solution.py:71
  55.2 0.8 collective-permute-done.8
  56.0 9.2 %collective-permute-start.9 = (f32[32,128]{1,0:T(8,128)S(1)}, f32[32,128]{1,0:T(8,128)S(1)}, u32[]{:S(2)}, u32[]{:S(2)}) collective-permute-start(f32[32,128]{1,0:T(8,128)S(1)} %fusion.293), channel_id=1, source_target_pairs={{0,32},{16,48},{32,0},{48,16},{64,96},{80,112},{96,64},{112,80},{1... | collective-permute-start | bytes 49160 | tf_op jit(solution)/shard_map/ppermute | solution.py:71
  65.2 1.7 %collective-permute-done.9 = f32[32,128]{1,0:T(8,128)S(1)} collective-permute-done((f32[32,128]{1,0:T(8,128)S(1)}, f32[32,128]{1,0:T(8,128)S(1)}, u32[]{:S(2)}, u32[]{:S(2)}) %collective-permute-start.9) | collective-permute-done | bytes 16416 | tf_op jit(solution)/shard_map/ppermute | solution.py:71
  66.9 9.1 %collective-permute-start.10 = (f32[32,128]{1,0:T(8,128)S(1)}, f32[32,128]{1,0:T(8,128)S(1)}, u32[]{:S(2)}, u32[]{:S(2)}) collective-permute-start(f32[32,128]{1,0:T(8,128)S(1)} %fusion.297), channel_id=1, source_target_pairs={{0,64},{16,80},{32,96},{48,112},{64,0},{80,16},{96,32},{112,48},{1... | collective-permute-start | bytes 49160 | tf_op jit(solution)/shard_map/ppermute | solution.py:71
  76.0 1.7 %collective-permute-done.10 = f32[32,128]{1,0:T(8,128)S(1)} collective-permute-done((f32[32,128]{1,0:T(8,128)S(1)}, f32[32,128]{1,0:T(8,128)S(1)}, u32[]{:S(2)}, u32[]{:S(2)}) %collective-permute-start.10) | collective-permute-done | bytes 16416 | tf_op jit(solution)/shard_map/ppermute | solution.py:71
  77.7 6.1 %collective-permute-start.11 = (f32[32,128]{1,0:T(8,128)S(1)}, f32[32,128]{1,0:T(8,128)S(1)}, u32[]{:S(2)}, u32[]{:S(2)}) collective-permute-start(f32[32,128]{1,0:T(8,128)S(1)} %add.1202), channel_id=1, source_target_pairs={{0,128},{16,144},{32,160},{48,176},{64,192},{80,208},{96,224},{112... | collective-permute-start | bytes 49160 | tf_op jit(solution)/shard_map/ppermute | solution.py:71
  83.8 1.7 %collective-permute-done.11 = f32[32,128]{1,0:T(8,128)S(1)} collective-permute-done((f32[32,128]{1,0:T(8,128)S(1)}, f32[32,128]{1,0:T(8,128)S(1)}, u32[]{:S(2)}, u32[]{:S(2)}) %collective-permute-start.11) | collective-permute-done | bytes 16416 | tf_op jit(solution)/shard_map/ppermute | solution.py:71
  85.5 12.2 %collective-permute-start.12 = (f32[32,128]{1,0:T(8,128)S(1)}, f32[32,128]{1,0:T(8,128)S(1)}, u32[]{:S(2)}, u32[]{:S(2)}) collective-permute-start(f32[32,128]{1,0:T(8,128)S(1)} %add.1203), channel_id=1, source_target_pairs={{0,256},{16,272},{32,288},{48,304},{64,320},{80,336},{96,352},{112... | collective-permute-start | bytes 49160 | tf_op jit(solution)/shard_map/ppermute | solution.py:71
  97.7 1.7 %collective-permute-done.12 = f32[32,128]{1,0:T(8,128)S(1)} collective-permute-done((f32[32,128]{1,0:T(8,128)S(1)}, f32[32,128]{1,0:T(8,128)S(1)}, u32[]{:S(2)}, u32[]{:S(2)}) %collective-permute-start.12) | collective-permute-done | bytes 16416 | tf_op jit(solution)/shard_map/ppermute | solution.py:71
  99.4 1.9 %collective-permute-start.13 = (f32[32,128]{1,0:T(8,128)S(1)}, f32[32,128]{1,0:T(8,128)S(1)}, u32[]{:S(2)}, u32[]{:S(2)}) collective-permute-start(f32[32,128]{1,0:T(8,128)S(1)} %add.1204), channel_id=1, source_target_pairs={{0,1},{1,0},{2,3},{3,2},{4,5},{5,4},{6,7},{7,6},{8,9},{9,8},{10,11... | collective-permute-start | bytes 49160 | tf_op jit(solution)/shard_map/ppermute | solution.py:71
  101.3 3.7 %collective-permute-done.13 = f32[32,128]{1,0:T(8,128)S(1)} collective-permute-done((f32[32,128]{1,0:T(8,128)S(1)}, f32[32,128]{1,0:T(8,128)S(1)}, u32[]{:S(2)}, u32[]{:S(2)}) %collective-permute-start.13) | collective-permute-done | bytes 16416 | tf_op jit(solution)/shard_map/ppermute | solution.py:71
  105.0 1.9 %collective-permute-start.14 = (f32[32,128]{1,0:T(8,128)S(1)}, f32[32,128]{1,0:T(8,128)S(1)}, u32[]{:S(2)}, u32[]{:S(2)}) collective-permute-start(f32[32,128]{1,0:T(8,128)S(1)} %add.1205), channel_id=1, source_target_pairs={{0,2},{1,3},{2,0},{3,1},{4,6},{5,7},{6,4},{7,5},{8,10},{9,11},{10,... | collective-permute-start | bytes 49160 | tf_op jit(solution)/shard_map/ppermute | solution.py:71
  106.9 4.6 %collective-permute-done.14 = f32[32,128]{1,0:T(8,128)S(1)} collective-permute-done((f32[32,128]{1,0:T(8,128)S(1)}, f32[32,128]{1,0:T(8,128)S(1)}, u32[]{:S(2)}, u32[]{:S(2)}) %collective-permute-start.14) | collective-permute-done | bytes 16416 | tf_op jit(solution)/shard_map/ppermute | solution.py:71
  111.5 3.1 %collective-permute-start.15 = (f32[32,128]{1,0:T(8,128)S(1)}, f32[32,128]{1,0:T(8,128)S(1)}, u32[]{:S(2)}, u32[]{:S(2)}) collective-permute-start(f32[32,128]{1,0:T(8,128)S(1)} %add.1206), channel_id=1, source_target_pairs={{0,4},{1,5},{2,6},{3,7},{4,0},{5,1},{6,2},{7,3},{8,12},{9,13},{10,... | collective-permute-start | bytes 49160 | tf_op jit(solution)/shard_map/ppermute | solution.py:71
  114.6 2.5 %collective-permute-done.15 = f32[32,128]{1,0:T(8,128)S(1)} collective-permute-done((f32[32,128]{1,0:T(8,128)S(1)}, f32[32,128]{1,0:T(8,128)S(1)}, u32[]{:S(2)}, u32[]{:S(2)}) %collective-permute-start.15) | collective-permute-done | bytes 16416 | tf_op jit(solution)/shard_map/ppermute | solution.py:71
  117.2 3.7 %collective-permute-start.16 = (f32[32,128]{1,0:T(8,128)S(1)}, f32[32,128]{1,0:T(8,128)S(1)}, u32[]{:S(2)}, u32[]{:S(2)}) collective-permute-start(f32[32,128]{1,0:T(8,128)S(1)} %add.1207), channel_id=1, source_target_pairs={{0,8},{1,9},{2,10},{3,11},{4,12},{5,13},{6,14},{7,15},{8,0},{9,1},... | collective-permute-start | bytes 49160 | tf_op jit(solution)/shard_map/ppermute | solution.py:71
  120.8 3.4 %collective-permute-done.16 = f32[32,128]{1,0:T(8,128)S(1)} collective-permute-done((f32[32,128]{1,0:T(8,128)S(1)}, f32[32,128]{1,0:T(8,128)S(1)}, u32[]{:S(2)}, u32[]{:S(2)}) %collective-permute-start.16) | collective-permute-done | bytes 16416 | tf_op jit(solution)/shard_map/ppermute | solution.py:71
  (83 shorter events, 6.8 us)
Async XLA Ops:
  3.0 6.9 %collective-permute-start.1 = (f32[208,128]{1,0:T(8,128)S(1)}, f32[208,128]{1,0:T(8,128)S(1)}, u32[]{:S(2)}, u32[]{:S(2)}) collective-permute-start(f32[208,128]{1,0:T(8,128)S(1)} %pad_maximum_fusion.2), channel_id=1, source_target_pairs={{16,0},{32,16},{48,32},{64,48},{80,64},{96,80},{112,96},{128,112},... | collective-permute-start | bytes 319496 | tf_op jit(solution)/shard_map/ppermute | solution.py:47
  4.3 5.6 %slice-start = ((f32[4,2,3,8,8,128]{5,4,3,2,1,0:T(8,128)}), f32[4,2,3,8,1,128]{5,4,3,2,1,0:T(1,128)S(1)}, s32[]{:S(2)}) async-start(f32[4,2,3,8,8,128]{5,4,3,2,1,0:T(8,128)} %param.9), calls=%async_computation | async-start | bytes 196608 | tf_op jit(solution)/shard_map/slice | solution.py:56
  4.3 5.6 %collective-permute-start = (f32[2,8,128]{2,1,0:T(8,128)S(1)}, f32[2,8,128]{2,1,0:T(8,128)S(1)}, u32[]{:S(2)}, u32[]{:S(2)}) collective-permute-start(f32[2,8,128]{2,1,0:T(8,128)S(1)} %get-tuple-element.23), channel_id=1, source_target_pairs={{0,16},{16,32},{32,48},{48,64},{64,80},{80,96},{96,112},{112,128},... | collective-permute-start | bytes 24584 | tf_op jit(solution)/shard_map/ppermute | solution.py:51
  9.6 0.8 copy-start
  10.0 9.4 %copy-start.2 = (f32[192,128]{1,0:T(8,128)}, f32[192,128]{1,0:T(8,128)S(1)}, u32[]{:S(2)}) copy-start(f32[192,128]{1,0:T(8,128)S(1)} %slice.1322) | copy-start | bytes 294916
  10.4 8.2 %collective-permute-start.3 = (f32[240,128]{1,0:T(8,128)S(1)}, f32[240,128]{1,0:T(8,128)S(1)}, u32[]{:S(2)}, u32[]{:S(2)}) collective-permute-start(f32[240,128]{1,0:T(8,128)S(1)} %pad_maximum_fusion.1), channel_id=1, source_target_pairs={{1,0},{2,1},{3,2},{4,3},{5,4},{6,5},{7,6},{8,7},{9,8},{10,9},{11,1... | collective-permute-start | bytes 368648 | tf_op jit(solution)/shard_map/ppermute | solution.py:47
  16.2 9.0 %collective-permute-start.2 = (f32[12,2,128]{2,1,0:T(2,128)S(1)}, f32[12,2,128]{2,1,0:T(2,128)S(1)}, u32[]{:S(2)}, u32[]{:S(2)}) collective-permute-start(f32[12,2,128]{2,1,0:T(2,128)S(1)} %get-tuple-element.16), channel_id=1, source_target_pairs={{0,1},{1,2},{2,3},{3,4},{4,5},{5,6},{6,7},{7,8},{8,9},{9,10},{10,1... | collective-permute-start | bytes 36872 | tf_op jit(solution)/shard_map/ppermute | solution.py:51
  19.3 6.1 %copy-start.3 = (s32[8,8,128]{2,1,0:T(8,128)S(1)}, s32[8,8,128]{2,1,0:T(8,128)}, u32[]{:S(2)}) copy-start(s32[8,8,128]{2,1,0:T(8,128)} %param.8) | copy-start | bytes 98308
  25.5 19.6 %copy-start.4 = (f32[63,64]{0,1:T(8,128)S(1)}, f32[63,64]{0,1:T(8,128)}, u32[]{:S(2)}) copy-start(f32[63,64]{0,1:T(8,128)} %constant.25.clone.1) | copy-start | bytes 48388
  27.5 8.0 %collective-permute-start.5 = (f32[2,8,128]{2,1,0:T(8,128)S(1)}, f32[2,8,128]{2,1,0:T(8,128)S(1)}, u32[]{:S(2)}, u32[]{:S(2)}) collective-permute-start(f32[2,8,128]{2,1,0:T(8,128)S(1)} %get-tuple-element.22), channel_id=1, source_target_pairs={{16,0},{32,16},{48,32},{64,48},{80,64},{96,80},{112,96},{128,112},... | collective-permute-start | bytes 24584 | tf_op jit(solution)/shard_map/ppermute | solution.py:29
  28.8 7.5 %collective-permute-start.4 = (f32[2,8,128]{2,1,0:T(8,128)S(1)}, f32[2,8,128]{2,1,0:T(8,128)S(1)}, u32[]{:S(2)}, u32[]{:S(2)}) collective-permute-start(f32[2,8,128]{2,1,0:T(8,128)S(1)} %get-tuple-element.21), channel_id=1, source_target_pairs={{0,16},{16,32},{32,48},{48,64},{64,80},{80,96},{96,112},{112,128},... | collective-permute-start | bytes 24584 | tf_op jit(solution)/shard_map/ppermute | solution.py:27
  36.4 8.9 %collective-permute-start.6 = (f32[12,2,128]{2,1,0:T(2,128)S(1)}, f32[12,2,128]{2,1,0:T(2,128)S(1)}, u32[]{:S(2)}, u32[]{:S(2)}) collective-permute-start(f32[12,2,128]{2,1,0:T(2,128)S(1)} %get-tuple-element.12), channel_id=1, source_target_pairs={{0,1},{1,2},{2,3},{3,4},{4,5},{5,6},{6,7},{7,8},{8,9},{9,10},{10,1... | collective-permute-start | bytes 36872 | tf_op jit(solution)/shard_map/ppermute | solution.py:27
  38.3 8.2 %collective-permute-start.7 = (f32[12,2,128]{2,1,0:T(2,128)S(1)}, f32[12,2,128]{2,1,0:T(2,128)S(1)}, u32[]{:S(2)}, u32[]{:S(2)}) collective-permute-start(f32[12,2,128]{2,1,0:T(2,128)S(1)} %get-tuple-element.13), channel_id=1, source_target_pairs={{1,0},{2,1},{3,2},{4,3},{5,4},{6,5},{7,6},{8,7},{9,8},{10,9},{11,1... | collective-permute-start | bytes 36872 | tf_op jit(solution)/shard_map/ppermute | solution.py:29
  47.2 77.6 %copy-start.1 = (f32[8,8,128]{2,1,0:T(8,128)}, f32[8,8,128]{2,1,0:T(8,128)S(1)}, u32[]{:S(2)}) copy-start(f32[8,8,128]{2,1,0:T(8,128)S(1)} %get-tuple-element.7) | copy-start | bytes 98308
  47.2 73.6 %copy-start.5 = (f32[64]{0:T(128)S(1)}, f32[64]{0:T(128)}, u32[]{:S(2)}) copy-start(f32[64]{0:T(128)} %param.13) | copy-start | bytes 772
  48.6 7.5 %collective-permute-start.8 = (f32[32,128]{1,0:T(8,128)S(1)}, f32[32,128]{1,0:T(8,128)S(1)}, u32[]{:S(2)}, u32[]{:S(2)}) collective-permute-start(f32[32,128]{1,0:T(8,128)S(1)} %pad_bitcast_fusion), channel_id=1, source_target_pairs={{0,16},{16,0},{32,48},{48,32},{64,80},{80,64},{96,112},{112,96},{1... | collective-permute-start | bytes 49160 | tf_op jit(solution)/shard_map/ppermute | solution.py:71
  56.0 10.9 %collective-permute-start.9 = (f32[32,128]{1,0:T(8,128)S(1)}, f32[32,128]{1,0:T(8,128)S(1)}, u32[]{:S(2)}, u32[]{:S(2)}) collective-permute-start(f32[32,128]{1,0:T(8,128)S(1)} %fusion.293), channel_id=1, source_target_pairs={{0,32},{16,48},{32,0},{48,16},{64,96},{80,112},{96,64},{112,80},{1... | collective-permute-start | bytes 49160 | tf_op jit(solution)/shard_map/ppermute | solution.py:71
  66.9 10.8 %collective-permute-start.10 = (f32[32,128]{1,0:T(8,128)S(1)}, f32[32,128]{1,0:T(8,128)S(1)}, u32[]{:S(2)}, u32[]{:S(2)}) collective-permute-start(f32[32,128]{1,0:T(8,128)S(1)} %fusion.297), channel_id=1, source_target_pairs={{0,64},{16,80},{32,96},{48,112},{64,0},{80,16},{96,32},{112,48},{1... | collective-permute-start | bytes 49160 | tf_op jit(solution)/shard_map/ppermute | solution.py:71
  77.7 7.8 %collective-permute-start.11 = (f32[32,128]{1,0:T(8,128)S(1)}, f32[32,128]{1,0:T(8,128)S(1)}, u32[]{:S(2)}, u32[]{:S(2)}) collective-permute-start(f32[32,128]{1,0:T(8,128)S(1)} %add.1202), channel_id=1, source_target_pairs={{0,128},{16,144},{32,160},{48,176},{64,192},{80,208},{96,224},{112... | collective-permute-start | bytes 49160 | tf_op jit(solution)/shard_map/ppermute | solution.py:71
  85.5 13.9 %collective-permute-start.12 = (f32[32,128]{1,0:T(8,128)S(1)}, f32[32,128]{1,0:T(8,128)S(1)}, u32[]{:S(2)}, u32[]{:S(2)}) collective-permute-start(f32[32,128]{1,0:T(8,128)S(1)} %add.1203), channel_id=1, source_target_pairs={{0,256},{16,272},{32,288},{48,304},{64,320},{80,336},{96,352},{112... | collective-permute-start | bytes 49160 | tf_op jit(solution)/shard_map/ppermute | solution.py:71
  99.4 5.6 %collective-permute-start.13 = (f32[32,128]{1,0:T(8,128)S(1)}, f32[32,128]{1,0:T(8,128)S(1)}, u32[]{:S(2)}, u32[]{:S(2)}) collective-permute-start(f32[32,128]{1,0:T(8,128)S(1)} %add.1204), channel_id=1, source_target_pairs={{0,1},{1,0},{2,3},{3,2},{4,5},{5,4},{6,7},{7,6},{8,9},{9,8},{10,11... | collective-permute-start | bytes 49160 | tf_op jit(solution)/shard_map/ppermute | solution.py:71
  105.0 6.5 %collective-permute-start.14 = (f32[32,128]{1,0:T(8,128)S(1)}, f32[32,128]{1,0:T(8,128)S(1)}, u32[]{:S(2)}, u32[]{:S(2)}) collective-permute-start(f32[32,128]{1,0:T(8,128)S(1)} %add.1205), channel_id=1, source_target_pairs={{0,2},{1,3},{2,0},{3,1},{4,6},{5,7},{6,4},{7,5},{8,10},{9,11},{10,... | collective-permute-start | bytes 49160 | tf_op jit(solution)/shard_map/ppermute | solution.py:71
  111.5 5.6 %collective-permute-start.15 = (f32[32,128]{1,0:T(8,128)S(1)}, f32[32,128]{1,0:T(8,128)S(1)}, u32[]{:S(2)}, u32[]{:S(2)}) collective-permute-start(f32[32,128]{1,0:T(8,128)S(1)} %add.1206), channel_id=1, source_target_pairs={{0,4},{1,5},{2,6},{3,7},{4,0},{5,1},{6,2},{7,3},{8,12},{9,13},{10,... | collective-permute-start | bytes 49160 | tf_op jit(solution)/shard_map/ppermute | solution.py:71
  117.2 7.1 %collective-permute-start.16 = (f32[32,128]{1,0:T(8,128)S(1)}, f32[32,128]{1,0:T(8,128)S(1)}, u32[]{:S(2)}, u32[]{:S(2)}) collective-permute-start(f32[32,128]{1,0:T(8,128)S(1)} %add.1207), channel_id=1, source_target_pairs={{0,8},{1,9},{2,10},{3,11},{4,12},{5,13},{6,14},{7,15},{8,0},{9,1},... | collective-permute-start | bytes 49160 | tf_op jit(solution)/shard_map/ppermute | solution.py:71

commit v14 on v11

--- a/solution.py
+++ b/solution.py
@@ -34,8 +34,7 @@
 
 
 def front_exchange(cells, basis_pairs, supports, width):
-    open_nodes = (1 - supports).astype(jnp.float32)
-    rim = basis_pairs[:, :, :, :1] * open_nodes[:1]
+    rim = basis_pairs[:, :, :, :1] * (1 - supports[:1]).astype(jnp.float32)
     rims = []
     for axis, dim in (("gx", 0), ("gy", 1)):
         count = lax.axis_size(axis)
@@ -53,7 +52,11 @@
         rims.append(received)
         if axis == "gx":
             rim = jnp.concatenate(
-                [basis_pairs[:, :, :, :, :1] * open_nodes[:, :1], received[:, :, :, :, :1]], axis=3
+                [
+                    basis_pairs[:, :, :, :, :1] * (1 - supports[:, :1]).astype(jnp.float32),
+                    received[:, :, :, :, :1],
+                ],
+                axis=3,
             )
     return cells, rims
 

time: 128 us -> 129 us (level)
  other arithmetic: 8.9 us -> 10.4 us
  transfers between devices with their start and end apart: 17 -> 17, of which waited for: 12 -> 12; matrix products, arithmetic and copies ran while one was open for 3% -> 4% of each run, Pallas kernels for 5% -> 5%
where the time goes in v14:
time: 129 us; the launch traced here: 126 us
  starting transfers between devices  81.7 us (63%)
  waiting for transfers between devices  24.7 us (19%)
  other arithmetic  10.4 us (8%)
  Pallas kernels  5.92 us (5%)
  local copies, waits for them, and re-layouts  2.53 us (2%)
    ppermute x9, starting transfers between devices, butterfly_sum(): lax.ppermute(value, axis, [(i, i ^ stride) for i in range(count)])  52.9 us
    ppermute x9, waiting for transfers between devices, butterfly_sum(): lax.ppermute(value, axis, [(i, i ^ stride) for i in range(count)])  22.1 us
    ppermute x2, starting transfers between devices, with_halo(): lax.ppermute(tail, axis, [(i, (i + 1) % count) for i in range(ends)])  8.7 us
    ppermute x2, starting transfers between devices, with_halo(): lax.ppermute(head, axis, [((i + 1) % count, i) for i in range(ends)])  8.09 us
    ppermute x2, starting transfers between devices, front_exchange(): lax.ppermute(packed, axis, [((i + 1) % count, i) for i in range(ends)])  7.07 us
    pallas_call x1, Pallas kernels, element_energies(): pl.pallas_call(mxu_energy_kernel, out_shape=(jax.ShapeDtypeStruct(cells,...  5.92 us
    ppermute x2, starting transfers between devices, front_exchange(): tail = lax.ppermute(tail, axis, [(i, (i + 1) % count) for i in range(ends)])  4.95 us
  transfers between devices with their start and end apart: 17, of which 12 were waited for; matrix products, arithmetic and copies ran while one was open for 4% of the time, Pallas kernels for 5%

profile of v14, /device:TPU:6, one launch (start us, length us, event | category | flops | bytes accessed | tf_op | source)
XLA Modules:
  0.0 126.3 jit_solution(17046558379437294463)
XLA Ops:
  2.0 0.9 slice_multiply_fusion
  3.0 1.3 %collective-permute-start.1 = (f32[208,128]{1,0:T(8,128)S(1)}, f32[208,128]{1,0:T(8,128)S(1)}, u32[]{:S(2)}, u32[]{:S(2)}) collective-permute-start(f32[208,128]{1,0:T(8,128)S(1)} %pad_maximum_fusion.2), channel_id=1, source_target_pairs={{16,0},{32,16},{48,32},{64,48},{80,64},{96,80},{112,96},{128,112},... | collective-permute-start | bytes 319496 | tf_op jit(solution)/shard_map/ppermute | solution.py:46
  4.3 3.0 %collective-permute-start = (f32[2,8,128]{2,1,0:T(8,128)S(1)}, f32[2,8,128]{2,1,0:T(8,128)S(1)}, u32[]{:S(2)}, u32[]{:S(2)}) collective-permute-start(f32[2,8,128]{2,1,0:T(8,128)S(1)} %get-tuple-element.23), channel_id=1, source_target_pairs={{0,16},{16,32},{32,48},{48,64},{64,80},{80,96},{96,112},{112,128},... | collective-permute-start | bytes 24584 | tf_op jit(solution)/shard_map/ppermute | solution.py:50
  8.8 2.2 %broadcast_multiply_fusion.fields_ref = f32[4,2,3,8,8,128]{5,4,3,2,1,0:T(8,128)} fusion(f32[4,2,3,8,8,128]{5,4,3,2,1,0:T(8,128)} %param.9, f32[8,8,128]{2,1,0:T(8,128)S(1)} %subtract_convert_fusion), kind=kLoop, calls=%fused_computation.6 | loop fusion | flops 196608 | bytes 1605632 | tf_op jit(solution)/shard_map/mul | solution.py:318
  11.8 5.8 %collective-permute-start.3 = (f32[240,128]{1,0:T(8,128)S(1)}, f32[240,128]{1,0:T(8,128)S(1)}, u32[]{:S(2)}, u32[]{:S(2)}) collective-permute-start(f32[240,128]{1,0:T(8,128)S(1)} %pad_maximum_fusion.1), channel_id=1, source_target_pairs={{1,0},{2,1},{3,2},{4,3},{5,4},{6,5},{7,6},{8,7},{9,8},{10,9},{11,1... | collective-permute-start | bytes 368648 | tf_op jit(solution)/shard_map/ppermute | solution.py:46
  17.6 1.9 %collective-permute-start.2 = (f32[12,2,128]{2,1,0:T(2,128)S(1)}, f32[12,2,128]{2,1,0:T(2,128)S(1)}, u32[]{:S(2)}, u32[]{:S(2)}) collective-permute-start(f32[12,2,128]{2,1,0:T(2,128)S(1)} %get-tuple-element.16), channel_id=1, source_target_pairs={{0,1},{1,2},{2,3},{3,4},{4,5},{5,6},{6,7},{7,8},{8,9},{9,10},{10,1... | collective-permute-start | bytes 36872 | tf_op jit(solution)/shard_map/ppermute | solution.py:50
  20.7 5.9 %shard_map.86 = (f32[8,8,128]{2,1,0:T(8,128)}, f32[8,8,128]{2,1,0:T(8,128)}) custom-call(f32[4,2,3,8,8,128]{5,4,3,2,1,0:T(8,128)} %broadcast_multiply_fusion.fields_ref, f32[4,2,3,1,8,128]{5,4,3,2,1,0:T(8,128)} %bitcast.75, f32[4,2,3,9,1,128]{5,4,3,2,1,0:T(1,128)} %bitcast.78, f32[24,24]{1,0:T(8,128)} %stiffness_ref.1, f32[24,24]{1,0:T(8,128)} %mass_ref.1), custom_call_target="tpu_custom_call" | custom-call | flops 607125504 | bytes 1065472 | tf_op jit(solution)/shard_map/pallas_call | solution.py:280
  26.8 2.0 %fusion.82 = (f32[8,8,128]{2,1,0:T(8,128)S(1)}, pred[8,8,128]{2,1,0:T(8,128)(4,1)S(1)}) fusion(f32[8,8,128]{2,1,0:T(8,128)} %get-tuple-element.4, f32[12,10,128]{2,1,0:T(8,128)S(1)} %get-tuple-element.15, f32[12,12,132]{2,1,0:T(8,128)S(1)} %select_maximum_fusion.4, f32[2,8,128]{2,1,0:T(8,128)S(1)} %slice_bitcast_fusion.1, f32[8,8,128]{2,1,0:T(8,128)S(1)} %copy-done, ...), kind=kLoop, calls=%fused_computation.111 | loop fusion | flops 3039232 | bytes 6176768 | tf_op jit(solution)/shard_map/div | solution.py:327
  28.8 1.3 %collective-permute-start.5 = (f32[2,8,128]{2,1,0:T(8,128)S(1)}, f32[2,8,128]{2,1,0:T(8,128)S(1)}, u32[]{:S(2)}, u32[]{:S(2)}) collective-permute-start(f32[2,8,128]{2,1,0:T(8,128)S(1)} %get-tuple-element.22), channel_id=1, source_target_pairs={{16,0},{32,16},{48,32},{64,48},{80,64},{96,80},{112,96},{128,112},... | collective-permute-start | bytes 24584 | tf_op jit(solution)/shard_map/ppermute | solution.py:29
  30.1 6.8 %collective-permute-start.4 = (f32[2,8,128]{2,1,0:T(8,128)S(1)}, f32[2,8,128]{2,1,0:T(8,128)S(1)}, u32[]{:S(2)}, u32[]{:S(2)}) collective-permute-start(f32[2,8,128]{2,1,0:T(8,128)S(1)} %get-tuple-element.21), channel_id=1, source_target_pairs={{0,16},{16,32},{32,48},{48,64},{64,80},{80,96},{96,112},{112,128},... | collective-permute-start | bytes 24584 | tf_op jit(solution)/shard_map/ppermute | solution.py:27
  37.7 1.9 %collective-permute-start.6 = (f32[12,2,128]{2,1,0:T(2,128)S(1)}, f32[12,2,128]{2,1,0:T(2,128)S(1)}, u32[]{:S(2)}, u32[]{:S(2)}) collective-permute-start(f32[12,2,128]{2,1,0:T(2,128)S(1)} %get-tuple-element.12), channel_id=1, source_target_pairs={{0,1},{1,2},{2,3},{3,4},{4,5},{5,6},{6,7},{7,8},{8,9},{9,10},{10,1... | collective-permute-start | bytes 36872 | tf_op jit(solution)/shard_map/ppermute | solution.py:27
  39.7 6.8 %collective-permute-start.7 = (f32[12,2,128]{2,1,0:T(2,128)S(1)}, f32[12,2,128]{2,1,0:T(2,128)S(1)}, u32[]{:S(2)}, u32[]{:S(2)}) collective-permute-start(f32[12,2,128]{2,1,0:T(2,128)S(1)} %get-tuple-element.13), channel_id=1, source_target_pairs={{1,0},{2,1},{3,2},{4,3},{5,4},{6,5},{7,6},{8,7},{9,8},{10,9},{11,1... | collective-permute-start | bytes 36872 | tf_op jit(solution)/shard_map/ppermute | solution.py:29
  46.6 1.2 collective-permute-done.7
  48.6 0.9 fusion.4
  49.9 1.9 %collective-permute-start.8 = (f32[32,128]{1,0:T(8,128)S(1)}, f32[32,128]{1,0:T(8,128)S(1)}, u32[]{:S(2)}, u32[]{:S(2)}) collective-permute-start(f32[32,128]{1,0:T(8,128)S(1)} %pad_bitcast_fusion), channel_id=1, source_target_pairs={{0,1},{1,0},{2,3},{3,2},{4,5},{5,4},{6,7},{7,6},{8,9},{9,8},{10,11... | collective-permute-start | bytes 49160 | tf_op jit(solution)/shard_map/ppermute | solution.py:74
  51.9 3.7 %collective-permute-done.8 = f32[32,128]{1,0:T(8,128)S(1)} collective-permute-done((f32[32,128]{1,0:T(8,128)S(1)}, f32[32,128]{1,0:T(8,128)S(1)}, u32[]{:S(2)}, u32[]{:S(2)}) %collective-permute-start.8) | collective-permute-done | bytes 16416 | tf_op jit(solution)/shard_map/ppermute | solution.py:74
  55.6 1.9 %collective-permute-start.9 = (f32[32,128]{1,0:T(8,128)S(1)}, f32[32,128]{1,0:T(8,128)S(1)}, u32[]{:S(2)}, u32[]{:S(2)}) collective-permute-start(f32[32,128]{1,0:T(8,128)S(1)} %fusion.293), channel_id=1, source_target_pairs={{0,2},{1,3},{2,0},{3,1},{4,6},{5,7},{6,4},{7,5},{8,10},{9,11},{10,... | collective-permute-start | bytes 49160 | tf_op jit(solution)/shard_map/ppermute | solution.py:74
  57.5 4.6 %collective-permute-done.9 = f32[32,128]{1,0:T(8,128)S(1)} collective-permute-done((f32[32,128]{1,0:T(8,128)S(1)}, f32[32,128]{1,0:T(8,128)S(1)}, u32[]{:S(2)}, u32[]{:S(2)}) %collective-permute-start.9) | collective-permute-done | bytes 16416 | tf_op jit(solution)/shard_map/ppermute | solution.py:74
  62.1 3.1 %collective-permute-start.10 = (f32[32,128]{1,0:T(8,128)S(1)}, f32[32,128]{1,0:T(8,128)S(1)}, u32[]{:S(2)}, u32[]{:S(2)}) collective-permute-start(f32[32,128]{1,0:T(8,128)S(1)} %fusion.297), channel_id=1, source_target_pairs={{0,4},{1,5},{2,6},{3,7},{4,0},{5,1},{6,2},{7,3},{8,12},{9,13},{10,... | collective-permute-start | bytes 49160 | tf_op jit(solution)/shard_map/ppermute | solution.py:74
  65.2 2.5 %collective-permute-done.10 = f32[32,128]{1,0:T(8,128)S(1)} collective-permute-done((f32[32,128]{1,0:T(8,128)S(1)}, f32[32,128]{1,0:T(8,128)S(1)}, u32[]{:S(2)}, u32[]{:S(2)}) %collective-permute-start.10) | collective-permute-done | bytes 16416 | tf_op jit(solution)/shard_map/ppermute | solution.py:74
  67.7 3.6 %collective-permute-start.11 = (f32[32,128]{1,0:T(8,128)S(1)}, f32[32,128]{1,0:T(8,128)S(1)}, u32[]{:S(2)}, u32[]{:S(2)}) collective-permute-start(f32[32,128]{1,0:T(8,128)S(1)} %add.1202), channel_id=1, source_target_pairs={{0,8},{1,9},{2,10},{3,11},{4,12},{5,13},{6,14},{7,15},{8,0},{9,1},... | collective-permute-start | bytes 49160 | tf_op jit(solution)/shard_map/ppermute | solution.py:74
  71.4 3.5 %collective-permute-done.11 = f32[32,128]{1,0:T(8,128)S(1)} collective-permute-done((f32[32,128]{1,0:T(8,128)S(1)}, f32[32,128]{1,0:T(8,128)S(1)}, u32[]{:S(2)}, u32[]{:S(2)}) %collective-permute-start.11) | collective-permute-done | bytes 16416 | tf_op jit(solution)/shard_map/ppermute | solution.py:74
  74.8 2.1 %collective-permute-start.12 = (f32[32,128]{1,0:T(8,128)S(1)}, f32[32,128]{1,0:T(8,128)S(1)}, u32[]{:S(2)}, u32[]{:S(2)}) collective-permute-start(f32[32,128]{1,0:T(8,128)S(1)} %add.1203), channel_id=1, source_target_pairs={{0,16},{16,0},{32,48},{48,32},{64,80},{80,64},{96,112},{112,96},{1... | collective-permute-start | bytes 49160 | tf_op jit(solution)/shard_map/ppermute | solution.py:74
  76.9 1.0 collective-permute-done.12
  77.9 13.7 %collective-permute-start.13 = (f32[32,128]{1,0:T(8,128)S(1)}, f32[32,128]{1,0:T(8,128)S(1)}, u32[]{:S(2)}, u32[]{:S(2)}) collective-permute-start(f32[32,128]{1,0:T(8,128)S(1)} %add.1204), channel_id=1, source_target_pairs={{0,32},{16,48},{32,0},{48,16},{64,96},{80,112},{96,64},{112,80},{1... | collective-permute-start | bytes 49160 | tf_op jit(solution)/shard_map/ppermute | solution.py:74
  91.6 1.7 %collective-permute-done.13 = f32[32,128]{1,0:T(8,128)S(1)} collective-permute-done((f32[32,128]{1,0:T(8,128)S(1)}, f32[32,128]{1,0:T(8,128)S(1)}, u32[]{:S(2)}, u32[]{:S(2)}) %collective-permute-start.13) | collective-permute-done | bytes 16416 | tf_op jit(solution)/shard_map/ppermute | solution.py:74
  93.3 9.0 %collective-permute-start.14 = (f32[32,128]{1,0:T(8,128)S(1)}, f32[32,128]{1,0:T(8,128)S(1)}, u32[]{:S(2)}, u32[]{:S(2)}) collective-permute-start(f32[32,128]{1,0:T(8,128)S(1)} %add.1205), channel_id=1, source_target_pairs={{0,64},{16,80},{32,96},{48,112},{64,0},{80,16},{96,32},{112,48},{1... | collective-permute-start | bytes 49160 | tf_op jit(solution)/shard_map/ppermute | solution.py:74
  102.3 1.7 %collective-permute-done.14 = f32[32,128]{1,0:T(8,128)S(1)} collective-permute-done((f32[32,128]{1,0:T(8,128)S(1)}, f32[32,128]{1,0:T(8,128)S(1)}, u32[]{:S(2)}, u32[]{:S(2)}) %collective-permute-start.14) | collective-permute-done | bytes 16416 | tf_op jit(solution)/shard_map/ppermute | solution.py:74
  104.0 6.1 %collective-permute-start.15 = (f32[32,128]{1,0:T(8,128)S(1)}, f32[32,128]{1,0:T(8,128)S(1)}, u32[]{:S(2)}, u32[]{:S(2)}) collective-permute-start(f32[32,128]{1,0:T(8,128)S(1)} %add.1206), channel_id=1, source_target_pairs={{0,128},{16,144},{32,160},{48,176},{64,192},{80,208},{96,224},{112... | collective-permute-start | bytes 49160 | tf_op jit(solution)/shard_map/ppermute | solution.py:74
  110.1 1.7 %collective-permute-done.15 = f32[32,128]{1,0:T(8,128)S(1)} collective-permute-done((f32[32,128]{1,0:T(8,128)S(1)}, f32[32,128]{1,0:T(8,128)S(1)}, u32[]{:S(2)}, u32[]{:S(2)}) %collective-permute-start.15) | collective-permute-done | bytes 16416 | tf_op jit(solution)/shard_map/ppermute | solution.py:74
  111.8 11.6 %collective-permute-start.16 = (f32[32,128]{1,0:T(8,128)S(1)}, f32[32,128]{1,0:T(8,128)S(1)}, u32[]{:S(2)}, u32[]{:S(2)}) collective-permute-start(f32[32,128]{1,0:T(8,128)S(1)} %add.1207), channel_id=1, source_target_pairs={{0,256},{16,272},{32,288},{48,304},{64,320},{80,336},{96,352},{112... | collective-permute-start | bytes 49160 | tf_op jit(solution)/shard_map/ppermute | solution.py:74
  123.4 1.7 %collective-permute-done.16 = f32[32,128]{1,0:T(8,128)S(1)} collective-permute-done((f32[32,128]{1,0:T(8,128)S(1)}, f32[32,128]{1,0:T(8,128)S(1)}, u32[]{:S(2)}, u32[]{:S(2)}) %collective-permute-start.16) | collective-permute-done | bytes 16416 | tf_op jit(solution)/shard_map/ppermute | solution.py:74
  (83 shorter events, 8.2 us)
Async XLA Ops:
  3.0 8.4 %collective-permute-start.1 = (f32[208,128]{1,0:T(8,128)S(1)}, f32[208,128]{1,0:T(8,128)S(1)}, u32[]{:S(2)}, u32[]{:S(2)}) collective-permute-start(f32[208,128]{1,0:T(8,128)S(1)} %pad_maximum_fusion.2), channel_id=1, source_target_pairs={{16,0},{32,16},{48,32},{64,48},{80,64},{96,80},{112,96},{128,112},... | collective-permute-start | bytes 319496 | tf_op jit(solution)/shard_map/ppermute | solution.py:46
  4.3 7.1 %collective-permute-start = (f32[2,8,128]{2,1,0:T(8,128)S(1)}, f32[2,8,128]{2,1,0:T(8,128)S(1)}, u32[]{:S(2)}, u32[]{:S(2)}) collective-permute-start(f32[2,8,128]{2,1,0:T(8,128)S(1)} %get-tuple-element.23), channel_id=1, source_target_pairs={{0,16},{16,32},{32,48},{48,64},{64,80},{80,96},{96,112},{112,128},... | collective-permute-start | bytes 24584 | tf_op jit(solution)/shard_map/ppermute | solution.py:50
  8.8 2.5 %slice-start = ((f32[4,2,3,8,8,128]{5,4,3,2,1,0:T(8,128)}), f32[4,2,3,8,1,128]{5,4,3,2,1,0:T(1,128)S(1)}, s32[]{:S(2)}) async-start(f32[4,2,3,8,8,128]{5,4,3,2,1,0:T(8,128)} %param.9), calls=%async_computation | async-start | bytes 196608 | tf_op jit(solution)/shard_map/slice | solution.py:56
  11.0 0.8 copy-start
  11.3 9.3 %copy-start.2 = (f32[192,128]{1,0:T(8,128)}, f32[192,128]{1,0:T(8,128)S(1)}, u32[]{:S(2)}) copy-start(f32[192,128]{1,0:T(8,128)S(1)} %slice.1320) | copy-start | bytes 294916
  11.8 8.2 %collective-permute-start.3 = (f32[240,128]{1,0:T(8,128)S(1)}, f32[240,128]{1,0:T(8,128)S(1)}, u32[]{:S(2)}, u32[]{:S(2)}) collective-permute-start(f32[240,128]{1,0:T(8,128)S(1)} %pad_maximum_fusion.1), channel_id=1, source_target_pairs={{1,0},{2,1},{3,2},{4,3},{5,4},{6,5},{7,6},{8,7},{9,8},{10,9},{11,1... | collective-permute-start | bytes 368648 | tf_op jit(solution)/shard_map/ppermute | solution.py:46
  17.6 9.0 %collective-permute-start.2 = (f32[12,2,128]{2,1,0:T(2,128)S(1)}, f32[12,2,128]{2,1,0:T(2,128)S(1)}, u32[]{:S(2)}, u32[]{:S(2)}) collective-permute-start(f32[12,2,128]{2,1,0:T(2,128)S(1)} %get-tuple-element.16), channel_id=1, source_target_pairs={{0,1},{1,2},{2,3},{3,4},{4,5},{5,6},{6,7},{7,8},{8,9},{9,10},{10,1... | collective-permute-start | bytes 36872 | tf_op jit(solution)/shard_map/ppermute | solution.py:50
  20.7 6.1 %copy-start.3 = (s32[8,8,128]{2,1,0:T(8,128)S(1)}, s32[8,8,128]{2,1,0:T(8,128)}, u32[]{:S(2)}) copy-start(s32[8,8,128]{2,1,0:T(8,128)} %param.8) | copy-start | bytes 98308
  26.8 19.7 %copy-start.4 = (f32[63,64]{0,1:T(8,128)S(1)}, f32[63,64]{0,1:T(8,128)}, u32[]{:S(2)}) copy-start(f32[63,64]{0,1:T(8,128)} %constant.23.clone.1) | copy-start | bytes 48388
  28.8 8.1 %collective-permute-start.5 = (f32[2,8,128]{2,1,0:T(8,128)S(1)}, f32[2,8,128]{2,1,0:T(8,128)S(1)}, u32[]{:S(2)}, u32[]{:S(2)}) collective-permute-start(f32[2,8,128]{2,1,0:T(8,128)S(1)} %get-tuple-element.22), channel_id=1, source_target_pairs={{16,0},{32,16},{48,32},{64,48},{80,64},{96,80},{112,96},{128,112},... | collective-permute-start | bytes 24584 | tf_op jit(solution)/shard_map/ppermute | solution.py:29
  30.1 7.6 %collective-permute-start.4 = (f32[2,8,128]{2,1,0:T(8,128)S(1)}, f32[2,8,128]{2,1,0:T(8,128)S(1)}, u32[]{:S(2)}, u32[]{:S(2)}) collective-permute-start(f32[2,8,128]{2,1,0:T(8,128)S(1)} %get-tuple-element.21), channel_id=1, source_target_pairs={{0,16},{16,32},{32,48},{48,64},{64,80},{80,96},{96,112},{112,128},... | collective-permute-start | bytes 24584 | tf_op jit(solution)/shard_map/ppermute | solution.py:27
  37.7 8.9 %collective-permute-start.6 = (f32[12,2,128]{2,1,0:T(2,128)S(1)}, f32[12,2,128]{2,1,0:T(2,128)S(1)}, u32[]{:S(2)}, u32[]{:S(2)}) collective-permute-start(f32[12,2,128]{2,1,0:T(2,128)S(1)} %get-tuple-element.12), channel_id=1, source_target_pairs={{0,1},{1,2},{2,3},{3,4},{4,5},{5,6},{6,7},{7,8},{8,9},{9,10},{10,1... | collective-permute-start | bytes 36872 | tf_op jit(solution)/shard_map/ppermute | solution.py:27
  39.7 8.2 %collective-permute-start.7 = (f32[12,2,128]{2,1,0:T(2,128)S(1)}, f32[12,2,128]{2,1,0:T(2,128)S(1)}, u32[]{:S(2)}, u32[]{:S(2)}) collective-permute-start(f32[12,2,128]{2,1,0:T(2,128)S(1)} %get-tuple-element.13), channel_id=1, source_target_pairs={{1,0},{2,1},{3,2},{4,3},{5,4},{6,5},{7,6},{8,7},{9,8},{10,9},{11,1... | collective-permute-start | bytes 36872 | tf_op jit(solution)/shard_map/ppermute | solution.py:29
  48.6 77.1 %copy-start.1 = (f32[8,8,128]{2,1,0:T(8,128)}, f32[8,8,128]{2,1,0:T(8,128)S(1)}, u32[]{:S(2)}) copy-start(f32[8,8,128]{2,1,0:T(8,128)S(1)} %get-tuple-element.7) | copy-start | bytes 98308
  48.6 74.8 %copy-start.5 = (f32[64]{0:T(128)S(1)}, f32[64]{0:T(128)}, u32[]{:S(2)}) copy-start(f32[64]{0:T(128)} %param.13) | copy-start | bytes 772
  49.9 5.6 %collective-permute-start.8 = (f32[32,128]{1,0:T(8,128)S(1)}, f32[32,128]{1,0:T(8,128)S(1)}, u32[]{:S(2)}, u32[]{:S(2)}) collective-permute-start(f32[32,128]{1,0:T(8,128)S(1)} %pad_bitcast_fusion), channel_id=1, source_target_pairs={{0,1},{1,0},{2,3},{3,2},{4,5},{5,4},{6,7},{7,6},{8,9},{9,8},{10,11... | collective-permute-start | bytes 49160 | tf_op jit(solution)/shard_map/ppermute | solution.py:74
  55.6 6.5 %collective-permute-start.9 = (f32[32,128]{1,0:T(8,128)S(1)}, f32[32,128]{1,0:T(8,128)S(1)}, u32[]{:S(2)}, u32[]{:S(2)}) collective-permute-start(f32[32,128]{1,0:T(8,128)S(1)} %fusion.293), channel_id=1, source_target_pairs={{0,2},{1,3},{2,0},{3,1},{4,6},{5,7},{6,4},{7,5},{8,10},{9,11},{10,... | collective-permute-start | bytes 49160 | tf_op jit(solution)/shard_map/ppermute | solution.py:74
  62.1 5.6 %collective-permute-start.10 = (f32[32,128]{1,0:T(8,128)S(1)}, f32[32,128]{1,0:T(8,128)S(1)}, u32[]{:S(2)}, u32[]{:S(2)}) collective-permute-start(f32[32,128]{1,0:T(8,128)S(1)} %fusion.297), channel_id=1, source_target_pairs={{0,4},{1,5},{2,6},{3,7},{4,0},{5,1},{6,2},{7,3},{8,12},{9,13},{10,... | collective-permute-start | bytes 49160 | tf_op jit(solution)/shard_map/ppermute | solution.py:74
  67.7 7.1 %collective-permute-start.11 = (f32[32,128]{1,0:T(8,128)S(1)}, f32[32,128]{1,0:T(8,128)S(1)}, u32[]{:S(2)}, u32[]{:S(2)}) collective-permute-start(f32[32,128]{1,0:T(8,128)S(1)} %add.1202), channel_id=1, source_target_pairs={{0,8},{1,9},{2,10},{3,11},{4,12},{5,13},{6,14},{7,15},{8,0},{9,1},... | collective-permute-start | bytes 49160 | tf_op jit(solution)/shard_map/ppermute | solution.py:74
  74.8 3.1 %collective-permute-start.12 = (f32[32,128]{1,0:T(8,128)S(1)}, f32[32,128]{1,0:T(8,128)S(1)}, u32[]{:S(2)}, u32[]{:S(2)}) collective-permute-start(f32[32,128]{1,0:T(8,128)S(1)} %add.1203), channel_id=1, source_target_pairs={{0,16},{16,0},{32,48},{48,32},{64,80},{80,64},{96,112},{112,96},{1... | collective-permute-start | bytes 49160 | tf_op jit(solution)/shard_map/ppermute | solution.py:74
  77.9 15.4 %collective-permute-start.13 = (f32[32,128]{1,0:T(8,128)S(1)}, f32[32,128]{1,0:T(8,128)S(1)}, u32[]{:S(2)}, u32[]{:S(2)}) collective-permute-start(f32[32,128]{1,0:T(8,128)S(1)} %add.1204), channel_id=1, source_target_pairs={{0,32},{16,48},{32,0},{48,16},{64,96},{80,112},{96,64},{112,80},{1... | collective-permute-start | bytes 49160 | tf_op jit(solution)/shard_map/ppermute | solution.py:74
  93.3 10.7 %collective-permute-start.14 = (f32[32,128]{1,0:T(8,128)S(1)}, f32[32,128]{1,0:T(8,128)S(1)}, u32[]{:S(2)}, u32[]{:S(2)}) collective-permute-start(f32[32,128]{1,0:T(8,128)S(1)} %add.1205), channel_id=1, source_target_pairs={{0,64},{16,80},{32,96},{48,112},{64,0},{80,16},{96,32},{112,48},{1... | collective-permute-start | bytes 49160 | tf_op jit(solution)/shard_map/ppermute | solution.py:74
  104.0 7.8 %collective-permute-start.15 = (f32[32,128]{1,0:T(8,128)S(1)}, f32[32,128]{1,0:T(8,128)S(1)}, u32[]{:S(2)}, u32[]{:S(2)}) collective-permute-start(f32[32,128]{1,0:T(8,128)S(1)} %add.1206), channel_id=1, source_target_pairs={{0,128},{16,144},{32,160},{48,176},{64,192},{80,208},{96,224},{112... | collective-permute-start | bytes 49160 | tf_op jit(solution)/shard_map/ppermute | solution.py:74
  111.8 13.3 %collective-permute-start.16 = (f32[32,128]{1,0:T(8,128)S(1)}, f32[32,128]{1,0:T(8,128)S(1)}, u32[]{:S(2)}, u32[]{:S(2)}) collective-permute-start(f32[32,128]{1,0:T(8,128)S(1)} %add.1207), channel_id=1, source_target_pairs={{0,256},{16,272},{32,288},{48,304},{64,320},{80,336},{96,352},{112... | collective-permute-start | bytes 49160 | tf_op jit(solution)/shard_map/ppermute | solution.py:74

commit v15 on v11

--- a/solution.py
+++ b/solution.py
@@ -35,27 +35,39 @@
 
 def front_exchange(cells, basis_pairs, supports, width):
     open_nodes = (1 - supports).astype(jnp.float32)
-    rim = basis_pairs[:, :, :, :1] * open_nodes[:1]
-    rims = []
+    count_x = lax.axis_size("gx")
+    count_y = lax.axis_size("gy")
+    lanes = cells.shape[-1]
+    rim_y = lax.ppermute(
+        basis_pairs[:, :, :, :, :1] * open_nodes[:, :1], "gy", [(i + 1, i) for i in range(count_y - 1)]
+    )
+    corner = lax.ppermute(
+        basis_pairs[:, :, :, :1, :1] * open_nodes[:1, :1],
+        ("gx", "gy"),
+        [
+            ((i + 1) * count_y + j + 1, i * count_y + j)
+            for i in range(count_x - 1)
+            for j in range(count_y - 1)
+        ],
+    )
+    rim_x = None
     for axis, dim in (("gx", 0), ("gy", 1)):
         count = lax.axis_size(axis)
         ends = count - 1
         head = lax.slice_in_dim(cells, 0, width, axis=dim)
         tail = lax.slice_in_dim(cells, cells.shape[dim] - width, cells.shape[dim], axis=dim)
-        lanes = cells.shape[-1]
-        packed = jnp.concatenate([head.reshape(-1, lanes), rim.reshape(-1, lanes)], axis=0)
-        packed = lax.ppermute(packed, axis, [((i + 1) % count, i) for i in range(ends)])
-        split = head.size // lanes
-        head = packed[:split].reshape(head.shape)
-        received = packed[split:].reshape(rim.shape)
+        if axis == "gx":
+            rim = basis_pairs[:, :, :, :1] * open_nodes[:1]
+            packed = jnp.concatenate([head.reshape(-1, lanes), rim.reshape(-1, lanes)], axis=0)
+            packed = lax.ppermute(packed, axis, [((i + 1) % count, i) for i in range(ends)])
+            split = head.size // lanes
+            head = packed[:split].reshape(head.shape)
+            rim_x = packed[split:].reshape(rim.shape)
+        else:
+            head = lax.ppermute(head, axis, [((i + 1) % count, i) for i in range(ends)])
         tail = lax.ppermute(tail, axis, [(i, (i + 1) % count) for i in range(ends)])
         cells = jnp.concatenate([tail, cells, head], axis=dim)
-        rims.append(received)
-        if axis == "gx":
-            rim = jnp.concatenate(
-                [basis_pairs[:, :, :, :, :1] * open_nodes[:, :1], received[:, :, :, :, :1]], axis=3
-            )
-    return cells, rims
+    return cells, (rim_x, jnp.concatenate([rim_y, corner], axis=3))
 
 
 def from_behind(value, axis, steps):

time: 128 us -> 137 us (1.070)
  starting transfers between devices: 82.3 us -> 90 us
  other arithmetic: 8.9 us -> 11.7 us
    ppermute x0 -> x3, starting transfers between devices: none -> 12.7 us  [the longest x1 5.78 us: front_exchange(): lax.ppermute(basis_pairs[:, :, :, :, :1] * open_nodes[:, :1], 'gy', [(i +...]
    ppermute x2 -> x1, starting transfers between devices: 7.07 us -> 1.29 us  [front_exchange(): lax.ppermute(packed, axis, [((i + 1) % count, i) for i in range(ends)])]
  transfers between devices with their start and end apart: 17 -> 19, of which waited for: 12 -> 11; matrix products, arithmetic and copies ran while one was open for 3% -> 4% of each run, Pallas kernels for 5% -> 4%
where the time goes in v15:
time: 137 us; the launch traced here: 135 us
  starting transfers between devices  90 us (66%)
  waiting for transfers between devices  24.3 us (18%)
  other arithmetic  11.7 us (9%)
  Pallas kernels  5.92 us (4%)
  local copies, waits for them, and re-layouts  2.15 us (2%)
    ppermute x9, starting transfers between devices, butterfly_sum(): lax.ppermute(value, axis, [(i, i ^ stride) for i in range(count)])  52.6 us
    ppermute x9, waiting for transfers between devices, butterfly_sum(): lax.ppermute(value, axis, [(i, i ^ stride) for i in range(count)])  22.3 us
    ppermute x2, starting transfers between devices, with_halo(): lax.ppermute(tail, axis, [(i, (i + 1) % count) for i in range(ends)])  9.15 us
    ppermute x2, starting transfers between devices, with_halo(): lax.ppermute(head, axis, [((i + 1) % count, i) for i in range(ends)])  7.91 us
    ppermute x2, starting transfers between devices, front_exchange(): tail = lax.ppermute(tail, axis, [(i, (i + 1) % count) for i in range(ends)])  6.29 us
    pallas_call x1, Pallas kernels, element_energies(): pl.pallas_call(mxu_energy_kernel, out_shape=(jax.ShapeDtypeStruct(cells,...  5.92 us
    ppermute x1, starting transfers between devices, front_exchange(): lax.ppermute(basis_pairs[:, :, :, :, :1] * open_nodes[:, :1], 'gy', [(i +...  5.78 us
    ppermute x1, starting transfers between devices, front_exchange(): head = lax.ppermute(head, axis, [((i + 1) % count, i) for i in range(ends)])  5.63 us
  transfers between devices with their start and end apart: 19, of which 11 were waited for; matrix products, arithmetic and copies ran while one was open for 4% of the time, Pallas kernels for 4%

profile of v15, /device:TPU:6, one launch (start us, length us, event | category | flops | bytes accessed | tf_op | source)
XLA Modules:
  0.0 135.2 jit_solution(4852052886913060475)
XLA Ops:
  3.0 1.3 collective-permute-start.1
  5.2 1.3 collective-permute-start.5
  6.5 1.2 slice_multiply_fusion
  7.7 5.8 %collective-permute-start.4 = (f32[4,2,3,8,1,128]{5,4,3,2,1,0:T(1,128)S(1)}, f32[4,2,3,8,1,128]{5,4,3,2,1,0:T(1,128)S(1)}, u32[]{:S(2)}, u32[]{:S(2)}) collective-permute-start(f32[4,2,3,8,1,128]{5,4,3,2,1,0:T(1,128)S(1)} %slice_multiply_fusion), channel_id=1, source_target_pairs={{1,0},{2,1},{3,2},{4,3},{5,4},{6,5},{7,6},{8,7},{9,8},{10,9},{11,1... | collective-permute-start | bytes 294920 | tf_op jit(solution)/shard_map/ppermute | solution.py:41
  13.5 3.4 %collective-permute-start = (f32[2,8,128]{2,1,0:T(8,128)S(1)}, f32[2,8,128]{2,1,0:T(8,128)S(1)}, u32[]{:S(2)}, u32[]{:S(2)}) collective-permute-start(f32[2,8,128]{2,1,0:T(8,128)S(1)} %get-tuple-element.23), channel_id=1, source_target_pairs={{0,16},{16,32},{32,48},{48,64},{64,80},{80,96},{96,112},{112,128},... | collective-permute-start | bytes 24584 | tf_op jit(solution)/shard_map/ppermute | solution.py:68
  16.9 2.1 %broadcast_multiply_fusion.fields_ref = f32[4,2,3,8,8,128]{5,4,3,2,1,0:T(8,128)} fusion(f32[4,2,3,8,8,128]{5,4,3,2,1,0:T(8,128)} %param.9, f32[8,8,128]{2,1,0:T(8,128)S(1)} %subtract_convert_fusion), kind=kLoop, calls=%fused_computation.6 | loop fusion | flops 196608 | bytes 1605632 | tf_op jit(solution)/shard_map/mul | solution.py:327
  20.2 2.9 %collective-permute-start.2 = (f32[12,2,128]{2,1,0:T(2,128)S(1)}, f32[12,2,128]{2,1,0:T(2,128)S(1)}, u32[]{:S(2)}, u32[]{:S(2)}) collective-permute-start(f32[12,2,128]{2,1,0:T(2,128)S(1)} %get-tuple-element.16), channel_id=1, source_target_pairs={{0,1},{1,2},{2,3},{3,4},{4,5},{5,6},{6,7},{7,8},{8,9},{9,10},{10,1... | collective-permute-start | bytes 36872 | tf_op jit(solution)/shard_map/ppermute | solution.py:68
  23.1 5.6 %collective-permute-start.3 = (f32[12,2,128]{2,1,0:T(2,128)S(1)}, f32[12,2,128]{2,1,0:T(2,128)S(1)}, u32[]{:S(2)}, u32[]{:S(2)}) collective-permute-start(f32[12,2,128]{2,1,0:T(2,128)S(1)} %get-tuple-element.17), channel_id=1, source_target_pairs={{1,0},{2,1},{3,2},{4,3},{5,4},{6,5},{7,6},{8,7},{9,8},{10,9},{11,1... | collective-permute-start | bytes 36872 | tf_op jit(solution)/shard_map/ppermute | solution.py:67
  29.4 5.9 %shard_map.86 = (f32[8,8,128]{2,1,0:T(8,128)}, f32[8,8,128]{2,1,0:T(8,128)}) custom-call(f32[4,2,3,8,8,128]{5,4,3,2,1,0:T(8,128)} %broadcast_multiply_fusion.fields_ref, f32[4,2,3,1,8,128]{5,4,3,2,1,0:T(8,128)} %bitcast.67, f32[4,2,3,9,1,128]{5,4,3,2,1,0:T(1,128)} %pad_maximum_fusion.rim_y_ref, f32[24,24]{1,0:T(8,128)} %stiffness_ref.1, f32[24,24]{1,0:T(8,128)} %mass_ref.1), custom_call_target="tpu_custom_call" | custom-call | flops 607125504 | bytes 1065472 | tf_op jit(solution)/shard_map/pallas_call | solution.py:289
  35.5 2.0 %fusion.82 = (f32[8,8,128]{2,1,0:T(8,128)S(1)}, pred[8,8,128]{2,1,0:T(8,128)(4,1)S(1)}) fusion(f32[8,8,128]{2,1,0:T(8,128)} %get-tuple-element.4, f32[12,10,128]{2,1,0:T(8,128)S(1)} %get-tuple-element.15, f32[12,12,132]{2,1,0:T(8,128)S(1)} %select_maximum_fusion.4, f32[2,8,128]{2,1,0:T(8,128)S(1)} %slice_bitcast_fusion, f32[8,8,128]{2,1,0:T(8,128)S(1)} %copy-done, ...), kind=kLoop, calls=%fused_computation.110 | loop fusion | flops 3039232 | bytes 6176768 | tf_op jit(solution)/shard_map/div | solution.py:336
  37.5 1.3 collective-permute-start.7
  38.8 7.2 %collective-permute-start.6 = (f32[2,8,128]{2,1,0:T(8,128)S(1)}, f32[2,8,128]{2,1,0:T(8,128)S(1)}, u32[]{:S(2)}, u32[]{:S(2)}) collective-permute-start(f32[2,8,128]{2,1,0:T(8,128)S(1)} %get-tuple-element.21), channel_id=1, source_target_pairs={{0,16},{16,32},{32,48},{48,64},{64,80},{80,96},{96,112},{112,128},... | collective-permute-start | bytes 24584 | tf_op jit(solution)/shard_map/ppermute | solution.py:27
  46.9 1.9 %collective-permute-start.8 = (f32[12,2,128]{2,1,0:T(2,128)S(1)}, f32[12,2,128]{2,1,0:T(2,128)S(1)}, u32[]{:S(2)}, u32[]{:S(2)}) collective-permute-start(f32[12,2,128]{2,1,0:T(2,128)S(1)} %get-tuple-element.12), channel_id=1, source_target_pairs={{0,1},{1,2},{2,3},{3,4},{4,5},{5,6},{6,7},{7,8},{8,9},{9,10},{10,1... | collective-permute-start | bytes 36872 | tf_op jit(solution)/shard_map/ppermute | solution.py:27
  48.8 6.6 %collective-permute-start.9 = (f32[12,2,128]{2,1,0:T(2,128)S(1)}, f32[12,2,128]{2,1,0:T(2,128)S(1)}, u32[]{:S(2)}, u32[]{:S(2)}) collective-permute-start(f32[12,2,128]{2,1,0:T(2,128)S(1)} %get-tuple-element.13), channel_id=1, source_target_pairs={{1,0},{2,1},{3,2},{4,3},{5,4},{6,5},{7,6},{8,7},{9,8},{10,9},{11,1... | collective-permute-start | bytes 36872 | tf_op jit(solution)/shard_map/ppermute | solution.py:29
  55.6 1.2 collective-permute-done.9
  58.9 1.9 %collective-permute-start.10 = (f32[32,128]{1,0:T(8,128)S(1)}, f32[32,128]{1,0:T(8,128)S(1)}, u32[]{:S(2)}, u32[]{:S(2)}) collective-permute-start(f32[32,128]{1,0:T(8,128)S(1)} %pad_bitcast_fusion), channel_id=1, source_target_pairs={{0,1},{1,0},{2,3},{3,2},{4,5},{5,4},{6,7},{7,6},{8,9},{9,8},{10,11... | collective-permute-start | bytes 49160 | tf_op jit(solution)/shard_map/ppermute | solution.py:83
  60.8 3.7 %collective-permute-done.10 = f32[32,128]{1,0:T(8,128)S(1)} collective-permute-done((f32[32,128]{1,0:T(8,128)S(1)}, f32[32,128]{1,0:T(8,128)S(1)}, u32[]{:S(2)}, u32[]{:S(2)}) %collective-permute-start.10) | collective-permute-done | bytes 16416 | tf_op jit(solution)/shard_map/ppermute | solution.py:83
  64.5 1.9 %collective-permute-start.11 = (f32[32,128]{1,0:T(8,128)S(1)}, f32[32,128]{1,0:T(8,128)S(1)}, u32[]{:S(2)}, u32[]{:S(2)}) collective-permute-start(f32[32,128]{1,0:T(8,128)S(1)} %fusion.293), channel_id=1, source_target_pairs={{0,2},{1,3},{2,0},{3,1},{4,6},{5,7},{6,4},{7,5},{8,10},{9,11},{10,... | collective-permute-start | bytes 49160 | tf_op jit(solution)/shard_map/ppermute | solution.py:83
  66.5 4.6 %collective-permute-done.11 = f32[32,128]{1,0:T(8,128)S(1)} collective-permute-done((f32[32,128]{1,0:T(8,128)S(1)}, f32[32,128]{1,0:T(8,128)S(1)}, u32[]{:S(2)}, u32[]{:S(2)}) %collective-permute-start.11) | collective-permute-done | bytes 16416 | tf_op jit(solution)/shard_map/ppermute | solution.py:83
  71.1 3.1 %collective-permute-start.12 = (f32[32,128]{1,0:T(8,128)S(1)}, f32[32,128]{1,0:T(8,128)S(1)}, u32[]{:S(2)}, u32[]{:S(2)}) collective-permute-start(f32[32,128]{1,0:T(8,128)S(1)} %fusion.297), channel_id=1, source_target_pairs={{0,4},{1,5},{2,6},{3,7},{4,0},{5,1},{6,2},{7,3},{8,12},{9,13},{10,... | collective-permute-start | bytes 49160 | tf_op jit(solution)/shard_map/ppermute | solution.py:83
  74.2 2.5 %collective-permute-done.12 = f32[32,128]{1,0:T(8,128)S(1)} collective-permute-done((f32[32,128]{1,0:T(8,128)S(1)}, f32[32,128]{1,0:T(8,128)S(1)}, u32[]{:S(2)}, u32[]{:S(2)}) %collective-permute-start.12) | collective-permute-done | bytes 16416 | tf_op jit(solution)/shard_map/ppermute | solution.py:83
  76.7 3.7 %collective-permute-start.13 = (f32[32,128]{1,0:T(8,128)S(1)}, f32[32,128]{1,0:T(8,128)S(1)}, u32[]{:S(2)}, u32[]{:S(2)}) collective-permute-start(f32[32,128]{1,0:T(8,128)S(1)} %add.1202), channel_id=1, source_target_pairs={{0,8},{1,9},{2,10},{3,11},{4,12},{5,13},{6,14},{7,15},{8,0},{9,1},... | collective-permute-start | bytes 49160 | tf_op jit(solution)/shard_map/ppermute | solution.py:83
  80.4 3.6 %collective-permute-done.13 = f32[32,128]{1,0:T(8,128)S(1)} collective-permute-done((f32[32,128]{1,0:T(8,128)S(1)}, f32[32,128]{1,0:T(8,128)S(1)}, u32[]{:S(2)}, u32[]{:S(2)}) %collective-permute-start.13) | collective-permute-done | bytes 16416 | tf_op jit(solution)/shard_map/ppermute | solution.py:83
  84.0 2.0 %collective-permute-start.14 = (f32[32,128]{1,0:T(8,128)S(1)}, f32[32,128]{1,0:T(8,128)S(1)}, u32[]{:S(2)}, u32[]{:S(2)}) collective-permute-start(f32[32,128]{1,0:T(8,128)S(1)} %add.1203), channel_id=1, source_target_pairs={{0,16},{16,0},{32,48},{48,32},{64,80},{80,64},{96,112},{112,96},{1... | collective-permute-start | bytes 49160 | tf_op jit(solution)/shard_map/ppermute | solution.py:83
  87.0 13.5 %collective-permute-start.15 = (f32[32,128]{1,0:T(8,128)S(1)}, f32[32,128]{1,0:T(8,128)S(1)}, u32[]{:S(2)}, u32[]{:S(2)}) collective-permute-start(f32[32,128]{1,0:T(8,128)S(1)} %add.1204), channel_id=1, source_target_pairs={{0,32},{16,48},{32,0},{48,16},{64,96},{80,112},{96,64},{112,80},{1... | collective-permute-start | bytes 49160 | tf_op jit(solution)/shard_map/ppermute | solution.py:83
  100.5 1.7 %collective-permute-done.15 = f32[32,128]{1,0:T(8,128)S(1)} collective-permute-done((f32[32,128]{1,0:T(8,128)S(1)}, f32[32,128]{1,0:T(8,128)S(1)}, u32[]{:S(2)}, u32[]{:S(2)}) %collective-permute-start.15) | collective-permute-done | bytes 16416 | tf_op jit(solution)/shard_map/ppermute | solution.py:83
  102.2 8.9 %collective-permute-start.16 = (f32[32,128]{1,0:T(8,128)S(1)}, f32[32,128]{1,0:T(8,128)S(1)}, u32[]{:S(2)}, u32[]{:S(2)}) collective-permute-start(f32[32,128]{1,0:T(8,128)S(1)} %add.1205), channel_id=1, source_target_pairs={{0,64},{16,80},{32,96},{48,112},{64,0},{80,16},{96,32},{112,48},{1... | collective-permute-start | bytes 49160 | tf_op jit(solution)/shard_map/ppermute | solution.py:83
  111.1 1.7 %collective-permute-done.16 = f32[32,128]{1,0:T(8,128)S(1)} collective-permute-done((f32[32,128]{1,0:T(8,128)S(1)}, f32[32,128]{1,0:T(8,128)S(1)}, u32[]{:S(2)}, u32[]{:S(2)}) %collective-permute-start.16) | collective-permute-done | bytes 16416 | tf_op jit(solution)/shard_map/ppermute | solution.py:83
  112.8 6.0 %collective-permute-start.17 = (f32[32,128]{1,0:T(8,128)S(1)}, f32[32,128]{1,0:T(8,128)S(1)}, u32[]{:S(2)}, u32[]{:S(2)}) collective-permute-start(f32[32,128]{1,0:T(8,128)S(1)} %add.1206), channel_id=1, source_target_pairs={{0,128},{16,144},{32,160},{48,176},{64,192},{80,208},{96,224},{112... | collective-permute-start | bytes 49160 | tf_op jit(solution)/shard_map/ppermute | solution.py:83
  118.8 1.7 %collective-permute-done.17 = f32[32,128]{1,0:T(8,128)S(1)} collective-permute-done((f32[32,128]{1,0:T(8,128)S(1)}, f32[32,128]{1,0:T(8,128)S(1)}, u32[]{:S(2)}, u32[]{:S(2)}) %collective-permute-start.17) | collective-permute-done | bytes 16416 | tf_op jit(solution)/shard_map/ppermute | solution.py:83
  120.5 11.7 %collective-permute-start.18 = (f32[32,128]{1,0:T(8,128)S(1)}, f32[32,128]{1,0:T(8,128)S(1)}, u32[]{:S(2)}, u32[]{:S(2)}) collective-permute-start(f32[32,128]{1,0:T(8,128)S(1)} %add.1207), channel_id=1, source_target_pairs={{0,256},{16,272},{32,288},{48,304},{64,320},{80,336},{96,352},{112... | collective-permute-start | bytes 49160 | tf_op jit(solution)/shard_map/ppermute | solution.py:83
  132.3 1.7 %collective-permute-done.18 = f32[32,128]{1,0:T(8,128)S(1)} collective-permute-done((f32[32,128]{1,0:T(8,128)S(1)}, f32[32,128]{1,0:T(8,128)S(1)}, u32[]{:S(2)}, u32[]{:S(2)}) %collective-permute-start.18) | collective-permute-done | bytes 16416 | tf_op jit(solution)/shard_map/ppermute | solution.py:83
  (80 shorter events, 10.4 us)
Async XLA Ops:
  3.0 17.1 %collective-permute-start.1 = (f32[208,128]{1,0:T(8,128)S(1)}, f32[208,128]{1,0:T(8,128)S(1)}, u32[]{:S(2)}, u32[]{:S(2)}) collective-permute-start(f32[208,128]{1,0:T(8,128)S(1)} %pad_maximum_fusion.1), channel_id=1, source_target_pairs={{16,0},{32,16},{48,32},{64,48},{80,64},{96,80},{112,96},{128,112},... | collective-permute-start | bytes 319496 | tf_op jit(solution)/shard_map/ppermute | solution.py:62
  5.2 14.1 %collective-permute-start.5 = (f32[4,2,3,1,1,128]{5,4,3,2,1,0:T(1,128)S(1)}, f32[4,2,3,1,1,128]{5,4,3,2,1,0:T(1,128)S(1)}, u32[]{:S(2)}, u32[]{:S(2)}) collective-permute-start(f32[4,2,3,1,1,128]{5,4,3,2,1,0:T(1,128)S(1)} %slice_multiply_fusion.258), channel_id=1, source_target_pairs={{17,0},{18,1},{19,2},{20,3},{21,4},{22,5},{23,6},{24,7},{25,8},{26... | collective-permute-start | bytes 36872 | tf_op jit(solution)/shard_map/ppermute | solution.py:44
  7.7 11.6 %collective-permute-start.4 = (f32[4,2,3,8,1,128]{5,4,3,2,1,0:T(1,128)S(1)}, f32[4,2,3,8,1,128]{5,4,3,2,1,0:T(1,128)S(1)}, u32[]{:S(2)}, u32[]{:S(2)}) collective-permute-start(f32[4,2,3,8,1,128]{5,4,3,2,1,0:T(1,128)S(1)} %slice_multiply_fusion), channel_id=1, source_target_pairs={{1,0},{2,1},{3,2},{4,3},{5,4},{6,5},{7,6},{8,7},{9,8},{10,9},{11,1... | collective-permute-start | bytes 294920 | tf_op jit(solution)/shard_map/ppermute | solution.py:41
  13.5 5.8 %copy-start = (f32[8,8,128]{2,1,0:T(8,128)S(1)}, f32[8,8,128]{2,1,0:T(8,128)}, u32[]{:S(2)}) copy-start(f32[8,8,128]{2,1,0:T(8,128)} %param.7) | copy-start | bytes 98308
  13.5 5.8 %collective-permute-start = (f32[2,8,128]{2,1,0:T(8,128)S(1)}, f32[2,8,128]{2,1,0:T(8,128)S(1)}, u32[]{:S(2)}, u32[]{:S(2)}) collective-permute-start(f32[2,8,128]{2,1,0:T(8,128)S(1)} %get-tuple-element.23), channel_id=1, source_target_pairs={{0,16},{16,32},{32,48},{48,64},{64,80},{80,96},{96,112},{112,128},... | collective-permute-start | bytes 24584 | tf_op jit(solution)/shard_map/ppermute | solution.py:68
  20.2 15.1 %collective-permute-start.2 = (f32[12,2,128]{2,1,0:T(2,128)S(1)}, f32[12,2,128]{2,1,0:T(2,128)S(1)}, u32[]{:S(2)}, u32[]{:S(2)}) collective-permute-start(f32[12,2,128]{2,1,0:T(2,128)S(1)} %get-tuple-element.16), channel_id=1, source_target_pairs={{0,1},{1,2},{2,3},{3,4},{4,5},{5,6},{6,7},{7,8},{8,9},{9,10},{10,1... | collective-permute-start | bytes 36872 | tf_op jit(solution)/shard_map/ppermute | solution.py:68
  23.1 12.2 %collective-permute-start.3 = (f32[12,2,128]{2,1,0:T(2,128)S(1)}, f32[12,2,128]{2,1,0:T(2,128)S(1)}, u32[]{:S(2)}, u32[]{:S(2)}) collective-permute-start(f32[12,2,128]{2,1,0:T(2,128)S(1)} %get-tuple-element.17), channel_id=1, source_target_pairs={{1,0},{2,1},{3,2},{4,3},{5,4},{6,5},{7,6},{8,7},{9,8},{10,9},{11,1... | collective-permute-start | bytes 36872 | tf_op jit(solution)/shard_map/ppermute | solution.py:67
  29.4 6.1 %copy-start.2 = (s32[8,8,128]{2,1,0:T(8,128)S(1)}, s32[8,8,128]{2,1,0:T(8,128)}, u32[]{:S(2)}) copy-start(s32[8,8,128]{2,1,0:T(8,128)} %param.8) | copy-start | bytes 98308
  35.5 20.0 %copy-start.3 = (f32[63,64]{0,1:T(8,128)S(1)}, f32[63,64]{0,1:T(8,128)}, u32[]{:S(2)}) copy-start(f32[63,64]{0,1:T(8,128)} %constant.25.clone.1) | copy-start | bytes 48388
  37.5 8.5 %collective-permute-start.7 = (f32[2,8,128]{2,1,0:T(8,128)S(1)}, f32[2,8,128]{2,1,0:T(8,128)S(1)}, u32[]{:S(2)}, u32[]{:S(2)}) collective-permute-start(f32[2,8,128]{2,1,0:T(8,128)S(1)} %get-tuple-element.22), channel_id=1, source_target_pairs={{16,0},{32,16},{48,32},{64,48},{80,64},{96,80},{112,96},{128,112},... | collective-permute-start | bytes 24584 | tf_op jit(solution)/shard_map/ppermute | solution.py:29
  38.8 8.1 %collective-permute-start.6 = (f32[2,8,128]{2,1,0:T(8,128)S(1)}, f32[2,8,128]{2,1,0:T(8,128)S(1)}, u32[]{:S(2)}, u32[]{:S(2)}) collective-permute-start(f32[2,8,128]{2,1,0:T(8,128)S(1)} %get-tuple-element.21), channel_id=1, source_target_pairs={{0,16},{16,32},{32,48},{48,64},{64,80},{80,96},{96,112},{112,128},... | collective-permute-start | bytes 24584 | tf_op jit(solution)/shard_map/ppermute | solution.py:27
  46.9 8.7 %collective-permute-start.8 = (f32[12,2,128]{2,1,0:T(2,128)S(1)}, f32[12,2,128]{2,1,0:T(2,128)S(1)}, u32[]{:S(2)}, u32[]{:S(2)}) collective-permute-start(f32[12,2,128]{2,1,0:T(2,128)S(1)} %get-tuple-element.12), channel_id=1, source_target_pairs={{0,1},{1,2},{2,3},{3,4},{4,5},{5,6},{6,7},{7,8},{8,9},{9,10},{10,1... | collective-permute-start | bytes 36872 | tf_op jit(solution)/shard_map/ppermute | solution.py:27
  48.8 8.0 %collective-permute-start.9 = (f32[12,2,128]{2,1,0:T(2,128)S(1)}, f32[12,2,128]{2,1,0:T(2,128)S(1)}, u32[]{:S(2)}, u32[]{:S(2)}) collective-permute-start(f32[12,2,128]{2,1,0:T(2,128)S(1)} %get-tuple-element.13), channel_id=1, source_target_pairs={{1,0},{2,1},{3,2},{4,3},{5,4},{6,5},{7,6},{8,7},{9,8},{10,9},{11,1... | collective-permute-start | bytes 36872 | tf_op jit(solution)/shard_map/ppermute | solution.py:29
  57.6 76.9 %copy-start.1 = (f32[8,8,128]{2,1,0:T(8,128)}, f32[8,8,128]{2,1,0:T(8,128)S(1)}, u32[]{:S(2)}) copy-start(f32[8,8,128]{2,1,0:T(8,128)S(1)} %get-tuple-element.7) | copy-start | bytes 98308
  57.6 74.7 %copy-start.4 = (f32[64]{0:T(128)S(1)}, f32[64]{0:T(128)}, u32[]{:S(2)}) copy-start(f32[64]{0:T(128)} %param.13) | copy-start | bytes 772
  58.9 5.6 %collective-permute-start.10 = (f32[32,128]{1,0:T(8,128)S(1)}, f32[32,128]{1,0:T(8,128)S(1)}, u32[]{:S(2)}, u32[]{:S(2)}) collective-permute-start(f32[32,128]{1,0:T(8,128)S(1)} %pad_bitcast_fusion), channel_id=1, source_target_pairs={{0,1},{1,0},{2,3},{3,2},{4,5},{5,4},{6,7},{7,6},{8,9},{9,8},{10,11... | collective-permute-start | bytes 49160 | tf_op jit(solution)/shard_map/ppermute | solution.py:83
  64.5 6.5 %collective-permute-start.11 = (f32[32,128]{1,0:T(8,128)S(1)}, f32[32,128]{1,0:T(8,128)S(1)}, u32[]{:S(2)}, u32[]{:S(2)}) collective-permute-start(f32[32,128]{1,0:T(8,128)S(1)} %fusion.293), channel_id=1, source_target_pairs={{0,2},{1,3},{2,0},{3,1},{4,6},{5,7},{6,4},{7,5},{8,10},{9,11},{10,... | collective-permute-start | bytes 49160 | tf_op jit(solution)/shard_map/ppermute | solution.py:83
  71.1 5.6 %collective-permute-start.12 = (f32[32,128]{1,0:T(8,128)S(1)}, f32[32,128]{1,0:T(8,128)S(1)}, u32[]{:S(2)}, u32[]{:S(2)}) collective-permute-start(f32[32,128]{1,0:T(8,128)S(1)} %fusion.297), channel_id=1, source_target_pairs={{0,4},{1,5},{2,6},{3,7},{4,0},{5,1},{6,2},{7,3},{8,12},{9,13},{10,... | collective-permute-start | bytes 49160 | tf_op jit(solution)/shard_map/ppermute | solution.py:83
  76.7 7.2 %collective-permute-start.13 = (f32[32,128]{1,0:T(8,128)S(1)}, f32[32,128]{1,0:T(8,128)S(1)}, u32[]{:S(2)}, u32[]{:S(2)}) collective-permute-start(f32[32,128]{1,0:T(8,128)S(1)} %add.1202), channel_id=1, source_target_pairs={{0,8},{1,9},{2,10},{3,11},{4,12},{5,13},{6,14},{7,15},{8,0},{9,1},... | collective-permute-start | bytes 49160 | tf_op jit(solution)/shard_map/ppermute | solution.py:83
  84.0 3.1 %collective-permute-start.14 = (f32[32,128]{1,0:T(8,128)S(1)}, f32[32,128]{1,0:T(8,128)S(1)}, u32[]{:S(2)}, u32[]{:S(2)}) collective-permute-start(f32[32,128]{1,0:T(8,128)S(1)} %add.1203), channel_id=1, source_target_pairs={{0,16},{16,0},{32,48},{48,32},{64,80},{80,64},{96,112},{112,96},{1... | collective-permute-start | bytes 49160 | tf_op jit(solution)/shard_map/ppermute | solution.py:83
  87.0 15.2 %collective-permute-start.15 = (f32[32,128]{1,0:T(8,128)S(1)}, f32[32,128]{1,0:T(8,128)S(1)}, u32[]{:S(2)}, u32[]{:S(2)}) collective-permute-start(f32[32,128]{1,0:T(8,128)S(1)} %add.1204), channel_id=1, source_target_pairs={{0,32},{16,48},{32,0},{48,16},{64,96},{80,112},{96,64},{112,80},{1... | collective-permute-start | bytes 49160 | tf_op jit(solution)/shard_map/ppermute | solution.py:83
  102.2 10.6 %collective-permute-start.16 = (f32[32,128]{1,0:T(8,128)S(1)}, f32[32,128]{1,0:T(8,128)S(1)}, u32[]{:S(2)}, u32[]{:S(2)}) collective-permute-start(f32[32,128]{1,0:T(8,128)S(1)} %add.1205), channel_id=1, source_target_pairs={{0,64},{16,80},{32,96},{48,112},{64,0},{80,16},{96,32},{112,48},{1... | collective-permute-start | bytes 49160 | tf_op jit(solution)/shard_map/ppermute | solution.py:83
  112.8 7.7 %collective-permute-start.17 = (f32[32,128]{1,0:T(8,128)S(1)}, f32[32,128]{1,0:T(8,128)S(1)}, u32[]{:S(2)}, u32[]{:S(2)}) collective-permute-start(f32[32,128]{1,0:T(8,128)S(1)} %add.1206), channel_id=1, source_target_pairs={{0,128},{16,144},{32,160},{48,176},{64,192},{80,208},{96,224},{112... | collective-permute-start | bytes 49160 | tf_op jit(solution)/shard_map/ppermute | solution.py:83
  120.5 13.4 %collective-permute-start.18 = (f32[32,128]{1,0:T(8,128)S(1)}, f32[32,128]{1,0:T(8,128)S(1)}, u32[]{:S(2)}, u32[]{:S(2)}) collective-permute-start(f32[32,128]{1,0:T(8,128)S(1)} %add.1207), channel_id=1, source_target_pairs={{0,256},{16,272},{32,288},{48,304},{64,320},{80,336},{96,352},{112... | collective-permute-start | bytes 49160 | tf_op jit(solution)/shard_map/ppermute | solution.py:83

commit v16 on v10

--- a/solution.py
+++ b/solution.py
@@ -22,14 +22,14 @@
         ends = count - 1
         head = lax.slice_in_dim(cells, 0, width, axis=dim)
         tail = lax.slice_in_dim(cells, cells.shape[dim] - width, cells.shape[dim], axis=dim)
-        cells = jnp.concatenate(
-            [
-                lax.ppermute(tail, axis, [(i, (i + 1) % count) for i in range(ends)]),
-                cells,
-                lax.ppermute(head, axis, [((i + 1) % count, i) for i in range(ends)]),
-            ],
-            axis=dim,
-        )
+        lanes = cells.shape[-1]
+        tail_in = lax.ppermute(
+            tail.reshape(-1, lanes), axis, [(i, (i + 1) % count) for i in range(ends)]
+        ).reshape(tail.shape)
+        head_in = lax.ppermute(
+            head.reshape(-1, lanes), axis, [((i + 1) % count, i) for i in range(ends)]
+        ).reshape(head.shape)
+        cells = jnp.concatenate([tail_in, cells, head_in], axis=dim)
     return cells
 
 
@@ -47,7 +47,9 @@
         split = head.size // lanes
         head = packed[:split].reshape(head.shape)
         rim = packed[split:].reshape(rim.shape)
-        tail = lax.ppermute(tail, axis, [(i, (i + 1) % count) for i in range(ends)])
+        tail = lax.ppermute(
+            tail.reshape(-1, lanes), axis, [(i, (i + 1) % count) for i in range(ends)]
+        ).reshape(tail.shape)
         cells = jnp.concatenate([tail, cells, head], axis=dim)
         fields = jnp.concatenate([fields, rim], axis=field_dim)
     return cells, fields

time: 127 us -> 132 us (1.039)
  waiting for transfers between devices: 25 us -> 30.8 us
    ppermute x6, waiting for transfers between devices: 2.59 us -> 8.47 us  [the longest x2 6.44 us: front_exchange(): lax.ppermute(tail.reshape(-1, lanes), axis, [(i, (i + 1) % count) for i i...]
  transfers between devices with their start and end apart: 17 -> 17, of which waited for: 13 -> 14; matrix products, arithmetic and copies ran while one was open for 1% -> 0% of each run, Pallas kernels for 5% -> 0%
where the time goes in v16:
time: 132 us; the launch traced here: 130 us
  starting transfers between devices  82.3 us (62%)
  waiting for transfers between devices  30.8 us (23%)
  other arithmetic  8.44 us (6%)
  Pallas kernels  6.22 us (5%)
    ppermute x9, starting transfers between devices, butterfly_sum(): lax.ppermute(value, axis, [(i, i ^ stride) for i in range(count)])  54.5 us
    ppermute x9, waiting for transfers between devices, butterfly_sum(): lax.ppermute(value, axis, [(i, i ^ stride) for i in range(count)])  21.9 us
    ppermute x2, starting transfers between devices, with_halo(): lax.ppermute(tail.reshape(-1, lanes), axis, [(i, (i + 1) % count) for i i...  7.93 us
    ppermute x2, starting transfers between devices, with_halo(): lax.ppermute(head.reshape(-1, lanes), axis, [((i + 1) % count, i) for i i...  7.91 us
    ppermute x2, starting transfers between devices, front_exchange(): lax.ppermute(packed, axis, [((i + 1) % count, i) for i in range(ends)])  7.07 us
    ppermute x2, waiting for transfers between devices, front_exchange(): lax.ppermute(tail.reshape(-1, lanes), axis, [(i, (i + 1) % count) for i i...  6.44 us
    pallas_call x1, Pallas kernels, element_energies(): pl.pallas_call(mxu_energy_kernel, out_shape=(jax.ShapeDtypeStruct(cells,...  6.22 us
    ppermute x2, starting transfers between devices, front_exchange(): lax.ppermute(tail.reshape(-1, lanes), axis, [(i, (i + 1) % count) for i i...  4.95 us
  transfers between devices with their start and end apart: 17, of which 14 were waited for; matrix products, arithmetic and copies ran while one was open for 0% of the time, Pallas kernels for 0%

profile of v16, /device:TPU:6, one launch (start us, length us, event | category | flops | bytes accessed | tf_op | source)
XLA Modules:
  0.0 129.6 jit_solution(5181717531456938840)
XLA Ops:
  1.4 1.2 broadcast_multiply_fusion
  2.7 1.3 collective-permute-start.1
  4.0 3.0 %collective-permute-start = (f32[16,128]{1,0:T(8,128)S(1)}, f32[16,128]{1,0:T(8,128)S(1)}, u32[]{:S(2)}, u32[]{:S(2)}) collective-permute-start(f32[16,128]{1,0:T(8,128)S(1)} %get-tuple-element.22), channel_id=1, source_target_pairs={{0,16},{16,32},{32,48},{48,64},{64,80},{80,96},{96,112},{112,128},... | collective-permute-start | bytes 24584 | tf_op jit(solution)/shard_map/ppermute | solution.py:50
  7.8 5.8 %collective-permute-start.3 = (f32[240,128]{1,0:T(8,128)S(1)}, f32[240,128]{1,0:T(8,128)S(1)}, u32[]{:S(2)}, u32[]{:S(2)}) collective-permute-start(f32[240,128]{1,0:T(8,128)S(1)} %pad_maximum_fusion.1), channel_id=1, source_target_pairs={{1,0},{2,1},{3,2},{4,3},{5,4},{6,5},{7,6},{8,7},{9,8},{10,9},{11,1... | collective-permute-start | bytes 368648 | tf_op jit(solution)/shard_map/ppermute | solution.py:46
  13.6 1.9 %collective-permute-start.2 = (f32[24,128]{1,0:T(8,128)S(1)}, f32[24,128]{1,0:T(8,128)S(1)}, u32[]{:S(2)}, u32[]{:S(2)}) collective-permute-start(f32[24,128]{1,0:T(8,128)S(1)} %bitcast.106), channel_id=1, source_target_pairs={{0,1},{1,2},{2,3},{3,4},{4,5},{5,6},{6,7},{7,8},{8,9},{9,10},{10,1... | collective-permute-start | bytes 36872 | tf_op jit(solution)/shard_map/ppermute | solution.py:50
  16.1 5.9 %collective-permute-done.2 = f32[24,128]{1,0:T(8,128)S(1)} collective-permute-done((f32[24,128]{1,0:T(8,128)S(1)}, f32[24,128]{1,0:T(8,128)S(1)}, u32[]{:S(2)}, u32[]{:S(2)}) %collective-permute-start.2) | collective-permute-done | bytes 12320 | tf_op jit(solution)/shard_map/ppermute | solution.py:50
  22.2 1.4 %pad_maximum_fusion.extended_ref = f32[4,2,3,9,9,128]{5,4,3,2,1,0:T(8,128)} fusion(f32[4,2,3,9,1,128]{5,4,3,2,1,0:T(1,128)S(1)} %bitcast.80, f32[4,2,3,1,8,128]{5,4,3,2,1,0:T(8,128)S(1)} %bitcast.79, f32[4,2,3,8,8,128]{5,4,3,2,1,0:T(8,128)S(1)} %broadcast_multiply_fusion), kind=kLoop, calls=%fused_computation.6 | loop fusion | flops 497664 | bytes 1990656 | tf_op jit(solution)/shard_map/concatenate | solution.py:54
  23.5 6.2 %shard_map.86 = (f32[8,8,128]{2,1,0:T(8,128)}, f32[8,8,128]{2,1,0:T(8,128)}) custom-call(f32[4,2,3,9,9,128]{5,4,3,2,1,0:T(8,128)} %pad_maximum_fusion.extended_ref, f32[24,24]{1,0:T(8,128)} %stiffness_ref.1, f32[24,24]{1,0:T(8,128)} %mass_ref.1), custom_call_target="tpu_custom_call" | custom-call | flops 607125504 | bytes 1065472 | tf_op jit(solution)/shard_map/pallas_call | solution.py:265
  29.7 2.0 %fusion.106 = (f32[8,8,128]{2,1,0:T(8,128)S(1)}, pred[8,8,128]{2,1,0:T(8,128)(4,1)S(1)}) fusion(f32[8,8,128]{2,1,0:T(8,128)} %get-tuple-element.4, f32[12,10,128]{2,1,0:T(8,128)S(1)} %get-tuple-element.15, f32[12,12,132]{2,1,0:T(8,128)S(1)} %select_maximum_fusion.4, f32[2,8,128]{2,1,0:T(8,128)S(1)} %slice_bitcast_fusion.2, f32[8,8,128]{2,1,0:T(8,128)S(1)} %copy-done, ...), kind=kLoop, calls=%fused_computation.136 | loop fusion | flops 3055616 | bytes 6119424 | tf_op jit(solution)/shard_map/div | solution.py:312
  31.8 1.3 collective-permute-start.5
  33.1 6.0 %collective-permute-start.4 = (f32[16,128]{1,0:T(8,128)S(1)}, f32[16,128]{1,0:T(8,128)S(1)}, u32[]{:S(2)}, u32[]{:S(2)}) collective-permute-start(f32[16,128]{1,0:T(8,128)S(1)} %get-tuple-element.20), channel_id=1, source_target_pairs={{0,16},{16,32},{32,48},{48,64},{64,80},{80,96},{96,112},{112,128},... | collective-permute-start | bytes 24584 | tf_op jit(solution)/shard_map/ppermute | solution.py:26
  39.9 1.9 %collective-permute-start.6 = (f32[24,128]{1,0:T(8,128)S(1)}, f32[24,128]{1,0:T(8,128)S(1)}, u32[]{:S(2)}, u32[]{:S(2)}) collective-permute-start(f32[24,128]{1,0:T(8,128)S(1)} %bitcast.108), channel_id=1, source_target_pairs={{0,1},{1,2},{2,3},{3,4},{4,5},{5,6},{6,7},{7,8},{8,9},{9,10},{10,1... | collective-permute-start | bytes 36872 | tf_op jit(solution)/shard_map/ppermute | solution.py:26
  41.8 6.6 %collective-permute-start.7 = (f32[24,128]{1,0:T(8,128)S(1)}, f32[24,128]{1,0:T(8,128)S(1)}, u32[]{:S(2)}, u32[]{:S(2)}) collective-permute-start(f32[24,128]{1,0:T(8,128)S(1)} %bitcast.107), channel_id=1, source_target_pairs={{1,0},{2,1},{3,2},{4,3},{5,4},{6,5},{7,6},{8,7},{9,8},{10,9},{11,1... | collective-permute-start | bytes 36872 | tf_op jit(solution)/shard_map/ppermute | solution.py:29
  48.6 1.2 collective-permute-done.7
  50.6 0.9 fusion.4
  51.9 1.9 %collective-permute-start.8 = (f32[32,128]{1,0:T(8,128)S(1)}, f32[32,128]{1,0:T(8,128)S(1)}, u32[]{:S(2)}, u32[]{:S(2)}) collective-permute-start(f32[32,128]{1,0:T(8,128)S(1)} %pad_bitcast_fusion), channel_id=1, source_target_pairs={{0,1},{1,0},{2,3},{3,2},{4,5},{5,4},{6,7},{7,6},{8,9},{9,8},{10,11... | collective-permute-start | bytes 49160 | tf_op jit(solution)/shard_map/ppermute | solution.py:68
  53.8 3.7 %collective-permute-done.8 = f32[32,128]{1,0:T(8,128)S(1)} collective-permute-done((f32[32,128]{1,0:T(8,128)S(1)}, f32[32,128]{1,0:T(8,128)S(1)}, u32[]{:S(2)}, u32[]{:S(2)}) %collective-permute-start.8) | collective-permute-done | bytes 16416 | tf_op jit(solution)/shard_map/ppermute | solution.py:68
  57.6 1.9 %collective-permute-start.9 = (f32[32,128]{1,0:T(8,128)S(1)}, f32[32,128]{1,0:T(8,128)S(1)}, u32[]{:S(2)}, u32[]{:S(2)}) collective-permute-start(f32[32,128]{1,0:T(8,128)S(1)} %fusion.296), channel_id=1, source_target_pairs={{0,2},{1,3},{2,0},{3,1},{4,6},{5,7},{6,4},{7,5},{8,10},{9,11},{10,... | collective-permute-start | bytes 49160 | tf_op jit(solution)/shard_map/ppermute | solution.py:68
  59.5 4.6 %collective-permute-done.9 = f32[32,128]{1,0:T(8,128)S(1)} collective-permute-done((f32[32,128]{1,0:T(8,128)S(1)}, f32[32,128]{1,0:T(8,128)S(1)}, u32[]{:S(2)}, u32[]{:S(2)}) %collective-permute-start.9) | collective-permute-done | bytes 16416 | tf_op jit(solution)/shard_map/ppermute | solution.py:68
  64.1 3.1 %collective-permute-start.10 = (f32[32,128]{1,0:T(8,128)S(1)}, f32[32,128]{1,0:T(8,128)S(1)}, u32[]{:S(2)}, u32[]{:S(2)}) collective-permute-start(f32[32,128]{1,0:T(8,128)S(1)} %fusion.298), channel_id=1, source_target_pairs={{0,4},{1,5},{2,6},{3,7},{4,0},{5,1},{6,2},{7,3},{8,12},{9,13},{10,... | collective-permute-start | bytes 49160 | tf_op jit(solution)/shard_map/ppermute | solution.py:68
  67.2 2.5 %collective-permute-done.10 = f32[32,128]{1,0:T(8,128)S(1)} collective-permute-done((f32[32,128]{1,0:T(8,128)S(1)}, f32[32,128]{1,0:T(8,128)S(1)}, u32[]{:S(2)}, u32[]{:S(2)}) %collective-permute-start.10) | collective-permute-done | bytes 16416 | tf_op jit(solution)/shard_map/ppermute | solution.py:68
  69.7 3.7 %collective-permute-start.11 = (f32[32,128]{1,0:T(8,128)S(1)}, f32[32,128]{1,0:T(8,128)S(1)}, u32[]{:S(2)}, u32[]{:S(2)}) collective-permute-start(f32[32,128]{1,0:T(8,128)S(1)} %add.1202), channel_id=1, source_target_pairs={{0,8},{1,9},{2,10},{3,11},{4,12},{5,13},{6,14},{7,15},{8,0},{9,1},... | collective-permute-start | bytes 49160 | tf_op jit(solution)/shard_map/ppermute | solution.py:68
  73.4 3.5 %collective-permute-done.11 = f32[32,128]{1,0:T(8,128)S(1)} collective-permute-done((f32[32,128]{1,0:T(8,128)S(1)}, f32[32,128]{1,0:T(8,128)S(1)}, u32[]{:S(2)}, u32[]{:S(2)}) %collective-permute-start.11) | collective-permute-done | bytes 16416 | tf_op jit(solution)/shard_map/ppermute | solution.py:68
  76.8 3.8 %collective-permute-start.12 = (f32[32,128]{1,0:T(8,128)S(1)}, f32[32,128]{1,0:T(8,128)S(1)}, u32[]{:S(2)}, u32[]{:S(2)}) collective-permute-start(f32[32,128]{1,0:T(8,128)S(1)} %add.1203), channel_id=1, source_target_pairs={{0,16},{16,0},{32,48},{48,32},{64,80},{80,64},{96,112},{112,96},{1... | collective-permute-start | bytes 49160 | tf_op jit(solution)/shard_map/ppermute | solution.py:68
  81.5 14.0 %collective-permute-start.13 = (f32[32,128]{1,0:T(8,128)S(1)}, f32[32,128]{1,0:T(8,128)S(1)}, u32[]{:S(2)}, u32[]{:S(2)}) collective-permute-start(f32[32,128]{1,0:T(8,128)S(1)} %add.1204), channel_id=1, source_target_pairs={{0,32},{16,48},{32,0},{48,16},{64,96},{80,112},{96,64},{112,80},{1... | collective-permute-start | bytes 49160 | tf_op jit(solution)/shard_map/ppermute | solution.py:68
  95.6 1.7 %collective-permute-done.13 = f32[32,128]{1,0:T(8,128)S(1)} collective-permute-done((f32[32,128]{1,0:T(8,128)S(1)}, f32[32,128]{1,0:T(8,128)S(1)}, u32[]{:S(2)}, u32[]{:S(2)}) %collective-permute-start.13) | collective-permute-done | bytes 16416 | tf_op jit(solution)/shard_map/ppermute | solution.py:68
  97.3 8.2 %collective-permute-start.14 = (f32[32,128]{1,0:T(8,128)S(1)}, f32[32,128]{1,0:T(8,128)S(1)}, u32[]{:S(2)}, u32[]{:S(2)}) collective-permute-start(f32[32,128]{1,0:T(8,128)S(1)} %add.1205), channel_id=1, source_target_pairs={{0,64},{16,80},{32,96},{48,112},{64,0},{80,16},{96,32},{112,48},{1... | collective-permute-start | bytes 49160 | tf_op jit(solution)/shard_map/ppermute | solution.py:68
  105.5 1.7 %collective-permute-done.14 = f32[32,128]{1,0:T(8,128)S(1)} collective-permute-done((f32[32,128]{1,0:T(8,128)S(1)}, f32[32,128]{1,0:T(8,128)S(1)}, u32[]{:S(2)}, u32[]{:S(2)}) %collective-permute-start.14) | collective-permute-done | bytes 16416 | tf_op jit(solution)/shard_map/ppermute | solution.py:68
  107.2 6.1 %collective-permute-start.15 = (f32[32,128]{1,0:T(8,128)S(1)}, f32[32,128]{1,0:T(8,128)S(1)}, u32[]{:S(2)}, u32[]{:S(2)}) collective-permute-start(f32[32,128]{1,0:T(8,128)S(1)} %add.1206), channel_id=1, source_target_pairs={{0,128},{16,144},{32,160},{48,176},{64,192},{80,208},{96,224},{112... | collective-permute-start | bytes 49160 | tf_op jit(solution)/shard_map/ppermute | solution.py:68
  113.3 1.7 %collective-permute-done.15 = f32[32,128]{1,0:T(8,128)S(1)} collective-permute-done((f32[32,128]{1,0:T(8,128)S(1)}, f32[32,128]{1,0:T(8,128)S(1)}, u32[]{:S(2)}, u32[]{:S(2)}) %collective-permute-start.15) | collective-permute-done | bytes 16416 | tf_op jit(solution)/shard_map/ppermute | solution.py:68
  115.0 11.7 %collective-permute-start.16 = (f32[32,128]{1,0:T(8,128)S(1)}, f32[32,128]{1,0:T(8,128)S(1)}, u32[]{:S(2)}, u32[]{:S(2)}) collective-permute-start(f32[32,128]{1,0:T(8,128)S(1)} %add.1207), channel_id=1, source_target_pairs={{0,256},{16,272},{32,288},{48,304},{64,320},{80,336},{96,352},{112... | collective-permute-start | bytes 49160 | tf_op jit(solution)/shard_map/ppermute | solution.py:68
  126.7 1.7 %collective-permute-done.16 = f32[32,128]{1,0:T(8,128)S(1)} collective-permute-done((f32[32,128]{1,0:T(8,128)S(1)}, f32[32,128]{1,0:T(8,128)S(1)}, u32[]{:S(2)}, u32[]{:S(2)}) %collective-permute-start.16) | collective-permute-done | bytes 16416 | tf_op jit(solution)/shard_map/ppermute | solution.py:68
  (74 shorter events, 6.3 us)
Async XLA Ops:
  0.6 2.0 %copy-start = (f32[8,8,128]{2,1,0:T(8,128)S(1)}, f32[8,8,128]{2,1,0:T(8,128)}, u32[]{:S(2)}) copy-start(f32[8,8,128]{2,1,0:T(8,128)} %param.7) | copy-start | bytes 98308
  2.7 4.5 %collective-permute-start.1 = (f32[208,128]{1,0:T(8,128)S(1)}, f32[208,128]{1,0:T(8,128)S(1)}, u32[]{:S(2)}, u32[]{:S(2)}) collective-permute-start(f32[208,128]{1,0:T(8,128)S(1)} %pad_maximum_fusion.3), channel_id=1, source_target_pairs={{16,0},{32,16},{48,32},{64,48},{80,64},{96,80},{112,96},{128,112},... | collective-permute-start | bytes 319496 | tf_op jit(solution)/shard_map/ppermute | solution.py:46
  4.0 3.8 %collective-permute-start = (f32[16,128]{1,0:T(8,128)S(1)}, f32[16,128]{1,0:T(8,128)S(1)}, u32[]{:S(2)}, u32[]{:S(2)}) collective-permute-start(f32[16,128]{1,0:T(8,128)S(1)} %get-tuple-element.22), channel_id=1, source_target_pairs={{0,16},{16,32},{32,48},{48,64},{64,80},{80,96},{96,112},{112,128},... | collective-permute-start | bytes 24584 | tf_op jit(solution)/shard_map/ppermute | solution.py:50
  7.8 8.2 %collective-permute-start.3 = (f32[240,128]{1,0:T(8,128)S(1)}, f32[240,128]{1,0:T(8,128)S(1)}, u32[]{:S(2)}, u32[]{:S(2)}) collective-permute-start(f32[240,128]{1,0:T(8,128)S(1)} %pad_maximum_fusion.1), channel_id=1, source_target_pairs={{1,0},{2,1},{3,2},{4,3},{5,4},{6,5},{7,6},{8,7},{9,8},{10,9},{11,1... | collective-permute-start | bytes 368648 | tf_op jit(solution)/shard_map/ppermute | solution.py:46
  13.6 8.3 %collective-permute-start.2 = (f32[24,128]{1,0:T(8,128)S(1)}, f32[24,128]{1,0:T(8,128)S(1)}, u32[]{:S(2)}, u32[]{:S(2)}) collective-permute-start(f32[24,128]{1,0:T(8,128)S(1)} %bitcast.106), channel_id=1, source_target_pairs={{0,1},{1,2},{2,3},{3,4},{4,5},{5,6},{6,7},{7,8},{8,9},{9,10},{10,1... | collective-permute-start | bytes 36872 | tf_op jit(solution)/shard_map/ppermute | solution.py:50
  23.5 6.2 %copy-start.2 = (s32[8,8,128]{2,1,0:T(8,128)S(1)}, s32[8,8,128]{2,1,0:T(8,128)}, u32[]{:S(2)}) copy-start(s32[8,8,128]{2,1,0:T(8,128)} %param.8) | copy-start | bytes 98308
  29.7 18.7 %copy-start.3 = (f32[63,64]{0,1:T(8,128)S(1)}, f32[63,64]{0,1:T(8,128)}, u32[]{:S(2)}) copy-start(f32[63,64]{0,1:T(8,128)} %constant.25.clone.1) | copy-start | bytes 48388
  31.8 7.3 %collective-permute-start.5 = (f32[16,128]{1,0:T(8,128)S(1)}, f32[16,128]{1,0:T(8,128)S(1)}, u32[]{:S(2)}, u32[]{:S(2)}) collective-permute-start(f32[16,128]{1,0:T(8,128)S(1)} %get-tuple-element.21), channel_id=1, source_target_pairs={{16,0},{32,16},{48,32},{64,48},{80,64},{96,80},{112,96},{128,112},... | collective-permute-start | bytes 24584 | tf_op jit(solution)/shard_map/ppermute | solution.py:29
  33.1 6.8 %collective-permute-start.4 = (f32[16,128]{1,0:T(8,128)S(1)}, f32[16,128]{1,0:T(8,128)S(1)}, u32[]{:S(2)}, u32[]{:S(2)}) collective-permute-start(f32[16,128]{1,0:T(8,128)S(1)} %get-tuple-element.20), channel_id=1, source_target_pairs={{0,16},{16,32},{32,48},{48,64},{64,80},{80,96},{96,112},{112,128},... | collective-permute-start | bytes 24584 | tf_op jit(solution)/shard_map/ppermute | solution.py:26
  39.9 8.7 %collective-permute-start.6 = (f32[24,128]{1,0:T(8,128)S(1)}, f32[24,128]{1,0:T(8,128)S(1)}, u32[]{:S(2)}, u32[]{:S(2)}) collective-permute-start(f32[24,128]{1,0:T(8,128)S(1)} %bitcast.108), channel_id=1, source_target_pairs={{0,1},{1,2},{2,3},{3,4},{4,5},{5,6},{6,7},{7,8},{8,9},{9,10},{10,1... | collective-permute-start | bytes 36872 | tf_op jit(solution)/shard_map/ppermute | solution.py:26
  41.8 8.0 %collective-permute-start.7 = (f32[24,128]{1,0:T(8,128)S(1)}, f32[24,128]{1,0:T(8,128)S(1)}, u32[]{:S(2)}, u32[]{:S(2)}) collective-permute-start(f32[24,128]{1,0:T(8,128)S(1)} %bitcast.107), channel_id=1, source_target_pairs={{1,0},{2,1},{3,2},{4,3},{5,4},{6,5},{7,6},{8,7},{9,8},{10,9},{11,1... | collective-permute-start | bytes 36872 | tf_op jit(solution)/shard_map/ppermute | solution.py:29
  50.0 76.7 %copy-start.4 = (f32[64]{0:T(128)S(1)}, f32[64]{0:T(128)}, u32[]{:S(2)}) copy-start(f32[64]{0:T(128)} %param.13) | copy-start | bytes 772
  50.6 79.0 %copy-start.1 = (f32[8,8,128]{2,1,0:T(8,128)}, f32[8,8,128]{2,1,0:T(8,128)S(1)}, u32[]{:S(2)}) copy-start(f32[8,8,128]{2,1,0:T(8,128)S(1)} %get-tuple-element.7) | copy-start | bytes 98308
  51.9 5.6 %collective-permute-start.8 = (f32[32,128]{1,0:T(8,128)S(1)}, f32[32,128]{1,0:T(8,128)S(1)}, u32[]{:S(2)}, u32[]{:S(2)}) collective-permute-start(f32[32,128]{1,0:T(8,128)S(1)} %pad_bitcast_fusion), channel_id=1, source_target_pairs={{0,1},{1,0},{2,3},{3,2},{4,5},{5,4},{6,7},{7,6},{8,9},{9,8},{10,11... | collective-permute-start | bytes 49160 | tf_op jit(solution)/shard_map/ppermute | solution.py:68
  57.6 6.5 %collective-permute-start.9 = (f32[32,128]{1,0:T(8,128)S(1)}, f32[32,128]{1,0:T(8,128)S(1)}, u32[]{:S(2)}, u32[]{:S(2)}) collective-permute-start(f32[32,128]{1,0:T(8,128)S(1)} %fusion.296), channel_id=1, source_target_pairs={{0,2},{1,3},{2,0},{3,1},{4,6},{5,7},{6,4},{7,5},{8,10},{9,11},{10,... | collective-permute-start | bytes 49160 | tf_op jit(solution)/shard_map/ppermute | solution.py:68
  64.1 5.6 %collective-permute-start.10 = (f32[32,128]{1,0:T(8,128)S(1)}, f32[32,128]{1,0:T(8,128)S(1)}, u32[]{:S(2)}, u32[]{:S(2)}) collective-permute-start(f32[32,128]{1,0:T(8,128)S(1)} %fusion.298), channel_id=1, source_target_pairs={{0,4},{1,5},{2,6},{3,7},{4,0},{5,1},{6,2},{7,3},{8,12},{9,13},{10,... | collective-permute-start | bytes 49160 | tf_op jit(solution)/shard_map/ppermute | solution.py:68
  69.7 7.1 %collective-permute-start.11 = (f32[32,128]{1,0:T(8,128)S(1)}, f32[32,128]{1,0:T(8,128)S(1)}, u32[]{:S(2)}, u32[]{:S(2)}) collective-permute-start(f32[32,128]{1,0:T(8,128)S(1)} %add.1202), channel_id=1, source_target_pairs={{0,8},{1,9},{2,10},{3,11},{4,12},{5,13},{6,14},{7,15},{8,0},{9,1},... | collective-permute-start | bytes 49160 | tf_op jit(solution)/shard_map/ppermute | solution.py:68
  76.8 4.7 %collective-permute-start.12 = (f32[32,128]{1,0:T(8,128)S(1)}, f32[32,128]{1,0:T(8,128)S(1)}, u32[]{:S(2)}, u32[]{:S(2)}) collective-permute-start(f32[32,128]{1,0:T(8,128)S(1)} %add.1203), channel_id=1, source_target_pairs={{0,16},{16,0},{32,48},{48,32},{64,80},{80,64},{96,112},{112,96},{1... | collective-permute-start | bytes 49160 | tf_op jit(solution)/shard_map/ppermute | solution.py:68
  81.5 15.8 %collective-permute-start.13 = (f32[32,128]{1,0:T(8,128)S(1)}, f32[32,128]{1,0:T(8,128)S(1)}, u32[]{:S(2)}, u32[]{:S(2)}) collective-permute-start(f32[32,128]{1,0:T(8,128)S(1)} %add.1204), channel_id=1, source_target_pairs={{0,32},{16,48},{32,0},{48,16},{64,96},{80,112},{96,64},{112,80},{1... | collective-permute-start | bytes 49160 | tf_op jit(solution)/shard_map/ppermute | solution.py:68
  97.3 9.9 %collective-permute-start.14 = (f32[32,128]{1,0:T(8,128)S(1)}, f32[32,128]{1,0:T(8,128)S(1)}, u32[]{:S(2)}, u32[]{:S(2)}) collective-permute-start(f32[32,128]{1,0:T(8,128)S(1)} %add.1205), channel_id=1, source_target_pairs={{0,64},{16,80},{32,96},{48,112},{64,0},{80,16},{96,32},{112,48},{1... | collective-permute-start | bytes 49160 | tf_op jit(solution)/shard_map/ppermute | solution.py:68
  107.2 7.8 %collective-permute-start.15 = (f32[32,128]{1,0:T(8,128)S(1)}, f32[32,128]{1,0:T(8,128)S(1)}, u32[]{:S(2)}, u32[]{:S(2)}) collective-permute-start(f32[32,128]{1,0:T(8,128)S(1)} %add.1206), channel_id=1, source_target_pairs={{0,128},{16,144},{32,160},{48,176},{64,192},{80,208},{96,224},{112... | collective-permute-start | bytes 49160 | tf_op jit(solution)/shard_map/ppermute | solution.py:68
  115.0 13.4 %collective-permute-start.16 = (f32[32,128]{1,0:T(8,128)S(1)}, f32[32,128]{1,0:T(8,128)S(1)}, u32[]{:S(2)}, u32[]{:S(2)}) collective-permute-start(f32[32,128]{1,0:T(8,128)S(1)} %add.1207), channel_id=1, source_target_pairs={{0,256},{16,272},{32,288},{48,304},{64,320},{80,336},{96,352},{112... | collective-permute-start | bytes 49160 | tf_op jit(solution)/shard_map/ppermute | solution.py:68

commit v17 on v10

--- a/solution.py
+++ b/solution.py
@@ -1,3 +1,4 @@
+import functools
 import math
 
 import jax
@@ -177,13 +178,8 @@
     lax.fori_loop(0, cells_x, over_x, 0)
 
 
-def mxu_energy_kernel(
-    extended_ref, stiffness_ref, mass_ref, stiff_out, mass_out, coupling_ref, state_rows,
-    adjoint_rows, products,
-):
-    pair_count = extended_ref.shape[0]
-    cells_x, cells_y, cells_z = stiff_out.shape
-    dofs = 3 * len(CORNERS)
+def coupling_kernel(cells_y, stiffness_ref, mass_ref, coupling_ref):
+    dofs = stiffness_ref.shape[0]
     wide = dofs * cells_y
     spread_rows = (
         lax.broadcasted_iota(jnp.int32, (wide, dofs), 0) // cells_y
@@ -206,6 +202,15 @@
             spread_rows, spread, precision=lax.Precision.HIGHEST, preferred_element_type=jnp.float32
         )
         coupling_ref[pl.ds(block * wide, wide), :] = jnp.where(same_y, spread, 0.0)
+
+
+def mxu_energy_kernel(
+    extended_ref, coupling_ref, stiff_out, mass_out, state_rows, adjoint_rows, products
+):
+    pair_count = extended_ref.shape[0]
+    cells_x, cells_y, cells_z = stiff_out.shape
+    dofs = 3 * len(CORNERS)
+    wide = dofs * cells_y
     lane = lax.broadcasted_iota(jnp.int32, (cells_y, cells_z), 1)
     inside = lane < cells_z - 1
     stiff_out[...] = jnp.zeros(stiff_out.shape, jnp.float32)
@@ -260,26 +265,31 @@
     voxels = cells[0] * cells[1] * cells[2]
     dofs = stiffness.shape[0]
     vmem = pl.BlockSpec(memory_space=pltpu.VMEM)
+    coupling = pl.pallas_call(
+        functools.partial(coupling_kernel, cells[1]),
+        out_shape=jax.ShapeDtypeStruct((2 * dofs * cells[1], dofs * cells[1]), jnp.float32),
+        in_specs=[vmem, vmem],
+        out_specs=vmem,
+    )(stiffness, mass_matrix)
     return pl.pallas_call(
         mxu_energy_kernel,
         out_shape=(
             jax.ShapeDtypeStruct(cells, jnp.float32),
             jax.ShapeDtypeStruct(cells, jnp.float32),
         ),
-        in_specs=[vmem, vmem, vmem],
+        in_specs=[vmem, vmem],
         out_specs=(vmem, vmem),
         scratch_shapes=[
-            pltpu.VMEM((2 * dofs * cells[1], dofs * cells[1]), jnp.float32),
             pltpu.VMEM((dofs * cells[1], cells[0] * cells[2]), jnp.float32),
             pltpu.VMEM((dofs * cells[1], cells[0] * cells[2]), jnp.float32),
             pltpu.VMEM((2 * dofs * cells[1], cells[0] * cells[2]), jnp.float32),
         ],
         cost_estimate=pl.CostEstimate(
             flops=pair_count * (4 * (dofs * cells[1]) ** 2 * cells[0] * cells[2] + 4 * dofs * voxels),
-            bytes_accessed=extended.size * 4 + 2 * stiffness.size * 4 + 2 * voxels * 4,
+            bytes_accessed=extended.size * 4 + coupling.size * 4 + 2 * voxels * 4,
             transcendentals=0,
         ),
-    )(extended, stiffness, mass_matrix)
+    )(extended, coupling)
 
 
 def shards(design, passive, basis_pairs, supports, stiffness, mass_matrix, volume_fraction):

time: 127 us -> 127 us (level)
  Pallas kernels: 6.22 us -> 7.78 us
    pallas_call x0 -> x1, Pallas kernels: none -> 2.16 us  [element_energies(): pl.pallas_call(functools.partial(coupling_kernel, cells[1]), out_shape=ja...]
  transfers between devices with their start and end apart: 17 -> 17, of which waited for: 13 -> 12; matrix products, arithmetic and copies ran while one was open for 1% -> 1% of each run, Pallas kernels for 5% -> 6%
where the time goes in v17:
time: 127 us; the launch traced here: 125 us
  starting transfers between devices  82.5 us (65%)
  waiting for transfers between devices  24.6 us (19%)
  other arithmetic  8.45 us (7%)
  Pallas kernels  7.78 us (6%)
    ppermute x9, starting transfers between devices, butterfly_sum(): lax.ppermute(value, axis, [(i, i ^ stride) for i in range(count)])  53.7 us
    ppermute x9, waiting for transfers between devices, butterfly_sum(): lax.ppermute(value, axis, [(i, i ^ stride) for i in range(count)])  22 us
    ppermute x2, starting transfers between devices, with_halo(): lax.ppermute(tail, axis, [(i, (i + 1) % count) for i in range(ends)])  8.65 us
    ppermute x2, starting transfers between devices, with_halo(): lax.ppermute(head, axis, [((i + 1) % count, i) for i in range(ends)])  8.09 us
    ppermute x2, starting transfers between devices, front_exchange(): lax.ppermute(packed, axis, [((i + 1) % count, i) for i in range(ends)])  7.07 us
    pallas_call x1, Pallas kernels, element_energies(): pl.pallas_call(mxu_energy_kernel, out_shape=(jax.ShapeDtypeStruct(cells,...  5.61 us
    ppermute x2, starting transfers between devices, front_exchange(): tail = lax.ppermute(tail, axis, [(i, (i + 1) % count) for i in range(ends)])  4.95 us
  transfers between devices with their start and end apart: 17, of which 12 were waited for; matrix products, arithmetic and copies ran while one was open for 1% of the time, Pallas kernels for 6%

profile of v17, /device:TPU:6, one launch (start us, length us, event | category | flops | bytes accessed | tf_op | source)
XLA Modules:
  0.0 125.1 jit_solution(15988660775075795797)
XLA Ops:
  1.4 1.2 broadcast_multiply_fusion
  2.7 1.3 %collective-permute-start.1 = (f32[208,128]{1,0:T(8,128)S(1)}, f32[208,128]{1,0:T(8,128)S(1)}, u32[]{:S(2)}, u32[]{:S(2)}) collective-permute-start(f32[208,128]{1,0:T(8,128)S(1)} %pad_maximum_fusion.3), channel_id=1, source_target_pairs={{16,0},{32,16},{48,32},{64,48},{80,64},{96,80},{112,96},{128,112},... | collective-permute-start | bytes 319496 | tf_op jit(solution)/shard_map/ppermute | solution.py:47
  4.0 3.0 %collective-permute-start = (f32[2,8,128]{2,1,0:T(8,128)S(1)}, f32[2,8,128]{2,1,0:T(8,128)S(1)}, u32[]{:S(2)}, u32[]{:S(2)}) collective-permute-start(f32[2,8,128]{2,1,0:T(8,128)S(1)} %get-tuple-element.23), channel_id=1, source_target_pairs={{0,16},{16,32},{32,48},{48,64},{64,80},{80,96},{96,112},{112,128},... | collective-permute-start | bytes 24584 | tf_op jit(solution)/shard_map/ppermute | solution.py:51
  7.3 2.2 %shard_map.86.coupling_ref = f32[384,192]{1,0:T(8,128)} custom-call(f32[24,24]{1,0:T(8,128)} %stiffness_ref.1, f32[24,24]{1,0:T(8,128)} %mass_ref.1), custom_call_target="tpu_custom_call" | custom-call | tf_op jit(solution)/shard_map/pallas_call | solution.py:268
  9.6 5.8 %collective-permute-start.3 = (f32[240,128]{1,0:T(8,128)S(1)}, f32[240,128]{1,0:T(8,128)S(1)}, u32[]{:S(2)}, u32[]{:S(2)}) collective-permute-start(f32[240,128]{1,0:T(8,128)S(1)} %pad_maximum_fusion.1), channel_id=1, source_target_pairs={{1,0},{2,1},{3,2},{4,3},{5,4},{6,5},{7,6},{8,7},{9,8},{10,9},{11,1... | collective-permute-start | bytes 368648 | tf_op jit(solution)/shard_map/ppermute | solution.py:47
  15.4 1.9 %collective-permute-start.2 = (f32[12,2,128]{2,1,0:T(2,128)S(1)}, f32[12,2,128]{2,1,0:T(2,128)S(1)}, u32[]{:S(2)}, u32[]{:S(2)}) collective-permute-start(f32[12,2,128]{2,1,0:T(2,128)S(1)} %get-tuple-element.16), channel_id=1, source_target_pairs={{0,1},{1,2},{2,3},{3,4},{4,5},{5,6},{6,7},{7,8},{8,9},{9,10},{10,1... | collective-permute-start | bytes 36872 | tf_op jit(solution)/shard_map/ppermute | solution.py:51
  17.8 1.4 %pad_maximum_fusion.extended_ref = f32[4,2,3,9,9,128]{5,4,3,2,1,0:T(8,128)} fusion(f32[4,2,3,9,1,128]{5,4,3,2,1,0:T(1,128)S(1)} %bitcast.65, f32[4,2,3,1,8,128]{5,4,3,2,1,0:T(8,128)S(1)} %bitcast.64, f32[4,2,3,8,8,128]{5,4,3,2,1,0:T(8,128)S(1)} %broadcast_multiply_fusion), kind=kLoop, calls=%fused_computation.6 | loop fusion | flops 497664 | bytes 1990656 | tf_op jit(solution)/shard_map/concatenate | solution.py:53
  19.2 5.6 %shard_map.87 = (f32[8,8,128]{2,1,0:T(8,128)}, f32[8,8,128]{2,1,0:T(8,128)}) custom-call(f32[4,2,3,9,9,128]{5,4,3,2,1,0:T(8,128)} %pad_maximum_fusion.extended_ref, f32[384,192]{1,0:T(8,128)} %shard_map.86.coupling_ref), custom_call_target="tpu_custom_call" | custom-call | flops 607125504 | bytes 1355776 | tf_op jit(solution)/shard_map/pallas_call | solution.py:274
  25.0 2.0 %fusion.82 = (f32[8,8,128]{2,1,0:T(8,128)S(1)}, pred[8,8,128]{2,1,0:T(8,128)(4,1)S(1)}) fusion(f32[8,8,128]{2,1,0:T(8,128)} %get-tuple-element.4, f32[12,10,128]{2,1,0:T(8,128)S(1)} %get-tuple-element.15, f32[12,12,132]{2,1,0:T(8,128)S(1)} %select_maximum_fusion.4, f32[2,8,128]{2,1,0:T(8,128)S(1)} %slice_bitcast_fusion, f32[8,8,128]{2,1,0:T(8,128)S(1)} %copy-done, ...), kind=kLoop, calls=%fused_computation.110 | loop fusion | flops 3039232 | bytes 6176768 | tf_op jit(solution)/shard_map/div | solution.py:320
  27.0 1.3 %collective-permute-start.5 = (f32[2,8,128]{2,1,0:T(8,128)S(1)}, f32[2,8,128]{2,1,0:T(8,128)S(1)}, u32[]{:S(2)}, u32[]{:S(2)}) collective-permute-start(f32[2,8,128]{2,1,0:T(8,128)S(1)} %get-tuple-element.22), channel_id=1, source_target_pairs={{16,0},{32,16},{48,32},{64,48},{80,64},{96,80},{112,96},{128,112},... | collective-permute-start | bytes 24584 | tf_op jit(solution)/shard_map/ppermute | solution.py:30
  28.3 6.7 %collective-permute-start.4 = (f32[2,8,128]{2,1,0:T(8,128)S(1)}, f32[2,8,128]{2,1,0:T(8,128)S(1)}, u32[]{:S(2)}, u32[]{:S(2)}) collective-permute-start(f32[2,8,128]{2,1,0:T(8,128)S(1)} %get-tuple-element.21), channel_id=1, source_target_pairs={{0,16},{16,32},{32,48},{48,64},{64,80},{80,96},{96,112},{112,128},... | collective-permute-start | bytes 24584 | tf_op jit(solution)/shard_map/ppermute | solution.py:28
  35.9 1.9 %collective-permute-start.6 = (f32[12,2,128]{2,1,0:T(2,128)S(1)}, f32[12,2,128]{2,1,0:T(2,128)S(1)}, u32[]{:S(2)}, u32[]{:S(2)}) collective-permute-start(f32[12,2,128]{2,1,0:T(2,128)S(1)} %get-tuple-element.12), channel_id=1, source_target_pairs={{0,1},{1,2},{2,3},{3,4},{4,5},{5,6},{6,7},{7,8},{8,9},{9,10},{10,1... | collective-permute-start | bytes 36872 | tf_op jit(solution)/shard_map/ppermute | solution.py:28
  37.8 6.8 %collective-permute-start.7 = (f32[12,2,128]{2,1,0:T(2,128)S(1)}, f32[12,2,128]{2,1,0:T(2,128)S(1)}, u32[]{:S(2)}, u32[]{:S(2)}) collective-permute-start(f32[12,2,128]{2,1,0:T(2,128)S(1)} %get-tuple-element.13), channel_id=1, source_target_pairs={{1,0},{2,1},{3,2},{4,3},{5,4},{6,5},{7,6},{8,7},{9,8},{10,9},{11,1... | collective-permute-start | bytes 36872 | tf_op jit(solution)/shard_map/ppermute | solution.py:30
  44.8 1.2 collective-permute-done.7
  46.8 0.9 fusion.4
  48.1 1.9 %collective-permute-start.8 = (f32[32,128]{1,0:T(8,128)S(1)}, f32[32,128]{1,0:T(8,128)S(1)}, u32[]{:S(2)}, u32[]{:S(2)}) collective-permute-start(f32[32,128]{1,0:T(8,128)S(1)} %pad_bitcast_fusion), channel_id=1, source_target_pairs={{0,1},{1,0},{2,3},{3,2},{4,5},{5,4},{6,7},{7,6},{8,9},{9,8},{10,11... | collective-permute-start | bytes 49160 | tf_op jit(solution)/shard_map/ppermute | solution.py:67
  50.0 3.7 %collective-permute-done.8 = f32[32,128]{1,0:T(8,128)S(1)} collective-permute-done((f32[32,128]{1,0:T(8,128)S(1)}, f32[32,128]{1,0:T(8,128)S(1)}, u32[]{:S(2)}, u32[]{:S(2)}) %collective-permute-start.8) | collective-permute-done | bytes 16416 | tf_op jit(solution)/shard_map/ppermute | solution.py:67
  53.7 1.9 %collective-permute-start.9 = (f32[32,128]{1,0:T(8,128)S(1)}, f32[32,128]{1,0:T(8,128)S(1)}, u32[]{:S(2)}, u32[]{:S(2)}) collective-permute-start(f32[32,128]{1,0:T(8,128)S(1)} %fusion.293), channel_id=1, source_target_pairs={{0,2},{1,3},{2,0},{3,1},{4,6},{5,7},{6,4},{7,5},{8,10},{9,11},{10,... | collective-permute-start | bytes 49160 | tf_op jit(solution)/shard_map/ppermute | solution.py:67
  55.7 4.6 %collective-permute-done.9 = f32[32,128]{1,0:T(8,128)S(1)} collective-permute-done((f32[32,128]{1,0:T(8,128)S(1)}, f32[32,128]{1,0:T(8,128)S(1)}, u32[]{:S(2)}, u32[]{:S(2)}) %collective-permute-start.9) | collective-permute-done | bytes 16416 | tf_op jit(solution)/shard_map/ppermute | solution.py:67
  60.3 3.1 %collective-permute-start.10 = (f32[32,128]{1,0:T(8,128)S(1)}, f32[32,128]{1,0:T(8,128)S(1)}, u32[]{:S(2)}, u32[]{:S(2)}) collective-permute-start(f32[32,128]{1,0:T(8,128)S(1)} %fusion.297), channel_id=1, source_target_pairs={{0,4},{1,5},{2,6},{3,7},{4,0},{5,1},{6,2},{7,3},{8,12},{9,13},{10,... | collective-permute-start | bytes 49160 | tf_op jit(solution)/shard_map/ppermute | solution.py:67
  63.4 2.5 %collective-permute-done.10 = f32[32,128]{1,0:T(8,128)S(1)} collective-permute-done((f32[32,128]{1,0:T(8,128)S(1)}, f32[32,128]{1,0:T(8,128)S(1)}, u32[]{:S(2)}, u32[]{:S(2)}) %collective-permute-start.10) | collective-permute-done | bytes 16416 | tf_op jit(solution)/shard_map/ppermute | solution.py:67
  65.9 3.6 %collective-permute-start.11 = (f32[32,128]{1,0:T(8,128)S(1)}, f32[32,128]{1,0:T(8,128)S(1)}, u32[]{:S(2)}, u32[]{:S(2)}) collective-permute-start(f32[32,128]{1,0:T(8,128)S(1)} %add.1202), channel_id=1, source_target_pairs={{0,8},{1,9},{2,10},{3,11},{4,12},{5,13},{6,14},{7,15},{8,0},{9,1},... | collective-permute-start | bytes 49160 | tf_op jit(solution)/shard_map/ppermute | solution.py:67
  69.5 3.5 %collective-permute-done.11 = f32[32,128]{1,0:T(8,128)S(1)} collective-permute-done((f32[32,128]{1,0:T(8,128)S(1)}, f32[32,128]{1,0:T(8,128)S(1)}, u32[]{:S(2)}, u32[]{:S(2)}) %collective-permute-start.11) | collective-permute-done | bytes 16416 | tf_op jit(solution)/shard_map/ppermute | solution.py:67
  73.0 2.2 %collective-permute-start.12 = (f32[32,128]{1,0:T(8,128)S(1)}, f32[32,128]{1,0:T(8,128)S(1)}, u32[]{:S(2)}, u32[]{:S(2)}) collective-permute-start(f32[32,128]{1,0:T(8,128)S(1)} %add.1203), channel_id=1, source_target_pairs={{0,16},{16,0},{32,48},{48,32},{64,80},{80,64},{96,112},{112,96},{1... | collective-permute-start | bytes 49160 | tf_op jit(solution)/shard_map/ppermute | solution.py:67
  76.1 13.7 %collective-permute-start.13 = (f32[32,128]{1,0:T(8,128)S(1)}, f32[32,128]{1,0:T(8,128)S(1)}, u32[]{:S(2)}, u32[]{:S(2)}) collective-permute-start(f32[32,128]{1,0:T(8,128)S(1)} %add.1204), channel_id=1, source_target_pairs={{0,32},{16,48},{32,0},{48,16},{64,96},{80,112},{96,64},{112,80},{1... | collective-permute-start | bytes 49160 | tf_op jit(solution)/shard_map/ppermute | solution.py:67
  89.8 1.7 %collective-permute-done.13 = f32[32,128]{1,0:T(8,128)S(1)} collective-permute-done((f32[32,128]{1,0:T(8,128)S(1)}, f32[32,128]{1,0:T(8,128)S(1)}, u32[]{:S(2)}, u32[]{:S(2)}) %collective-permute-start.13) | collective-permute-done | bytes 16416 | tf_op jit(solution)/shard_map/ppermute | solution.py:67
  91.5 9.4 %collective-permute-start.14 = (f32[32,128]{1,0:T(8,128)S(1)}, f32[32,128]{1,0:T(8,128)S(1)}, u32[]{:S(2)}, u32[]{:S(2)}) collective-permute-start(f32[32,128]{1,0:T(8,128)S(1)} %add.1205), channel_id=1, source_target_pairs={{0,64},{16,80},{32,96},{48,112},{64,0},{80,16},{96,32},{112,48},{1... | collective-permute-start | bytes 49160 | tf_op jit(solution)/shard_map/ppermute | solution.py:67
  100.9 1.7 %collective-permute-done.14 = f32[32,128]{1,0:T(8,128)S(1)} collective-permute-done((f32[32,128]{1,0:T(8,128)S(1)}, f32[32,128]{1,0:T(8,128)S(1)}, u32[]{:S(2)}, u32[]{:S(2)}) %collective-permute-start.14) | collective-permute-done | bytes 16416 | tf_op jit(solution)/shard_map/ppermute | solution.py:67
  102.6 6.1 %collective-permute-start.15 = (f32[32,128]{1,0:T(8,128)S(1)}, f32[32,128]{1,0:T(8,128)S(1)}, u32[]{:S(2)}, u32[]{:S(2)}) collective-permute-start(f32[32,128]{1,0:T(8,128)S(1)} %add.1206), channel_id=1, source_target_pairs={{0,128},{16,144},{32,160},{48,176},{64,192},{80,208},{96,224},{112... | collective-permute-start | bytes 49160 | tf_op jit(solution)/shard_map/ppermute | solution.py:67
  108.7 1.7 %collective-permute-done.15 = f32[32,128]{1,0:T(8,128)S(1)} collective-permute-done((f32[32,128]{1,0:T(8,128)S(1)}, f32[32,128]{1,0:T(8,128)S(1)}, u32[]{:S(2)}, u32[]{:S(2)}) %collective-permute-start.15) | collective-permute-done | bytes 16416 | tf_op jit(solution)/shard_map/ppermute | solution.py:67
  110.4 11.8 %collective-permute-start.16 = (f32[32,128]{1,0:T(8,128)S(1)}, f32[32,128]{1,0:T(8,128)S(1)}, u32[]{:S(2)}, u32[]{:S(2)}) collective-permute-start(f32[32,128]{1,0:T(8,128)S(1)} %add.1207), channel_id=1, source_target_pairs={{0,256},{16,272},{32,288},{48,304},{64,320},{80,336},{96,352},{112... | collective-permute-start | bytes 49160 | tf_op jit(solution)/shard_map/ppermute | solution.py:67
  122.3 1.7 %collective-permute-done.16 = f32[32,128]{1,0:T(8,128)S(1)} collective-permute-done((f32[32,128]{1,0:T(8,128)S(1)}, f32[32,128]{1,0:T(8,128)S(1)}, u32[]{:S(2)}, u32[]{:S(2)}) %collective-permute-start.16) | collective-permute-done | bytes 16416 | tf_op jit(solution)/shard_map/ppermute | solution.py:67
  (76 shorter events, 6.0 us)
Async XLA Ops:
  0.6 2.0 %copy-start = (f32[8,8,128]{2,1,0:T(8,128)S(1)}, f32[8,8,128]{2,1,0:T(8,128)}, u32[]{:S(2)}) copy-start(f32[8,8,128]{2,1,0:T(8,128)} %param.7) | copy-start | bytes 98308
  2.7 6.8 %collective-permute-start.1 = (f32[208,128]{1,0:T(8,128)S(1)}, f32[208,128]{1,0:T(8,128)S(1)}, u32[]{:S(2)}, u32[]{:S(2)}) collective-permute-start(f32[208,128]{1,0:T(8,128)S(1)} %pad_maximum_fusion.3), channel_id=1, source_target_pairs={{16,0},{32,16},{48,32},{64,48},{80,64},{96,80},{112,96},{128,112},... | collective-permute-start | bytes 319496 | tf_op jit(solution)/shard_map/ppermute | solution.py:47
  4.0 5.5 %collective-permute-start = (f32[2,8,128]{2,1,0:T(8,128)S(1)}, f32[2,8,128]{2,1,0:T(8,128)S(1)}, u32[]{:S(2)}, u32[]{:S(2)}) collective-permute-start(f32[2,8,128]{2,1,0:T(8,128)S(1)} %get-tuple-element.23), channel_id=1, source_target_pairs={{0,16},{16,32},{32,48},{48,64},{64,80},{80,96},{96,112},{112,128},... | collective-permute-start | bytes 24584 | tf_op jit(solution)/shard_map/ppermute | solution.py:51
  9.6 8.2 %collective-permute-start.3 = (f32[240,128]{1,0:T(8,128)S(1)}, f32[240,128]{1,0:T(8,128)S(1)}, u32[]{:S(2)}, u32[]{:S(2)}) collective-permute-start(f32[240,128]{1,0:T(8,128)S(1)} %pad_maximum_fusion.1), channel_id=1, source_target_pairs={{1,0},{2,1},{3,2},{4,3},{5,4},{6,5},{7,6},{8,7},{9,8},{10,9},{11,1... | collective-permute-start | bytes 368648 | tf_op jit(solution)/shard_map/ppermute | solution.py:47
  15.4 9.4 %collective-permute-start.2 = (f32[12,2,128]{2,1,0:T(2,128)S(1)}, f32[12,2,128]{2,1,0:T(2,128)S(1)}, u32[]{:S(2)}, u32[]{:S(2)}) collective-permute-start(f32[12,2,128]{2,1,0:T(2,128)S(1)} %get-tuple-element.16), channel_id=1, source_target_pairs={{0,1},{1,2},{2,3},{3,4},{4,5},{5,6},{6,7},{7,8},{8,9},{9,10},{10,1... | collective-permute-start | bytes 36872 | tf_op jit(solution)/shard_map/ppermute | solution.py:51
  19.2 5.8 %copy-start.2 = (s32[8,8,128]{2,1,0:T(8,128)S(1)}, s32[8,8,128]{2,1,0:T(8,128)}, u32[]{:S(2)}) copy-start(s32[8,8,128]{2,1,0:T(8,128)} %param.8) | copy-start | bytes 98308
  25.0 19.6 %copy-start.3 = (f32[63,64]{0,1:T(8,128)S(1)}, f32[63,64]{0,1:T(8,128)}, u32[]{:S(2)}) copy-start(f32[63,64]{0,1:T(8,128)} %constant.25.clone.1) | copy-start | bytes 48388
  27.0 8.0 %collective-permute-start.5 = (f32[2,8,128]{2,1,0:T(8,128)S(1)}, f32[2,8,128]{2,1,0:T(8,128)S(1)}, u32[]{:S(2)}, u32[]{:S(2)}) collective-permute-start(f32[2,8,128]{2,1,0:T(8,128)S(1)} %get-tuple-element.22), channel_id=1, source_target_pairs={{16,0},{32,16},{48,32},{64,48},{80,64},{96,80},{112,96},{128,112},... | collective-permute-start | bytes 24584 | tf_op jit(solution)/shard_map/ppermute | solution.py:30
  28.3 7.6 %collective-permute-start.4 = (f32[2,8,128]{2,1,0:T(8,128)S(1)}, f32[2,8,128]{2,1,0:T(8,128)S(1)}, u32[]{:S(2)}, u32[]{:S(2)}) collective-permute-start(f32[2,8,128]{2,1,0:T(8,128)S(1)} %get-tuple-element.21), channel_id=1, source_target_pairs={{0,16},{16,32},{32,48},{48,64},{64,80},{80,96},{96,112},{112,128},... | collective-permute-start | bytes 24584 | tf_op jit(solution)/shard_map/ppermute | solution.py:28
  35.9 8.9 %collective-permute-start.6 = (f32[12,2,128]{2,1,0:T(2,128)S(1)}, f32[12,2,128]{2,1,0:T(2,128)S(1)}, u32[]{:S(2)}, u32[]{:S(2)}) collective-permute-start(f32[12,2,128]{2,1,0:T(2,128)S(1)} %get-tuple-element.12), channel_id=1, source_target_pairs={{0,1},{1,2},{2,3},{3,4},{4,5},{5,6},{6,7},{7,8},{8,9},{9,10},{10,1... | collective-permute-start | bytes 36872 | tf_op jit(solution)/shard_map/ppermute | solution.py:28
  37.8 8.2 %collective-permute-start.7 = (f32[12,2,128]{2,1,0:T(2,128)S(1)}, f32[12,2,128]{2,1,0:T(2,128)S(1)}, u32[]{:S(2)}, u32[]{:S(2)}) collective-permute-start(f32[12,2,128]{2,1,0:T(2,128)S(1)} %get-tuple-element.13), channel_id=1, source_target_pairs={{1,0},{2,1},{3,2},{4,3},{5,4},{6,5},{7,6},{8,7},{9,8},{10,9},{11,1... | collective-permute-start | bytes 36872 | tf_op jit(solution)/shard_map/ppermute | solution.py:30
  46.2 76.0 %copy-start.4 = (f32[64]{0:T(128)S(1)}, f32[64]{0:T(128)}, u32[]{:S(2)}) copy-start(f32[64]{0:T(128)} %param.13) | copy-start | bytes 772
  46.8 78.4 %copy-start.1 = (f32[8,8,128]{2,1,0:T(8,128)}, f32[8,8,128]{2,1,0:T(8,128)S(1)}, u32[]{:S(2)}) copy-start(f32[8,8,128]{2,1,0:T(8,128)S(1)} %get-tuple-element.7) | copy-start | bytes 98308
  48.1 5.6 %collective-permute-start.8 = (f32[32,128]{1,0:T(8,128)S(1)}, f32[32,128]{1,0:T(8,128)S(1)}, u32[]{:S(2)}, u32[]{:S(2)}) collective-permute-start(f32[32,128]{1,0:T(8,128)S(1)} %pad_bitcast_fusion), channel_id=1, source_target_pairs={{0,1},{1,0},{2,3},{3,2},{4,5},{5,4},{6,7},{7,6},{8,9},{9,8},{10,11... | collective-permute-start | bytes 49160 | tf_op jit(solution)/shard_map/ppermute | solution.py:67
  53.7 6.5 %collective-permute-start.9 = (f32[32,128]{1,0:T(8,128)S(1)}, f32[32,128]{1,0:T(8,128)S(1)}, u32[]{:S(2)}, u32[]{:S(2)}) collective-permute-start(f32[32,128]{1,0:T(8,128)S(1)} %fusion.293), channel_id=1, source_target_pairs={{0,2},{1,3},{2,0},{3,1},{4,6},{5,7},{6,4},{7,5},{8,10},{9,11},{10,... | collective-permute-start | bytes 49160 | tf_op jit(solution)/shard_map/ppermute | solution.py:67
  60.3 5.6 %collective-permute-start.10 = (f32[32,128]{1,0:T(8,128)S(1)}, f32[32,128]{1,0:T(8,128)S(1)}, u32[]{:S(2)}, u32[]{:S(2)}) collective-permute-start(f32[32,128]{1,0:T(8,128)S(1)} %fusion.297), channel_id=1, source_target_pairs={{0,4},{1,5},{2,6},{3,7},{4,0},{5,1},{6,2},{7,3},{8,12},{9,13},{10,... | collective-permute-start | bytes 49160 | tf_op jit(solution)/shard_map/ppermute | solution.py:67
  65.9 7.1 %collective-permute-start.11 = (f32[32,128]{1,0:T(8,128)S(1)}, f32[32,128]{1,0:T(8,128)S(1)}, u32[]{:S(2)}, u32[]{:S(2)}) collective-permute-start(f32[32,128]{1,0:T(8,128)S(1)} %add.1202), channel_id=1, source_target_pairs={{0,8},{1,9},{2,10},{3,11},{4,12},{5,13},{6,14},{7,15},{8,0},{9,1},... | collective-permute-start | bytes 49160 | tf_op jit(solution)/shard_map/ppermute | solution.py:67
  73.0 3.1 %collective-permute-start.12 = (f32[32,128]{1,0:T(8,128)S(1)}, f32[32,128]{1,0:T(8,128)S(1)}, u32[]{:S(2)}, u32[]{:S(2)}) collective-permute-start(f32[32,128]{1,0:T(8,128)S(1)} %add.1203), channel_id=1, source_target_pairs={{0,16},{16,0},{32,48},{48,32},{64,80},{80,64},{96,112},{112,96},{1... | collective-permute-start | bytes 49160 | tf_op jit(solution)/shard_map/ppermute | solution.py:67
  76.1 15.4 %collective-permute-start.13 = (f32[32,128]{1,0:T(8,128)S(1)}, f32[32,128]{1,0:T(8,128)S(1)}, u32[]{:S(2)}, u32[]{:S(2)}) collective-permute-start(f32[32,128]{1,0:T(8,128)S(1)} %add.1204), channel_id=1, source_target_pairs={{0,32},{16,48},{32,0},{48,16},{64,96},{80,112},{96,64},{112,80},{1... | collective-permute-start | bytes 49160 | tf_op jit(solution)/shard_map/ppermute | solution.py:67
  91.5 11.1 %collective-permute-start.14 = (f32[32,128]{1,0:T(8,128)S(1)}, f32[32,128]{1,0:T(8,128)S(1)}, u32[]{:S(2)}, u32[]{:S(2)}) collective-permute-start(f32[32,128]{1,0:T(8,128)S(1)} %add.1205), channel_id=1, source_target_pairs={{0,64},{16,80},{32,96},{48,112},{64,0},{80,16},{96,32},{112,48},{1... | collective-permute-start | bytes 49160 | tf_op jit(solution)/shard_map/ppermute | solution.py:67
  102.6 7.8 %collective-permute-start.15 = (f32[32,128]{1,0:T(8,128)S(1)}, f32[32,128]{1,0:T(8,128)S(1)}, u32[]{:S(2)}, u32[]{:S(2)}) collective-permute-start(f32[32,128]{1,0:T(8,128)S(1)} %add.1206), channel_id=1, source_target_pairs={{0,128},{16,144},{32,160},{48,176},{64,192},{80,208},{96,224},{112... | collective-permute-start | bytes 49160 | tf_op jit(solution)/shard_map/ppermute | solution.py:67
  110.4 13.5 %collective-permute-start.16 = (f32[32,128]{1,0:T(8,128)S(1)}, f32[32,128]{1,0:T(8,128)S(1)}, u32[]{:S(2)}, u32[]{:S(2)}) collective-permute-start(f32[32,128]{1,0:T(8,128)S(1)} %add.1207), channel_id=1, source_target_pairs={{0,256},{16,272},{32,288},{48,304},{64,320},{80,336},{96,352},{112... | collective-permute-start | bytes 49160 | tf_op jit(solution)/shard_map/ppermute | solution.py:67

commit v18 on v10

--- a/solution.py
+++ b/solution.py
@@ -307,7 +307,7 @@
         PENALTY_SCALE * physical * physical * stiff_energy - OMEGA_SQUARED * mass_energy
     )
     raw_sensitivity = jnp.where(passive == 1, 0.0, raw_sensitivity)
-    scaled_wide = with_halo(raw_sensitivity / weight_sum, (("gx", 0), ("gy", 1)), 2)
+    scaled_wide = with_halo(raw_sensitivity / weight_sum, (("gy", 1), ("gx", 0)), 2)
     scaled_wide = jnp.pad(scaled_wide, ((0, 0), (0, 0), (2, 2)))
     sensitivity = stencil(scaled_wide, block_shape)
     benefit = jnp.maximum(-sensitivity, 0.0)

time: 127 us -> 130 us (1.024)
  waiting for transfers between devices: 25 us -> 40.9 us
  starting transfers between devices: 83.6 us -> 72 us
    ppermute x9, starting transfers between devices: 54.9 us -> 45.3 us  [butterfly_sum(): lax.ppermute(value, axis, [(i, i ^ stride) for i in range(count)])]
    ppermute x2, waiting for transfers between devices: 1.25 us -> 9.98 us  [with_halo(): lax.ppermute(head, axis, [((i + 1) % count, i) for i in range(ends)])]
    ppermute x2, waiting for transfers between devices: 0.8 us -> 6.31 us  [with_halo(): lax.ppermute(tail, axis, [(i, (i + 1) % count) for i in range(ends)])]
    ppermute x2, starting transfers between devices: 9.13 us -> 6.2 us  [with_halo(): lax.ppermute(tail, axis, [(i, (i + 1) % count) for i in range(ends)])]
    ppermute x9, waiting for transfers between devices: 21.9 us -> 23.6 us  [butterfly_sum(): lax.ppermute(value, axis, [(i, i ^ stride) for i in range(count)])]
where the time goes in v18:
time: 130 us; the launch traced here: 129 us
  starting transfers between devices  72 us (55%)
  waiting for transfers between devices  40.9 us (31%)
  other arithmetic  8.44 us (6%)
  Pallas kernels  6.22 us (5%)
    ppermute x9, starting transfers between devices, butterfly_sum(): lax.ppermute(value, axis, [(i, i ^ stride) for i in range(count)])  45.3 us
    ppermute x9, waiting for transfers between devices, butterfly_sum(): lax.ppermute(value, axis, [(i, i ^ stride) for i in range(count)])  23.6 us
    ppermute x2, waiting for transfers between devices, with_halo(): lax.ppermute(head, axis, [((i + 1) % count, i) for i in range(ends)])  9.98 us
    ppermute x2, starting transfers between devices, with_halo(): lax.ppermute(head, axis, [((i + 1) % count, i) for i in range(ends)])  8.45 us
    ppermute x2, starting transfers between devices, front_exchange(): lax.ppermute(packed, axis, [((i + 1) % count, i) for i in range(ends)])  7.07 us
    ppermute x2, waiting for transfers between devices, with_halo(): lax.ppermute(tail, axis, [(i, (i + 1) % count) for i in range(ends)])  6.31 us
    pallas_call x1, Pallas kernels, element_energies(): pl.pallas_call(mxu_energy_kernel, out_shape=(jax.ShapeDtypeStruct(cells,...  6.22 us
    ppermute x2, starting transfers between devices, with_halo(): lax.ppermute(tail, axis, [(i, (i + 1) % count) for i in range(ends)])  6.2 us
  transfers between devices with their start and end apart: 17, of which 13 were waited for; matrix products, arithmetic and copies ran while one was open for 1% of the time, Pallas kernels for 5%

profile of v18, /device:TPU:6, one launch (start us, length us, event | category | flops | bytes accessed | tf_op | source)
XLA Modules:
  0.0 129.4 jit_solution(1517481909734685820)
XLA Ops:
  1.4 1.2 broadcast_multiply_fusion
  2.7 1.3 collective-permute-start.1
  4.0 3.0 %collective-permute-start = (f32[2,8,128]{2,1,0:T(8,128)S(1)}, f32[2,8,128]{2,1,0:T(8,128)S(1)}, u32[]{:S(2)}, u32[]{:S(2)}) collective-permute-start(f32[2,8,128]{2,1,0:T(8,128)S(1)} %get-tuple-element.23), channel_id=1, source_target_pairs={{0,16},{16,32},{32,48},{48,64},{64,80},{80,96},{96,112},{112,128},... | collective-permute-start | bytes 24584 | tf_op jit(solution)/shard_map/ppermute | solution.py:50
  7.9 5.8 %collective-permute-start.3 = (f32[240,128]{1,0:T(8,128)S(1)}, f32[240,128]{1,0:T(8,128)S(1)}, u32[]{:S(2)}, u32[]{:S(2)}) collective-permute-start(f32[240,128]{1,0:T(8,128)S(1)} %pad_maximum_fusion.1), channel_id=1, source_target_pairs={{1,0},{2,1},{3,2},{4,3},{5,4},{6,5},{7,6},{8,7},{9,8},{10,9},{11,1... | collective-permute-start | bytes 368648 | tf_op jit(solution)/shard_map/ppermute | solution.py:46
  13.8 1.9 %collective-permute-start.2 = (f32[12,2,128]{2,1,0:T(2,128)S(1)}, f32[12,2,128]{2,1,0:T(2,128)S(1)}, u32[]{:S(2)}, u32[]{:S(2)}) collective-permute-start(f32[12,2,128]{2,1,0:T(2,128)S(1)} %get-tuple-element.16), channel_id=1, source_target_pairs={{0,1},{1,2},{2,3},{3,4},{4,5},{5,6},{6,7},{7,8},{8,9},{9,10},{10,1... | collective-permute-start | bytes 36872 | tf_op jit(solution)/shard_map/ppermute | solution.py:50
  16.2 1.4 %pad_maximum_fusion.extended_ref = f32[4,2,3,9,9,128]{5,4,3,2,1,0:T(8,128)} fusion(f32[4,2,3,9,1,128]{5,4,3,2,1,0:T(1,128)S(1)} %bitcast.65, f32[4,2,3,1,8,128]{5,4,3,2,1,0:T(8,128)S(1)} %bitcast.64, f32[4,2,3,8,8,128]{5,4,3,2,1,0:T(8,128)S(1)} %broadcast_multiply_fusion), kind=kLoop, calls=%fused_computation.6 | loop fusion | flops 497664 | bytes 1990656 | tf_op jit(solution)/shard_map/concatenate | solution.py:52
  17.5 6.2 %shard_map.86 = (f32[8,8,128]{2,1,0:T(8,128)}, f32[8,8,128]{2,1,0:T(8,128)}) custom-call(f32[4,2,3,9,9,128]{5,4,3,2,1,0:T(8,128)} %pad_maximum_fusion.extended_ref, f32[24,24]{1,0:T(8,128)} %stiffness_ref.1, f32[24,24]{1,0:T(8,128)} %mass_ref.1), custom_call_target="tpu_custom_call" | custom-call | flops 607125504 | bytes 1065472 | tf_op jit(solution)/shard_map/pallas_call | solution.py:263
  24.0 2.0 %fusion.34 = (f32[8,8,128]{2,1,0:T(8,128)S(1)}, pred[8,8,128]{2,1,0:T(8,128)(4,1)S(1)}) fusion(f32[8,8,128]{2,1,0:T(8,128)} %get-tuple-element.4, f32[12,10,128]{2,1,0:T(8,128)S(1)} %get-tuple-element.15, f32[12,12,132]{2,1,0:T(8,128)S(1)} %select_maximum_fusion.4, f32[2,8,128]{2,1,0:T(8,128)S(1)} %slice_bitcast_fusion, f32[8,8,128]{2,1,0:T(8,128)S(1)} %copy-done, ...), kind=kLoop, calls=%fused_computation.62 | loop fusion | flops 3039232 | bytes 6176768 | tf_op jit(solution)/shard_map/div | solution.py:310
  26.0 7.2 %collective-permute-start.5 = (f32[8,2,128]{2,1,0:T(2,128)S(1)}, f32[8,2,128]{2,1,0:T(2,128)S(1)}, u32[]{:S(2)}, u32[]{:S(2)}) collective-permute-start(f32[8,2,128]{2,1,0:T(2,128)S(1)} %get-tuple-element.22), channel_id=1, source_target_pairs={{1,0},{2,1},{3,2},{4,3},{5,4},{6,5},{7,6},{8,7},{9,8},{10,9},{11,1... | collective-permute-start | bytes 24584 | tf_op jit(solution)/shard_map/ppermute | solution.py:29
  33.2 1.9 %collective-permute-start.4 = (f32[8,2,128]{2,1,0:T(2,128)S(1)}, f32[8,2,128]{2,1,0:T(2,128)S(1)}, u32[]{:S(2)}, u32[]{:S(2)}) collective-permute-start(f32[8,2,128]{2,1,0:T(2,128)S(1)} %get-tuple-element.21), channel_id=1, source_target_pairs={{0,1},{1,2},{2,3},{3,4},{4,5},{5,6},{6,7},{7,8},{8,9},{9,10},{10,1... | collective-permute-start | bytes 24584 | tf_op jit(solution)/shard_map/ppermute | solution.py:27
  35.1 6.3 %collective-permute-done.4 = f32[8,2,128]{2,1,0:T(2,128)S(1)} collective-permute-done((f32[8,2,128]{2,1,0:T(2,128)S(1)}, f32[8,2,128]{2,1,0:T(2,128)S(1)}, u32[]{:S(2)}, u32[]{:S(2)}) %collective-permute-start.4) | collective-permute-done | bytes 8224 | tf_op jit(solution)/shard_map/ppermute | solution.py:27
  41.4 4.3 %collective-permute-start.6 = (f32[2,12,128]{2,1,0:T(8,128)S(1)}, f32[2,12,128]{2,1,0:T(8,128)S(1)}, u32[]{:S(2)}, u32[]{:S(2)}) collective-permute-start(f32[2,12,128]{2,1,0:T(8,128)S(1)} %get-tuple-element.12), channel_id=1, source_target_pairs={{0,16},{16,32},{32,48},{48,64},{64,80},{80,96},{96,112},{112,128},... | collective-permute-start | bytes 36872 | tf_op jit(solution)/shard_map/ppermute | solution.py:27
  45.7 1.3 collective-permute-start.7
  47.1 10.0 %collective-permute-done.7 = f32[2,12,128]{2,1,0:T(8,128)S(1)} collective-permute-done((f32[2,12,128]{2,1,0:T(8,128)S(1)}, f32[2,12,128]{2,1,0:T(8,128)S(1)}, u32[]{:S(2)}, u32[]{:S(2)}) %collective-permute-start.7) | collective-permute-done | bytes 12320 | tf_op jit(solution)/shard_map/ppermute | solution.py:29
  57.9 0.9 fusion.4
  59.2 1.9 %collective-permute-start.8 = (f32[32,128]{1,0:T(8,128)S(1)}, f32[32,128]{1,0:T(8,128)S(1)}, u32[]{:S(2)}, u32[]{:S(2)}) collective-permute-start(f32[32,128]{1,0:T(8,128)S(1)} %pad_bitcast_fusion), channel_id=1, source_target_pairs={{0,1},{1,0},{2,3},{3,2},{4,5},{5,4},{6,7},{7,6},{8,9},{9,8},{10,11... | collective-permute-start | bytes 49160 | tf_op jit(solution)/shard_map/ppermute | solution.py:66
  61.1 3.7 %collective-permute-done.8 = f32[32,128]{1,0:T(8,128)S(1)} collective-permute-done((f32[32,128]{1,0:T(8,128)S(1)}, f32[32,128]{1,0:T(8,128)S(1)}, u32[]{:S(2)}, u32[]{:S(2)}) %collective-permute-start.8) | collective-permute-done | bytes 16416 | tf_op jit(solution)/shard_map/ppermute | solution.py:66
  64.8 1.9 %collective-permute-start.9 = (f32[32,128]{1,0:T(8,128)S(1)}, f32[32,128]{1,0:T(8,128)S(1)}, u32[]{:S(2)}, u32[]{:S(2)}) collective-permute-start(f32[32,128]{1,0:T(8,128)S(1)} %fusion.295), channel_id=1, source_target_pairs={{0,2},{1,3},{2,0},{3,1},{4,6},{5,7},{6,4},{7,5},{8,10},{9,11},{10,... | collective-permute-start | bytes 49160 | tf_op jit(solution)/shard_map/ppermute | solution.py:66
  66.7 4.6 %collective-permute-done.9 = f32[32,128]{1,0:T(8,128)S(1)} collective-permute-done((f32[32,128]{1,0:T(8,128)S(1)}, f32[32,128]{1,0:T(8,128)S(1)}, u32[]{:S(2)}, u32[]{:S(2)}) %collective-permute-start.9) | collective-permute-done | bytes 16416 | tf_op jit(solution)/shard_map/ppermute | solution.py:66
  71.3 2.4 %collective-permute-start.10 = (f32[32,128]{1,0:T(8,128)S(1)}, f32[32,128]{1,0:T(8,128)S(1)}, u32[]{:S(2)}, u32[]{:S(2)}) collective-permute-start(f32[32,128]{1,0:T(8,128)S(1)} %fusion.299), channel_id=1, source_target_pairs={{0,4},{1,5},{2,6},{3,7},{4,0},{5,1},{6,2},{7,3},{8,12},{9,13},{10,... | collective-permute-start | bytes 49160 | tf_op jit(solution)/shard_map/ppermute | solution.py:66
  73.8 3.2 %collective-permute-done.10 = f32[32,128]{1,0:T(8,128)S(1)} collective-permute-done((f32[32,128]{1,0:T(8,128)S(1)}, f32[32,128]{1,0:T(8,128)S(1)}, u32[]{:S(2)}, u32[]{:S(2)}) %collective-permute-start.10) | collective-permute-done | bytes 16416 | tf_op jit(solution)/shard_map/ppermute | solution.py:66
  77.0 3.0 %collective-permute-start.11 = (f32[32,128]{1,0:T(8,128)S(1)}, f32[32,128]{1,0:T(8,128)S(1)}, u32[]{:S(2)}, u32[]{:S(2)}) collective-permute-start(f32[32,128]{1,0:T(8,128)S(1)} %add.1202), channel_id=1, source_target_pairs={{0,8},{1,9},{2,10},{3,11},{4,12},{5,13},{6,14},{7,15},{8,0},{9,1},... | collective-permute-start | bytes 49160 | tf_op jit(solution)/shard_map/ppermute | solution.py:66
  80.0 4.1 %collective-permute-done.11 = f32[32,128]{1,0:T(8,128)S(1)} collective-permute-done((f32[32,128]{1,0:T(8,128)S(1)}, f32[32,128]{1,0:T(8,128)S(1)}, u32[]{:S(2)}, u32[]{:S(2)}) %collective-permute-start.11) | collective-permute-done | bytes 16416 | tf_op jit(solution)/shard_map/ppermute | solution.py:66
  84.1 3.7 %collective-permute-start.12 = (f32[32,128]{1,0:T(8,128)S(1)}, f32[32,128]{1,0:T(8,128)S(1)}, u32[]{:S(2)}, u32[]{:S(2)}) collective-permute-start(f32[32,128]{1,0:T(8,128)S(1)} %add.1203), channel_id=1, source_target_pairs={{0,16},{16,0},{32,48},{48,32},{64,80},{80,64},{96,112},{112,96},{1... | collective-permute-start | bytes 49160 | tf_op jit(solution)/shard_map/ppermute | solution.py:66
  88.6 7.5 %collective-permute-start.13 = (f32[32,128]{1,0:T(8,128)S(1)}, f32[32,128]{1,0:T(8,128)S(1)}, u32[]{:S(2)}, u32[]{:S(2)}) collective-permute-start(f32[32,128]{1,0:T(8,128)S(1)} %add.1204), channel_id=1, source_target_pairs={{0,32},{16,48},{32,0},{48,16},{64,96},{80,112},{96,64},{112,80},{1... | collective-permute-start | bytes 49160 | tf_op jit(solution)/shard_map/ppermute | solution.py:66
  96.2 2.0 %collective-permute-done.13 = f32[32,128]{1,0:T(8,128)S(1)} collective-permute-done((f32[32,128]{1,0:T(8,128)S(1)}, f32[32,128]{1,0:T(8,128)S(1)}, u32[]{:S(2)}, u32[]{:S(2)}) %collective-permute-start.13) | collective-permute-done | bytes 16416 | tf_op jit(solution)/shard_map/ppermute | solution.py:66
  98.2 7.2 %collective-permute-start.14 = (f32[32,128]{1,0:T(8,128)S(1)}, f32[32,128]{1,0:T(8,128)S(1)}, u32[]{:S(2)}, u32[]{:S(2)}) collective-permute-start(f32[32,128]{1,0:T(8,128)S(1)} %add.1205), channel_id=1, source_target_pairs={{0,64},{16,80},{32,96},{48,112},{64,0},{80,16},{96,32},{112,48},{1... | collective-permute-start | bytes 49160 | tf_op jit(solution)/shard_map/ppermute | solution.py:66
  105.3 1.7 %collective-permute-done.14 = f32[32,128]{1,0:T(8,128)S(1)} collective-permute-done((f32[32,128]{1,0:T(8,128)S(1)}, f32[32,128]{1,0:T(8,128)S(1)}, u32[]{:S(2)}, u32[]{:S(2)}) %collective-permute-start.14) | collective-permute-done | bytes 16416 | tf_op jit(solution)/shard_map/ppermute | solution.py:66
  107.1 6.5 %collective-permute-start.15 = (f32[32,128]{1,0:T(8,128)S(1)}, f32[32,128]{1,0:T(8,128)S(1)}, u32[]{:S(2)}, u32[]{:S(2)}) collective-permute-start(f32[32,128]{1,0:T(8,128)S(1)} %add.1206), channel_id=1, source_target_pairs={{0,128},{16,144},{32,160},{48,176},{64,192},{80,208},{96,224},{112... | collective-permute-start | bytes 49160 | tf_op jit(solution)/shard_map/ppermute | solution.py:66
  113.6 1.7 %collective-permute-done.15 = f32[32,128]{1,0:T(8,128)S(1)} collective-permute-done((f32[32,128]{1,0:T(8,128)S(1)}, f32[32,128]{1,0:T(8,128)S(1)}, u32[]{:S(2)}, u32[]{:S(2)}) %collective-permute-start.15) | collective-permute-done | bytes 16416 | tf_op jit(solution)/shard_map/ppermute | solution.py:66
  115.3 11.2 %collective-permute-start.16 = (f32[32,128]{1,0:T(8,128)S(1)}, f32[32,128]{1,0:T(8,128)S(1)}, u32[]{:S(2)}, u32[]{:S(2)}) collective-permute-start(f32[32,128]{1,0:T(8,128)S(1)} %add.1207), channel_id=1, source_target_pairs={{0,256},{16,272},{32,288},{48,304},{64,320},{80,336},{96,352},{112... | collective-permute-start | bytes 49160 | tf_op jit(solution)/shard_map/ppermute | solution.py:66
  126.5 1.7 %collective-permute-done.16 = f32[32,128]{1,0:T(8,128)S(1)} collective-permute-done((f32[32,128]{1,0:T(8,128)S(1)}, f32[32,128]{1,0:T(8,128)S(1)}, u32[]{:S(2)}, u32[]{:S(2)}) %collective-permute-start.16) | collective-permute-done | bytes 16416 | tf_op jit(solution)/shard_map/ppermute | solution.py:66
  (75 shorter events, 5.6 us)
Async XLA Ops:
  0.6 2.0 %copy-start = (f32[8,8,128]{2,1,0:T(8,128)S(1)}, f32[8,8,128]{2,1,0:T(8,128)}, u32[]{:S(2)}) copy-start(f32[8,8,128]{2,1,0:T(8,128)} %param.7) | copy-start | bytes 98308
  2.7 5.2 %collective-permute-start.1 = (f32[208,128]{1,0:T(8,128)S(1)}, f32[208,128]{1,0:T(8,128)S(1)}, u32[]{:S(2)}, u32[]{:S(2)}) collective-permute-start(f32[208,128]{1,0:T(8,128)S(1)} %pad_maximum_fusion.3), channel_id=1, source_target_pairs={{16,0},{32,16},{48,32},{64,48},{80,64},{96,80},{112,96},{128,112},... | collective-permute-start | bytes 319496 | tf_op jit(solution)/shard_map/ppermute | solution.py:46
  4.0 3.8 %collective-permute-start = (f32[2,8,128]{2,1,0:T(8,128)S(1)}, f32[2,8,128]{2,1,0:T(8,128)S(1)}, u32[]{:S(2)}, u32[]{:S(2)}) collective-permute-start(f32[2,8,128]{2,1,0:T(8,128)S(1)} %get-tuple-element.23), channel_id=1, source_target_pairs={{0,16},{16,32},{32,48},{48,64},{64,80},{80,96},{96,112},{112,128},... | collective-permute-start | bytes 24584 | tf_op jit(solution)/shard_map/ppermute | solution.py:50
  7.9 8.2 %collective-permute-start.3 = (f32[240,128]{1,0:T(8,128)S(1)}, f32[240,128]{1,0:T(8,128)S(1)}, u32[]{:S(2)}, u32[]{:S(2)}) collective-permute-start(f32[240,128]{1,0:T(8,128)S(1)} %pad_maximum_fusion.1), channel_id=1, source_target_pairs={{1,0},{2,1},{3,2},{4,3},{5,4},{6,5},{7,6},{8,7},{9,8},{10,9},{11,1... | collective-permute-start | bytes 368648 | tf_op jit(solution)/shard_map/ppermute | solution.py:46
  13.8 10.0 %collective-permute-start.2 = (f32[12,2,128]{2,1,0:T(2,128)S(1)}, f32[12,2,128]{2,1,0:T(2,128)S(1)}, u32[]{:S(2)}, u32[]{:S(2)}) collective-permute-start(f32[12,2,128]{2,1,0:T(2,128)S(1)} %get-tuple-element.16), channel_id=1, source_target_pairs={{0,1},{1,2},{2,3},{3,4},{4,5},{5,6},{6,7},{7,8},{8,9},{9,10},{10,1... | collective-permute-start | bytes 36872 | tf_op jit(solution)/shard_map/ppermute | solution.py:50
  17.5 6.4 %copy-start.2 = (s32[8,8,128]{2,1,0:T(8,128)S(1)}, s32[8,8,128]{2,1,0:T(8,128)}, u32[]{:S(2)}) copy-start(s32[8,8,128]{2,1,0:T(8,128)} %param.8) | copy-start | bytes 98308
  24.0 23.0 %copy-start.3 = (f32[63,64]{0,1:T(8,128)S(1)}, f32[63,64]{0,1:T(8,128)}, u32[]{:S(2)}) copy-start(f32[63,64]{0,1:T(8,128)} %constant.25.clone.1) | copy-start | bytes 48388
  26.0 9.1 %collective-permute-start.5 = (f32[8,2,128]{2,1,0:T(2,128)S(1)}, f32[8,2,128]{2,1,0:T(2,128)S(1)}, u32[]{:S(2)}, u32[]{:S(2)}) collective-permute-start(f32[8,2,128]{2,1,0:T(2,128)S(1)} %get-tuple-element.22), channel_id=1, source_target_pairs={{1,0},{2,1},{3,2},{4,3},{5,4},{6,5},{7,6},{8,7},{9,8},{10,9},{11,1... | collective-permute-start | bytes 24584 | tf_op jit(solution)/shard_map/ppermute | solution.py:29
  33.2 8.2 %collective-permute-start.4 = (f32[8,2,128]{2,1,0:T(2,128)S(1)}, f32[8,2,128]{2,1,0:T(2,128)S(1)}, u32[]{:S(2)}, u32[]{:S(2)}) collective-permute-start(f32[8,2,128]{2,1,0:T(2,128)S(1)} %get-tuple-element.21), channel_id=1, source_target_pairs={{0,1},{1,2},{2,3},{3,4},{4,5},{5,6},{6,7},{7,8},{8,9},{9,10},{10,1... | collective-permute-start | bytes 24584 | tf_op jit(solution)/shard_map/ppermute | solution.py:27
  41.4 5.7 %collective-permute-start.6 = (f32[2,12,128]{2,1,0:T(8,128)S(1)}, f32[2,12,128]{2,1,0:T(8,128)S(1)}, u32[]{:S(2)}, u32[]{:S(2)}) collective-permute-start(f32[2,12,128]{2,1,0:T(8,128)S(1)} %get-tuple-element.12), channel_id=1, source_target_pairs={{0,16},{16,32},{32,48},{48,64},{64,80},{80,96},{96,112},{112,128},... | collective-permute-start | bytes 36872 | tf_op jit(solution)/shard_map/ppermute | solution.py:27
  45.7 11.4 %collective-permute-start.7 = (f32[2,12,128]{2,1,0:T(8,128)S(1)}, f32[2,12,128]{2,1,0:T(8,128)S(1)}, u32[]{:S(2)}, u32[]{:S(2)}) collective-permute-start(f32[2,12,128]{2,1,0:T(8,128)S(1)} %get-tuple-element.13), channel_id=1, source_target_pairs={{16,0},{32,16},{48,32},{64,48},{80,64},{96,80},{112,96},{128,112},... | collective-permute-start | bytes 36872 | tf_op jit(solution)/shard_map/ppermute | solution.py:29
  57.3 69.2 %copy-start.4 = (f32[64]{0:T(128)S(1)}, f32[64]{0:T(128)}, u32[]{:S(2)}) copy-start(f32[64]{0:T(128)} %param.13) | copy-start | bytes 772
  57.9 71.5 %copy-start.1 = (f32[8,8,128]{2,1,0:T(8,128)}, f32[8,8,128]{2,1,0:T(8,128)S(1)}, u32[]{:S(2)}) copy-start(f32[8,8,128]{2,1,0:T(8,128)S(1)} %get-tuple-element.7) | copy-start | bytes 98308
  59.2 5.6 %collective-permute-start.8 = (f32[32,128]{1,0:T(8,128)S(1)}, f32[32,128]{1,0:T(8,128)S(1)}, u32[]{:S(2)}, u32[]{:S(2)}) collective-permute-start(f32[32,128]{1,0:T(8,128)S(1)} %pad_bitcast_fusion), channel_id=1, source_target_pairs={{0,1},{1,0},{2,3},{3,2},{4,5},{5,4},{6,7},{7,6},{8,9},{9,8},{10,11... | collective-permute-start | bytes 49160 | tf_op jit(solution)/shard_map/ppermute | solution.py:66
  64.8 6.5 %collective-permute-start.9 = (f32[32,128]{1,0:T(8,128)S(1)}, f32[32,128]{1,0:T(8,128)S(1)}, u32[]{:S(2)}, u32[]{:S(2)}) collective-permute-start(f32[32,128]{1,0:T(8,128)S(1)} %fusion.295), channel_id=1, source_target_pairs={{0,2},{1,3},{2,0},{3,1},{4,6},{5,7},{6,4},{7,5},{8,10},{9,11},{10,... | collective-permute-start | bytes 49160 | tf_op jit(solution)/shard_map/ppermute | solution.py:66
  71.3 5.6 %collective-permute-start.10 = (f32[32,128]{1,0:T(8,128)S(1)}, f32[32,128]{1,0:T(8,128)S(1)}, u32[]{:S(2)}, u32[]{:S(2)}) collective-permute-start(f32[32,128]{1,0:T(8,128)S(1)} %fusion.299), channel_id=1, source_target_pairs={{0,4},{1,5},{2,6},{3,7},{4,0},{5,1},{6,2},{7,3},{8,12},{9,13},{10,... | collective-permute-start | bytes 49160 | tf_op jit(solution)/shard_map/ppermute | solution.py:66
  77.0 7.1 %collective-permute-start.11 = (f32[32,128]{1,0:T(8,128)S(1)}, f32[32,128]{1,0:T(8,128)S(1)}, u32[]{:S(2)}, u32[]{:S(2)}) collective-permute-start(f32[32,128]{1,0:T(8,128)S(1)} %add.1202), channel_id=1, source_target_pairs={{0,8},{1,9},{2,10},{3,11},{4,12},{5,13},{6,14},{7,15},{8,0},{9,1},... | collective-permute-start | bytes 49160 | tf_op jit(solution)/shard_map/ppermute | solution.py:66
  84.1 4.5 %collective-permute-start.12 = (f32[32,128]{1,0:T(8,128)S(1)}, f32[32,128]{1,0:T(8,128)S(1)}, u32[]{:S(2)}, u32[]{:S(2)}) collective-permute-start(f32[32,128]{1,0:T(8,128)S(1)} %add.1203), channel_id=1, source_target_pairs={{0,16},{16,0},{32,48},{48,32},{64,80},{80,64},{96,112},{112,96},{1... | collective-permute-start | bytes 49160 | tf_op jit(solution)/shard_map/ppermute | solution.py:66
  88.6 9.5 %collective-permute-start.13 = (f32[32,128]{1,0:T(8,128)S(1)}, f32[32,128]{1,0:T(8,128)S(1)}, u32[]{:S(2)}, u32[]{:S(2)}) collective-permute-start(f32[32,128]{1,0:T(8,128)S(1)} %add.1204), channel_id=1, source_target_pairs={{0,32},{16,48},{32,0},{48,16},{64,96},{80,112},{96,64},{112,80},{1... | collective-permute-start | bytes 49160 | tf_op jit(solution)/shard_map/ppermute | solution.py:66
  98.2 8.9 %collective-permute-start.14 = (f32[32,128]{1,0:T(8,128)S(1)}, f32[32,128]{1,0:T(8,128)S(1)}, u32[]{:S(2)}, u32[]{:S(2)}) collective-permute-start(f32[32,128]{1,0:T(8,128)S(1)} %add.1205), channel_id=1, source_target_pairs={{0,64},{16,80},{32,96},{48,112},{64,0},{80,16},{96,32},{112,48},{1... | collective-permute-start | bytes 49160 | tf_op jit(solution)/shard_map/ppermute | solution.py:66
  107.1 8.2 %collective-permute-start.15 = (f32[32,128]{1,0:T(8,128)S(1)}, f32[32,128]{1,0:T(8,128)S(1)}, u32[]{:S(2)}, u32[]{:S(2)}) collective-permute-start(f32[32,128]{1,0:T(8,128)S(1)} %add.1206), channel_id=1, source_target_pairs={{0,128},{16,144},{32,160},{48,176},{64,192},{80,208},{96,224},{112... | collective-permute-start | bytes 49160 | tf_op jit(solution)/shard_map/ppermute | solution.py:66
  115.3 12.9 %collective-permute-start.16 = (f32[32,128]{1,0:T(8,128)S(1)}, f32[32,128]{1,0:T(8,128)S(1)}, u32[]{:S(2)}, u32[]{:S(2)}) collective-permute-start(f32[32,128]{1,0:T(8,128)S(1)} %add.1207), channel_id=1, source_target_pairs={{0,256},{16,272},{32,288},{48,304},{64,320},{80,336},{96,352},{112... | collective-permute-start | bytes 49160 | tf_op jit(solution)/shard_map/ppermute | solution.py:66

commit v19 on v10

--- a/solution.py
+++ b/solution.py
@@ -33,14 +33,14 @@
     return cells
 
 
-def front_exchange(cells, fields, width):
+def front_exchange(cells, fields, width, first_rim):
     for axis, dim in (("gx", 0), ("gy", 1)):
         count = lax.axis_size(axis)
         ends = count - 1
         field_dim = dim + 3
         head = lax.slice_in_dim(cells, 0, width, axis=dim)
         tail = lax.slice_in_dim(cells, cells.shape[dim] - width, cells.shape[dim], axis=dim)
-        rim = lax.slice_in_dim(fields, 0, 1, axis=field_dim)
+        rim = first_rim if axis == "gx" else lax.slice_in_dim(fields, 0, 1, axis=field_dim)
         lanes = cells.shape[-1]
         packed = jnp.concatenate([head.reshape(-1, lanes), rim.reshape(-1, lanes)], axis=0)
         packed = lax.ppermute(packed, axis, [((i + 1) % count, i) for i in range(ends)])
@@ -299,7 +299,8 @@
     inside = valid_x[:, None, None] * valid_y[None, :, None] * valid_z[None, None, :]
     weight_sum = stencil(inside, block_shape)
     fields = basis_pairs * (1 - supports).astype(jnp.float32)
-    design_wide, extended = front_exchange(design, fields, 2)
+    first_rim = basis_pairs[:, :, :, :1] * (1 - supports[:1]).astype(jnp.float32)
+    design_wide, extended = front_exchange(design, fields, 2, first_rim)
     design_wide = jnp.pad(design_wide, ((0, 0), (0, 0), (2, 2)))
     physical = jnp.where(passive == 1, 1.0, stencil(design_wide, block_shape) / weight_sum)
     stiff_energy, mass_energy = element_energies(extended, stiffness, mass_matrix)

time: 127 us -> 128 us (level)
  other arithmetic: 8.45 us -> 10 us
  starting transfers between devices: 83.6 us -> 82.3 us
    mul x0 -> x2, other arithmetic: none -> 1.6 us  [shards(): basis_pairs[:, :, :, :1] * (1 - supports[:1]).astype(jnp.float32)]
  transfers between devices with their start and end apart: 17 -> 17, of which waited for: 13 -> 12; matrix products, arithmetic and copies ran while one was open for 1% -> 3% of each run, Pallas kernels for 5% -> 5%
where the time goes in v19:
time: 128 us; the launch traced here: 126 us
  starting transfers between devices  82.3 us (64%)
  waiting for transfers between devices  24.7 us (19%)
  other arithmetic  10 us (8%)
  Pallas kernels  6.22 us (5%)
  local copies, waits for them, and re-layouts  1.51 us (1%)
    ppermute x9, starting transfers between devices, butterfly_sum(): lax.ppermute(value, axis, [(i, i ^ stride) for i in range(count)])  53.6 us
    ppermute x9, waiting for transfers between devices, butterfly_sum(): lax.ppermute(value, axis, [(i, i ^ stride) for i in range(count)])  22.1 us
    ppermute x2, starting transfers between devices, with_halo(): lax.ppermute(tail, axis, [(i, (i + 1) % count) for i in range(ends)])  8.62 us
    ppermute x2, starting transfers between devices, with_halo(): lax.ppermute(head, axis, [((i + 1) % count, i) for i in range(ends)])  8.09 us
    ppermute x2, starting transfers between devices, front_exchange(): lax.ppermute(packed, axis, [((i + 1) % count, i) for i in range(ends)])  7.07 us
    pallas_call x1, Pallas kernels, element_energies(): pl.pallas_call(mxu_energy_kernel, out_shape=(jax.ShapeDtypeStruct(cells,...  6.22 us
    ppermute x2, starting transfers between devices, front_exchange(): tail = lax.ppermute(tail, axis, [(i, (i + 1) % count) for i in range(ends)])  4.95 us
  transfers between devices with their start and end apart: 17, of which 12 were waited for; matrix products, arithmetic and copies ran while one was open for 3% of the time, Pallas kernels for 5%

profile of v19, /device:TPU:6, one launch (start us, length us, event | category | flops | bytes accessed | tf_op | source)
XLA Modules:
  0.0 125.9 jit_solution(15337391712150841321)
XLA Ops:
  2.0 0.9 slice_multiply_fusion
  3.0 1.3 %collective-permute-start.1 = (f32[208,128]{1,0:T(8,128)S(1)}, f32[208,128]{1,0:T(8,128)S(1)}, u32[]{:S(2)}, u32[]{:S(2)}) collective-permute-start(f32[208,128]{1,0:T(8,128)S(1)} %pad_maximum_fusion.3), channel_id=1, source_target_pairs={{16,0},{32,16},{48,32},{64,48},{80,64},{96,80},{112,96},{128,112},... | collective-permute-start | bytes 319496 | tf_op jit(solution)/shard_map/ppermute | solution.py:46
  4.3 3.0 %collective-permute-start = (f32[2,8,128]{2,1,0:T(8,128)S(1)}, f32[2,8,128]{2,1,0:T(8,128)S(1)}, u32[]{:S(2)}, u32[]{:S(2)}) collective-permute-start(f32[2,8,128]{2,1,0:T(8,128)S(1)} %get-tuple-element.23), channel_id=1, source_target_pairs={{0,16},{16,32},{32,48},{48,64},{64,80},{80,96},{96,112},{112,128},... | collective-permute-start | bytes 24584 | tf_op jit(solution)/shard_map/ppermute | solution.py:50
  8.1 1.2 broadcast_multiply_fusion
  9.7 5.8 %collective-permute-start.3 = (f32[240,128]{1,0:T(8,128)S(1)}, f32[240,128]{1,0:T(8,128)S(1)}, u32[]{:S(2)}, u32[]{:S(2)}) collective-permute-start(f32[240,128]{1,0:T(8,128)S(1)} %pad_maximum_fusion.1), channel_id=1, source_target_pairs={{1,0},{2,1},{3,2},{4,3},{5,4},{6,5},{7,6},{8,7},{9,8},{10,9},{11,1... | collective-permute-start | bytes 368648 | tf_op jit(solution)/shard_map/ppermute | solution.py:46
  15.5 1.9 %collective-permute-start.2 = (f32[12,2,128]{2,1,0:T(2,128)S(1)}, f32[12,2,128]{2,1,0:T(2,128)S(1)}, u32[]{:S(2)}, u32[]{:S(2)}) collective-permute-start(f32[12,2,128]{2,1,0:T(2,128)S(1)} %get-tuple-element.16), channel_id=1, source_target_pairs={{0,1},{1,2},{2,3},{3,4},{4,5},{5,6},{6,7},{7,8},{8,9},{9,10},{10,1... | collective-permute-start | bytes 36872 | tf_op jit(solution)/shard_map/ppermute | solution.py:50
  18.0 1.4 %pad_maximum_fusion.extended_ref = f32[4,2,3,9,9,128]{5,4,3,2,1,0:T(8,128)} fusion(f32[4,2,3,9,1,128]{5,4,3,2,1,0:T(1,128)S(1)} %bitcast.67, f32[4,2,3,1,8,128]{5,4,3,2,1,0:T(8,128)S(1)} %bitcast.66, f32[4,2,3,8,8,128]{5,4,3,2,1,0:T(8,128)S(1)} %broadcast_multiply_fusion), kind=kLoop, calls=%fused_computation.6 | loop fusion | flops 497664 | bytes 1990656 | tf_op jit(solution)/shard_map/concatenate | solution.py:52
  19.4 6.2 %shard_map.86 = (f32[8,8,128]{2,1,0:T(8,128)}, f32[8,8,128]{2,1,0:T(8,128)}) custom-call(f32[4,2,3,9,9,128]{5,4,3,2,1,0:T(8,128)} %pad_maximum_fusion.extended_ref, f32[24,24]{1,0:T(8,128)} %stiffness_ref.1, f32[24,24]{1,0:T(8,128)} %mass_ref.1), custom_call_target="tpu_custom_call" | custom-call | flops 607125504 | bytes 1065472 | tf_op jit(solution)/shard_map/pallas_call | solution.py:263
  25.8 2.0 %fusion.82 = (f32[8,8,128]{2,1,0:T(8,128)S(1)}, pred[8,8,128]{2,1,0:T(8,128)(4,1)S(1)}) fusion(f32[8,8,128]{2,1,0:T(8,128)} %get-tuple-element.4, f32[12,10,128]{2,1,0:T(8,128)S(1)} %get-tuple-element.15, f32[12,12,132]{2,1,0:T(8,128)S(1)} %select_maximum_fusion.4, f32[2,8,128]{2,1,0:T(8,128)S(1)} %slice_bitcast_fusion, f32[8,8,128]{2,1,0:T(8,128)S(1)} %copy-done, ...), kind=kLoop, calls=%fused_computation.111 | loop fusion | flops 3039232 | bytes 6176768 | tf_op jit(solution)/shard_map/div | solution.py:311
  27.8 1.3 %collective-permute-start.5 = (f32[2,8,128]{2,1,0:T(8,128)S(1)}, f32[2,8,128]{2,1,0:T(8,128)S(1)}, u32[]{:S(2)}, u32[]{:S(2)}) collective-permute-start(f32[2,8,128]{2,1,0:T(8,128)S(1)} %get-tuple-element.22), channel_id=1, source_target_pairs={{16,0},{32,16},{48,32},{64,48},{80,64},{96,80},{112,96},{128,112},... | collective-permute-start | bytes 24584 | tf_op jit(solution)/shard_map/ppermute | solution.py:29
  29.1 6.7 %collective-permute-start.4 = (f32[2,8,128]{2,1,0:T(8,128)S(1)}, f32[2,8,128]{2,1,0:T(8,128)S(1)}, u32[]{:S(2)}, u32[]{:S(2)}) collective-permute-start(f32[2,8,128]{2,1,0:T(8,128)S(1)} %get-tuple-element.21), channel_id=1, source_target_pairs={{0,16},{16,32},{32,48},{48,64},{64,80},{80,96},{96,112},{112,128},... | collective-permute-start | bytes 24584 | tf_op jit(solution)/shard_map/ppermute | solution.py:27
  36.6 1.9 %collective-permute-start.6 = (f32[12,2,128]{2,1,0:T(2,128)S(1)}, f32[12,2,128]{2,1,0:T(2,128)S(1)}, u32[]{:S(2)}, u32[]{:S(2)}) collective-permute-start(f32[12,2,128]{2,1,0:T(2,128)S(1)} %get-tuple-element.12), channel_id=1, source_target_pairs={{0,1},{1,2},{2,3},{3,4},{4,5},{5,6},{6,7},{7,8},{8,9},{9,10},{10,1... | collective-permute-start | bytes 36872 | tf_op jit(solution)/shard_map/ppermute | solution.py:27
  38.6 6.8 %collective-permute-start.7 = (f32[12,2,128]{2,1,0:T(2,128)S(1)}, f32[12,2,128]{2,1,0:T(2,128)S(1)}, u32[]{:S(2)}, u32[]{:S(2)}) collective-permute-start(f32[12,2,128]{2,1,0:T(2,128)S(1)} %get-tuple-element.13), channel_id=1, source_target_pairs={{1,0},{2,1},{3,2},{4,3},{5,4},{6,5},{7,6},{8,7},{9,8},{10,9},{11,1... | collective-permute-start | bytes 36872 | tf_op jit(solution)/shard_map/ppermute | solution.py:29
  45.5 1.2 collective-permute-done.7
  47.5 0.9 fusion.4
  48.8 1.9 %collective-permute-start.8 = (f32[32,128]{1,0:T(8,128)S(1)}, f32[32,128]{1,0:T(8,128)S(1)}, u32[]{:S(2)}, u32[]{:S(2)}) collective-permute-start(f32[32,128]{1,0:T(8,128)S(1)} %pad_bitcast_fusion), channel_id=1, source_target_pairs={{0,1},{1,0},{2,3},{3,2},{4,5},{5,4},{6,7},{7,6},{8,9},{9,8},{10,11... | collective-permute-start | bytes 49160 | tf_op jit(solution)/shard_map/ppermute | solution.py:66
  50.8 3.7 %collective-permute-done.8 = f32[32,128]{1,0:T(8,128)S(1)} collective-permute-done((f32[32,128]{1,0:T(8,128)S(1)}, f32[32,128]{1,0:T(8,128)S(1)}, u32[]{:S(2)}, u32[]{:S(2)}) %collective-permute-start.8) | collective-permute-done | bytes 16416 | tf_op jit(solution)/shard_map/ppermute | solution.py:66
  54.5 1.9 %collective-permute-start.9 = (f32[32,128]{1,0:T(8,128)S(1)}, f32[32,128]{1,0:T(8,128)S(1)}, u32[]{:S(2)}, u32[]{:S(2)}) collective-permute-start(f32[32,128]{1,0:T(8,128)S(1)} %fusion.293), channel_id=1, source_target_pairs={{0,2},{1,3},{2,0},{3,1},{4,6},{5,7},{6,4},{7,5},{8,10},{9,11},{10,... | collective-permute-start | bytes 49160 | tf_op jit(solution)/shard_map/ppermute | solution.py:66
  56.4 4.6 %collective-permute-done.9 = f32[32,128]{1,0:T(8,128)S(1)} collective-permute-done((f32[32,128]{1,0:T(8,128)S(1)}, f32[32,128]{1,0:T(8,128)S(1)}, u32[]{:S(2)}, u32[]{:S(2)}) %collective-permute-start.9) | collective-permute-done | bytes 16416 | tf_op jit(solution)/shard_map/ppermute | solution.py:66
  61.0 3.1 %collective-permute-start.10 = (f32[32,128]{1,0:T(8,128)S(1)}, f32[32,128]{1,0:T(8,128)S(1)}, u32[]{:S(2)}, u32[]{:S(2)}) collective-permute-start(f32[32,128]{1,0:T(8,128)S(1)} %fusion.297), channel_id=1, source_target_pairs={{0,4},{1,5},{2,6},{3,7},{4,0},{5,1},{6,2},{7,3},{8,12},{9,13},{10,... | collective-permute-start | bytes 49160 | tf_op jit(solution)/shard_map/ppermute | solution.py:66
  64.1 2.5 %collective-permute-done.10 = f32[32,128]{1,0:T(8,128)S(1)} collective-permute-done((f32[32,128]{1,0:T(8,128)S(1)}, f32[32,128]{1,0:T(8,128)S(1)}, u32[]{:S(2)}, u32[]{:S(2)}) %collective-permute-start.10) | collective-permute-done | bytes 16416 | tf_op jit(solution)/shard_map/ppermute | solution.py:66
  66.6 3.6 %collective-permute-start.11 = (f32[32,128]{1,0:T(8,128)S(1)}, f32[32,128]{1,0:T(8,128)S(1)}, u32[]{:S(2)}, u32[]{:S(2)}) collective-permute-start(f32[32,128]{1,0:T(8,128)S(1)} %add.1202), channel_id=1, source_target_pairs={{0,8},{1,9},{2,10},{3,11},{4,12},{5,13},{6,14},{7,15},{8,0},{9,1},... | collective-permute-start | bytes 49160 | tf_op jit(solution)/shard_map/ppermute | solution.py:66
  70.3 3.5 %collective-permute-done.11 = f32[32,128]{1,0:T(8,128)S(1)} collective-permute-done((f32[32,128]{1,0:T(8,128)S(1)}, f32[32,128]{1,0:T(8,128)S(1)}, u32[]{:S(2)}, u32[]{:S(2)}) %collective-permute-start.11) | collective-permute-done | bytes 16416 | tf_op jit(solution)/shard_map/ppermute | solution.py:66
  73.8 2.4 %collective-permute-start.12 = (f32[32,128]{1,0:T(8,128)S(1)}, f32[32,128]{1,0:T(8,128)S(1)}, u32[]{:S(2)}, u32[]{:S(2)}) collective-permute-start(f32[32,128]{1,0:T(8,128)S(1)} %add.1203), channel_id=1, source_target_pairs={{0,16},{16,0},{32,48},{48,32},{64,80},{80,64},{96,112},{112,96},{1... | collective-permute-start | bytes 49160 | tf_op jit(solution)/shard_map/ppermute | solution.py:66
  77.0 13.9 %collective-permute-start.13 = (f32[32,128]{1,0:T(8,128)S(1)}, f32[32,128]{1,0:T(8,128)S(1)}, u32[]{:S(2)}, u32[]{:S(2)}) collective-permute-start(f32[32,128]{1,0:T(8,128)S(1)} %add.1204), channel_id=1, source_target_pairs={{0,32},{16,48},{32,0},{48,16},{64,96},{80,112},{96,64},{112,80},{1... | collective-permute-start | bytes 49160 | tf_op jit(solution)/shard_map/ppermute | solution.py:66
  90.8 1.7 %collective-permute-done.13 = f32[32,128]{1,0:T(8,128)S(1)} collective-permute-done((f32[32,128]{1,0:T(8,128)S(1)}, f32[32,128]{1,0:T(8,128)S(1)}, u32[]{:S(2)}, u32[]{:S(2)}) %collective-permute-start.13) | collective-permute-done | bytes 16416 | tf_op jit(solution)/shard_map/ppermute | solution.py:66
  92.5 9.4 %collective-permute-start.14 = (f32[32,128]{1,0:T(8,128)S(1)}, f32[32,128]{1,0:T(8,128)S(1)}, u32[]{:S(2)}, u32[]{:S(2)}) collective-permute-start(f32[32,128]{1,0:T(8,128)S(1)} %add.1205), channel_id=1, source_target_pairs={{0,64},{16,80},{32,96},{48,112},{64,0},{80,16},{96,32},{112,48},{1... | collective-permute-start | bytes 49160 | tf_op jit(solution)/shard_map/ppermute | solution.py:66
  102.0 1.7 %collective-permute-done.14 = f32[32,128]{1,0:T(8,128)S(1)} collective-permute-done((f32[32,128]{1,0:T(8,128)S(1)}, f32[32,128]{1,0:T(8,128)S(1)}, u32[]{:S(2)}, u32[]{:S(2)}) %collective-permute-start.14) | collective-permute-done | bytes 16416 | tf_op jit(solution)/shard_map/ppermute | solution.py:66
  103.7 6.1 %collective-permute-start.15 = (f32[32,128]{1,0:T(8,128)S(1)}, f32[32,128]{1,0:T(8,128)S(1)}, u32[]{:S(2)}, u32[]{:S(2)}) collective-permute-start(f32[32,128]{1,0:T(8,128)S(1)} %add.1206), channel_id=1, source_target_pairs={{0,128},{16,144},{32,160},{48,176},{64,192},{80,208},{96,224},{112... | collective-permute-start | bytes 49160 | tf_op jit(solution)/shard_map/ppermute | solution.py:66
  109.8 1.7 %collective-permute-done.15 = f32[32,128]{1,0:T(8,128)S(1)} collective-permute-done((f32[32,128]{1,0:T(8,128)S(1)}, f32[32,128]{1,0:T(8,128)S(1)}, u32[]{:S(2)}, u32[]{:S(2)}) %collective-permute-start.15) | collective-permute-done | bytes 16416 | tf_op jit(solution)/shard_map/ppermute | solution.py:66
  111.5 11.3 %collective-permute-start.16 = (f32[32,128]{1,0:T(8,128)S(1)}, f32[32,128]{1,0:T(8,128)S(1)}, u32[]{:S(2)}, u32[]{:S(2)}) collective-permute-start(f32[32,128]{1,0:T(8,128)S(1)} %add.1207), channel_id=1, source_target_pairs={{0,256},{16,272},{32,288},{48,304},{64,320},{80,336},{96,352},{112... | collective-permute-start | bytes 49160 | tf_op jit(solution)/shard_map/ppermute | solution.py:66
  122.8 1.9 %collective-permute-done.16 = f32[32,128]{1,0:T(8,128)S(1)} collective-permute-done((f32[32,128]{1,0:T(8,128)S(1)}, f32[32,128]{1,0:T(8,128)S(1)}, u32[]{:S(2)}, u32[]{:S(2)}) %collective-permute-start.16) | collective-permute-done | bytes 16416 | tf_op jit(solution)/shard_map/ppermute | solution.py:66
  (76 shorter events, 7.4 us)
Async XLA Ops:
  2.0 7.6 %copy-start = (f32[8,8,128]{2,1,0:T(8,128)S(1)}, f32[8,8,128]{2,1,0:T(8,128)}, u32[]{:S(2)}) copy-start(f32[8,8,128]{2,1,0:T(8,128)} %param.7) | copy-start | bytes 98308
  3.0 6.6 %collective-permute-start.1 = (f32[208,128]{1,0:T(8,128)S(1)}, f32[208,128]{1,0:T(8,128)S(1)}, u32[]{:S(2)}, u32[]{:S(2)}) collective-permute-start(f32[208,128]{1,0:T(8,128)S(1)} %pad_maximum_fusion.3), channel_id=1, source_target_pairs={{16,0},{32,16},{48,32},{64,48},{80,64},{96,80},{112,96},{128,112},... | collective-permute-start | bytes 319496 | tf_op jit(solution)/shard_map/ppermute | solution.py:46
  4.3 5.3 %collective-permute-start = (f32[2,8,128]{2,1,0:T(8,128)S(1)}, f32[2,8,128]{2,1,0:T(8,128)S(1)}, u32[]{:S(2)}, u32[]{:S(2)}) collective-permute-start(f32[2,8,128]{2,1,0:T(8,128)S(1)} %get-tuple-element.23), channel_id=1, source_target_pairs={{0,16},{16,32},{32,48},{48,64},{64,80},{80,96},{96,112},{112,128},... | collective-permute-start | bytes 24584 | tf_op jit(solution)/shard_map/ppermute | solution.py:50
  9.7 8.3 %collective-permute-start.3 = (f32[240,128]{1,0:T(8,128)S(1)}, f32[240,128]{1,0:T(8,128)S(1)}, u32[]{:S(2)}, u32[]{:S(2)}) collective-permute-start(f32[240,128]{1,0:T(8,128)S(1)} %pad_maximum_fusion.1), channel_id=1, source_target_pairs={{1,0},{2,1},{3,2},{4,3},{5,4},{6,5},{7,6},{8,7},{9,8},{10,9},{11,1... | collective-permute-start | bytes 368648 | tf_op jit(solution)/shard_map/ppermute | solution.py:46
  15.5 10.1 %collective-permute-start.2 = (f32[12,2,128]{2,1,0:T(2,128)S(1)}, f32[12,2,128]{2,1,0:T(2,128)S(1)}, u32[]{:S(2)}, u32[]{:S(2)}) collective-permute-start(f32[12,2,128]{2,1,0:T(2,128)S(1)} %get-tuple-element.16), channel_id=1, source_target_pairs={{0,1},{1,2},{2,3},{3,4},{4,5},{5,6},{6,7},{7,8},{8,9},{9,10},{10,1... | collective-permute-start | bytes 36872 | tf_op jit(solution)/shard_map/ppermute | solution.py:50
  19.3 6.4 %copy-start.2 = (s32[8,8,128]{2,1,0:T(8,128)S(1)}, s32[8,8,128]{2,1,0:T(8,128)}, u32[]{:S(2)}) copy-start(s32[8,8,128]{2,1,0:T(8,128)} %param.8) | copy-start | bytes 98308
  25.8 19.6 %copy-start.3 = (f32[63,64]{0,1:T(8,128)S(1)}, f32[63,64]{0,1:T(8,128)}, u32[]{:S(2)}) copy-start(f32[63,64]{0,1:T(8,128)} %constant.24.clone.1) | copy-start | bytes 48388
  27.8 8.0 %collective-permute-start.5 = (f32[2,8,128]{2,1,0:T(8,128)S(1)}, f32[2,8,128]{2,1,0:T(8,128)S(1)}, u32[]{:S(2)}, u32[]{:S(2)}) collective-permute-start(f32[2,8,128]{2,1,0:T(8,128)S(1)} %get-tuple-element.22), channel_id=1, source_target_pairs={{16,0},{32,16},{48,32},{64,48},{80,64},{96,80},{112,96},{128,112},... | collective-permute-start | bytes 24584 | tf_op jit(solution)/shard_map/ppermute | solution.py:29
  29.1 7.5 %collective-permute-start.4 = (f32[2,8,128]{2,1,0:T(8,128)S(1)}, f32[2,8,128]{2,1,0:T(8,128)S(1)}, u32[]{:S(2)}, u32[]{:S(2)}) collective-permute-start(f32[2,8,128]{2,1,0:T(8,128)S(1)} %get-tuple-element.21), channel_id=1, source_target_pairs={{0,16},{16,32},{32,48},{48,64},{64,80},{80,96},{96,112},{112,128},... | collective-permute-start | bytes 24584 | tf_op jit(solution)/shard_map/ppermute | solution.py:27
  36.6 8.9 %collective-permute-start.6 = (f32[12,2,128]{2,1,0:T(2,128)S(1)}, f32[12,2,128]{2,1,0:T(2,128)S(1)}, u32[]{:S(2)}, u32[]{:S(2)}) collective-permute-start(f32[12,2,128]{2,1,0:T(2,128)S(1)} %get-tuple-element.12), channel_id=1, source_target_pairs={{0,1},{1,2},{2,3},{3,4},{4,5},{5,6},{6,7},{7,8},{8,9},{9,10},{10,1... | collective-permute-start | bytes 36872 | tf_op jit(solution)/shard_map/ppermute | solution.py:27
  38.6 8.2 %collective-permute-start.7 = (f32[12,2,128]{2,1,0:T(2,128)S(1)}, f32[12,2,128]{2,1,0:T(2,128)S(1)}, u32[]{:S(2)}, u32[]{:S(2)}) collective-permute-start(f32[12,2,128]{2,1,0:T(2,128)S(1)} %get-tuple-element.13), channel_id=1, source_target_pairs={{1,0},{2,1},{3,2},{4,3},{5,4},{6,5},{7,6},{8,7},{9,8},{10,9},{11,1... | collective-permute-start | bytes 36872 | tf_op jit(solution)/shard_map/ppermute | solution.py:29
  47.0 75.8 %copy-start.4 = (f32[64]{0:T(128)S(1)}, f32[64]{0:T(128)}, u32[]{:S(2)}) copy-start(f32[64]{0:T(128)} %param.13) | copy-start | bytes 772
  47.5 78.4 %copy-start.1 = (f32[8,8,128]{2,1,0:T(8,128)}, f32[8,8,128]{2,1,0:T(8,128)S(1)}, u32[]{:S(2)}) copy-start(f32[8,8,128]{2,1,0:T(8,128)S(1)} %get-tuple-element.7) | copy-start | bytes 98308
  48.8 5.6 %collective-permute-start.8 = (f32[32,128]{1,0:T(8,128)S(1)}, f32[32,128]{1,0:T(8,128)S(1)}, u32[]{:S(2)}, u32[]{:S(2)}) collective-permute-start(f32[32,128]{1,0:T(8,128)S(1)} %pad_bitcast_fusion), channel_id=1, source_target_pairs={{0,1},{1,0},{2,3},{3,2},{4,5},{5,4},{6,7},{7,6},{8,9},{9,8},{10,11... | collective-permute-start | bytes 49160 | tf_op jit(solution)/shard_map/ppermute | solution.py:66
  54.5 6.5 %collective-permute-start.9 = (f32[32,128]{1,0:T(8,128)S(1)}, f32[32,128]{1,0:T(8,128)S(1)}, u32[]{:S(2)}, u32[]{:S(2)}) collective-permute-start(f32[32,128]{1,0:T(8,128)S(1)} %fusion.293), channel_id=1, source_target_pairs={{0,2},{1,3},{2,0},{3,1},{4,6},{5,7},{6,4},{7,5},{8,10},{9,11},{10,... | collective-permute-start | bytes 49160 | tf_op jit(solution)/shard_map/ppermute | solution.py:66
  61.0 5.6 %collective-permute-start.10 = (f32[32,128]{1,0:T(8,128)S(1)}, f32[32,128]{1,0:T(8,128)S(1)}, u32[]{:S(2)}, u32[]{:S(2)}) collective-permute-start(f32[32,128]{1,0:T(8,128)S(1)} %fusion.297), channel_id=1, source_target_pairs={{0,4},{1,5},{2,6},{3,7},{4,0},{5,1},{6,2},{7,3},{8,12},{9,13},{10,... | collective-permute-start | bytes 49160 | tf_op jit(solution)/shard_map/ppermute | solution.py:66
  66.6 7.1 %collective-permute-start.11 = (f32[32,128]{1,0:T(8,128)S(1)}, f32[32,128]{1,0:T(8,128)S(1)}, u32[]{:S(2)}, u32[]{:S(2)}) collective-permute-start(f32[32,128]{1,0:T(8,128)S(1)} %add.1202), channel_id=1, source_target_pairs={{0,8},{1,9},{2,10},{3,11},{4,12},{5,13},{6,14},{7,15},{8,0},{9,1},... | collective-permute-start | bytes 49160 | tf_op jit(solution)/shard_map/ppermute | solution.py:66
  73.8 3.2 %collective-permute-start.12 = (f32[32,128]{1,0:T(8,128)S(1)}, f32[32,128]{1,0:T(8,128)S(1)}, u32[]{:S(2)}, u32[]{:S(2)}) collective-permute-start(f32[32,128]{1,0:T(8,128)S(1)} %add.1203), channel_id=1, source_target_pairs={{0,16},{16,0},{32,48},{48,32},{64,80},{80,64},{96,112},{112,96},{1... | collective-permute-start | bytes 49160 | tf_op jit(solution)/shard_map/ppermute | solution.py:66
  77.0 15.6 %collective-permute-start.13 = (f32[32,128]{1,0:T(8,128)S(1)}, f32[32,128]{1,0:T(8,128)S(1)}, u32[]{:S(2)}, u32[]{:S(2)}) collective-permute-start(f32[32,128]{1,0:T(8,128)S(1)} %add.1204), channel_id=1, source_target_pairs={{0,32},{16,48},{32,0},{48,16},{64,96},{80,112},{96,64},{112,80},{1... | collective-permute-start | bytes 49160 | tf_op jit(solution)/shard_map/ppermute | solution.py:66
  92.5 11.1 %collective-permute-start.14 = (f32[32,128]{1,0:T(8,128)S(1)}, f32[32,128]{1,0:T(8,128)S(1)}, u32[]{:S(2)}, u32[]{:S(2)}) collective-permute-start(f32[32,128]{1,0:T(8,128)S(1)} %add.1205), channel_id=1, source_target_pairs={{0,64},{16,80},{32,96},{48,112},{64,0},{80,16},{96,32},{112,48},{1... | collective-permute-start | bytes 49160 | tf_op jit(solution)/shard_map/ppermute | solution.py:66
  103.7 7.8 %collective-permute-start.15 = (f32[32,128]{1,0:T(8,128)S(1)}, f32[32,128]{1,0:T(8,128)S(1)}, u32[]{:S(2)}, u32[]{:S(2)}) collective-permute-start(f32[32,128]{1,0:T(8,128)S(1)} %add.1206), channel_id=1, source_target_pairs={{0,128},{16,144},{32,160},{48,176},{64,192},{80,208},{96,224},{112... | collective-permute-start | bytes 49160 | tf_op jit(solution)/shard_map/ppermute | solution.py:66
  111.5 13.1 %collective-permute-start.16 = (f32[32,128]{1,0:T(8,128)S(1)}, f32[32,128]{1,0:T(8,128)S(1)}, u32[]{:S(2)}, u32[]{:S(2)}) collective-permute-start(f32[32,128]{1,0:T(8,128)S(1)} %add.1207), channel_id=1, source_target_pairs={{0,256},{16,272},{32,288},{48,304},{64,320},{80,336},{96,352},{112... | collective-permute-start | bytes 49160 | tf_op jit(solution)/shard_map/ppermute | solution.py:66
